TPU v7x, 128 devices: a whole 4x4x4 slice. The times are simulated.
128 devices in a mesh: row: 4 (over x), col: 2 (over core), layer: 16 (over z, y).
Axes of the slice: x: 4, y: 4, z: 4, core: 2. Of those that a mesh axis runs over, the one named last changes fastest.
Arguments:
- left_blocks: bfloat16 [4, 2, 16, 48, 128, 128], P('row', 'col', 'layer'), may hold values from -0.8984375 to 0.8984375
- left_rows: int32 [4, 2, 16, 48], P('row', 'col', 'layer'), may hold values from 0 to 7
- right_blocks: bfloat16 [4, 2, 16, 48, 128, 128], P('row', 'col', 'layer'), may hold values from -0.8984375 to 0.8984375
- right_cols: int32 [4, 2, 16, 48], P('row', 'col', 'layer'), may hold values from 0 to 31
- pair_left: int32 [4, 2, 16, 4, 192], P('row', 'col', 'layer'), may hold values from 0 to 47
- pair_right: int32 [4, 2, 16, 4, 192], P('row', 'col', 'layer'), may hold values from 0 to 47
- pair_count: int32 [4, 2, 16, 4], P('row', 'col', 'layer'), may hold values from 24 to 192, as said below
Outputs:
- product: float32 [2, 4, 256, 128, 128], P('col', 'row', 'layer')
Inputs may be any that keep to these rules, and one draw needn't show every extreme that they name: `pair_count`: for each grid position and layer exactly one piece has 192 pairs and the others at most 48; over all pieces one grid position and layer has at most 336 pairs, and one reaches that number.
All inputs are finite; a program needn't handle non-finite values.
Results may differ from a plain program's by a relative error of at most 0.0003.
Values may be sent and summed in bfloat16 or wider, within the bound.
No kernel may reach another device: no remote copies, remote signals or barrier semaphores. Data moves between devices by JAX's collectives and lax.ppermute only.
A program may use at most 192 MiB of HBM per device.

v0:
```python
import jax
import jax.numpy as jnp
from jax import lax
from jax.experimental import pallas as pl
from jax.experimental.pallas import tpu as pltpu
from jax.sharding import PartitionSpec as P

SLAB = 128
ROWS_GROUP = 8


def pair_kernel(slots_left, slots_right, counts, left_ids, right_ids, right_pick,
                left_lists, right_lists, totals):
    list_count = left_lists.shape[0]
    slab_width = totals.shape[0] // ROWS_GROUP
    block_size = totals.shape[-1]

    def clear(t, carry):
        totals[t] = jnp.zeros((block_size, block_size), jnp.float32)
        return carry

    lax.fori_loop(0, totals.shape[0], clear, 0)

    for u in range(list_count):
        v = right_pick[u]

        def add_pair(j, carry, u=u, v=v):
            i = slots_left[u, j]
            k = slots_right[u, j]
            t = left_ids[u, i] * slab_width + right_ids[v, k]
            term = jnp.dot(left_lists[u, i], right_lists[v, k],
                           preferred_element_type=jnp.float32)
            totals[t] = totals[t] + term
            return carry

        lax.fori_loop(0, counts[u], add_pair, 0)


def pair_products(slots_left, slots_right, counts, left_ids, right_ids, right_pick,
                  left_lists, right_lists, targets):
    block_size = left_lists.shape[-1]
    smem = pl.BlockSpec(memory_space=pltpu.SMEM)
    vmem = pl.BlockSpec(memory_space=pltpu.VMEM)
    return pl.pallas_call(
        pair_kernel,
        out_shape=jax.ShapeDtypeStruct((targets, block_size, block_size), jnp.float32),
        in_specs=[smem] * 6 + [vmem, vmem],
        out_specs=vmem,
        compiler_params=pltpu.CompilerParams(vmem_limit_bytes=60 * 1024 * 1024),
    )(slots_left, slots_right, counts, left_ids, right_ids, right_pick, left_lists, right_lists)


def on_device(left_blocks, left_rows, right_blocks, right_cols, pair_left, pair_right, pair_count):
    block_size = left_blocks.shape[-1]
    left_cap = left_blocks.shape[3]
    right_cap = right_blocks.shape[3]
    piece_count = lax.axis_size("row")
    col_count = lax.axis_size("col")
    slab_width = SLAB // piece_count
    targets = ROWS_GROUP * slab_width
    row_here = lax.axis_index("row")
    col_here = lax.axis_index("col")
    left_lists = lax.all_gather(left_blocks.reshape(left_cap, block_size, block_size), "row")
    left_ids = lax.all_gather(left_rows.reshape(left_cap), "row")
    right_lists = lax.all_gather(right_blocks.reshape(right_cap, block_size, block_size), "col")
    right_ids = lax.all_gather(right_cols.reshape(right_cap), "col")
    owners = jnp.arange(piece_count, dtype=jnp.int32)
    piece_of = (owners + col_here) % piece_count
    right_pick = (piece_of - row_here) % col_count
    slots_left = jnp.take(pair_left.reshape(piece_count, -1), piece_of, axis=0)
    slots_right = jnp.take(pair_right.reshape(piece_count, -1), piece_of, axis=0)
    counts = jnp.take(pair_count.reshape(piece_count), piece_of, axis=0)
    totals = pair_products(slots_left, slots_right, counts, left_ids, right_ids, right_pick,
                           left_lists, right_lists, targets)
    owned = lax.psum_scatter(totals, "layer", scatter_dimension=0, tiled=True)
    return owned.reshape(1, 1, -1, block_size, block_size)


def solution(mesh):
    in_specs = (
        P("row", "col", "layer", None, None, None),
        P("row", "col", "layer", None),
        P("row", "col", "layer", None, None, None),
        P("row", "col", "layer", None),
        P("row", "col", "layer", None, None),
        P("row", "col", "layer", None, None),
        P("row", "col", "layer", None),
    )
    out_specs = P("col", "row", "layer", None, None)
    return jax.shard_map(
        on_device, mesh=mesh, in_specs=in_specs, out_specs=out_specs, check_vma=False
    )
```

profile of v0, /device:TPU:26, one launch (start us, length us, event | category | flops | bytes accessed | tf_op | source)
XLA Modules:
  0.0 266.9 jit_solution(8242207177255215017)
XLA Ops:
  6.5 0.0 copy-start
  6.5 0.0 copy-start.2
  6.5 0.0 copy-start.1
  6.5 0.0 copy-start.4
  6.5 0.0 copy-start.3
  6.5 0.0 all-gather.9.cloned.1.call-start
  6.6 0.7 all-gather.9.cloned.1.call-update
  7.3 0.0 all-gather.7.cloned.1.call-start
  7.3 0.7 all-gather.7.cloned.1.call-update
  8.0 0.0 reduce-scatter.2.cloned.1.call-start
  8.1 0.0 copy-done
  8.1 0.6 gather_fusion.2
  8.7 0.0 copy-done.2
  8.7 0.6 gather_fusion.1
  9.3 0.0 copy-done.1
  9.3 0.6 gather_fusion
  9.9 0.0 copy-done.4
  9.9 1.7 all-gather.1
  11.7 0.0 copy-done.3
  11.7 8.2 %all-gather = s32[4,1,1,48]{3,2,1,0:T(1,128)} all-gather(s32[1,1,1,48]{3,2,1,0:T(1,128)S(1)} %copy-done.3), channel_id=2, replica_groups=mesh['row'=4,'col'=2,'layer'=16] {'row'}, dimensions={0}, use_global_device_ids=true | all-gather | bytes 960 | tf_op jit(solution)/shard_map/all_gather | solution.py:64
  19.9 0.6 and_select_fusion
  20.5 0.7 broadcast_select_fusion
  21.2 4.9 %all-gather.9.cloned.1.call-done = bf16[2,1,1,48,128,128]{5,4,3,2,1,0:T(8,128)(2,1)} async-done(((bf16[1,1,1,48,128,128]{5,4,3,2,1,0:T(8,128)(2,1)}), bf16[2,1,1,48,128,128]{5,4,3,2,1,0:T(8,128)(2,1)}) %all-gather.9.cloned.1.call-update) | async-done | bytes 3145744 | tf_op jit(solution)/shard_map/all_gather | solution.py:65
  26.1 68.3 %all-gather.7.cloned.1.call-done = bf16[4,1,1,48,128,128]{5,4,3,2,1,0:T(8,128)(2,1)} async-done(((bf16[1,1,1,48,128,128]{5,4,3,2,1,0:T(8,128)(2,1)}), bf16[4,1,1,48,128,128]{5,4,3,2,1,0:T(8,128)(2,1)}) %all-gather.7.cloned.1.call-update) | async-done | bytes 6291472 | tf_op jit(solution)/shard_map/all_gather | solution.py:63
  94.4 49.0 %shard_map.73 = f32[256,128,128]{2,1,0:T(8,128)} custom-call(s32[4,192]{1,0:T(4,128)} %get-tuple-element.7.slots_left, s32[4,192]{1,0:T(4,128)} %get-tuple-element.6.slots_right, s32[4]{0:T(128)} %get-tuple-element.9.counts, s32[4,48]{1,0:T(4,128)} %bitcast.15, s32[2,48]{1,0:T(2,128)} %bitcast.16, s32[4]{0:T(128)} %get-tuple-element.8.right_pick, ...), custom_call_target="tpu_custom_call" | custom-call | tf_op jit(solution)/shard_map/pallas_call | solution.py:44
  143.4 0.0 reduce-scatter.2.cloned.1.call-update
  143.4 117.0 %reduce-scatter.2.cloned.1.call-done = f32[16,128,128]{2,1,0:T(8,128)} async-done(((f32[256,128,128]{2,1,0:T(8,128)}), f32[16,128,128]{2,1,0:T(8,128)}) %reduce-scatter.2.cloned.1.call-update) | async-done | bytes 1048592 | tf_op jit(solution)/shard_map/reduce_scatter | solution.py:75
  (5 shorter events, 0.1 us)
Async XLA Ops:
  6.5 1.6 copy-start
  6.5 2.2 copy-start.2
  6.5 2.8 %copy-start.1 = (s32[1,1,1,4]{3,2,1,0:T(1,128)S(1)}, s32[1,1,1,4]{3,2,1,0:T(1,128)}, u32[]{:S(2)}) copy-start(s32[1,1,1,4]{3,2,1,0:T(1,128)} %param.15) | copy-start | bytes 52
  6.5 3.4 %copy-start.4 = (s32[1,1,1,48]{3,2,1,0:T(1,128)S(1)}, s32[1,1,1,48]{3,2,1,0:T(1,128)}, u32[]{:S(2)}) copy-start(s32[1,1,1,48]{3,2,1,0:T(1,128)} %param.12) | copy-start | bytes 580
  6.5 5.1 %copy-start.3 = (s32[1,1,1,48]{3,2,1,0:T(1,128)S(1)}, s32[1,1,1,48]{3,2,1,0:T(1,128)}, u32[]{:S(2)}) copy-start(s32[1,1,1,48]{3,2,1,0:T(1,128)} %param.10) | copy-start | bytes 580
  6.5 19.5 %all-gather.9.cloned.1.call-start = ((), (), s32[]{:S(2)}) async-start(), calls=%async_computation.3 | async-start | bytes 4718592 | tf_op jit(solution)/shard_map/all_gather | solution.py:65
  7.3 87.1 %all-gather.7.cloned.1.call-start = ((), (), s32[]{:S(2)}) async-start(), calls=%async_computation.2 | async-start | bytes 7864320 | tf_op jit(solution)/shard_map/all_gather | solution.py:63
  8.0 252.4 %reduce-scatter.2.cloned.1.call-start = ((), (), s32[]{:S(2)}) async-start(), calls=%async_computation.1 | async-start | bytes 17825792 | tf_op jit(solution)/shard_map/reduce_scatter | solution.py:75
Sparse Core Ops, SparseCore 0:
  9.0 16.9 all-gather.8
  27.7 66.6 all-gather.6
  143.5 116.8 reduce-scatter.1
where the time goes:
time: 269 us; the launch traced here: 267 us
  waiting for transfers between devices  192 us (71%)
  Pallas kernels  49 us (18%)
  between operations  13.2 us (5%)
  blocking collectives  9.94 us (4%)
    reduce_scatter x1, waiting for transfers between devices, on_device(): owned = lax.psum_scatter(totals, 'layer', scatter_dimension=0, tiled=True)  117 us
    all_gather x1, waiting for transfers between devices, on_device(): lax.all_gather(left_blocks.reshape(left_cap, block_size, block_size), 'row')  68.3 us
    pallas_call x1, Pallas kernels, pair_products(): pl.pallas_call(pair_kernel, out_shape=jax.ShapeDtypeStruct((targets, bloc...  49 us
    all_gather x1, blocking collectives, on_device(): left_ids = lax.all_gather(left_rows.reshape(left_cap), 'row')  8.21 us
  transfers between devices with their start and end apart: 3, of which 3 were waited for; matrix products, arithmetic and copies ran while one was open for 1% of the time, Pallas kernels for 0%

commit v1 on v0

v1 whole, which is shorter than its diff:
```python
import jax
import jax.numpy as jnp
from jax import lax
from jax.experimental import pallas as pl
from jax.experimental.pallas import tpu as pltpu
from jax.sharding import PartitionSpec as P

SLAB = 128
ROWS_GROUP = 8
UNROLL = 4


def make_pair_kernel(has_start, right_pick):
    def pair_kernel(slots_left, slots_right, counts, left_ids, right_ids, *refs):
        if has_start:
            left_lists, right_lists, start, totals = refs
        else:
            left_lists, right_lists, totals = refs
        list_count = left_lists.shape[0]
        slab_width = totals.shape[0] // ROWS_GROUP
        block_size = totals.shape[-1]

        if has_start:
            totals[...] = start[...]
        else:
            def clear(t, carry):
                totals[t] = jnp.zeros((block_size, block_size), jnp.float32)
                return carry

            lax.fori_loop(0, totals.shape[0], clear, 0)

        for u in range(list_count):
            v = right_pick[u]

            def one_term(j, u=u, v=v):
                i = slots_left[u, j]
                k = slots_right[u, j]
                t = left_ids[u, i] * slab_width + right_ids[v, k]
                term = jnp.dot(left_lists[u, i], right_lists[v, k],
                               preferred_element_type=jnp.float32)
                return t, term

            def add_group(g, carry):
                made = [one_term(g * UNROLL + q) for q in range(UNROLL)]
                for t, term in made:
                    totals[t] = totals[t] + term
                return carry

            def add_single(j, carry):
                t, term = one_term(j)
                totals[t] = totals[t] + term
                return carry

            count = counts[u]
            groups = count // UNROLL
            lax.fori_loop(0, groups, add_group, 0)
            lax.fori_loop(groups * UNROLL, count, add_single, 0)

    return pair_kernel


def pair_products(slots_left, slots_right, counts, left_ids, right_ids,
                  left_lists, right_lists, right_pick, start=None, targets=None):
    block_size = left_lists.shape[-1]
    smem = pl.BlockSpec(memory_space=pltpu.SMEM)
    vmem = pl.BlockSpec(memory_space=pltpu.VMEM)
    operands = [slots_left, slots_right, counts, left_ids, right_ids, left_lists, right_lists]
    if start is not None:
        operands.append(start)
        targets = start.shape[0]
    return pl.pallas_call(
        make_pair_kernel(start is not None, right_pick),
        out_shape=jax.ShapeDtypeStruct((targets, block_size, block_size), jnp.float32),
        in_specs=[smem] * 5 + [vmem] * (len(operands) - 5),
        out_specs=vmem,
        input_output_aliases={7: 0} if start is not None else {},
        compiler_params=pltpu.CompilerParams(vmem_limit_bytes=60 * 1024 * 1024),
    )(*operands)


def shifted(value, axis, steps):
    count = lax.axis_size(axis)
    pairs = [(source, (source + steps) % count) for source in range(count)]
    return lax.ppermute(value, axis, pairs)


def on_device(left_blocks, left_rows, right_blocks, right_cols, pair_left, pair_right, pair_count):
    block_size = left_blocks.shape[-1]
    left_cap = left_blocks.shape[3]
    right_cap = right_blocks.shape[3]
    piece_count = lax.axis_size("row")
    slab_width = SLAB // piece_count
    targets = ROWS_GROUP * slab_width
    row_here = lax.axis_index("row")
    col_here = lax.axis_index("col")
    own_left = (left_blocks.reshape(left_cap, block_size, block_size), left_rows.reshape(left_cap))
    own_right = (right_blocks.reshape(right_cap, block_size, block_size), right_cols.reshape(right_cap))

    from_below = shifted(own_left, "row", 1)
    from_above = shifted(own_left, "row", -1)
    half = left_cap // 2
    far_low = shifted(jax.tree.map(lambda a: a[:half], from_below), "row", 1)
    far_high = shifted(jax.tree.map(lambda a: a[half:], from_above), "row", -1)
    far = jax.tree.map(lambda a, b: jnp.concatenate([a, b]), far_low, far_high)
    other_right = shifted(own_right, "col", 1)

    slots_left_all = pair_left.reshape(piece_count, -1)
    slots_right_all = pair_right.reshape(piece_count, -1)
    counts_all = pair_count.reshape(piece_count)

    def pieces_for(offsets):
        piece = (row_here + col_here + jnp.array(offsets, jnp.int32)) % piece_count
        return (jnp.take(slots_left_all, piece, axis=0), jnp.take(slots_right_all, piece, axis=0),
                jnp.take(counts_all, piece, axis=0))

    sl, sr, cn = pieces_for([0])
    totals = pair_products(sl, sr, cn, own_left[1][None], own_right[1][None],
                           own_left[0][None], own_right[0][None], (0,), targets=targets)
    sl, sr, cn = pieces_for([2, -1, 1])
    left_stack = jnp.stack([far[0], from_below[0], from_above[0]])
    left_id_stack = jnp.stack([far[1], from_below[1], from_above[1]])
    right_stack = jnp.stack([own_right[0], other_right[0]])
    right_id_stack = jnp.stack([own_right[1], other_right[1]])
    totals = pair_products(sl, sr, cn, left_id_stack, right_id_stack,
                           left_stack, right_stack, (0, 1, 1), start=totals)
    owned = lax.psum_scatter(totals, "layer", scatter_dimension=0, tiled=True)
    return owned.reshape(1, 1, -1, block_size, block_size)


def solution(mesh):
    in_specs = (
        P("row", "col", "layer", None, None, None),
        P("row", "col", "layer", None),
        P("row", "col", "layer", None, None, None),
        P("row", "col", "layer", None),
        P("row", "col", "layer", None, None),
        P("row", "col", "layer", None, None),
        P("row", "col", "layer", None),
    )
    out_specs = P("col", "row", "layer", None, None)
    return jax.shard_map(
        on_device, mesh=mesh, in_specs=in_specs, out_specs=out_specs, check_vma=False
    )
```

time: 269 us -> 234 us (0.87)
  waiting for transfers between devices: 192 us -> 155 us
  Pallas kernels: 49 us -> 38.4 us
  blocking collectives: 9.94 us -> 0 us
  other arithmetic: 1.33 us -> 11.2 us
  starting transfers between devices: 0.11 us -> 9.83 us
  local copies, waits for them, and re-layouts: 1.78 us -> 4.76 us
    all_gather x2 -> x0, waiting for transfers between devices: 73.2 us -> none  [the longest x1 68.3 us: on_device(): lax.all_gather(left_blocks.reshape(left_cap, block_size, block_size), 'row')]
    ppermute x0 -> x10, waiting for transfers between devices: none -> 34.8 us  [shifted(): return lax.ppermute(value, axis, pairs)]
    pallas_call x1 -> x2, Pallas kernels: 49 us -> 38.4 us  [pair_products(): pl.pallas_call(make_pair_kernel(start is not None, right_pick), out_shape...]
    all_gather x2 -> x0, blocking collectives: 9.94 us -> none  [the longest x1 8.21 us: on_device(): left_ids = lax.all_gather(left_rows.reshape(left_cap), 'row')]
    ppermute x0 -> x10, starting transfers between devices: none -> 9.82 us  [shifted(): return lax.ppermute(value, axis, pairs)]
    another operation x0 -> x6, other arithmetic: none -> 8.66 us  [the longest x2 4.06 us: on_device(): left_stack = jnp.stack([far[0], from_below[0], from_above[0]])]
    reduce_scatter x1, waiting for transfers between devices: 117 us -> 120 us  [on_device(): owned = lax.psum_scatter(totals, 'layer', scatter_dimension=0, tiled=True)]
  transfers between devices with their start and end apart: 3 -> 11, of which waited for: 3 -> 5; matrix products, arithmetic and copies ran while one was open for 1% -> 5% of each run, Pallas kernels for 0% -> 8%
where the time goes in v1:
time: 234 us; the launch traced here: 233 us
  waiting for transfers between devices  155 us (66%)
  Pallas kernels  38.4 us (16%)
  between operations  14 us (6%)
  other arithmetic  11.2 us (5%)
  starting transfers between devices  9.83 us (4%)
  local copies, waits for them, and re-layouts  4.76 us (2%)
    reduce_scatter x1, waiting for transfers between devices, on_device(): owned = lax.psum_scatter(totals, 'layer', scatter_dimension=0, tiled=True)  120 us
    pallas_call x2, Pallas kernels, pair_products(): pl.pallas_call(make_pair_kernel(start is not None, right_pick), out_shape...  38.4 us
    ppermute x10, waiting for transfers between devices, shifted(): return lax.ppermute(value, axis, pairs)  34.8 us
    ppermute x10, starting transfers between devices, shifted(): return lax.ppermute(value, axis, pairs)  9.82 us
  transfers between devices with their start and end apart: 11, of which 5 were waited for; matrix products, arithmetic and copies ran while one was open for 5% of the time, Pallas kernels for 8%

profile of v1, /device:TPU:26, one launch (start us, length us, event | category | flops | bytes accessed | tf_op | source)
XLA Modules:
  0.0 233.4 jit_solution(729791960268131451)
XLA Ops:
  6.5 0.0 copy-start
  6.5 0.0 reduce-scatter.2.cloned.1.call-start
  6.5 0.5 collective-permute-start.7
  7.1 1.5 collective-permute-start.5
  8.6 0.0 collective-permute-start.9
  8.6 0.5 collective-permute-start.4
  9.1 1.3 collective-permute-start.2
  10.3 0.7 compare_and_fusion
  11.0 0.0 copy-done
  11.0 0.6 gather_fusion
  11.7 0.6 broadcast_select_fusion.4.counts
  12.3 30.6 %collective-permute-done.7 = bf16[48,128,128]{2,1,0:T(8,128)(2,1)S(1)} collective-permute-done((bf16[48,128,128]{2,1,0:T(8,128)(2,1)}, bf16[48,128,128]{2,1,0:T(8,128)(2,1)S(1)}, u32[]{:S(2)}, u32[]{:S(2)}) %collective-permute-start.7) | collective-permute-done | bytes 1572896 | tf_op jit(solution)/shard_map/ppermute | solution.py:84
  42.9 1.0 slice.35
  43.8 0.9 collective-permute-start.8
  44.8 0.0 collective-permute-done.5
  44.8 1.1 slice.34
  45.9 1.1 collective-permute-start.6
  47.0 0.0 copy-done.4
  47.0 0.6 broadcast_select_fusion.2
  47.6 0.6 constant_dynamic-slice_fusion
  48.2 0.6 gather_fusion.2
  48.7 0.6 gather_fusion.1
  49.9 0.7 broadcast_select_fusion
  50.5 0.0 copy-start.1
  50.5 18.0 %shard_map.91.refs_2_ = f32[256,128,128]{2,1,0:T(8,128)} custom-call(s32[1,192]{1,0:T(1,128)} %get-tuple-element.34.slots_left, s32[1,192]{1,0:T(1,128)} %get-tuple-element.33.slots_right, s32[1]{0:T(128)S(6)} %select_n.56.counts, s32[1,48]{1,0:T(1,128)} %bitcast.44, s32[1,48]{1,0:T(1,128)} %bitcast.41, bf16[1,48,128,128]{3,2,1,0:T(8,128)(2,1)} %bitcast.35, ...), custom_call_target="tpu_custom_call" | custom-call | tf_op jit(solution)/shard_map/pallas_call | solution.py:71
  68.6 0.0 collective-permute-done.4
  68.6 1.9 collective-permute-start
  70.5 0.6 pad_add_fusion.1.right_ids
  71.1 0.0 collective-permute-done.2
  71.1 0.1 slice.13
  71.2 0.6 collective-permute-start.3
  71.8 0.8 collective-permute-done
  72.6 1.4 collective-permute-start.1
  74.0 0.7 collective-permute-done.3
  74.7 2.7 %collective-permute-done.1 = s32[24]{0:T(128)S(1)} collective-permute-done((s32[24]{0:T(128)S(1)}, s32[24]{0:T(128)S(1)}, u32[]{:S(2)}, u32[]{:S(2)}) %collective-permute-start.1) | collective-permute-done | bytes 128 | tf_op jit(solution)/shard_map/ppermute | solution.py:84
  77.4 0.1 add_bitcast_fusion
  77.5 0.6 pad_add_fusion.left_ids
  78.1 0.0 collective-permute-done.9
  78.1 0.0 copy-done.1
  78.1 3.3 %pad_maximum_fusion.1.refs_1_ = bf16[2,48,128,128]{3,2,1,0:T(8,128)(2,1)} fusion(bf16[1,48,128,128]{3,2,1,0:T(8,128)(2,1)} %bitcast.16, bf16[1,48,128,128]{3,2,1,0:T(8,128)(2,1)S(1)} %bitcast.30), kind=kLoop, calls=%fused_computation.4 | loop fusion | flops 1572864 | bytes 6291456 | tf_op jit(solution)/shard_map/stack | solution.py:122
  81.4 0.0 collective-permute-done.8
  81.4 0.0 collective-permute-done.6
  81.4 1.6 maximum_bitcast_fusion
  83.0 0.2 copy-done.3
  83.3 2.4 %pad_maximum_fusion.refs_0_ = bf16[3,48,128,128]{3,2,1,0:T(8,128)(2,1)} fusion(bf16[1,48,128,128]{3,2,1,0:T(8,128)(2,1)S(1)} %bitcast.31, bf16[1,48,128,128]{3,2,1,0:T(8,128)(2,1)S(1)} %bitcast.32, bf16[1,48,128,128]{3,2,1,0:T(8,128)(2,1)S(1)} %maximum_bitcast_fusion), kind=kLoop, calls=%fused_computation.3 | loop fusion | flops 4718592 | bytes 9437184 | tf_op jit(solution)/shard_map/stack | solution.py:120
  85.7 20.4 %shard_map.92 = f32[256,128,128]{2,1,0:T(8,128)} custom-call(s32[3,192]{1,0:T(4,128)} %get-tuple-element.32.slots_left, s32[3,192]{1,0:T(4,128)} %get-tuple-element.31.slots_right, s32[3]{0:T(128)} %broadcast_select_fusion.4.counts, s32[3,48]{1,0:T(4,128)} %pad_add_fusion.left_ids, s32[2,48]{1,0:T(2,128)} %pad_add_fusion.1.right_ids, ...), custom_call_target="tpu_custom_call", output_to_operand_aliasing={{}: (7, {})} | custom-call | tf_op jit(solution)/shard_map/pallas_call | solution.py:71
  106.1 0.0 reduce-scatter.2.cloned.1.call-update
  106.1 120.4 %reduce-scatter.2.cloned.1.call-done = f32[16,128,128]{2,1,0:T(8,128)} async-done(((f32[256,128,128]{2,1,0:T(8,128)}), f32[16,128,128]{2,1,0:T(8,128)}) %reduce-scatter.2.cloned.1.call-update) | async-done | bytes 1048592 | tf_op jit(solution)/shard_map/reduce_scatter | solution.py:126
  (11 shorter events, 0.0 us)
Async XLA Ops:
  6.5 4.5 %copy-start = (s32[1,1,1,4]{3,2,1,0:T(1,128)S(1)}, s32[1,1,1,4]{3,2,1,0:T(1,128)}, u32[]{:S(2)}) copy-start(s32[1,1,1,4]{3,2,1,0:T(1,128)} %param.19) | copy-start | bytes 52
  6.5 220.0 %reduce-scatter.2.cloned.1.call-start = ((), (), s32[]{:S(2)}) async-start(), calls=%async_computation.1 | async-start | bytes 17825792 | tf_op jit(solution)/shard_map/reduce_scatter | solution.py:126
  6.5 36.4 %collective-permute-start.7 = (bf16[48,128,128]{2,1,0:T(8,128)(2,1)}, bf16[48,128,128]{2,1,0:T(8,128)(2,1)S(1)}, u32[]{:S(2)}, u32[]{:S(2)}) collective-permute-start(bf16[48,128,128]{2,1,0:T(8,128)(2,1)} %bitcast.33), channel_id=1, source_target_pairs={{0,96},{32,0},{64,32},{96,64},{1,97},{33,1},{65,33},{97,65},{2,98}... | collective-permute-start | bytes 4718600 | tf_op jit(solution)/shard_map/ppermute | solution.py:84
  7.1 37.7 %collective-permute-start.5 = (bf16[48,128,128]{2,1,0:T(8,128)(2,1)}, bf16[48,128,128]{2,1,0:T(8,128)(2,1)S(1)}, u32[]{:S(2)}, u32[]{:S(2)}) collective-permute-start(bf16[48,128,128]{2,1,0:T(8,128)(2,1)} %bitcast.34), channel_id=1, source_target_pairs={{0,32},{32,64},{64,96},{96,0},{1,33},{33,65},{65,97},{97,1},{2,34}... | collective-permute-start | bytes 4718600 | tf_op jit(solution)/shard_map/ppermute | solution.py:84
  8.6 69.5 %collective-permute-start.9 = (bf16[48,128,128]{2,1,0:T(8,128)(2,1)}, bf16[48,128,128]{2,1,0:T(8,128)(2,1)}, u32[]{:S(2)}, u32[]{:S(2)}) collective-permute-start(bf16[48,128,128]{2,1,0:T(8,128)(2,1)} %bitcast.28), channel_id=1, source_target_pairs={{0,16},{16,0},{1,17},{17,1},{2,18},{18,2},{3,19},{19,3},{4,20},{20... | collective-permute-start | bytes 4718600 | tf_op jit(solution)/shard_map/ppermute | solution.py:84
  8.6 60.0 %collective-permute-start.4 = (s32[48]{0:T(128)}, s32[48]{0:T(128)S(1)}, u32[]{:S(2)}, u32[]{:S(2)}) collective-permute-start(s32[48]{0:T(128)} %bitcast.40), channel_id=1, source_target_pairs={{0,16},{16,0},{1,17},{17,1},{2,18},{18,2},{3,19},{19,3},{4,20},{20... | collective-permute-start | bytes 584 | tf_op jit(solution)/shard_map/ppermute | solution.py:84
  9.1 62.0 %collective-permute-start.2 = (s32[48]{0:T(128)}, s32[48]{0:T(128)S(1)}, u32[]{:S(2)}, u32[]{:S(2)}) collective-permute-start(s32[48]{0:T(128)} %bitcast.43), channel_id=1, source_target_pairs={{0,96},{32,0},{64,32},{96,64},{1,97},{33,1},{65,33},{97,65},{2,98}... | collective-permute-start | bytes 584 | tf_op jit(solution)/shard_map/ppermute | solution.py:84
  12.3 34.7 %copy-start.4 = (s32[1,1,1,4,192]{4,3,2,1,0:T(4,128)S(1)}, s32[1,1,1,4,192]{4,3,2,1,0:T(4,128)}, u32[]{:S(2)}) copy-start(s32[1,1,1,4,192]{4,3,2,1,0:T(4,128)} %param.18) | copy-start | bytes 9220
  12.3 34.7 %copy-start.5 = (s32[1,1,1,4,192]{4,3,2,1,0:T(4,128)S(1)}, s32[1,1,1,4,192]{4,3,2,1,0:T(4,128)}, u32[]{:S(2)}) copy-start(s32[1,1,1,4,192]{4,3,2,1,0:T(4,128)} %param.17) | copy-start | bytes 9220
  43.8 37.6 %collective-permute-start.8 = (bf16[24,128,128]{2,1,0:T(8,128)(2,1)}, bf16[24,128,128]{2,1,0:T(8,128)(2,1)}, u32[]{:S(2)}, u32[]{:S(2)}) collective-permute-start(bf16[24,128,128]{2,1,0:T(8,128)(2,1)} %slice.35), channel_id=1, source_target_pairs={{0,96},{32,0},{64,32},{96,64},{1,97},{33,1},{65,33},{97,65},{2,98}... | collective-permute-start | bytes 2359304 | tf_op jit(solution)/shard_map/ppermute | solution.py:84
  44.8 5.8 %copy-start.2 = (bf16[48,128,128]{2,1,0:T(8,128)(2,1)}, bf16[48,128,128]{2,1,0:T(8,128)(2,1)S(1)}, u32[]{:S(2)}) copy-start(bf16[48,128,128]{2,1,0:T(8,128)(2,1)S(1)} %collective-permute-done.5) | copy-start | bytes 4718596
  45.9 35.5 %collective-permute-start.6 = (bf16[24,128,128]{2,1,0:T(8,128)(2,1)}, bf16[24,128,128]{2,1,0:T(8,128)(2,1)}, u32[]{:S(2)}, u32[]{:S(2)}) collective-permute-start(bf16[24,128,128]{2,1,0:T(8,128)(2,1)} %slice.34), channel_id=1, source_target_pairs={{0,32},{32,64},{64,96},{96,0},{1,33},{33,65},{65,97},{97,1},{2,34}... | collective-permute-start | bytes 2359304 | tf_op jit(solution)/shard_map/ppermute | solution.py:84
  50.5 18.0 %copy-start.7 = (s32[1,1,1,48]{3,2,1,0:T(1,128)S(1)}, s32[1,1,1,48]{3,2,1,0:T(1,128)}, u32[]{:S(2)}) copy-start(s32[1,1,1,48]{3,2,1,0:T(1,128)} %param.14) | copy-start | bytes 580
  50.5 20.0 %copy-start.6 = (s32[1,1,1,48]{3,2,1,0:T(1,128)S(1)}, s32[1,1,1,48]{3,2,1,0:T(1,128)}, u32[]{:S(2)}) copy-start(s32[1,1,1,48]{3,2,1,0:T(1,128)} %param.16) | copy-start | bytes 580
  50.5 27.5 %copy-start.1 = (bf16[1,1,1,48,128,128]{5,4,3,2,1,0:T(8,128)(2,1)S(1)}, bf16[1,1,1,48,128,128]{5,4,3,2,1,0:T(8,128)(2,1)}, u32[]{:S(2)}) copy-start(bf16[1,1,1,48,128,128]{5,4,3,2,1,0:T(8,128)(2,1)} %param.15) | copy-start | bytes 4718596
  68.6 4.1 %collective-permute-start = (s32[48]{0:T(128)S(1)}, s32[48]{0:T(128)S(1)}, u32[]{:S(2)}, u32[]{:S(2)}) collective-permute-start(s32[48]{0:T(128)S(1)} %bitcast.45), channel_id=1, source_target_pairs={{0,32},{32,64},{64,96},{96,0},{1,33},{33,65},{65,97},{97,1},{2,34}... | collective-permute-start | bytes 584 | tf_op jit(solution)/shard_map/ppermute | solution.py:84
  71.2 3.5 %collective-permute-start.3 = (s32[24]{0:T(128)S(1)}, s32[24]{0:T(128)S(1)}, u32[]{:S(2)}, u32[]{:S(2)}) collective-permute-start(s32[24]{0:T(128)S(1)} %slice.13), channel_id=1, source_target_pairs={{0,96},{32,0},{64,32},{96,64},{1,97},{33,1},{65,33},{97,65},{2,98}... | collective-permute-start | bytes 296 | tf_op jit(solution)/shard_map/ppermute | solution.py:84
  72.6 4.7 %collective-permute-start.1 = (s32[24]{0:T(128)S(1)}, s32[24]{0:T(128)S(1)}, u32[]{:S(2)}, u32[]{:S(2)}) collective-permute-start(s32[24]{0:T(128)S(1)} %bitcast.47), channel_id=1, source_target_pairs={{0,32},{32,64},{64,96},{96,0},{1,33},{33,65},{65,97},{97,1},{2,34}... | collective-permute-start | bytes 296 | tf_op jit(solution)/shard_map/ppermute | solution.py:84
  81.4 1.9 copy-start.3
Sparse Core Ops, SparseCore 0:
  106.2 120.2 reduce-scatter.1

commit v2 on v1

--- a/solution.py
+++ b/solution.py
@@ -10,18 +10,16 @@
 UNROLL = 4
 
 
-def make_pair_kernel(has_start, right_pick):
+def make_pair_kernel(has_start, right_pick, list_count, right_count):
     def pair_kernel(slots_left, slots_right, counts, left_ids, right_ids, *refs):
-        if has_start:
-            left_lists, right_lists, start, totals = refs
-        else:
-            left_lists, right_lists, totals = refs
-        list_count = left_lists.shape[0]
+        left_lists = refs[:list_count]
+        right_lists = refs[list_count:list_count + right_count]
+        totals = refs[-1]
         slab_width = totals.shape[0] // ROWS_GROUP
         block_size = totals.shape[-1]
 
         if has_start:
-            totals[...] = start[...]
+            totals[...] = refs[-2][...]
         else:
             def clear(t, carry):
                 totals[t] = jnp.zeros((block_size, block_size), jnp.float32)
@@ -31,22 +29,23 @@
 
         for u in range(list_count):
             v = right_pick[u]
+            left_list = left_lists[u]
+            right_list = right_lists[v]
 
-            def one_term(j, u=u, v=v):
+            def one_term(j, u=u, v=v, left_list=left_list, right_list=right_list):
                 i = slots_left[u, j]
                 k = slots_right[u, j]
                 t = left_ids[u, i] * slab_width + right_ids[v, k]
-                term = jnp.dot(left_lists[u, i], right_lists[v, k],
-                               preferred_element_type=jnp.float32)
+                term = jnp.dot(left_list[i], right_list[k], preferred_element_type=jnp.float32)
                 return t, term
 
-            def add_group(g, carry):
+            def add_group(g, carry, one_term=one_term):
                 made = [one_term(g * UNROLL + q) for q in range(UNROLL)]
                 for t, term in made:
                     totals[t] = totals[t] + term
                 return carry
 
-            def add_single(j, carry):
+            def add_single(j, carry, one_term=one_term):
                 t, term = one_term(j)
                 totals[t] = totals[t] + term
                 return carry
@@ -61,19 +60,19 @@
 
 def pair_products(slots_left, slots_right, counts, left_ids, right_ids,
                   left_lists, right_lists, right_pick, start=None, targets=None):
-    block_size = left_lists.shape[-1]
+    block_size = left_lists[0].shape[-1]
     smem = pl.BlockSpec(memory_space=pltpu.SMEM)
     vmem = pl.BlockSpec(memory_space=pltpu.VMEM)
-    operands = [slots_left, slots_right, counts, left_ids, right_ids, left_lists, right_lists]
+    operands = [slots_left, slots_right, counts, left_ids, right_ids, *left_lists, *right_lists]
     if start is not None:
         operands.append(start)
         targets = start.shape[0]
     return pl.pallas_call(
-        make_pair_kernel(start is not None, right_pick),
+        make_pair_kernel(start is not None, right_pick, len(left_lists), len(right_lists)),
         out_shape=jax.ShapeDtypeStruct((targets, block_size, block_size), jnp.float32),
         in_specs=[smem] * 5 + [vmem] * (len(operands) - 5),
         out_specs=vmem,
-        input_output_aliases={7: 0} if start is not None else {},
+        input_output_aliases={len(operands) - 1: 0} if start is not None else {},
         compiler_params=pltpu.CompilerParams(vmem_limit_bytes=60 * 1024 * 1024),
     )(*operands)
 
@@ -113,16 +112,17 @@
         return (jnp.take(slots_left_all, piece, axis=0), jnp.take(slots_right_all, piece, axis=0),
                 jnp.take(counts_all, piece, axis=0))
 
+    right_lists = (own_right[0], other_right[0])
+    right_id_stack = jnp.stack([own_right[1], other_right[1]])
     sl, sr, cn = pieces_for([0])
     totals = pair_products(sl, sr, cn, own_left[1][None], own_right[1][None],
-                           own_left[0][None], own_right[0][None], (0,), targets=targets)
-    sl, sr, cn = pieces_for([2, -1, 1])
-    left_stack = jnp.stack([far[0], from_below[0], from_above[0]])
-    left_id_stack = jnp.stack([far[1], from_below[1], from_above[1]])
-    right_stack = jnp.stack([own_right[0], other_right[0]])
-    right_id_stack = jnp.stack([own_right[1], other_right[1]])
-    totals = pair_products(sl, sr, cn, left_id_stack, right_id_stack,
-                           left_stack, right_stack, (0, 1, 1), start=totals)
+                           (own_left[0],), (own_right[0],), (0,), targets=targets)
+    sl, sr, cn = pieces_for([-1, 1])
+    totals = pair_products(sl, sr, cn, jnp.stack([from_below[1], from_above[1]]), right_id_stack,
+                           (from_below[0], from_above[0]), right_lists, (1, 1), start=totals)
+    sl, sr, cn = pieces_for([2])
+    totals = pair_products(sl, sr, cn, far[1][None], right_id_stack,
+                           (far[0],), right_lists, (0,), start=totals)
     owned = lax.psum_scatter(totals, "layer", scatter_dimension=0, tiled=True)
     return owned.reshape(1, 1, -1, block_size, block_size)
 

time: 234 us -> 242 us (1.034)
  Pallas kernels: 38.4 us -> 51.2 us
  other arithmetic: 11.2 us -> 7.8 us
  starting transfers between devices: 9.83 us -> 7.21 us
    pallas_call x2 -> x3, Pallas kernels: 38.4 us -> 51.2 us  [pair_products(): pl.pallas_call(make_pair_kernel(start is not None, right_pick, len(left_l...]
    another operation x5 -> x1, other arithmetic: 8.07 us -> 0.55 us  [on_device(): jnp.stack([from_below[1], from_above[1]])]
    concatenate x0 -> x1, other arithmetic: none -> 2.68 us  [on_device(): far = jax.tree.map(lambda a, b: jnp.concatenate([a, b]), far_low, far_high)]
    ppermute x10, starting transfers between devices: 9.82 us -> 7.2 us  [shifted(): return lax.ppermute(value, axis, pairs)]
  transfers between devices with their start and end apart: 11 -> 11, of which waited for: 5 -> 5; matrix products, arithmetic and copies ran while one was open for 5% -> 4% of each run, Pallas kernels for 8% -> 15%
where the time goes in v2:
time: 242 us; the launch traced here: 240 us
  waiting for transfers between devices  153 us (63%)
  Pallas kernels  51.2 us (21%)
  between operations  14.6 us (6%)
  other arithmetic  7.8 us (3%)
  starting transfers between devices  7.21 us (3%)
  local copies, waits for them, and re-layouts  6.73 us (3%)
    reduce_scatter x1, waiting for transfers between devices, on_device(): owned = lax.psum_scatter(totals, 'layer', scatter_dimension=0, tiled=True)  120 us
    pallas_call x3, Pallas kernels, pair_products(): pl.pallas_call(make_pair_kernel(start is not None, right_pick, len(left_l...  51.2 us
    ppermute x10, waiting for transfers between devices, shifted(): return lax.ppermute(value, axis, pairs)  32.6 us
    ppermute x10, starting transfers between devices, shifted(): return lax.ppermute(value, axis, pairs)  7.2 us
  transfers between devices with their start and end apart: 11, of which 5 were waited for; matrix products, arithmetic and copies ran while one was open for 4% of the time, Pallas kernels for 15%

profile of v2, /device:TPU:26, one launch (start us, length us, event | category | flops | bytes accessed | tf_op | source)
XLA Modules:
  0.0 240.2 jit_solution(2081645264095942071)
XLA Ops:
  6.5 0.0 reduce-scatter.2.cloned.1.call-start
  6.5 1.5 collective-permute-start.5
  8.0 0.5 collective-permute-start.7
  8.6 0.0 collective-permute-start.9
  8.6 1.5 collective-permute-start
  10.1 0.5 collective-permute-start.2
  10.6 0.7 compare_and_fusion
  11.3 1.4 broadcast_select_fusion.2
  12.7 0.0 copy-start
  12.7 30.2 %collective-permute-done.5.refs_0_ = bf16[48,128,128]{2,1,0:T(8,128)(2,1)S(1)} collective-permute-done((bf16[48,128,128]{2,1,0:T(8,128)(2,1)}, bf16[48,128,128]{2,1,0:T(8,128)(2,1)S(1)}, u32[]{:S(2)}, u32[]{:S(2)}) %collective-permute-start.5) | collective-permute-done | bytes 1572896 | tf_op jit(solution)/shard_map/ppermute | solution.py:83
  42.9 1.0 slice.39
  43.9 1.5 collective-permute-start.6
  45.4 0.0 collective-permute-done.7.refs_1_
  45.4 2.1 slice.40
  47.5 0.0 copy-done.2
  47.5 0.5 collective-permute-start.8
  48.0 0.0 copy-done.3
  48.1 0.6 gather_fusion.1
  48.6 0.0 copy-done.4
  48.6 0.6 gather_fusion.2
  49.2 0.0 copy-done
  49.2 0.6 gather_fusion
  49.8 0.6 constant_dynamic-slice_fusion.4
  51.6 0.6 broadcast_select_fusion.6.counts
  52.2 0.7 broadcast_select_fusion
  52.9 17.9 %shard_map.100.refs_4_ = f32[256,128,128]{2,1,0:T(8,128)} custom-call(s32[1,192]{1,0:T(1,128)} %get-tuple-element.51.slots_left, s32[1,192]{1,0:T(1,128)} %get-tuple-element.42.slots_right, s32[1]{0:T(128)S(6)} %select_n.69.counts, s32[1,48]{1,0:T(1,128)} %bitcast.40, s32[1,48]{1,0:T(1,128)} %bitcast.35, bf16[48,128,128]{2,1,0:T(8,128)(2,1)} %bitcast.30, ...), custom_call_target="tpu_custom_call" | custom-call | tf_op jit(solution)/shard_map/pallas_call | solution.py:70
  70.8 0.0 collective-permute-done.2
  70.8 0.0 copy-done.5
  70.8 0.1 collective-permute-start.4
  70.9 0.1 slice.13
  70.9 0.0 collective-permute-done
  70.9 0.0 collective-permute-start.3
  71.0 1.0 collective-permute-done.4
  72.0 1.0 collective-permute-start.1
  73.0 0.6 pad_add_fusion.right_ids
  73.6 0.6 pad_add_fusion.1.left_ids
  74.1 0.4 collective-permute-done.3
  74.5 1.0 collective-permute-done.1
  75.5 0.7 add_bitcast_fusion.left_ids
  76.2 0.0 collective-permute-done.9.refs_3_.refs_2_
  76.2 1.2 copy-done.1
  77.3 17.6 %shard_map.101.refs_3_ = f32[256,128,128]{2,1,0:T(8,128)} custom-call(s32[2,192]{1,0:T(2,128)} %get-tuple-element.49.slots_left, s32[2,192]{1,0:T(2,128)} %get-tuple-element.48.slots_right, s32[2]{0:T(128)} %broadcast_select_fusion.6.counts, s32[2,48]{1,0:T(2,128)} %pad_add_fusion.1.left_ids, ...), custom_call_target="tpu_custom_call", output_to_operand_aliasing={{}: (9, {})} | custom-call | tf_op jit(solution)/shard_map/pallas_call | solution.py:70
  94.9 0.0 collective-permute-done.6
  94.9 0.0 collective-permute-done.8
  94.9 2.7 %pad_maximum_fusion.refs_0_ = bf16[48,128,128]{2,1,0:T(8,128)(2,1)} fusion(bf16[24,128,128]{2,1,0:T(8,128)(2,1)} %collective-permute-done.8, bf16[24,128,128]{2,1,0:T(8,128)(2,1)} %collective-permute-done.6), kind=kLoop, calls=%fused_computation.3 | loop fusion | flops 786432 | bytes 3145728 | tf_op jit(solution)/shard_map/concatenate | solution.py:103
  97.6 15.7 %shard_map.102 = f32[256,128,128]{2,1,0:T(8,128)} custom-call(s32[1,192]{1,0:T(1,128)} %get-tuple-element.50.slots_left, s32[1,192]{1,0:T(1,128)} %get-tuple-element.43.slots_right, s32[1]{0:T(128)S(6)} %select_n.63.counts, s32[1,48]{1,0:T(1,128)} %add_bitcast_fusion.left_ids, s32[2,48]{1,0:T(2,128)} %pad_add_fusion.right_ids, ...), custom_call_target="tpu_custom_call", output_to_operand_aliasing={{}: (8, {})} | custom-call | tf_op jit(solution)/shard_map/pallas_call | solution.py:70
  113.3 0.0 reduce-scatter.2.cloned.1.call-update
  113.4 120.0 %reduce-scatter.2.cloned.1.call-done = f32[16,128,128]{2,1,0:T(8,128)} async-done(((f32[256,128,128]{2,1,0:T(8,128)}), f32[16,128,128]{2,1,0:T(8,128)}) %reduce-scatter.2.cloned.1.call-update) | async-done | bytes 1048592 | tf_op jit(solution)/shard_map/reduce_scatter | solution.py:126
  (6 shorter events, 0.0 us)
Async XLA Ops:
  6.5 226.8 %reduce-scatter.2.cloned.1.call-start = ((), (), s32[]{:S(2)}) async-start(), calls=%async_computation.1 | async-start | bytes 17825792 | tf_op jit(solution)/shard_map/reduce_scatter | solution.py:126
  6.5 36.4 %collective-permute-start.5 = (bf16[48,128,128]{2,1,0:T(8,128)(2,1)}, bf16[48,128,128]{2,1,0:T(8,128)(2,1)S(1)}, u32[]{:S(2)}, u32[]{:S(2)}) collective-permute-start(bf16[48,128,128]{2,1,0:T(8,128)(2,1)} %bitcast.28), channel_id=1, source_target_pairs={{0,32},{32,64},{64,96},{96,0},{1,33},{33,65},{65,97},{97,1},{2,34}... | collective-permute-start | bytes 4718600 | tf_op jit(solution)/shard_map/ppermute | solution.py:83
  8.0 37.4 %collective-permute-start.7 = (bf16[48,128,128]{2,1,0:T(8,128)(2,1)}, bf16[48,128,128]{2,1,0:T(8,128)(2,1)}, u32[]{:S(2)}, u32[]{:S(2)}) collective-permute-start(bf16[48,128,128]{2,1,0:T(8,128)(2,1)} %bitcast.29), channel_id=1, source_target_pairs={{0,96},{32,0},{64,32},{96,64},{1,97},{33,1},{65,33},{97,65},{2,98}... | collective-permute-start | bytes 4718600 | tf_op jit(solution)/shard_map/ppermute | solution.py:83
  8.6 67.6 %collective-permute-start.9 = (bf16[48,128,128]{2,1,0:T(8,128)(2,1)}, bf16[48,128,128]{2,1,0:T(8,128)(2,1)S(1)}, u32[]{:S(2)}, u32[]{:S(2)}) collective-permute-start(bf16[48,128,128]{2,1,0:T(8,128)(2,1)} %bitcast.24), channel_id=1, source_target_pairs={{0,16},{16,0},{1,17},{17,1},{2,18},{18,2},{3,19},{19,3},{4,20},{20... | collective-permute-start | bytes 4718600 | tf_op jit(solution)/shard_map/ppermute | solution.py:83
  8.6 62.4 %collective-permute-start = (s32[48]{0:T(128)}, s32[48]{0:T(128)S(1)}, u32[]{:S(2)}, u32[]{:S(2)}) collective-permute-start(s32[48]{0:T(128)} %bitcast.38), channel_id=1, source_target_pairs={{0,32},{32,64},{64,96},{96,0},{1,33},{33,65},{65,97},{97,1},{2,34}... | collective-permute-start | bytes 584 | tf_op jit(solution)/shard_map/ppermute | solution.py:83
  10.1 60.7 %collective-permute-start.2 = (s32[48]{0:T(128)}, s32[48]{0:T(128)S(1)}, u32[]{:S(2)}, u32[]{:S(2)}) collective-permute-start(s32[48]{0:T(128)} %bitcast.39), channel_id=1, source_target_pairs={{0,96},{32,0},{64,32},{96,64},{1,97},{33,1},{65,33},{97,65},{2,98}... | collective-permute-start | bytes 584 | tf_op jit(solution)/shard_map/ppermute | solution.py:83
  12.7 35.4 %copy-start.3 = (s32[1,1,1,4,192]{4,3,2,1,0:T(4,128)S(1)}, s32[1,1,1,4,192]{4,3,2,1,0:T(4,128)}, u32[]{:S(2)}) copy-start(s32[1,1,1,4,192]{4,3,2,1,0:T(4,128)} %param.18) | copy-start | bytes 9220
  12.7 36.0 %copy-start.4 = (s32[1,1,1,4,192]{4,3,2,1,0:T(4,128)S(1)}, s32[1,1,1,4,192]{4,3,2,1,0:T(4,128)}, u32[]{:S(2)}) copy-start(s32[1,1,1,4,192]{4,3,2,1,0:T(4,128)} %param.19) | copy-start | bytes 9220
  12.7 36.5 %copy-start = (s32[1,1,1,4]{3,2,1,0:T(1,128)S(1)}, s32[1,1,1,4]{3,2,1,0:T(1,128)}, u32[]{:S(2)}) copy-start(s32[1,1,1,4]{3,2,1,0:T(1,128)} %param.20) | copy-start | bytes 52
  42.9 4.6 %copy-start.2 = (bf16[48,128,128]{2,1,0:T(8,128)(2,1)}, bf16[48,128,128]{2,1,0:T(8,128)(2,1)S(1)}, u32[]{:S(2)}) copy-start(bf16[48,128,128]{2,1,0:T(8,128)(2,1)S(1)} %collective-permute-done.5.refs_0_) | copy-start | bytes 4718596
  43.9 51.0 %collective-permute-start.6 = (bf16[24,128,128]{2,1,0:T(8,128)(2,1)}, bf16[24,128,128]{2,1,0:T(8,128)(2,1)}, u32[]{:S(2)}, u32[]{:S(2)}) collective-permute-start(bf16[24,128,128]{2,1,0:T(8,128)(2,1)} %slice.39), channel_id=1, source_target_pairs={{0,32},{32,64},{64,96},{96,0},{1,33},{33,65},{65,97},{97,1},{2,34}... | collective-permute-start | bytes 2359304 | tf_op jit(solution)/shard_map/ppermute | solution.py:83
  47.5 47.4 %collective-permute-start.8 = (bf16[24,128,128]{2,1,0:T(8,128)(2,1)}, bf16[24,128,128]{2,1,0:T(8,128)(2,1)}, u32[]{:S(2)}, u32[]{:S(2)}) collective-permute-start(bf16[24,128,128]{2,1,0:T(8,128)(2,1)} %slice.40), channel_id=1, source_target_pairs={{0,96},{32,0},{64,32},{96,64},{1,97},{33,1},{65,33},{97,65},{2,98}... | collective-permute-start | bytes 2359304 | tf_op jit(solution)/shard_map/ppermute | solution.py:83
  52.9 17.9 %copy-start.5 = (s32[1,1,1,48]{3,2,1,0:T(1,128)S(1)}, s32[1,1,1,48]{3,2,1,0:T(1,128)}, u32[]{:S(2)}) copy-start(s32[1,1,1,48]{3,2,1,0:T(1,128)} %param.17) | copy-start | bytes 580
  70.8 1.2 collective-permute-start.4
  70.9 3.6 %collective-permute-start.3 = (s32[24]{0:T(128)S(1)}, s32[24]{0:T(128)S(1)}, u32[]{:S(2)}, u32[]{:S(2)}) collective-permute-start(s32[24]{0:T(128)S(1)} %slice.13), channel_id=1, source_target_pairs={{0,96},{32,0},{64,32},{96,64},{1,97},{33,1},{65,33},{97,65},{2,98}... | collective-permute-start | bytes 296 | tf_op jit(solution)/shard_map/ppermute | solution.py:83
  72.0 3.5 %collective-permute-start.1 = (s32[24]{0:T(128)S(1)}, s32[24]{0:T(128)S(1)}, u32[]{:S(2)}, u32[]{:S(2)}) collective-permute-start(s32[24]{0:T(128)S(1)} %bitcast.41), channel_id=1, source_target_pairs={{0,32},{32,64},{64,96},{96,0},{1,33},{33,65},{65,97},{97,1},{2,34}... | collective-permute-start | bytes 296 | tf_op jit(solution)/shard_map/ppermute | solution.py:83
  76.2 1.2 copy-start.1
Sparse Core Ops, SparseCore 0:
  113.5 119.8 reduce-scatter.1

commit v3 on v2

--- a/solution.py
+++ b/solution.py
@@ -8,6 +8,17 @@
 SLAB = 128
 ROWS_GROUP = 8
 UNROLL = 4
+
+
+def placed(t):
+    owner = t // 16
+    block = t % 16
+    quarter = block // 4
+    z_o = owner // 4
+    y_o = owner % 4
+    first = jnp.where(quarter < 2, y_o, z_o)
+    second = jnp.where(quarter < 2, z_o, y_o)
+    return quarter * 64 + first * 16 + second * 4 + block % 4
 
 
 def make_pair_kernel(has_start, right_pick, list_count, right_count):
@@ -35,7 +46,7 @@
             def one_term(j, u=u, v=v, left_list=left_list, right_list=right_list):
                 i = slots_left[u, j]
                 k = slots_right[u, j]
-                t = left_ids[u, i] * slab_width + right_ids[v, k]
+                t = placed(left_ids[u, i] * slab_width + right_ids[v, k])
                 term = jnp.dot(left_list[i], right_list[k], preferred_element_type=jnp.float32)
                 return t, term
 
@@ -83,6 +94,40 @@
     return lax.ppermute(value, axis, pairs)
 
 
+def ring_pairs(step_y, step_z):
+    return [(z * 4 + y, ((z + step_z) % 4) * 4 + (y + step_y) % 4) for z in range(4) for y in range(4)]
+
+
+def ring_pass(chunks, here, pairs, sign):
+    count = chunks.shape[0]
+    acc = lax.dynamic_index_in_dim(chunks, (here - sign) % count, 0, keepdims=False)
+    for step in range(count - 1):
+        acc = lax.ppermute(acc, "layer", pairs)
+        acc = acc + lax.dynamic_index_in_dim(chunks, (here - sign * (step + 2)) % count, 0,
+                                             keepdims=False)
+    return acc
+
+
+def ring_reduce_scatter(totals):
+    block_size = totals.shape[-1]
+    layer_here = lax.axis_index("layer")
+    y_here = layer_here % 4
+    z_here = layer_here // 4
+    routes = [
+        ((y_here, ring_pairs(1, 0), 1), (z_here, ring_pairs(0, 1), 1)),
+        ((y_here, ring_pairs(-1, 0), -1), (z_here, ring_pairs(0, -1), -1)),
+        ((z_here, ring_pairs(0, 1), 1), (y_here, ring_pairs(1, 0), 1)),
+        ((z_here, ring_pairs(0, -1), -1), (y_here, ring_pairs(-1, 0), -1)),
+    ]
+    quarters = totals.reshape(4, 4, 16, block_size, block_size)
+    results = []
+    for quarter, (first, second) in enumerate(routes):
+        part = ring_pass(quarters[quarter], *first)
+        part = ring_pass(part.reshape(4, 4, block_size, block_size), *second)
+        results.append(part)
+    return jnp.concatenate(results)
+
+
 def on_device(left_blocks, left_rows, right_blocks, right_cols, pair_left, pair_right, pair_count):
     block_size = left_blocks.shape[-1]
     left_cap = left_blocks.shape[3]
@@ -117,13 +162,12 @@
     sl, sr, cn = pieces_for([0])
     totals = pair_products(sl, sr, cn, own_left[1][None], own_right[1][None],
                            (own_left[0],), (own_right[0],), (0,), targets=targets)
-    sl, sr, cn = pieces_for([-1, 1])
-    totals = pair_products(sl, sr, cn, jnp.stack([from_below[1], from_above[1]]), right_id_stack,
-                           (from_below[0], from_above[0]), right_lists, (1, 1), start=totals)
-    sl, sr, cn = pieces_for([2])
-    totals = pair_products(sl, sr, cn, far[1][None], right_id_stack,
-                           (far[0],), right_lists, (0,), start=totals)
-    owned = lax.psum_scatter(totals, "layer", scatter_dimension=0, tiled=True)
+    sl, sr, cn = pieces_for([-1, 1, 2])
+    left_id_stack = jnp.stack([from_below[1], from_above[1], far[1]])
+    totals = pair_products(sl, sr, cn, left_id_stack, right_id_stack,
+                           (from_below[0], from_above[0], far[0]), right_lists, (1, 1, 0),
+                           start=totals)
+    owned = ring_reduce_scatter(totals)
     return owned.reshape(1, 1, -1, block_size, block_size)
 
 

time: 242 us -> 238 us (0.983)
  waiting for transfers between devices: 153 us -> 81 us
  starting transfers between devices: 7.21 us -> 59.8 us
  other arithmetic: 7.8 us -> 32.5 us
  local copies, waits for them, and re-layouts: 6.73 us -> 23.9 us
  between operations: 14.6 us -> 0.94 us
  Pallas kernels: 51.2 us -> 38.4 us
    reduce_scatter x1 -> x0, waiting for transfers between devices: 120 us -> none  [on_device(): owned = lax.psum_scatter(totals, 'layer', scatter_dimension=0, tiled=True)]
    ppermute x0 -> x24, starting transfers between devices: none -> 50.5 us  [ring_pass(): acc = lax.ppermute(acc, 'layer', pairs)]
    ppermute x0 -> x24, waiting for transfers between devices: none -> 50.2 us  [ring_pass(): acc = lax.ppermute(acc, 'layer', pairs)]
    add x0 -> x24, other arithmetic: none -> 24.3 us  [ring_pass(): acc + lax.dynamic_index_in_dim(chunks, (here - sign * (step + 2)) % count...]
    pallas_call x3 -> x2, Pallas kernels: 51.2 us -> 38.4 us  [pair_products(): pl.pallas_call(make_pair_kernel(start is not None, right_pick, len(left_l...]
    slice x0 -> x1, local copies, waits for them, and re-layouts: none -> 11 us  [ring_reduce_scatter(): part = ring_pass(quarters[quarter], *first)]
    squeeze x0 -> x8, local copies, waits for them, and re-layouts: none -> 5.06 us  [ring_pass(): lax.dynamic_index_in_dim(chunks, (here - sign) % count, 0, keepdims=False)]
  transfers between devices with their start and end apart: 11 -> 34, of which waited for: 5 -> 14; matrix products, arithmetic and copies ran while one was open for 4% -> 18% of each run, Pallas kernels for 15% -> 5%
where the time goes in v3:
time: 238 us; the launch traced here: 236 us
  waiting for transfers between devices  81 us (34%)
  starting transfers between devices  59.8 us (25%)
  Pallas kernels  38.4 us (16%)
  other arithmetic  32.5 us (14%)
  local copies, waits for them, and re-layouts  23.9 us (10%)
    ppermute x24, starting transfers between devices, ring_pass(): acc = lax.ppermute(acc, 'layer', pairs)  50.5 us
    ppermute x24, waiting for transfers between devices, ring_pass(): acc = lax.ppermute(acc, 'layer', pairs)  50.2 us
    pallas_call x2, Pallas kernels, pair_products(): pl.pallas_call(make_pair_kernel(start is not None, right_pick, len(left_l...  38.4 us
    ppermute x10, waiting for transfers between devices, shifted(): return lax.ppermute(value, axis, pairs)  30.8 us
    add x24, other arithmetic, ring_pass(): acc + lax.dynamic_index_in_dim(chunks, (here - sign * (step + 2)) % count...  24.3 us
    slice x1, local copies, waits for them, and re-layouts, ring_reduce_scatter(): part = ring_pass(quarters[quarter], *first)  11 us
    ppermute x10, starting transfers between devices, shifted(): return lax.ppermute(value, axis, pairs)  9.32 us
    squeeze x8, local copies, waits for them, and re-layouts, ring_pass(): lax.dynamic_index_in_dim(chunks, (here - sign) % count, 0, keepdims=False)  5.06 us
  transfers between devices with their start and end apart: 34, of which 14 were waited for; matrix products, arithmetic and copies ran while one was open for 18% of the time, Pallas kernels for 5%

profile of v3, /device:TPU:26, one launch (start us, length us, event | category | flops | bytes accessed | tf_op | source)
XLA Modules:
  0.0 236.4 jit_solution(949689679741977605)
XLA Ops:
  0.0 1.5 collective-permute-start.5
  2.0 1.7 collective-permute-start.1
  7.3 1.3 broadcast_select_fusion.2
  8.6 27.8 %collective-permute-done.5.refs_0_ = bf16[48,128,128]{2,1,0:T(8,128)(2,1)S(1)} collective-permute-done((bf16[48,128,128]{2,1,0:T(8,128)(2,1)}, bf16[48,128,128]{2,1,0:T(8,128)(2,1)S(1)}, u32[]{:S(2)}, u32[]{:S(2)}) %collective-permute-start.5) | collective-permute-done | bytes 1572896 | tf_op jit(solution)/shard_map/ppermute | solution.py:94
  37.4 1.5 collective-permute-start.7
  43.5 10.9 %shard_map.91.refs_5_ = f32[256,128,128]{2,1,0:T(8,128)} custom-call(s32[1,192]{1,0:T(1,128)} %get-tuple-element.38.slots_left, s32[1,192]{1,0:T(1,128)} %get-tuple-element.37.slots_right, s32[1]{0:T(128)S(6)} %select_n.228.counts, s32[1,48]{1,0:T(1,128)} %bitcast.141, s32[1,48]{1,0:T(1,128)} %bitcast.136, bf16[48,128,128]{2,1,0:T(8,128)(2,1)} %bitcast.131, ...), custom_call_target="tpu_custom_call" | custom-call | tf_op jit(solution)/shard_map/pallas_call | solution.py:81
  54.6 3.2 %collective-permute-start.3 = (s32[24]{0:T(128)S(1)}, s32[24]{0:T(128)S(1)}, u32[]{:S(2)}, u32[]{:S(2)}) collective-permute-start(s32[24]{0:T(128)S(1)} %slice.29), channel_id=1, source_target_pairs={{0,96},{32,0},{64,32},{96,64},{1,97},{33,1},{65,33},{97,65},{2,98}... | collective-permute-start | bytes 296 | tf_op jit(solution)/shard_map/ppermute | solution.py:94
  59.1 2.2 collective-permute-done.2
  62.0 2.7 %pad_maximum_fusion.refs_2_ = bf16[48,128,128]{2,1,0:T(8,128)(2,1)} fusion(bf16[24,128,128]{2,1,0:T(8,128)(2,1)} %collective-permute-done.8, bf16[24,128,128]{2,1,0:T(8,128)(2,1)} %collective-permute-done.7), kind=kLoop, calls=%fused_computation.3 | loop fusion | flops 786432 | bytes 3145728 | tf_op jit(solution)/shard_map/concatenate | solution.py:148
  64.7 27.4 %shard_map.92 = f32[256,128,128]{2,1,0:T(8,128)} custom-call(s32[3,192]{1,0:T(4,128)} %get-tuple-element.36.slots_left, s32[3,192]{1,0:T(4,128)} %get-tuple-element.35.slots_right, s32[3]{0:T(128)} %broadcast_select_fusion.4.counts, s32[3,48]{1,0:T(4,128)} %pad_add_fusion.left_ids, ...), custom_call_target="tpu_custom_call", output_to_operand_aliasing={{}: (10, {})} | custom-call | tf_op jit(solution)/shard_map/pallas_call | solution.py:81
  92.1 11.0 %fusion.1 = (f32[64,128,128]{2,1,0:T(8,128)S(1)}, f32[64,128,128]{2,1,0:T(8,128)}, f32[64,128,128]{2,1,0:T(8,128)}, f32[64,128,128]{2,1,0:T(8,128)}) fusion(f32[256,128,128]{2,1,0:T(8,128)} %shard_map.92), kind=kLoop, calls=%fused_computation.55 | loop fusion | bytes 33554432 | tf_op jit(solution)/shard_map/slice | solution.py:125
  103.1 2.0 copy-done.2
  105.2 5.4 %collective-permute-start.10 = (f32[16,128,128]{2,1,0:T(8,128)S(1)}, f32[16,128,128]{2,1,0:T(8,128)}, u32[]{:S(2)}, u32[]{:S(2)}) collective-permute-start(f32[16,128,128]{2,1,0:T(8,128)S(1)} %dynamic-slice_bitcast_fusion.3), channel_id=1, source_target_pairs={{0,1},{1,2},{2,3},{3,0},{4,5},{5,6},{6,7},{7,4},{8,9},{9,10},{10,1... | collective-permute-start | bytes 3145736 | tf_op jit(solution)/shard_map/ppermute | solution.py:105
  110.6 1.3 dynamic-slice_bitcast_fusion.2
  112.9 1.3 dynamic-slice_bitcast_fusion.1
  114.2 2.2 collective-permute-start.22
  116.4 2.3 dynamic-slice_bitcast_fusion
  118.6 3.2 %collective-permute-start.28 = (f32[16,128,128]{2,1,0:T(8,128)}, f32[16,128,128]{2,1,0:T(8,128)}, u32[]{:S(2)}, u32[]{:S(2)}) collective-permute-start(f32[16,128,128]{2,1,0:T(8,128)} %dynamic-slice_bitcast_fusion), channel_id=1, source_target_pairs={{0,12},{1,13},{2,14},{3,15},{4,0},{5,1},{6,2},{7,3},{8,4},{9,5},{1... | collective-permute-start | bytes 3145736 | tf_op jit(solution)/shard_map/ppermute | solution.py:105
  121.9 11.4 %collective-permute-done.10 = f32[16,128,128]{2,1,0:T(8,128)} collective-permute-done((f32[16,128,128]{2,1,0:T(8,128)S(1)}, f32[16,128,128]{2,1,0:T(8,128)}, u32[]{:S(2)}, u32[]{:S(2)}) %collective-permute-start.10) | collective-permute-done | bytes 1048608 | tf_op jit(solution)/shard_map/ppermute | solution.py:105
  133.3 2.7 %bitcast_add_fusion.11 = f32[16,128,128]{2,1,0:T(8,128)} fusion(f32[16,128,128]{2,1,0:T(8,128)} %collective-permute-done.10, f32[4,16,128,128]{3,2,1,0:T(8,128)} %bitcast.107, s32[]{:T(128)S(6)} %select_n.233), kind=kLoop, calls=%fused_computation.16 | loop fusion | flops 262144 | bytes 3145732 | tf_op jit(solution)/shard_map/add | solution.py:106
  136.0 3.8 %collective-permute-start.11 = (f32[16,128,128]{2,1,0:T(8,128)}, f32[16,128,128]{2,1,0:T(8,128)}, u32[]{:S(2)}, u32[]{:S(2)}) collective-permute-start(f32[16,128,128]{2,1,0:T(8,128)} %bitcast_add_fusion.11), channel_id=1, source_target_pairs={{0,1},{1,2},{2,3},{3,0},{4,5},{5,6},{6,7},{7,4},{8,9},{9,10},{10,1... | collective-permute-start | bytes 3145736 | tf_op jit(solution)/shard_map/ppermute | solution.py:105
  139.8 2.7 %bitcast_add_fusion.8 = f32[16,128,128]{2,1,0:T(8,128)} fusion(f32[16,128,128]{2,1,0:T(8,128)} %collective-permute-done.16, f32[4,16,128,128]{3,2,1,0:T(8,128)} %bitcast.103, s32[]{:T(128)S(6)} %select_n.250), kind=kLoop, calls=%fused_computation.13 | loop fusion | flops 262144 | bytes 3145732 | tf_op jit(solution)/shard_map/add | solution.py:106
  143.2 1.7 bitcast_add_fusion.5
  145.8 2.6 %bitcast_add_fusion.2 = f32[16,128,128]{2,1,0:T(8,128)} fusion(f32[16,128,128]{2,1,0:T(8,128)} %collective-permute-done.28, f32[4,16,128,128]{3,2,1,0:T(8,128)} %bitcast.95, s32[]{:T(128)S(6)} %select_n.258), kind=kLoop, calls=%fused_computation.7 | loop fusion | flops 262144 | bytes 3145732 | tf_op jit(solution)/shard_map/add | solution.py:106
  148.4 4.0 %collective-permute-start.29 = (f32[16,128,128]{2,1,0:T(8,128)}, f32[16,128,128]{2,1,0:T(8,128)}, u32[]{:S(2)}, u32[]{:S(2)}) collective-permute-start(f32[16,128,128]{2,1,0:T(8,128)} %bitcast_add_fusion.2), channel_id=1, source_target_pairs={{0,12},{1,13},{2,14},{3,15},{4,0},{5,1},{6,2},{7,3},{8,4},{9,5},{1... | collective-permute-start | bytes 3145736 | tf_op jit(solution)/shard_map/ppermute | solution.py:105
  152.5 9.5 %collective-permute-done.11 = f32[16,128,128]{2,1,0:T(8,128)} collective-permute-done((f32[16,128,128]{2,1,0:T(8,128)}, f32[16,128,128]{2,1,0:T(8,128)}, u32[]{:S(2)}, u32[]{:S(2)}) %collective-permute-start.11) | collective-permute-done | bytes 1048608 | tf_op jit(solution)/shard_map/ppermute | solution.py:105
  162.0 2.7 %bitcast_add_fusion.10 = f32[16,128,128]{2,1,0:T(8,128)} fusion(f32[16,128,128]{2,1,0:T(8,128)} %collective-permute-done.11, f32[4,16,128,128]{3,2,1,0:T(8,128)} %bitcast.108, s32[]{:T(128)S(6)} %select_n.235), kind=kLoop, calls=%fused_computation.15 | loop fusion | flops 262144 | bytes 3145732 | tf_op jit(solution)/shard_map/add | solution.py:106
  164.6 3.7 %collective-permute-start.12 = (f32[16,128,128]{2,1,0:T(8,128)}, f32[16,128,128]{2,1,0:T(8,128)S(1)}, u32[]{:S(2)}, u32[]{:S(2)}) collective-permute-start(f32[16,128,128]{2,1,0:T(8,128)} %bitcast_add_fusion.10), channel_id=1, source_target_pairs={{0,1},{1,2},{2,3},{3,0},{4,5},{5,6},{6,7},{7,4},{8,9},{9,10},{10,1... | collective-permute-start | bytes 3145736 | tf_op jit(solution)/shard_map/ppermute | solution.py:105
  168.3 2.7 %bitcast_add_fusion.7 = f32[16,128,128]{2,1,0:T(8,128)} fusion(f32[16,128,128]{2,1,0:T(8,128)} %collective-permute-done.17, f32[4,16,128,128]{3,2,1,0:T(8,128)} %bitcast.104, s32[]{:T(128)S(6)} %select_n.252), kind=kLoop, calls=%fused_computation.12 | loop fusion | flops 262144 | bytes 3145732 | tf_op jit(solution)/shard_map/add | solution.py:106
  171.0 1.6 collective-permute-done.23
  172.6 1.4 bitcast_add_fusion.4
  174.8 1.7 bitcast_add_fusion.1
  176.5 3.8 %collective-permute-start.30 = (f32[16,128,128]{2,1,0:T(8,128)S(1)}, f32[16,128,128]{2,1,0:T(8,128)S(1)}, u32[]{:S(2)}, u32[]{:S(2)}) collective-permute-start(f32[16,128,128]{2,1,0:T(8,128)S(1)} %bitcast_add_fusion.1), channel_id=1, source_target_pairs={{0,12},{1,13},{2,14},{3,15},{4,0},{5,1},{6,2},{7,3},{8,4},{9,5},{1... | collective-permute-start | bytes 3145736 | tf_op jit(solution)/shard_map/ppermute | solution.py:105
  180.2 9.4 %collective-permute-done.12 = f32[16,128,128]{2,1,0:T(8,128)S(1)} collective-permute-done((f32[16,128,128]{2,1,0:T(8,128)}, f32[16,128,128]{2,1,0:T(8,128)S(1)}, u32[]{:S(2)}, u32[]{:S(2)}) %collective-permute-start.12) | collective-permute-done | bytes 1048608 | tf_op jit(solution)/shard_map/ppermute | solution.py:105
  189.7 1.4 bitcast_add_fusion.9
  191.8 3.9 %collective-permute-done.18 = f32[16,128,128]{2,1,0:T(8,128)} collective-permute-done((f32[16,128,128]{2,1,0:T(8,128)}, f32[16,128,128]{2,1,0:T(8,128)}, u32[]{:S(2)}, u32[]{:S(2)}) %collective-permute-start.18) | collective-permute-done | bytes 1048608 | tf_op jit(solution)/shard_map/ppermute | solution.py:105
  195.7 1.7 bitcast_add_fusion.6
  197.4 6.3 %collective-permute-start.19 = (f32[4,128,128]{2,1,0:T(8,128)S(1)}, f32[4,128,128]{2,1,0:T(8,128)S(1)}, u32[]{:S(2)}, u32[]{:S(2)}) collective-permute-start(f32[4,128,128]{2,1,0:T(8,128)S(1)} %dynamic-slice_bitcast_fusion.6), channel_id=1, source_target_pairs={{0,12},{1,13},{2,14},{3,15},{4,0},{5,1},{6,2},{7,3},{8,4},{9,5},{1... | collective-permute-start | bytes 786440 | tf_op jit(solution)/shard_map/ppermute | solution.py:105
  203.7 1.4 bitcast_add_fusion.3
  205.2 1.8 collective-permute-start.25
  207.0 1.4 bitcast_add_fusion
  209.0 3.3 %collective-permute-start.20 = (f32[4,128,128]{2,1,0:T(8,128)S(1)}, f32[4,128,128]{2,1,0:T(8,128)S(1)}, u32[]{:S(2)}, u32[]{:S(2)}) collective-permute-start(f32[4,128,128]{2,1,0:T(8,128)S(1)} %bitcast_add_fusion.20), channel_id=1, source_target_pairs={{0,12},{1,13},{2,14},{3,15},{4,0},{5,1},{6,2},{7,3},{8,4},{9,5},{1... | collective-permute-start | bytes 786440 | tf_op jit(solution)/shard_map/ppermute | solution.py:105
  212.3 3.0 %collective-permute-start.26 = (f32[4,128,128]{2,1,0:T(8,128)S(1)}, f32[4,128,128]{2,1,0:T(8,128)S(1)}, u32[]{:S(2)}, u32[]{:S(2)}) collective-permute-start(f32[4,128,128]{2,1,0:T(8,128)S(1)} %bitcast_add_fusion.17), channel_id=1, source_target_pairs={{0,1},{1,2},{2,3},{3,0},{4,5},{5,6},{6,7},{7,4},{8,9},{9,10},{10,1... | collective-permute-start | bytes 786440 | tf_op jit(solution)/shard_map/ppermute | solution.py:105
  215.3 2.1 collective-permute-done.31
  217.7 3.3 %collective-permute-start.21 = (f32[4,128,128]{2,1,0:T(8,128)S(1)}, f32[4,128,128]{2,1,0:T(8,128)S(1)}, u32[]{:S(2)}, u32[]{:S(2)}) collective-permute-start(f32[4,128,128]{2,1,0:T(8,128)S(1)} %bitcast_add_fusion.19), channel_id=1, source_target_pairs={{0,12},{1,13},{2,14},{3,15},{4,0},{5,1},{6,2},{7,3},{8,4},{9,5},{1... | collective-permute-start | bytes 786440 | tf_op jit(solution)/shard_map/ppermute | solution.py:105
  221.1 3.3 %collective-permute-start.27 = (f32[4,128,128]{2,1,0:T(8,128)S(1)}, f32[4,128,128]{2,1,0:T(8,128)S(1)}, u32[]{:S(2)}, u32[]{:S(2)}) collective-permute-start(f32[4,128,128]{2,1,0:T(8,128)S(1)} %bitcast_add_fusion.16), channel_id=1, source_target_pairs={{0,1},{1,2},{2,3},{3,0},{4,5},{5,6},{6,7},{7,4},{8,9},{9,10},{10,1... | collective-permute-start | bytes 786440 | tf_op jit(solution)/shard_map/ppermute | solution.py:105
  224.4 3.2 %collective-permute-done.32 = f32[4,128,128]{2,1,0:T(8,128)S(1)} collective-permute-done((f32[4,128,128]{2,1,0:T(8,128)S(1)}, f32[4,128,128]{2,1,0:T(8,128)S(1)}, u32[]{:S(2)}, u32[]{:S(2)}) %collective-permute-start.32) | collective-permute-done | bytes 262176 | tf_op jit(solution)/shard_map/ppermute | solution.py:105
  228.3 7.0 %collective-permute-done.33 = f32[4,128,128]{2,1,0:T(8,128)S(1)} collective-permute-done((f32[4,128,128]{2,1,0:T(8,128)S(1)}, f32[4,128,128]{2,1,0:T(8,128)S(1)}, u32[]{:S(2)}, u32[]{:S(2)}) %collective-permute-start.33) | collective-permute-done | bytes 262176 | tf_op jit(solution)/shard_map/ppermute | solution.py:105
  (84 shorter events, 18.2 us)
Async XLA Ops:
  0.0 40.4 %copy-start = (s32[1,1,1,4]{3,2,1,0:T(1,128)S(1)}, s32[1,1,1,4]{3,2,1,0:T(1,128)}, u32[]{:S(2)}) copy-start(s32[1,1,1,4]{3,2,1,0:T(1,128)} %param.19) | copy-start | bytes 52
  0.0 36.4 %collective-permute-start.5 = (bf16[48,128,128]{2,1,0:T(8,128)(2,1)}, bf16[48,128,128]{2,1,0:T(8,128)(2,1)S(1)}, u32[]{:S(2)}, u32[]{:S(2)}) collective-permute-start(bf16[48,128,128]{2,1,0:T(8,128)(2,1)} %bitcast.129), channel_id=1, source_target_pairs={{0,32},{32,64},{64,96},{96,0},{1,33},{33,65},{65,97},{97,1},{2,34}... | collective-permute-start | bytes 4718600 | tf_op jit(solution)/shard_map/ppermute | solution.py:94
  1.5 37.4 %collective-permute-start.6 = (bf16[48,128,128]{2,1,0:T(8,128)(2,1)}, bf16[48,128,128]{2,1,0:T(8,128)(2,1)S(1)}, u32[]{:S(2)}, u32[]{:S(2)}) collective-permute-start(bf16[48,128,128]{2,1,0:T(8,128)(2,1)} %bitcast.130), channel_id=1, source_target_pairs={{0,96},{32,0},{64,32},{96,64},{1,97},{33,1},{65,33},{97,65},{2,98}... | collective-permute-start | bytes 4718600 | tf_op jit(solution)/shard_map/ppermute | solution.py:94
  2.0 62.7 %collective-permute-start.9 = (bf16[48,128,128]{2,1,0:T(8,128)(2,1)}, bf16[48,128,128]{2,1,0:T(8,128)(2,1)}, u32[]{:S(2)}, u32[]{:S(2)}) collective-permute-start(bf16[48,128,128]{2,1,0:T(8,128)(2,1)} %bitcast.110), channel_id=1, source_target_pairs={{0,16},{16,0},{1,17},{17,1},{2,18},{18,2},{3,19},{19,3},{4,20},{20... | collective-permute-start | bytes 4718600 | tf_op jit(solution)/shard_map/ppermute | solution.py:94
  2.0 52.4 %collective-permute-start.1 = (s32[48]{0:T(128)}, s32[48]{0:T(128)S(1)}, u32[]{:S(2)}, u32[]{:S(2)}) collective-permute-start(s32[48]{0:T(128)} %bitcast.139), channel_id=1, source_target_pairs={{0,96},{32,0},{64,32},{96,64},{1,97},{33,1},{65,33},{97,65},{2,98}... | collective-permute-start | bytes 584 | tf_op jit(solution)/shard_map/ppermute | solution.py:94
  3.8 50.8 %collective-permute-start = (s32[48]{0:T(128)}, s32[48]{0:T(128)S(1)}, u32[]{:S(2)}, u32[]{:S(2)}) collective-permute-start(s32[48]{0:T(128)} %bitcast.140), channel_id=1, source_target_pairs={{0,32},{32,64},{64,96},{96,0},{1,33},{33,65},{65,97},{97,1},{2,34}... | collective-permute-start | bytes 584 | tf_op jit(solution)/shard_map/ppermute | solution.py:94
  36.4 18.1 %copy-start.3 = (bf16[48,128,128]{2,1,0:T(8,128)(2,1)}, bf16[48,128,128]{2,1,0:T(8,128)(2,1)S(1)}, u32[]{:S(2)}) copy-start(bf16[48,128,128]{2,1,0:T(8,128)(2,1)S(1)} %collective-permute-done.5.refs_0_) | copy-start | bytes 4718596
  37.4 24.6 %collective-permute-start.7 = (bf16[24,128,128]{2,1,0:T(8,128)(2,1)}, bf16[24,128,128]{2,1,0:T(8,128)(2,1)}, u32[]{:S(2)}, u32[]{:S(2)}) collective-permute-start(bf16[24,128,128]{2,1,0:T(8,128)(2,1)} %slice.54), channel_id=1, source_target_pairs={{0,32},{32,64},{64,96},{96,0},{1,33},{33,65},{65,97},{97,1},{2,34}... | collective-permute-start | bytes 2359304 | tf_op jit(solution)/shard_map/ppermute | solution.py:94
  38.9 15.5 %copy-start.4 = (bf16[48,128,128]{2,1,0:T(8,128)(2,1)}, bf16[48,128,128]{2,1,0:T(8,128)(2,1)S(1)}, u32[]{:S(2)}) copy-start(bf16[48,128,128]{2,1,0:T(8,128)(2,1)S(1)} %collective-permute-done.6.refs_1_) | copy-start | bytes 4718596
  39.9 22.1 %collective-permute-start.8 = (bf16[24,128,128]{2,1,0:T(8,128)(2,1)}, bf16[24,128,128]{2,1,0:T(8,128)(2,1)}, u32[]{:S(2)}, u32[]{:S(2)}) collective-permute-start(bf16[24,128,128]{2,1,0:T(8,128)(2,1)} %slice.55), channel_id=1, source_target_pairs={{0,96},{32,0},{64,32},{96,64},{1,97},{33,1},{65,33},{97,65},{2,98}... | collective-permute-start | bytes 2359304 | tf_op jit(solution)/shard_map/ppermute | solution.py:94
  43.5 10.9 %copy-start.5 = (s32[1,1,1,48]{3,2,1,0:T(1,128)S(1)}, s32[1,1,1,48]{3,2,1,0:T(1,128)}, u32[]{:S(2)}) copy-start(s32[1,1,1,48]{3,2,1,0:T(1,128)} %param.16) | copy-start | bytes 580
  54.4 3.3 %collective-permute-start.4 = (s32[48]{0:T(128)S(1)}, s32[48]{0:T(128)S(1)}, u32[]{:S(2)}, u32[]{:S(2)}) collective-permute-start(s32[48]{0:T(128)S(1)} %bitcast.137), channel_id=1, source_target_pairs={{0,16},{16,0},{1,17},{17,1},{2,18},{18,2},{3,19},{19,3},{4,20},{20... | collective-permute-start | bytes 584 | tf_op jit(solution)/shard_map/ppermute | solution.py:94
  54.6 4.5 %collective-permute-start.3 = (s32[24]{0:T(128)S(1)}, s32[24]{0:T(128)S(1)}, u32[]{:S(2)}, u32[]{:S(2)}) collective-permute-start(s32[24]{0:T(128)S(1)} %slice.29), channel_id=1, source_target_pairs={{0,96},{32,0},{64,32},{96,64},{1,97},{33,1},{65,33},{97,65},{2,98}... | collective-permute-start | bytes 296 | tf_op jit(solution)/shard_map/ppermute | solution.py:94
  57.8 3.5 %collective-permute-start.2 = (s32[24]{0:T(128)S(1)}, s32[24]{0:T(128)S(1)}, u32[]{:S(2)}, u32[]{:S(2)}) collective-permute-start(s32[24]{0:T(128)S(1)} %bitcast.143), channel_id=1, source_target_pairs={{0,32},{32,64},{64,96},{96,0},{1,33},{33,65},{65,97},{97,1},{2,34}... | collective-permute-start | bytes 296 | tf_op jit(solution)/shard_map/ppermute | solution.py:94
  103.1 2.0 copy-start.2
  105.2 28.1 %collective-permute-start.10 = (f32[16,128,128]{2,1,0:T(8,128)S(1)}, f32[16,128,128]{2,1,0:T(8,128)}, u32[]{:S(2)}, u32[]{:S(2)}) collective-permute-start(f32[16,128,128]{2,1,0:T(8,128)S(1)} %dynamic-slice_bitcast_fusion.3), channel_id=1, source_target_pairs={{0,1},{1,2},{2,3},{3,0},{4,5},{5,6},{6,7},{7,4},{8,9},{9,10},{10,1... | collective-permute-start | bytes 3145736 | tf_op jit(solution)/shard_map/ppermute | solution.py:105
  111.9 27.9 %collective-permute-start.16 = (f32[16,128,128]{2,1,0:T(8,128)S(1)}, f32[16,128,128]{2,1,0:T(8,128)}, u32[]{:S(2)}, u32[]{:S(2)}) collective-permute-start(f32[16,128,128]{2,1,0:T(8,128)S(1)} %dynamic-slice_bitcast_fusion.2), channel_id=1, source_target_pairs={{0,3},{1,0},{2,1},{3,2},{4,7},{5,4},{6,5},{7,6},{8,11},{9,8},{10,9... | collective-permute-start | bytes 3145736 | tf_op jit(solution)/shard_map/ppermute | solution.py:105
  114.2 29.0 %collective-permute-start.22 = (f32[16,128,128]{2,1,0:T(8,128)S(1)}, f32[16,128,128]{2,1,0:T(8,128)}, u32[]{:S(2)}, u32[]{:S(2)}) collective-permute-start(f32[16,128,128]{2,1,0:T(8,128)S(1)} %dynamic-slice_bitcast_fusion.1), channel_id=1, source_target_pairs={{0,4},{1,5},{2,6},{3,7},{4,8},{5,9},{6,10},{7,11},{8,12},{9,13},{1... | collective-permute-start | bytes 3145736 | tf_op jit(solution)/shard_map/ppermute | solution.py:105
  118.6 27.1 %collective-permute-start.28 = (f32[16,128,128]{2,1,0:T(8,128)}, f32[16,128,128]{2,1,0:T(8,128)}, u32[]{:S(2)}, u32[]{:S(2)}) collective-permute-start(f32[16,128,128]{2,1,0:T(8,128)} %dynamic-slice_bitcast_fusion), channel_id=1, source_target_pairs={{0,12},{1,13},{2,14},{3,15},{4,0},{5,1},{6,2},{7,3},{8,4},{9,5},{1... | collective-permute-start | bytes 3145736 | tf_op jit(solution)/shard_map/ppermute | solution.py:105
  136.0 26.0 %collective-permute-start.11 = (f32[16,128,128]{2,1,0:T(8,128)}, f32[16,128,128]{2,1,0:T(8,128)}, u32[]{:S(2)}, u32[]{:S(2)}) collective-permute-start(f32[16,128,128]{2,1,0:T(8,128)} %bitcast_add_fusion.11), channel_id=1, source_target_pairs={{0,1},{1,2},{2,3},{3,0},{4,5},{5,6},{6,7},{7,4},{8,9},{9,10},{10,1... | collective-permute-start | bytes 3145736 | tf_op jit(solution)/shard_map/ppermute | solution.py:105
  142.4 25.9 %collective-permute-start.17 = (f32[16,128,128]{2,1,0:T(8,128)}, f32[16,128,128]{2,1,0:T(8,128)}, u32[]{:S(2)}, u32[]{:S(2)}) collective-permute-start(f32[16,128,128]{2,1,0:T(8,128)} %bitcast_add_fusion.8), channel_id=1, source_target_pairs={{0,3},{1,0},{2,1},{3,2},{4,7},{5,4},{6,5},{7,6},{8,11},{9,8},{10,9... | collective-permute-start | bytes 3145736 | tf_op jit(solution)/shard_map/ppermute | solution.py:105
  144.9 27.7 %collective-permute-start.23 = (f32[16,128,128]{2,1,0:T(8,128)S(1)}, f32[16,128,128]{2,1,0:T(8,128)S(1)}, u32[]{:S(2)}, u32[]{:S(2)}) collective-permute-start(f32[16,128,128]{2,1,0:T(8,128)S(1)} %bitcast_add_fusion.5), channel_id=1, source_target_pairs={{0,4},{1,5},{2,6},{3,7},{4,8},{5,9},{6,10},{7,11},{8,12},{9,13},{1... | collective-permute-start | bytes 3145736 | tf_op jit(solution)/shard_map/ppermute | solution.py:105
  148.4 26.4 %collective-permute-start.29 = (f32[16,128,128]{2,1,0:T(8,128)}, f32[16,128,128]{2,1,0:T(8,128)}, u32[]{:S(2)}, u32[]{:S(2)}) collective-permute-start(f32[16,128,128]{2,1,0:T(8,128)} %bitcast_add_fusion.2), channel_id=1, source_target_pairs={{0,12},{1,13},{2,14},{3,15},{4,0},{5,1},{6,2},{7,3},{8,4},{9,5},{1... | collective-permute-start | bytes 3145736 | tf_op jit(solution)/shard_map/ppermute | solution.py:105
  164.6 25.0 %collective-permute-start.12 = (f32[16,128,128]{2,1,0:T(8,128)}, f32[16,128,128]{2,1,0:T(8,128)S(1)}, u32[]{:S(2)}, u32[]{:S(2)}) collective-permute-start(f32[16,128,128]{2,1,0:T(8,128)} %bitcast_add_fusion.10), channel_id=1, source_target_pairs={{0,1},{1,2},{2,3},{3,0},{4,5},{5,6},{6,7},{7,4},{8,9},{9,10},{10,1... | collective-permute-start | bytes 3145736 | tf_op jit(solution)/shard_map/ppermute | solution.py:105
  171.0 24.7 %collective-permute-start.18 = (f32[16,128,128]{2,1,0:T(8,128)}, f32[16,128,128]{2,1,0:T(8,128)}, u32[]{:S(2)}, u32[]{:S(2)}) collective-permute-start(f32[16,128,128]{2,1,0:T(8,128)} %bitcast_add_fusion.7), channel_id=1, source_target_pairs={{0,3},{1,0},{2,1},{3,2},{4,7},{5,4},{6,5},{7,6},{8,11},{9,8},{10,9... | collective-permute-start | bytes 3145736 | tf_op jit(solution)/shard_map/ppermute | solution.py:105
  174.0 29.7 %collective-permute-start.24 = (f32[16,128,128]{2,1,0:T(8,128)S(1)}, f32[16,128,128]{2,1,0:T(8,128)S(1)}, u32[]{:S(2)}, u32[]{:S(2)}) collective-permute-start(f32[16,128,128]{2,1,0:T(8,128)S(1)} %bitcast_add_fusion.4), channel_id=1, source_target_pairs={{0,4},{1,5},{2,6},{3,7},{4,8},{5,9},{6,10},{7,11},{8,12},{9,13},{1... | collective-permute-start | bytes 3145736 | tf_op jit(solution)/shard_map/ppermute | solution.py:105
  176.5 30.5 %collective-permute-start.30 = (f32[16,128,128]{2,1,0:T(8,128)S(1)}, f32[16,128,128]{2,1,0:T(8,128)S(1)}, u32[]{:S(2)}, u32[]{:S(2)}) collective-permute-start(f32[16,128,128]{2,1,0:T(8,128)S(1)} %bitcast_add_fusion.1), channel_id=1, source_target_pairs={{0,12},{1,13},{2,14},{3,15},{4,0},{5,1},{6,2},{7,3},{8,4},{9,5},{1... | collective-permute-start | bytes 3145736 | tf_op jit(solution)/shard_map/ppermute | solution.py:105
  191.1 17.7 %collective-permute-start.13 = (f32[4,128,128]{2,1,0:T(8,128)S(1)}, f32[4,128,128]{2,1,0:T(8,128)S(1)}, u32[]{:S(2)}, u32[]{:S(2)}) collective-permute-start(f32[4,128,128]{2,1,0:T(8,128)S(1)} %dynamic-slice_bitcast_fusion.7), channel_id=1, source_target_pairs={{0,4},{1,5},{2,6},{3,7},{4,8},{5,9},{6,10},{7,11},{8,12},{9,13},{1... | collective-permute-start | bytes 786440 | tf_op jit(solution)/shard_map/ppermute | solution.py:105
  197.4 11.5 %collective-permute-start.19 = (f32[4,128,128]{2,1,0:T(8,128)S(1)}, f32[4,128,128]{2,1,0:T(8,128)S(1)}, u32[]{:S(2)}, u32[]{:S(2)}) collective-permute-start(f32[4,128,128]{2,1,0:T(8,128)S(1)} %dynamic-slice_bitcast_fusion.6), channel_id=1, source_target_pairs={{0,12},{1,13},{2,14},{3,15},{4,0},{5,1},{6,2},{7,3},{8,4},{9,5},{1... | collective-permute-start | bytes 786440 | tf_op jit(solution)/shard_map/ppermute | solution.py:105
  205.2 7.1 %collective-permute-start.25 = (f32[4,128,128]{2,1,0:T(8,128)S(1)}, f32[4,128,128]{2,1,0:T(8,128)S(1)}, u32[]{:S(2)}, u32[]{:S(2)}) collective-permute-start(f32[4,128,128]{2,1,0:T(8,128)S(1)} %dynamic-slice_bitcast_fusion.5), channel_id=1, source_target_pairs={{0,1},{1,2},{2,3},{3,0},{4,5},{5,6},{6,7},{7,4},{8,9},{9,10},{10,1... | collective-permute-start | bytes 786440 | tf_op jit(solution)/shard_map/ppermute | solution.py:105
  208.4 9.0 %collective-permute-start.31 = (f32[4,128,128]{2,1,0:T(8,128)S(1)}, f32[4,128,128]{2,1,0:T(8,128)S(1)}, u32[]{:S(2)}, u32[]{:S(2)}) collective-permute-start(f32[4,128,128]{2,1,0:T(8,128)S(1)} %dynamic-slice_bitcast_fusion.4), channel_id=1, source_target_pairs={{0,3},{1,0},{2,1},{3,2},{4,7},{5,4},{6,5},{7,6},{8,11},{9,8},{10,9... | collective-permute-start | bytes 786440 | tf_op jit(solution)/shard_map/ppermute | solution.py:105
  208.8 8.7 %collective-permute-start.14 = (f32[4,128,128]{2,1,0:T(8,128)S(1)}, f32[4,128,128]{2,1,0:T(8,128)S(1)}, u32[]{:S(2)}, u32[]{:S(2)}) collective-permute-start(f32[4,128,128]{2,1,0:T(8,128)S(1)} %bitcast_add_fusion.23), channel_id=1, source_target_pairs={{0,4},{1,5},{2,6},{3,7},{4,8},{5,9},{6,10},{7,11},{8,12},{9,13},{1... | collective-permute-start | bytes 786440 | tf_op jit(solution)/shard_map/ppermute | solution.py:105
  209.0 8.7 %collective-permute-start.20 = (f32[4,128,128]{2,1,0:T(8,128)S(1)}, f32[4,128,128]{2,1,0:T(8,128)S(1)}, u32[]{:S(2)}, u32[]{:S(2)}) collective-permute-start(f32[4,128,128]{2,1,0:T(8,128)S(1)} %bitcast_add_fusion.20), channel_id=1, source_target_pairs={{0,12},{1,13},{2,14},{3,15},{4,0},{5,1},{6,2},{7,3},{8,4},{9,5},{1... | collective-permute-start | bytes 786440 | tf_op jit(solution)/shard_map/ppermute | solution.py:105
  212.3 8.8 %collective-permute-start.26 = (f32[4,128,128]{2,1,0:T(8,128)S(1)}, f32[4,128,128]{2,1,0:T(8,128)S(1)}, u32[]{:S(2)}, u32[]{:S(2)}) collective-permute-start(f32[4,128,128]{2,1,0:T(8,128)S(1)} %bitcast_add_fusion.17), channel_id=1, source_target_pairs={{0,1},{1,2},{2,3},{3,0},{4,5},{5,6},{6,7},{7,4},{8,9},{9,10},{10,1... | collective-permute-start | bytes 786440 | tf_op jit(solution)/shard_map/ppermute | solution.py:105
  217.4 19.0 %copy-start.1 = (s32[1,1,1,4]{3,2,1,0:T(1,128)S(1)}, s32[1,1,1,4]{3,2,1,0:T(1,128)}, u32[]{:S(2)}) copy-start(s32[1,1,1,4]{3,2,1,0:T(1,128)} %param.19) | copy-start | bytes 52
  217.5 10.2 %collective-permute-start.32 = (f32[4,128,128]{2,1,0:T(8,128)S(1)}, f32[4,128,128]{2,1,0:T(8,128)S(1)}, u32[]{:S(2)}, u32[]{:S(2)}) collective-permute-start(f32[4,128,128]{2,1,0:T(8,128)S(1)} %bitcast_add_fusion.14), channel_id=1, source_target_pairs={{0,3},{1,0},{2,1},{3,2},{4,7},{5,4},{6,5},{7,6},{8,11},{9,8},{10,9... | collective-permute-start | bytes 786440 | tf_op jit(solution)/shard_map/ppermute | solution.py:105
  217.6 10.1 %collective-permute-start.15 = (f32[4,128,128]{2,1,0:T(8,128)S(1)}, f32[4,128,128]{2,1,0:T(8,128)S(1)}, u32[]{:S(2)}, u32[]{:S(2)}) collective-permute-start(f32[4,128,128]{2,1,0:T(8,128)S(1)} %bitcast_add_fusion.22), channel_id=1, source_target_pairs={{0,4},{1,5},{2,6},{3,7},{4,8},{5,9},{6,10},{7,11},{8,12},{9,13},{1... | collective-permute-start | bytes 786440 | tf_op jit(solution)/shard_map/ppermute | solution.py:105
  217.7 10.1 %collective-permute-start.21 = (f32[4,128,128]{2,1,0:T(8,128)S(1)}, f32[4,128,128]{2,1,0:T(8,128)S(1)}, u32[]{:S(2)}, u32[]{:S(2)}) collective-permute-start(f32[4,128,128]{2,1,0:T(8,128)S(1)} %bitcast_add_fusion.19), channel_id=1, source_target_pairs={{0,12},{1,13},{2,14},{3,15},{4,0},{5,1},{6,2},{7,3},{8,4},{9,5},{1... | collective-permute-start | bytes 786440 | tf_op jit(solution)/shard_map/ppermute | solution.py:105
  221.1 7.2 %collective-permute-start.27 = (f32[4,128,128]{2,1,0:T(8,128)S(1)}, f32[4,128,128]{2,1,0:T(8,128)S(1)}, u32[]{:S(2)}, u32[]{:S(2)}) collective-permute-start(f32[4,128,128]{2,1,0:T(8,128)S(1)} %bitcast_add_fusion.16), channel_id=1, source_target_pairs={{0,1},{1,2},{2,3},{3,0},{4,5},{5,6},{6,7},{7,4},{8,9},{9,10},{10,1... | collective-permute-start | bytes 786440 | tf_op jit(solution)/shard_map/ppermute | solution.py:105
  227.7 7.7 %collective-permute-start.33 = (f32[4,128,128]{2,1,0:T(8,128)S(1)}, f32[4,128,128]{2,1,0:T(8,128)S(1)}, u32[]{:S(2)}, u32[]{:S(2)}) collective-permute-start(f32[4,128,128]{2,1,0:T(8,128)S(1)} %bitcast_add_fusion.13), channel_id=1, source_target_pairs={{0,3},{1,0},{2,1},{3,2},{4,7},{5,4},{6,5},{7,6},{8,11},{9,8},{10,9... | collective-permute-start | bytes 786440 | tf_op jit(solution)/shard_map/ppermute | solution.py:105

commit v4 on v2

--- a/solution.py
+++ b/solution.py
@@ -19,7 +19,7 @@
         block_size = totals.shape[-1]
 
         if has_start:
-            totals[...] = refs[-2][...]
+            pltpu.sync_copy(refs[-2], totals)
         else:
             def clear(t, carry):
                 totals[t] = jnp.zeros((block_size, block_size), jnp.float32)
@@ -70,9 +70,9 @@
     return pl.pallas_call(
         make_pair_kernel(start is not None, right_pick, len(left_lists), len(right_lists)),
         out_shape=jax.ShapeDtypeStruct((targets, block_size, block_size), jnp.float32),
-        in_specs=[smem] * 5 + [vmem] * (len(operands) - 5),
+        in_specs=[smem] * 5 + [vmem] * (len(left_lists) + len(right_lists))
+        + [pl.BlockSpec(memory_space=pl.ANY)] * (start is not None),
         out_specs=vmem,
-        input_output_aliases={len(operands) - 1: 0} if start is not None else {},
         compiler_params=pltpu.CompilerParams(vmem_limit_bytes=60 * 1024 * 1024),
     )(*operands)
 
@@ -97,10 +97,6 @@
 
     from_below = shifted(own_left, "row", 1)
     from_above = shifted(own_left, "row", -1)
-    half = left_cap // 2
-    far_low = shifted(jax.tree.map(lambda a: a[:half], from_below), "row", 1)
-    far_high = shifted(jax.tree.map(lambda a: a[half:], from_above), "row", -1)
-    far = jax.tree.map(lambda a, b: jnp.concatenate([a, b]), far_low, far_high)
     other_right = shifted(own_right, "col", 1)
 
     slots_left_all = pair_left.reshape(piece_count, -1)
@@ -117,12 +113,16 @@
     sl, sr, cn = pieces_for([0])
     totals = pair_products(sl, sr, cn, own_left[1][None], own_right[1][None],
                            (own_left[0],), (own_right[0],), (0,), targets=targets)
-    sl, sr, cn = pieces_for([-1, 1])
-    totals = pair_products(sl, sr, cn, jnp.stack([from_below[1], from_above[1]]), right_id_stack,
-                           (from_below[0], from_above[0]), right_lists, (1, 1), start=totals)
-    sl, sr, cn = pieces_for([2])
-    totals = pair_products(sl, sr, cn, far[1][None], right_id_stack,
-                           (far[0],), right_lists, (0,), start=totals)
+    totals, from_below, from_above = lax.optimization_barrier((totals, from_below, from_above))
+    half = left_cap // 2
+    far_low = shifted(jax.tree.map(lambda a: a[:half], from_below), "row", 1)
+    far_high = shifted(jax.tree.map(lambda a: a[half:], from_above), "row", -1)
+    sl, sr, cn = pieces_for([-1, 1, 2])
+    far = jax.tree.map(lambda a, b: jnp.concatenate([a, b]), far_low, far_high)
+    left_id_stack = jnp.stack([from_below[1], from_above[1], far[1]])
+    totals = pair_products(sl, sr, cn, left_id_stack, right_id_stack,
+                           (from_below[0], from_above[0], far[0]), right_lists, (1, 1, 0),
+                           start=totals)
     owned = lax.psum_scatter(totals, "layer", scatter_dimension=0, tiled=True)
     return owned.reshape(1, 1, -1, block_size, block_size)
 

time: 242 us -> 220 us (0.909)
  Pallas kernels: 51.2 us -> 37.5 us
  waiting for transfers between devices: 153 us -> 147 us
    pallas_call x3 -> x2, Pallas kernels: 51.2 us -> 37.5 us  [pair_products(): pl.pallas_call(make_pair_kernel(start is not None, right_pick, len(left_l...]
    reduce_scatter x1, waiting for transfers between devices: 120 us -> 115 us  [on_device(): owned = lax.psum_scatter(totals, 'layer', scatter_dimension=0, tiled=True)]
  transfers between devices with their start and end apart: 11 -> 11, of which waited for: 5 -> 5; matrix products, arithmetic and copies ran while one was open for 4% -> 5% of each run, Pallas kernels for 15% -> 5%
where the time goes in v4:
time: 220 us; the launch traced here: 219 us
  waiting for transfers between devices  147 us (67%)
  Pallas kernels  37.5 us (17%)
  between operations  14.1 us (6%)
  starting transfers between devices  9.01 us (4%)
  other arithmetic  6.9 us (3%)
  local copies, waits for them, and re-layouts  4.59 us (2%)
    reduce_scatter x1, waiting for transfers between devices, on_device(): owned = lax.psum_scatter(totals, 'layer', scatter_dimension=0, tiled=True)  115 us
    pallas_call x2, Pallas kernels, pair_products(): pl.pallas_call(make_pair_kernel(start is not None, right_pick, len(left_l...  37.5 us
    ppermute x10, waiting for transfers between devices, shifted(): return lax.ppermute(value, axis, pairs)  32.3 us
    ppermute x10, starting transfers between devices, shifted(): return lax.ppermute(value, axis, pairs)  9.01 us
  transfers between devices with their start and end apart: 11, of which 5 were waited for; matrix products, arithmetic and copies ran while one was open for 5% of the time, Pallas kernels for 5%

profile of v4, /device:TPU:26, one launch (start us, length us, event | category | flops | bytes accessed | tf_op | source)
XLA Modules:
  0.0 219.0 jit_solution(10720827629373244742)
XLA Ops:
  6.5 0.0 copy-start
  6.5 0.0 reduce-scatter.2.cloned.1.call-start
  6.5 0.5 collective-permute-start.2
  7.1 1.5 collective-permute-start
  8.6 0.0 collective-permute-start.9
  8.6 1.3 collective-permute-start.3
  9.8 0.8 collective-permute-start.1
  10.6 0.0 copy-done
  10.6 0.6 constant_dynamic-slice_fusion
  11.8 1.3 broadcast_select_fusion.2
  13.1 0.7 compare_and_fusion
  13.8 0.0 copy-start.5
  13.8 10.9 %shard_map.91.refs_5_ = f32[256,128,128]{2,1,0:T(8,128)} custom-call(s32[1,192]{1,0:T(1,128)} %get-tuple-element.44.slots_left, s32[1,192]{1,0:T(1,128)} %get-tuple-element.43.slots_right, s32[1]{0:T(128)S(6)} %select_n.56.counts, s32[1,48]{1,0:T(1,128)} %bitcast.36, s32[1,48]{1,0:T(1,128)} %bitcast.31, bf16[48,128,128]{2,1,0:T(8,128)(2,1)} %bitcast.26, ...), custom_call_target="tpu_custom_call" | custom-call | tf_op jit(solution)/shard_map/pallas_call | solution.py:70
  24.7 18.2 %collective-permute-done.3 = s32[48]{0:T(128)S(1)} collective-permute-done((s32[48]{0:T(128)}, s32[48]{0:T(128)S(1)}, u32[]{:S(2)}, u32[]{:S(2)}) %collective-permute-start.3) | collective-permute-done | bytes 224 | tf_op jit(solution)/shard_map/ppermute | solution.py:83
  43.0 0.0 copy-done.5
  43.0 0.0 collective-permute-start.6
  43.0 1.3 collective-permute-done.1
  44.3 0.0 collective-permute-done.2.refs_1_
  44.3 0.0 collective-permute-done.refs_0_
  44.3 0.0 copy-start.2
  44.3 1.0 slice.14
  45.3 1.1 slice.15
  46.4 0.0 copy-done.1
  46.4 0.0 copy-done.2
  46.4 2.9 %collective-permute-start.8 = (bf16[24,128,128]{2,1,0:T(8,128)(2,1)}, bf16[24,128,128]{2,1,0:T(8,128)(2,1)}, u32[]{:S(2)}, u32[]{:S(2)}) collective-permute-start(bf16[24,128,128]{2,1,0:T(8,128)(2,1)} %slice.15), channel_id=1, source_target_pairs={{0,96},{32,0},{64,32},{96,64},{1,97},{33,1},{65,33},{97,65},{2,98}... | collective-permute-start | bytes 2359304 | tf_op jit(solution)/shard_map/ppermute | solution.py:83
  49.4 0.0 collective-permute-start.7
  49.4 0.0 copy-done.3
  49.4 0.6 gather_fusion.2
  50.0 0.6 gather_fusion.1
  50.5 0.6 gather_fusion
  51.2 0.7 broadcast_select_fusion
  51.8 0.6 broadcast_select_fusion.4.counts
  52.4 0.0 collective-permute-done.6
  52.4 0.6 pad_add_fusion.1.right_ids
  53.0 0.1 slice.13
  53.1 2.0 collective-permute-start.5
  55.1 0.0 collective-permute-start.4
  55.1 10.3 %collective-permute-done.5 = s32[24]{0:T(128)S(1)} collective-permute-done((s32[24]{0:T(128)S(1)}, s32[24]{0:T(128)S(1)}, u32[]{:S(2)}, u32[]{:S(2)}) %collective-permute-start.5) | collective-permute-done | bytes 128 | tf_op jit(solution)/shard_map/ppermute | solution.py:83
  65.4 2.4 %collective-permute-done.4 = s32[24]{0:T(128)S(1)} collective-permute-done((s32[24]{0:T(128)S(1)}, s32[24]{0:T(128)S(1)}, u32[]{:S(2)}, u32[]{:S(2)}) %collective-permute-start.4) | collective-permute-done | bytes 128 | tf_op jit(solution)/shard_map/ppermute | solution.py:83
  67.9 0.1 add_bitcast_fusion
  67.9 0.6 pad_add_fusion.left_ids
  68.5 0.0 collective-permute-done.8
  68.5 0.0 collective-permute-done.7
  68.5 2.4 %pad_maximum_fusion.refs_2_ = bf16[48,128,128]{2,1,0:T(8,128)(2,1)} fusion(bf16[24,128,128]{2,1,0:T(8,128)(2,1)} %collective-permute-done.8, bf16[24,128,128]{2,1,0:T(8,128)(2,1)S(1)} %collective-permute-done.7), kind=kLoop, calls=%fused_computation.3 | loop fusion | flops 786432 | bytes 3145728 | tf_op jit(solution)/shard_map/concatenate | solution.py:121
  70.9 0.0 collective-permute-done.9.refs_4_
  71.0 26.6 %shard_map.92 = f32[256,128,128]{2,1,0:T(8,128)} custom-call(s32[3,192]{1,0:T(4,128)} %get-tuple-element.42.slots_left, s32[3,192]{1,0:T(4,128)} %get-tuple-element.41.slots_right, s32[3]{0:T(128)} %broadcast_select_fusion.4.counts, s32[3,48]{1,0:T(4,128)} %pad_add_fusion.left_ids, s32[2,48]{1,0:T(2,128)} %pad_add_fusion.1.right_ids, ...), custom_call_target="tpu_custom_call" | custom-call | tf_op jit(solution)/shard_map/pallas_call | solution.py:70
  97.6 0.0 reduce-scatter.2.cloned.1.call-update
  97.6 114.5 %reduce-scatter.2.cloned.1.call-done = f32[16,128,128]{2,1,0:T(8,128)} async-done(((f32[256,128,128]{2,1,0:T(8,128)}), f32[16,128,128]{2,1,0:T(8,128)}) %reduce-scatter.2.cloned.1.call-update) | async-done | bytes 1048592 | tf_op jit(solution)/shard_map/reduce_scatter | solution.py:126
  (5 shorter events, 0.0 us)
Async XLA Ops:
  6.5 4.1 %copy-start = (s32[1,1,1,4]{3,2,1,0:T(1,128)S(1)}, s32[1,1,1,4]{3,2,1,0:T(1,128)}, u32[]{:S(2)}) copy-start(s32[1,1,1,4]{3,2,1,0:T(1,128)} %param.19) | copy-start | bytes 52
  6.5 205.6 %reduce-scatter.2.cloned.1.call-start = ((), (), s32[]{:S(2)}) async-start(), calls=%async_computation.1 | async-start | bytes 17825792 | tf_op jit(solution)/shard_map/reduce_scatter | solution.py:126
  6.5 37.7 %collective-permute-start.2 = (bf16[48,128,128]{2,1,0:T(8,128)(2,1)}, bf16[48,128,128]{2,1,0:T(8,128)(2,1)S(1)}, u32[]{:S(2)}, u32[]{:S(2)}) collective-permute-start(bf16[48,128,128]{2,1,0:T(8,128)(2,1)} %bitcast.24), channel_id=1, source_target_pairs={{0,96},{32,0},{64,32},{96,64},{1,97},{33,1},{65,33},{97,65},{2,98}... | collective-permute-start | bytes 4718600 | tf_op jit(solution)/shard_map/ppermute | solution.py:83
  7.1 37.2 %collective-permute-start = (bf16[48,128,128]{2,1,0:T(8,128)(2,1)}, bf16[48,128,128]{2,1,0:T(8,128)(2,1)S(1)}, u32[]{:S(2)}, u32[]{:S(2)}) collective-permute-start(bf16[48,128,128]{2,1,0:T(8,128)(2,1)} %bitcast.25), channel_id=1, source_target_pairs={{0,32},{32,64},{64,96},{96,0},{1,33},{33,65},{65,97},{97,1},{2,34}... | collective-permute-start | bytes 4718600 | tf_op jit(solution)/shard_map/ppermute | solution.py:83
  8.6 62.4 %collective-permute-start.9 = (bf16[48,128,128]{2,1,0:T(8,128)(2,1)}, bf16[48,128,128]{2,1,0:T(8,128)(2,1)}, u32[]{:S(2)}, u32[]{:S(2)}) collective-permute-start(bf16[48,128,128]{2,1,0:T(8,128)(2,1)} %bitcast.21), channel_id=1, source_target_pairs={{0,16},{16,0},{1,17},{17,1},{2,18},{18,2},{3,19},{19,3},{4,20},{20... | collective-permute-start | bytes 4718600 | tf_op jit(solution)/shard_map/ppermute | solution.py:83
  8.6 34.4 %collective-permute-start.3 = (s32[48]{0:T(128)}, s32[48]{0:T(128)S(1)}, u32[]{:S(2)}, u32[]{:S(2)}) collective-permute-start(s32[48]{0:T(128)} %bitcast.34), channel_id=1, source_target_pairs={{0,96},{32,0},{64,32},{96,64},{1,97},{33,1},{65,33},{97,65},{2,98}... | collective-permute-start | bytes 584 | tf_op jit(solution)/shard_map/ppermute | solution.py:83
  9.8 34.4 %collective-permute-start.1 = (s32[48]{0:T(128)}, s32[48]{0:T(128)S(1)}, u32[]{:S(2)}, u32[]{:S(2)}) collective-permute-start(s32[48]{0:T(128)} %bitcast.35), channel_id=1, source_target_pairs={{0,32},{32,64},{64,96},{96,0},{1,33},{33,65},{65,97},{97,1},{2,34}... | collective-permute-start | bytes 584 | tf_op jit(solution)/shard_map/ppermute | solution.py:83
  13.8 29.1 %copy-start.5 = (s32[1,1,1,48]{3,2,1,0:T(1,128)S(1)}, s32[1,1,1,48]{3,2,1,0:T(1,128)}, u32[]{:S(2)}) copy-start(s32[1,1,1,48]{3,2,1,0:T(1,128)} %param.16) | copy-start | bytes 580
  43.0 6.4 %copy-start.3 = (s32[1,1,1,4,192]{4,3,2,1,0:T(4,128)S(1)}, s32[1,1,1,4,192]{4,3,2,1,0:T(4,128)}, u32[]{:S(2)}) copy-start(s32[1,1,1,4,192]{4,3,2,1,0:T(4,128)} %param.18) | copy-start | bytes 9220
  43.0 7.0 %copy-start.4 = (s32[1,1,1,4,192]{4,3,2,1,0:T(4,128)S(1)}, s32[1,1,1,4,192]{4,3,2,1,0:T(4,128)}, u32[]{:S(2)}) copy-start(s32[1,1,1,4,192]{4,3,2,1,0:T(4,128)} %param.17) | copy-start | bytes 9220
  43.0 9.4 %collective-permute-start.6 = (s32[48]{0:T(128)S(1)}, s32[48]{0:T(128)S(1)}, u32[]{:S(2)}, u32[]{:S(2)}) collective-permute-start(s32[48]{0:T(128)S(1)} %bitcast.32), channel_id=1, source_target_pairs={{0,16},{16,0},{1,17},{17,1},{2,18},{18,2},{3,19},{19,3},{4,20},{20... | collective-permute-start | bytes 584 | tf_op jit(solution)/shard_map/ppermute | solution.py:83
  44.3 2.2 copy-start.1
  44.3 2.2 copy-start.2
  46.4 22.1 %collective-permute-start.8 = (bf16[24,128,128]{2,1,0:T(8,128)(2,1)}, bf16[24,128,128]{2,1,0:T(8,128)(2,1)}, u32[]{:S(2)}, u32[]{:S(2)}) collective-permute-start(bf16[24,128,128]{2,1,0:T(8,128)(2,1)} %slice.15), channel_id=1, source_target_pairs={{0,96},{32,0},{64,32},{96,64},{1,97},{33,1},{65,33},{97,65},{2,98}... | collective-permute-start | bytes 2359304 | tf_op jit(solution)/shard_map/ppermute | solution.py:83
  49.4 19.2 %collective-permute-start.7 = (bf16[24,128,128]{2,1,0:T(8,128)(2,1)}, bf16[24,128,128]{2,1,0:T(8,128)(2,1)S(1)}, u32[]{:S(2)}, u32[]{:S(2)}) collective-permute-start(bf16[24,128,128]{2,1,0:T(8,128)(2,1)} %slice.14), channel_id=1, source_target_pairs={{0,32},{32,64},{64,96},{96,0},{1,33},{33,65},{65,97},{97,1},{2,34}... | collective-permute-start | bytes 2359304 | tf_op jit(solution)/shard_map/ppermute | solution.py:83
  53.1 12.4 %collective-permute-start.5 = (s32[24]{0:T(128)S(1)}, s32[24]{0:T(128)S(1)}, u32[]{:S(2)}, u32[]{:S(2)}) collective-permute-start(s32[24]{0:T(128)S(1)} %slice.13), channel_id=1, source_target_pairs={{0,96},{32,0},{64,32},{96,64},{1,97},{33,1},{65,33},{97,65},{2,98}... | collective-permute-start | bytes 296 | tf_op jit(solution)/shard_map/ppermute | solution.py:83
  55.1 12.8 %collective-permute-start.4 = (s32[24]{0:T(128)S(1)}, s32[24]{0:T(128)S(1)}, u32[]{:S(2)}, u32[]{:S(2)}) collective-permute-start(s32[24]{0:T(128)S(1)} %bitcast.38), channel_id=1, source_target_pairs={{0,32},{32,64},{64,96},{96,0},{1,33},{33,65},{65,97},{97,1},{2,34}... | collective-permute-start | bytes 296 | tf_op jit(solution)/shard_map/ppermute | solution.py:83
Sparse Core Ops, SparseCore 0:
  97.7 114.3 reduce-scatter.1

commit v5 on v4

--- a/solution.py
+++ b/solution.py
@@ -8,6 +8,14 @@
 SLAB = 128
 ROWS_GROUP = 8
 UNROLL = 4
+parts = 2
+
+
+def placed(t, parts):
+    owner = t // 16
+    block = t % 16
+    width = 16 // parts
+    return (block // width) * (16 * width) + owner * width + block % width
 
 
 def make_pair_kernel(has_start, right_pick, list_count, right_count):
@@ -35,7 +43,7 @@
             def one_term(j, u=u, v=v, left_list=left_list, right_list=right_list):
                 i = slots_left[u, j]
                 k = slots_right[u, j]
-                t = left_ids[u, i] * slab_width + right_ids[v, k]
+                t = placed(left_ids[u, i] * slab_width + right_ids[v, k], parts)
                 term = jnp.dot(left_list[i], right_list[k], preferred_element_type=jnp.float32)
                 return t, term
 
@@ -123,7 +131,11 @@
     totals = pair_products(sl, sr, cn, left_id_stack, right_id_stack,
                            (from_below[0], from_above[0], far[0]), right_lists, (1, 1, 0),
                            start=totals)
-    owned = lax.psum_scatter(totals, "layer", scatter_dimension=0, tiled=True)
+    width = targets // parts
+    owned = jnp.concatenate([
+        lax.psum_scatter(totals[part * width:(part + 1) * width], "layer", scatter_dimension=0,
+                         tiled=True)
+        for part in range(parts)])
     return owned.reshape(1, 1, -1, block_size, block_size)
 
 

time: 220 us -> 294 us (1.34)
  waiting for transfers between devices: 147 us -> 209 us
  local copies, waits for them, and re-layouts: 4.59 us -> 15.4 us
    reduce_scatter x1 -> x2, waiting for transfers between devices: 115 us -> 175 us  [on_device(): lax.psum_scatter(totals[part * width:(part + 1) * width], 'layer', scatte...]
    slice x0 -> x1, local copies, waits for them, and re-layouts: none -> 10.8 us  [on_device(): totals[part * width:(part + 1) * width]]
  transfers between devices with their start and end apart: 11 -> 12, of which waited for: 5 -> 6; matrix products, arithmetic and copies ran while one was open for 5% -> 4% of each run, Pallas kernels for 5% -> 4%
where the time goes in v5:
time: 294 us; the launch traced here: 293 us
  waiting for transfers between devices  209 us (71%)
  Pallas kernels  37.1 us (13%)
  local copies, waits for them, and re-layouts  15.4 us (5%)
  between operations  14.1 us (5%)
  other arithmetic  9.11 us (3%)
  starting transfers between devices  9.05 us (3%)
    reduce_scatter x2, waiting for transfers between devices, on_device(): lax.psum_scatter(totals[part * width:(part + 1) * width], 'layer', scatte...  175 us
    pallas_call x2, Pallas kernels, pair_products(): pl.pallas_call(make_pair_kernel(start is not None, right_pick, len(left_l...  37.1 us
    ppermute x10, waiting for transfers between devices, shifted(): return lax.ppermute(value, axis, pairs)  32.6 us
    slice x1, local copies, waits for them, and re-layouts, on_device(): totals[part * width:(part + 1) * width]  10.8 us
    ppermute x10, starting transfers between devices, shifted(): return lax.ppermute(value, axis, pairs)  9.01 us
  transfers between devices with their start and end apart: 12, of which 6 were waited for; matrix products, arithmetic and copies ran while one was open for 4% of the time, Pallas kernels for 4%

profile of v5, /device:TPU:26, one launch (start us, length us, event | category | flops | bytes accessed | tf_op | source)
XLA Modules:
  0.0 293.4 jit_solution(13422115559987950981)
XLA Ops:
  6.5 0.0 copy-start
  6.5 0.0 reduce-scatter.3.cloned.1.call-start
  6.5 0.5 collective-permute-start.2
  7.1 1.5 collective-permute-start
  8.6 0.0 collective-permute-start.9
  8.6 1.3 collective-permute-start.3
  9.8 0.8 collective-permute-start.1
  10.6 0.6 constant_dynamic-slice_fusion
  11.8 1.3 broadcast_select_fusion.2
  13.1 0.7 compare_and_fusion
  13.8 10.7 %shard_map.91.refs_5_ = f32[256,128,128]{2,1,0:T(8,128)} custom-call(s32[1,192]{1,0:T(1,128)} %get-tuple-element.46.slots_left, s32[1,192]{1,0:T(1,128)} %get-tuple-element.45.slots_right, s32[1]{0:T(128)S(6)} %select_n.56.counts, s32[1,48]{1,0:T(1,128)} %bitcast.37, s32[1,48]{1,0:T(1,128)} %bitcast.32, bf16[48,128,128]{2,1,0:T(8,128)(2,1)} %bitcast.27, ...), custom_call_target="tpu_custom_call" | custom-call | tf_op jit(solution)/shard_map/pallas_call | solution.py:78
  24.5 18.4 %collective-permute-done.3 = s32[48]{0:T(128)S(1)} collective-permute-done((s32[48]{0:T(128)}, s32[48]{0:T(128)S(1)}, u32[]{:S(2)}, u32[]{:S(2)}) %collective-permute-start.3) | collective-permute-done | bytes 224 | tf_op jit(solution)/shard_map/ppermute | solution.py:91
  43.0 0.0 collective-permute-start.6
  43.0 1.3 collective-permute-done.1
  44.3 0.0 collective-permute-done.2.refs_1_
  44.3 0.0 collective-permute-done.refs_0_
  44.3 0.0 copy-start.2
  44.3 1.1 slice.20
  45.3 1.1 slice.21
  46.4 0.0 copy-done.1
  46.4 2.9 collective-permute-start.8
  49.4 0.0 collective-permute-start.7
  49.4 0.6 gather_fusion.2
  50.0 0.6 gather_fusion.1
  50.5 0.6 gather_fusion
  51.2 0.7 broadcast_select_fusion
  51.8 0.5 broadcast_select_fusion.4.counts
  52.3 0.0 collective-permute-done.6
  52.4 0.6 pad_add_fusion.1.right_ids
  52.9 0.1 slice.19
  53.0 2.0 collective-permute-start.5
  55.0 0.0 collective-permute-start.4
  55.0 10.4 %collective-permute-done.5 = s32[24]{0:T(128)S(1)} collective-permute-done((s32[24]{0:T(128)S(1)}, s32[24]{0:T(128)S(1)}, u32[]{:S(2)}, u32[]{:S(2)}) %collective-permute-start.5) | collective-permute-done | bytes 128 | tf_op jit(solution)/shard_map/ppermute | solution.py:91
  65.4 2.4 collective-permute-done.4
  67.9 0.1 add_bitcast_fusion
  67.9 0.6 pad_add_fusion.left_ids
  68.5 0.0 collective-permute-done.8
  68.5 0.0 collective-permute-done.7
  68.5 2.4 pad_maximum_fusion.refs_2_
  71.0 0.0 collective-permute-done.9.refs_4_
  71.0 26.4 %shard_map.92 = f32[256,128,128]{2,1,0:T(8,128)} custom-call(s32[3,192]{1,0:T(4,128)} %get-tuple-element.44.slots_left, s32[3,192]{1,0:T(4,128)} %get-tuple-element.43.slots_right, s32[3]{0:T(128)} %broadcast_select_fusion.4.counts, s32[3,48]{1,0:T(4,128)} %pad_add_fusion.left_ids, s32[2,48]{1,0:T(2,128)} %pad_add_fusion.1.right_ids, ...), custom_call_target="tpu_custom_call" | custom-call | tf_op jit(solution)/shard_map/pallas_call | solution.py:78
  97.4 10.8 %fusion.1 = (f32[128,128,128]{2,1,0:T(8,128)}, f32[128,128,128]{2,1,0:T(8,128)}) fusion(f32[256,128,128]{2,1,0:T(8,128)} %shard_map.92), kind=kLoop, calls=%fused_computation.21 | loop fusion | bytes 33554432 | tf_op jit(solution)/shard_map/slice | solution.py:136
  108.2 0.0 reduce-scatter.3.cloned.1.call-update
  108.2 0.0 reduce-scatter.5.cloned.1.call-start
  108.2 0.7 reduce-scatter.5.cloned.1.call-update
  108.9 87.5 %reduce-scatter.3.cloned.1.call-done = f32[8,128,128]{2,1,0:T(8,128)} async-done(((f32[128,128,128]{2,1,0:T(8,128)}), f32[8,128,128]{2,1,0:T(8,128)}) %reduce-scatter.3.cloned.1.call-update) | async-done | bytes 524304 | tf_op jit(solution)/shard_map/reduce_scatter | solution.py:136
  196.4 87.8 %reduce-scatter.5.cloned.1.call-done = f32[8,128,128]{2,1,0:T(8,128)} async-done(((f32[128,128,128]{2,1,0:T(8,128)}), f32[8,128,128]{2,1,0:T(8,128)}) %reduce-scatter.5.cloned.1.call-update) | async-done | bytes 524304 | tf_op jit(solution)/shard_map/reduce_scatter | solution.py:136
  284.3 2.3 maximum_bitcast_fusion
  (10 shorter events, 0.0 us)
Async XLA Ops:
  6.5 4.1 %copy-start = (s32[1,1,1,4]{3,2,1,0:T(1,128)S(1)}, s32[1,1,1,4]{3,2,1,0:T(1,128)}, u32[]{:S(2)}) copy-start(s32[1,1,1,4]{3,2,1,0:T(1,128)} %param.19) | copy-start | bytes 52
  6.5 189.9 %reduce-scatter.3.cloned.1.call-start = ((), (), s32[]{:S(2)}) async-start(), calls=%async_computation.2 | async-start | bytes 8912896 | tf_op jit(solution)/shard_map/reduce_scatter | solution.py:136
  6.5 37.7 %collective-permute-start.2 = (bf16[48,128,128]{2,1,0:T(8,128)(2,1)}, bf16[48,128,128]{2,1,0:T(8,128)(2,1)S(1)}, u32[]{:S(2)}, u32[]{:S(2)}) collective-permute-start(bf16[48,128,128]{2,1,0:T(8,128)(2,1)} %bitcast.25), channel_id=1, source_target_pairs={{0,96},{32,0},{64,32},{96,64},{1,97},{33,1},{65,33},{97,65},{2,98}... | collective-permute-start | bytes 4718600 | tf_op jit(solution)/shard_map/ppermute | solution.py:91
  7.1 37.2 %collective-permute-start = (bf16[48,128,128]{2,1,0:T(8,128)(2,1)}, bf16[48,128,128]{2,1,0:T(8,128)(2,1)S(1)}, u32[]{:S(2)}, u32[]{:S(2)}) collective-permute-start(bf16[48,128,128]{2,1,0:T(8,128)(2,1)} %bitcast.26), channel_id=1, source_target_pairs={{0,32},{32,64},{64,96},{96,0},{1,33},{33,65},{65,97},{97,1},{2,34}... | collective-permute-start | bytes 4718600 | tf_op jit(solution)/shard_map/ppermute | solution.py:91
  8.6 62.4 %collective-permute-start.9 = (bf16[48,128,128]{2,1,0:T(8,128)(2,1)}, bf16[48,128,128]{2,1,0:T(8,128)(2,1)}, u32[]{:S(2)}, u32[]{:S(2)}) collective-permute-start(bf16[48,128,128]{2,1,0:T(8,128)(2,1)} %bitcast.22), channel_id=1, source_target_pairs={{0,16},{16,0},{1,17},{17,1},{2,18},{18,2},{3,19},{19,3},{4,20},{20... | collective-permute-start | bytes 4718600 | tf_op jit(solution)/shard_map/ppermute | solution.py:91
  8.6 34.4 %collective-permute-start.3 = (s32[48]{0:T(128)}, s32[48]{0:T(128)S(1)}, u32[]{:S(2)}, u32[]{:S(2)}) collective-permute-start(s32[48]{0:T(128)} %bitcast.35), channel_id=1, source_target_pairs={{0,96},{32,0},{64,32},{96,64},{1,97},{33,1},{65,33},{97,65},{2,98}... | collective-permute-start | bytes 584 | tf_op jit(solution)/shard_map/ppermute | solution.py:91
  9.8 34.4 %collective-permute-start.1 = (s32[48]{0:T(128)}, s32[48]{0:T(128)S(1)}, u32[]{:S(2)}, u32[]{:S(2)}) collective-permute-start(s32[48]{0:T(128)} %bitcast.36), channel_id=1, source_target_pairs={{0,32},{32,64},{64,96},{96,0},{1,33},{33,65},{65,97},{97,1},{2,34}... | collective-permute-start | bytes 584 | tf_op jit(solution)/shard_map/ppermute | solution.py:91
  13.8 29.1 %copy-start.5 = (s32[1,1,1,48]{3,2,1,0:T(1,128)S(1)}, s32[1,1,1,48]{3,2,1,0:T(1,128)}, u32[]{:S(2)}) copy-start(s32[1,1,1,48]{3,2,1,0:T(1,128)} %param.16) | copy-start | bytes 580
  43.0 6.4 %copy-start.3 = (s32[1,1,1,4,192]{4,3,2,1,0:T(4,128)S(1)}, s32[1,1,1,4,192]{4,3,2,1,0:T(4,128)}, u32[]{:S(2)}) copy-start(s32[1,1,1,4,192]{4,3,2,1,0:T(4,128)} %param.18) | copy-start | bytes 9220
  43.0 7.0 %copy-start.4 = (s32[1,1,1,4,192]{4,3,2,1,0:T(4,128)S(1)}, s32[1,1,1,4,192]{4,3,2,1,0:T(4,128)}, u32[]{:S(2)}) copy-start(s32[1,1,1,4,192]{4,3,2,1,0:T(4,128)} %param.17) | copy-start | bytes 9220
  43.0 9.4 %collective-permute-start.6 = (s32[48]{0:T(128)S(1)}, s32[48]{0:T(128)S(1)}, u32[]{:S(2)}, u32[]{:S(2)}) collective-permute-start(s32[48]{0:T(128)S(1)} %bitcast.33), channel_id=1, source_target_pairs={{0,16},{16,0},{1,17},{17,1},{2,18},{18,2},{3,19},{19,3},{4,20},{20... | collective-permute-start | bytes 584 | tf_op jit(solution)/shard_map/ppermute | solution.py:91
  44.3 2.2 copy-start.1
  44.3 2.2 copy-start.2
  46.4 22.1 %collective-permute-start.8 = (bf16[24,128,128]{2,1,0:T(8,128)(2,1)}, bf16[24,128,128]{2,1,0:T(8,128)(2,1)}, u32[]{:S(2)}, u32[]{:S(2)}) collective-permute-start(bf16[24,128,128]{2,1,0:T(8,128)(2,1)} %slice.21), channel_id=1, source_target_pairs={{0,96},{32,0},{64,32},{96,64},{1,97},{33,1},{65,33},{97,65},{2,98}... | collective-permute-start | bytes 2359304 | tf_op jit(solution)/shard_map/ppermute | solution.py:91
  49.4 19.2 %collective-permute-start.7 = (bf16[24,128,128]{2,1,0:T(8,128)(2,1)}, bf16[24,128,128]{2,1,0:T(8,128)(2,1)S(1)}, u32[]{:S(2)}, u32[]{:S(2)}) collective-permute-start(bf16[24,128,128]{2,1,0:T(8,128)(2,1)} %slice.20), channel_id=1, source_target_pairs={{0,32},{32,64},{64,96},{96,0},{1,33},{33,65},{65,97},{97,1},{2,34}... | collective-permute-start | bytes 2359304 | tf_op jit(solution)/shard_map/ppermute | solution.py:91
  53.0 12.4 %collective-permute-start.5 = (s32[24]{0:T(128)S(1)}, s32[24]{0:T(128)S(1)}, u32[]{:S(2)}, u32[]{:S(2)}) collective-permute-start(s32[24]{0:T(128)S(1)} %slice.19), channel_id=1, source_target_pairs={{0,96},{32,0},{64,32},{96,64},{1,97},{33,1},{65,33},{97,65},{2,98}... | collective-permute-start | bytes 296 | tf_op jit(solution)/shard_map/ppermute | solution.py:91
  55.0 12.8 %collective-permute-start.4 = (s32[24]{0:T(128)S(1)}, s32[24]{0:T(128)S(1)}, u32[]{:S(2)}, u32[]{:S(2)}) collective-permute-start(s32[24]{0:T(128)S(1)} %bitcast.39), channel_id=1, source_target_pairs={{0,32},{32,64},{64,96},{96,0},{1,33},{33,65},{65,97},{97,1},{2,34}... | collective-permute-start | bytes 296 | tf_op jit(solution)/shard_map/ppermute | solution.py:91
  108.2 176.1 %reduce-scatter.5.cloned.1.call-start = ((), (), s32[]{:S(2)}) async-start(), calls=%async_computation.3 | async-start | bytes 8912896 | tf_op jit(solution)/shard_map/reduce_scatter | solution.py:136
Sparse Core Ops, SparseCore 0:
  108.3 88.0 reduce-scatter.2
  199.8 84.3 reduce-scatter.4

commit v6 on v4

--- a/solution.py
+++ b/solution.py
@@ -7,7 +7,7 @@
 
 SLAB = 128
 ROWS_GROUP = 8
-UNROLL = 4
+UNROLL = 16
 
 
 def make_pair_kernel(has_start, right_pick, list_count, right_count):

time: 220 us -> 215 us (0.977)
  Pallas kernels: 37.5 us -> 32.6 us
    pallas_call x2, Pallas kernels: 37.5 us -> 32.6 us  [pair_products(): pl.pallas_call(make_pair_kernel(start is not None, right_pick, len(left_l...]
  transfers between devices with their start and end apart: 11 -> 11, of which waited for: 5 -> 5; matrix products, arithmetic and copies ran while one was open for 5% -> 5% of each run, Pallas kernels for 5% -> 6%
where the time goes in v6:
time: 215 us; the launch traced here: 213 us
  waiting for transfers between devices  146 us (68%)
  Pallas kernels  32.6 us (15%)
  between operations  14.1 us (7%)
  starting transfers between devices  9.01 us (4%)
  other arithmetic  6.9 us (3%)
  local copies, waits for them, and re-layouts  4.59 us (2%)
    reduce_scatter x1, waiting for transfers between devices, on_device(): owned = lax.psum_scatter(totals, 'layer', scatter_dimension=0, tiled=True)  116 us
    pallas_call x2, Pallas kernels, pair_products(): pl.pallas_call(make_pair_kernel(start is not None, right_pick, len(left_l...  32.6 us
    ppermute x10, waiting for transfers between devices, shifted(): return lax.ppermute(value, axis, pairs)  30.4 us
    ppermute x10, starting transfers between devices, shifted(): return lax.ppermute(value, axis, pairs)  9.01 us
  transfers between devices with their start and end apart: 11, of which 5 were waited for; matrix products, arithmetic and copies ran while one was open for 5% of the time, Pallas kernels for 6%

profile of v6, /device:TPU:26, one launch (start us, length us, event | category | flops | bytes accessed | tf_op | source)
XLA Modules:
  0.0 213.4 jit_solution(1922159111213215357)
XLA Ops:
  6.5 0.0 copy-start
  6.5 0.0 reduce-scatter.2.cloned.1.call-start
  6.5 0.5 collective-permute-start.2
  7.1 1.5 collective-permute-start
  8.6 0.0 collective-permute-start.9
  8.6 1.3 collective-permute-start.3
  9.8 0.8 collective-permute-start.1
  10.6 0.0 copy-done
  10.6 0.6 constant_dynamic-slice_fusion
  11.8 1.3 broadcast_select_fusion.2
  13.1 0.7 compare_and_fusion
  13.8 0.0 copy-start.5
  13.8 12.8 %shard_map.91.refs_5_ = f32[256,128,128]{2,1,0:T(8,128)} custom-call(s32[1,192]{1,0:T(1,128)} %get-tuple-element.44.slots_left, s32[1,192]{1,0:T(1,128)} %get-tuple-element.43.slots_right, s32[1]{0:T(128)S(6)} %select_n.56.counts, s32[1,48]{1,0:T(1,128)} %bitcast.36, s32[1,48]{1,0:T(1,128)} %bitcast.31, bf16[48,128,128]{2,1,0:T(8,128)(2,1)} %bitcast.26, ...), custom_call_target="tpu_custom_call" | custom-call | tf_op jit(solution)/shard_map/pallas_call | solution.py:70
  26.6 16.3 %collective-permute-done.3 = s32[48]{0:T(128)S(1)} collective-permute-done((s32[48]{0:T(128)}, s32[48]{0:T(128)S(1)}, u32[]{:S(2)}, u32[]{:S(2)}) %collective-permute-start.3) | collective-permute-done | bytes 224 | tf_op jit(solution)/shard_map/ppermute | solution.py:83
  43.0 0.0 copy-done.5
  43.0 0.0 collective-permute-start.6
  43.0 1.3 collective-permute-done.1
  44.3 0.0 collective-permute-done.2.refs_1_
  44.3 0.0 collective-permute-done.refs_0_
  44.3 0.0 copy-start.2
  44.3 1.0 slice.14
  45.3 1.1 slice.15
  46.4 0.0 copy-done.1
  46.4 0.0 copy-done.2
  46.4 2.9 %collective-permute-start.8 = (bf16[24,128,128]{2,1,0:T(8,128)(2,1)}, bf16[24,128,128]{2,1,0:T(8,128)(2,1)}, u32[]{:S(2)}, u32[]{:S(2)}) collective-permute-start(bf16[24,128,128]{2,1,0:T(8,128)(2,1)} %slice.15), channel_id=1, source_target_pairs={{0,96},{32,0},{64,32},{96,64},{1,97},{33,1},{65,33},{97,65},{2,98}... | collective-permute-start | bytes 2359304 | tf_op jit(solution)/shard_map/ppermute | solution.py:83
  49.4 0.0 collective-permute-start.7
  49.4 0.0 copy-done.3
  49.4 0.6 gather_fusion.2
  50.0 0.6 gather_fusion.1
  50.5 0.6 gather_fusion
  51.2 0.7 broadcast_select_fusion
  51.8 0.6 broadcast_select_fusion.4.counts
  52.4 0.0 collective-permute-done.6
  52.4 0.6 pad_add_fusion.1.right_ids
  53.0 0.1 slice.13
  53.1 2.0 collective-permute-start.5
  55.1 0.0 collective-permute-start.4
  55.1 10.3 %collective-permute-done.5 = s32[24]{0:T(128)S(1)} collective-permute-done((s32[24]{0:T(128)S(1)}, s32[24]{0:T(128)S(1)}, u32[]{:S(2)}, u32[]{:S(2)}) %collective-permute-start.5) | collective-permute-done | bytes 128 | tf_op jit(solution)/shard_map/ppermute | solution.py:83
  65.4 2.4 %collective-permute-done.4 = s32[24]{0:T(128)S(1)} collective-permute-done((s32[24]{0:T(128)S(1)}, s32[24]{0:T(128)S(1)}, u32[]{:S(2)}, u32[]{:S(2)}) %collective-permute-start.4) | collective-permute-done | bytes 128 | tf_op jit(solution)/shard_map/ppermute | solution.py:83
  67.9 0.1 add_bitcast_fusion
  67.9 0.6 pad_add_fusion.left_ids
  68.5 0.0 collective-permute-done.8
  68.5 0.0 collective-permute-done.7
  68.5 2.4 %pad_maximum_fusion.refs_2_ = bf16[48,128,128]{2,1,0:T(8,128)(2,1)} fusion(bf16[24,128,128]{2,1,0:T(8,128)(2,1)} %collective-permute-done.8, bf16[24,128,128]{2,1,0:T(8,128)(2,1)S(1)} %collective-permute-done.7), kind=kLoop, calls=%fused_computation.3 | loop fusion | flops 786432 | bytes 3145728 | tf_op jit(solution)/shard_map/concatenate | solution.py:121
  70.9 0.0 collective-permute-done.9.refs_4_
  71.0 19.8 %shard_map.92 = f32[256,128,128]{2,1,0:T(8,128)} custom-call(s32[3,192]{1,0:T(4,128)} %get-tuple-element.42.slots_left, s32[3,192]{1,0:T(4,128)} %get-tuple-element.41.slots_right, s32[3]{0:T(128)} %broadcast_select_fusion.4.counts, s32[3,48]{1,0:T(4,128)} %pad_add_fusion.left_ids, s32[2,48]{1,0:T(2,128)} %pad_add_fusion.1.right_ids, ...), custom_call_target="tpu_custom_call" | custom-call | tf_op jit(solution)/shard_map/pallas_call | solution.py:70
  90.8 0.0 reduce-scatter.2.cloned.1.call-update
  90.8 115.8 %reduce-scatter.2.cloned.1.call-done = f32[16,128,128]{2,1,0:T(8,128)} async-done(((f32[256,128,128]{2,1,0:T(8,128)}), f32[16,128,128]{2,1,0:T(8,128)}) %reduce-scatter.2.cloned.1.call-update) | async-done | bytes 1048592 | tf_op jit(solution)/shard_map/reduce_scatter | solution.py:126
  (5 shorter events, 0.0 us)
Async XLA Ops:
  6.5 4.1 %copy-start = (s32[1,1,1,4]{3,2,1,0:T(1,128)S(1)}, s32[1,1,1,4]{3,2,1,0:T(1,128)}, u32[]{:S(2)}) copy-start(s32[1,1,1,4]{3,2,1,0:T(1,128)} %param.19) | copy-start | bytes 52
  6.5 200.0 %reduce-scatter.2.cloned.1.call-start = ((), (), s32[]{:S(2)}) async-start(), calls=%async_computation.1 | async-start | bytes 17825792 | tf_op jit(solution)/shard_map/reduce_scatter | solution.py:126
  6.5 37.7 %collective-permute-start.2 = (bf16[48,128,128]{2,1,0:T(8,128)(2,1)}, bf16[48,128,128]{2,1,0:T(8,128)(2,1)S(1)}, u32[]{:S(2)}, u32[]{:S(2)}) collective-permute-start(bf16[48,128,128]{2,1,0:T(8,128)(2,1)} %bitcast.24), channel_id=1, source_target_pairs={{0,96},{32,0},{64,32},{96,64},{1,97},{33,1},{65,33},{97,65},{2,98}... | collective-permute-start | bytes 4718600 | tf_op jit(solution)/shard_map/ppermute | solution.py:83
  7.1 37.2 %collective-permute-start = (bf16[48,128,128]{2,1,0:T(8,128)(2,1)}, bf16[48,128,128]{2,1,0:T(8,128)(2,1)S(1)}, u32[]{:S(2)}, u32[]{:S(2)}) collective-permute-start(bf16[48,128,128]{2,1,0:T(8,128)(2,1)} %bitcast.25), channel_id=1, source_target_pairs={{0,32},{32,64},{64,96},{96,0},{1,33},{33,65},{65,97},{97,1},{2,34}... | collective-permute-start | bytes 4718600 | tf_op jit(solution)/shard_map/ppermute | solution.py:83
  8.6 62.4 %collective-permute-start.9 = (bf16[48,128,128]{2,1,0:T(8,128)(2,1)}, bf16[48,128,128]{2,1,0:T(8,128)(2,1)}, u32[]{:S(2)}, u32[]{:S(2)}) collective-permute-start(bf16[48,128,128]{2,1,0:T(8,128)(2,1)} %bitcast.21), channel_id=1, source_target_pairs={{0,16},{16,0},{1,17},{17,1},{2,18},{18,2},{3,19},{19,3},{4,20},{20... | collective-permute-start | bytes 4718600 | tf_op jit(solution)/shard_map/ppermute | solution.py:83
  8.6 34.4 %collective-permute-start.3 = (s32[48]{0:T(128)}, s32[48]{0:T(128)S(1)}, u32[]{:S(2)}, u32[]{:S(2)}) collective-permute-start(s32[48]{0:T(128)} %bitcast.34), channel_id=1, source_target_pairs={{0,96},{32,0},{64,32},{96,64},{1,97},{33,1},{65,33},{97,65},{2,98}... | collective-permute-start | bytes 584 | tf_op jit(solution)/shard_map/ppermute | solution.py:83
  9.8 34.4 %collective-permute-start.1 = (s32[48]{0:T(128)}, s32[48]{0:T(128)S(1)}, u32[]{:S(2)}, u32[]{:S(2)}) collective-permute-start(s32[48]{0:T(128)} %bitcast.35), channel_id=1, source_target_pairs={{0,32},{32,64},{64,96},{96,0},{1,33},{33,65},{65,97},{97,1},{2,34}... | collective-permute-start | bytes 584 | tf_op jit(solution)/shard_map/ppermute | solution.py:83
  13.8 29.1 %copy-start.5 = (s32[1,1,1,48]{3,2,1,0:T(1,128)S(1)}, s32[1,1,1,48]{3,2,1,0:T(1,128)}, u32[]{:S(2)}) copy-start(s32[1,1,1,48]{3,2,1,0:T(1,128)} %param.16) | copy-start | bytes 580
  43.0 6.4 %copy-start.3 = (s32[1,1,1,4,192]{4,3,2,1,0:T(4,128)S(1)}, s32[1,1,1,4,192]{4,3,2,1,0:T(4,128)}, u32[]{:S(2)}) copy-start(s32[1,1,1,4,192]{4,3,2,1,0:T(4,128)} %param.18) | copy-start | bytes 9220
  43.0 7.0 %copy-start.4 = (s32[1,1,1,4,192]{4,3,2,1,0:T(4,128)S(1)}, s32[1,1,1,4,192]{4,3,2,1,0:T(4,128)}, u32[]{:S(2)}) copy-start(s32[1,1,1,4,192]{4,3,2,1,0:T(4,128)} %param.17) | copy-start | bytes 9220
  43.0 9.4 %collective-permute-start.6 = (s32[48]{0:T(128)S(1)}, s32[48]{0:T(128)S(1)}, u32[]{:S(2)}, u32[]{:S(2)}) collective-permute-start(s32[48]{0:T(128)S(1)} %bitcast.32), channel_id=1, source_target_pairs={{0,16},{16,0},{1,17},{17,1},{2,18},{18,2},{3,19},{19,3},{4,20},{20... | collective-permute-start | bytes 584 | tf_op jit(solution)/shard_map/ppermute | solution.py:83
  44.3 2.2 %copy-start.1 = (bf16[48,128,128]{2,1,0:T(8,128)(2,1)}, bf16[48,128,128]{2,1,0:T(8,128)(2,1)S(1)}, u32[]{:S(2)}) copy-start(bf16[48,128,128]{2,1,0:T(8,128)(2,1)S(1)} %collective-permute-done.2.refs_1_) | copy-start | bytes 4718596
  44.3 2.2 %copy-start.2 = (bf16[48,128,128]{2,1,0:T(8,128)(2,1)}, bf16[48,128,128]{2,1,0:T(8,128)(2,1)S(1)}, u32[]{:S(2)}) copy-start(bf16[48,128,128]{2,1,0:T(8,128)(2,1)S(1)} %collective-permute-done.refs_0_) | copy-start | bytes 4718596
  46.4 22.1 %collective-permute-start.8 = (bf16[24,128,128]{2,1,0:T(8,128)(2,1)}, bf16[24,128,128]{2,1,0:T(8,128)(2,1)}, u32[]{:S(2)}, u32[]{:S(2)}) collective-permute-start(bf16[24,128,128]{2,1,0:T(8,128)(2,1)} %slice.15), channel_id=1, source_target_pairs={{0,96},{32,0},{64,32},{96,64},{1,97},{33,1},{65,33},{97,65},{2,98}... | collective-permute-start | bytes 2359304 | tf_op jit(solution)/shard_map/ppermute | solution.py:83
  49.4 19.2 %collective-permute-start.7 = (bf16[24,128,128]{2,1,0:T(8,128)(2,1)}, bf16[24,128,128]{2,1,0:T(8,128)(2,1)S(1)}, u32[]{:S(2)}, u32[]{:S(2)}) collective-permute-start(bf16[24,128,128]{2,1,0:T(8,128)(2,1)} %slice.14), channel_id=1, source_target_pairs={{0,32},{32,64},{64,96},{96,0},{1,33},{33,65},{65,97},{97,1},{2,34}... | collective-permute-start | bytes 2359304 | tf_op jit(solution)/shard_map/ppermute | solution.py:83
  53.1 12.4 %collective-permute-start.5 = (s32[24]{0:T(128)S(1)}, s32[24]{0:T(128)S(1)}, u32[]{:S(2)}, u32[]{:S(2)}) collective-permute-start(s32[24]{0:T(128)S(1)} %slice.13), channel_id=1, source_target_pairs={{0,96},{32,0},{64,32},{96,64},{1,97},{33,1},{65,33},{97,65},{2,98}... | collective-permute-start | bytes 296 | tf_op jit(solution)/shard_map/ppermute | solution.py:83
  55.1 12.8 %collective-permute-start.4 = (s32[24]{0:T(128)S(1)}, s32[24]{0:T(128)S(1)}, u32[]{:S(2)}, u32[]{:S(2)}) collective-permute-start(s32[24]{0:T(128)S(1)} %bitcast.38), channel_id=1, source_target_pairs={{0,32},{32,64},{64,96},{96,0},{1,33},{33,65},{65,97},{97,1},{2,34}... | collective-permute-start | bytes 296 | tf_op jit(solution)/shard_map/ppermute | solution.py:83
Sparse Core Ops, SparseCore 0:
  90.9 115.6 reduce-scatter.1

commit v7 on v6

--- a/solution.py
+++ b/solution.py
@@ -10,33 +10,62 @@
 UNROLL = 16
 
 
-def make_pair_kernel(has_start, right_pick, list_count, right_count):
+def make_pair_kernel(right_pick, sources):
+    list_count = len(right_pick)
+    operand_count = sum(len(parts) for parts in sources)
+
     def pair_kernel(slots_left, slots_right, counts, left_ids, right_ids, *refs):
-        left_lists = refs[:list_count]
-        right_lists = refs[list_count:list_count + right_count]
-        totals = refs[-1]
+        operands = refs[:operand_count]
+        right_hbm = refs[operand_count:operand_count + 2]
+        totals = refs[operand_count + 2]
+        left_lists, right_lists, sems = refs[operand_count + 3:]
         slab_width = totals.shape[0] // ROWS_GROUP
         block_size = totals.shape[-1]
 
-        if has_start:
-            pltpu.sync_copy(refs[-2], totals)
-        else:
-            def clear(t, carry):
-                totals[t] = jnp.zeros((block_size, block_size), jnp.float32)
-                return carry
+        right_copies = [pltpu.make_async_copy(right_hbm[v], right_lists.at[v], sems.at[v])
+                        for v in range(2)]
+        left_copies = []
+        position = 0
+        for u, parts in enumerate(sources):
+            copies = []
+            offset = 0
+            for part in parts:
+                size = operands[position].shape[0]
+                copies.append(pltpu.make_async_copy(
+                    operands[position], left_lists.at[u, pl.ds(offset, size)],
+                    sems.at[2 + position]))
+                offset += size
+                position += 1
+            left_copies.append(copies)
+        started = set()
+        for u in range(list_count):
+            for copy in left_copies[u]:
+                copy.start()
+            if right_pick[u] not in started:
+                right_copies[right_pick[u]].start()
+                started.add(right_pick[u])
 
-            lax.fori_loop(0, totals.shape[0], clear, 0)
+        def clear(t, carry):
+            totals[t] = jnp.zeros((block_size, block_size), jnp.float32)
+            return carry
 
+        lax.fori_loop(0, totals.shape[0], clear, 0)
+
+        waited = set()
         for u in range(list_count):
             v = right_pick[u]
-            left_list = left_lists[u]
-            right_list = right_lists[v]
+            for copy in left_copies[u]:
+                copy.wait()
+            if v not in waited:
+                right_copies[v].wait()
+                waited.add(v)
 
-            def one_term(j, u=u, v=v, left_list=left_list, right_list=right_list):
+            def one_term(j, u=u, v=v):
                 i = slots_left[u, j]
                 k = slots_right[u, j]
                 t = left_ids[u, i] * slab_width + right_ids[v, k]
-                term = jnp.dot(left_list[i], right_list[k], preferred_element_type=jnp.float32)
+                term = jnp.dot(left_lists[u, i], right_lists[v, k],
+                               preferred_element_type=jnp.float32)
                 return t, term
 
             def add_group(g, carry, one_term=one_term):
@@ -59,22 +88,24 @@
 
 
 def pair_products(slots_left, slots_right, counts, left_ids, right_ids,
-                  left_lists, right_lists, right_pick, start=None, targets=None):
-    block_size = left_lists[0].shape[-1]
+                  left_sources, right_lists, right_pick, targets):
+    block_size = right_lists[0].shape[-1]
+    list_cap = right_lists[0].shape[0]
     smem = pl.BlockSpec(memory_space=pltpu.SMEM)
-    vmem = pl.BlockSpec(memory_space=pltpu.VMEM)
-    operands = [slots_left, slots_right, counts, left_ids, right_ids, *left_lists, *right_lists]
-    if start is not None:
-        operands.append(start)
-        targets = start.shape[0]
+    hbm = pl.BlockSpec(memory_space=pl.ANY)
+    flat = [part for parts in left_sources for part in parts]
     return pl.pallas_call(
-        make_pair_kernel(start is not None, right_pick, len(left_lists), len(right_lists)),
+        make_pair_kernel(right_pick, [tuple(range(len(parts))) for parts in left_sources]),
         out_shape=jax.ShapeDtypeStruct((targets, block_size, block_size), jnp.float32),
-        in_specs=[smem] * 5 + [vmem] * (len(left_lists) + len(right_lists))
-        + [pl.BlockSpec(memory_space=pl.ANY)] * (start is not None),
-        out_specs=vmem,
+        in_specs=[smem] * 5 + [hbm] * (len(flat) + len(right_lists)),
+        out_specs=pl.BlockSpec(memory_space=pltpu.VMEM),
+        scratch_shapes=[
+            pltpu.VMEM((len(left_sources), list_cap, block_size, block_size), jnp.bfloat16),
+            pltpu.VMEM((len(right_lists), list_cap, block_size, block_size), jnp.bfloat16),
+            pltpu.SemaphoreType.DMA((2 + len(flat),)),
+        ],
         compiler_params=pltpu.CompilerParams(vmem_limit_bytes=60 * 1024 * 1024),
-    )(*operands)
+    )(slots_left, slots_right, counts, left_ids, right_ids, *flat, *right_lists)
 
 
 def shifted(value, axis, steps):
@@ -108,21 +139,17 @@
         return (jnp.take(slots_left_all, piece, axis=0), jnp.take(slots_right_all, piece, axis=0),
                 jnp.take(counts_all, piece, axis=0))
 
-    right_lists = (own_right[0], other_right[0])
-    right_id_stack = jnp.stack([own_right[1], other_right[1]])
-    sl, sr, cn = pieces_for([0])
-    totals = pair_products(sl, sr, cn, own_left[1][None], own_right[1][None],
-                           (own_left[0],), (own_right[0],), (0,), targets=targets)
-    totals, from_below, from_above = lax.optimization_barrier((totals, from_below, from_above))
     half = left_cap // 2
     far_low = shifted(jax.tree.map(lambda a: a[:half], from_below), "row", 1)
     far_high = shifted(jax.tree.map(lambda a: a[half:], from_above), "row", -1)
-    sl, sr, cn = pieces_for([-1, 1, 2])
-    far = jax.tree.map(lambda a, b: jnp.concatenate([a, b]), far_low, far_high)
-    left_id_stack = jnp.stack([from_below[1], from_above[1], far[1]])
+    far_ids = jnp.concatenate([far_low[1], far_high[1]])
+    sl, sr, cn = pieces_for([0, -1, 1, 2])
+    left_id_stack = jnp.stack([own_left[1], from_below[1], from_above[1], far_ids])
+    right_id_stack = jnp.stack([own_right[1], other_right[1]])
     totals = pair_products(sl, sr, cn, left_id_stack, right_id_stack,
-                           (from_below[0], from_above[0], far[0]), right_lists, (1, 1, 0),
-                           start=totals)
+                           ((own_left[0],), (from_below[0],), (from_above[0],),
+                            (far_low[0], far_high[0])),
+                           (own_right[0], other_right[0]), (0, 1, 1, 0), targets)
     owned = lax.psum_scatter(totals, "layer", scatter_dimension=0, tiled=True)
     return owned.reshape(1, 1, -1, block_size, block_size)
 

time: 215 us -> 211 us (0.981)
  waiting for transfers between devices: 146 us -> 165 us
  Pallas kernels: 32.6 us -> 16.2 us
  other arithmetic: 6.9 us -> 3.11 us
    ppermute x10, waiting for transfers between devices: 30.4 us -> 49.3 us  [shifted(): return lax.ppermute(value, axis, pairs)]
    pallas_call x2 -> x1, Pallas kernels: 32.6 us -> 16.2 us  [pair_products(): pl.pallas_call(make_pair_kernel(right_pick, [tuple(range(len(parts))) for...]
    concatenate x1 -> x0, other arithmetic: 2.4 us -> none  [on_device(): far = jax.tree.map(lambda a, b: jnp.concatenate([a, b]), far_low, far_high)]
  transfers between devices with their start and end apart: 11 -> 11, of which waited for: 5 -> 4; matrix products, arithmetic and copies ran while one was open for 5% -> 3% of each run, Pallas kernels for 6% -> 0%
where the time goes in v7:
time: 211 us; the launch traced here: 210 us
  waiting for transfers between devices  165 us (78%)
  Pallas kernels  16.2 us (8%)
  between operations  13.5 us (6%)
  starting transfers between devices  8.35 us (4%)
  local copies, waits for them, and re-layouts  3.96 us (2%)
  other arithmetic  3.11 us (1%)
    reduce_scatter x1, waiting for transfers between devices, on_device(): owned = lax.psum_scatter(totals, 'layer', scatter_dimension=0, tiled=True)  115 us
    ppermute x10, waiting for transfers between devices, shifted(): return lax.ppermute(value, axis, pairs)  49.3 us
    pallas_call x1, Pallas kernels, pair_products(): pl.pallas_call(make_pair_kernel(right_pick, [tuple(range(len(parts))) for...  16.2 us
    ppermute x10, starting transfers between devices, shifted(): return lax.ppermute(value, axis, pairs)  8.35 us
  transfers between devices with their start and end apart: 11, of which 4 were waited for; matrix products, arithmetic and copies ran while one was open for 3% of the time, Pallas kernels for 0%

profile of v7, /device:TPU:26, one launch (start us, length us, event | category | flops | bytes accessed | tf_op | source)
XLA Modules:
  0.0 209.6 jit_solution(16561133191407619362)
XLA Ops:
  6.5 0.0 copy-start
  6.5 0.0 reduce-scatter.2.cloned.1.call-start
  6.5 0.5 collective-permute-start.6
  7.1 1.5 collective-permute-start.5
  8.6 0.0 collective-permute-start.9
  8.6 0.5 collective-permute-start.4
  9.1 1.3 collective-permute-start.1
  10.3 0.7 compare_and_fusion
  11.0 0.0 copy-start.1
  11.0 0.0 copy-start.4
  11.0 0.0 copy-start.6
  11.1 0.0 copy-start.5
  11.1 31.8 %collective-permute-done.6.refs_2_ = bf16[48,128,128]{2,1,0:T(8,128)(2,1)S(1)} collective-permute-done((bf16[48,128,128]{2,1,0:T(8,128)(2,1)}, bf16[48,128,128]{2,1,0:T(8,128)(2,1)S(1)}, u32[]{:S(2)}, u32[]{:S(2)}) %collective-permute-start.6) | collective-permute-done | bytes 1572896 | tf_op jit(solution)/shard_map/ppermute | solution.py:114
  42.9 1.0 slice.23
  43.9 0.9 collective-permute-start.8
  44.8 0.0 collective-permute-done.5.refs_1_
  44.8 1.1 slice.22
  45.9 0.0 copy-done.2
  45.9 1.1 collective-permute-start.7
  47.0 0.0 copy-done.1
  47.0 0.6 gather_fusion
  47.7 0.0 copy-done
  47.7 0.6 gather_fusion.2
  48.2 0.0 copy-done.4
  48.2 0.6 gather_fusion.1
  48.8 0.7 broadcast_select_fusion
  49.5 0.5 broadcast_select_fusion.2.counts
  50.0 0.0 collective-permute-done.1
  50.0 0.0 copy-done.6
  50.0 1.9 collective-permute-start
  51.9 0.1 slice.13
  51.9 0.0 collective-permute-done.4
  51.9 0.6 collective-permute-start.3
  52.6 13.6 %collective-permute-done = s32[48]{0:T(128)S(1)} collective-permute-done((s32[48]{0:T(128)S(1)}, s32[48]{0:T(128)S(1)}, u32[]{:S(2)}, u32[]{:S(2)}) %collective-permute-start) | collective-permute-done | bytes 224 | tf_op jit(solution)/shard_map/ppermute | solution.py:114
  66.2 0.0 collective-permute-start.2
  66.2 0.0 copy-done.5
  66.2 0.6 pad_add_fusion.1.right_ids
  66.8 0.0 collective-permute-done.3
  66.8 3.9 %collective-permute-done.2 = s32[24]{0:T(128)S(1)} collective-permute-done((s32[24]{0:T(128)S(1)}, s32[24]{0:T(128)S(1)}, u32[]{:S(2)}, u32[]{:S(2)}) %collective-permute-start.2) | collective-permute-done | bytes 128 | tf_op jit(solution)/shard_map/ppermute | solution.py:114
  70.7 0.1 add_bitcast_fusion
  70.7 0.6 pad_add_fusion.left_ids
  71.3 0.0 collective-permute-done.9.refs_6_
  71.3 0.0 collective-permute-done.8.refs_4_
  71.3 0.0 collective-permute-done.7.refs_3_
  71.4 0.0 copy-done.3
  71.4 16.2 %shard_map.82 = f32[256,128,128]{2,1,0:T(8,128)} custom-call(s32[4,192]{1,0:T(4,128)} %get-tuple-element.9.slots_left, s32[4,192]{1,0:T(4,128)} %get-tuple-element.8.slots_right, s32[4]{0:T(128)} %broadcast_select_fusion.2.counts, s32[4,48]{1,0:T(4,128)} %pad_add_fusion.left_ids, s32[2,48]{1,0:T(2,128)} %pad_add_fusion.1.right_ids, ...), custom_call_target="tpu_custom_call" | custom-call | tf_op jit(solution)/shard_map/pallas_call | solution.py:97
  87.6 0.0 reduce-scatter.2.cloned.1.call-update
  87.6 115.2 %reduce-scatter.2.cloned.1.call-done = f32[16,128,128]{2,1,0:T(8,128)} async-done(((f32[256,128,128]{2,1,0:T(8,128)}), f32[16,128,128]{2,1,0:T(8,128)}) %reduce-scatter.2.cloned.1.call-update) | async-done | bytes 1048592 | tf_op jit(solution)/shard_map/reduce_scatter | solution.py:153
  (3 shorter events, 0.0 us)
Async XLA Ops:
  6.5 41.1 %copy-start = (s32[1,1,1,4,192]{4,3,2,1,0:T(4,128)S(1)}, s32[1,1,1,4,192]{4,3,2,1,0:T(4,128)}, u32[]{:S(2)}) copy-start(s32[1,1,1,4,192]{4,3,2,1,0:T(4,128)} %param.15) | copy-start | bytes 9220
  6.5 196.3 %reduce-scatter.2.cloned.1.call-start = ((), (), s32[]{:S(2)}) async-start(), calls=%async_computation.1 | async-start | bytes 17825792 | tf_op jit(solution)/shard_map/reduce_scatter | solution.py:153
  6.5 36.4 %collective-permute-start.6 = (bf16[48,128,128]{2,1,0:T(8,128)(2,1)}, bf16[48,128,128]{2,1,0:T(8,128)(2,1)S(1)}, u32[]{:S(2)}, u32[]{:S(2)}) collective-permute-start(bf16[48,128,128]{2,1,0:T(8,128)(2,1)} %bitcast.18), channel_id=1, source_target_pairs={{0,96},{32,0},{64,32},{96,64},{1,97},{33,1},{65,33},{97,65},{2,98}... | collective-permute-start | bytes 4718600 | tf_op jit(solution)/shard_map/ppermute | solution.py:114
  7.1 37.8 %collective-permute-start.5 = (bf16[48,128,128]{2,1,0:T(8,128)(2,1)}, bf16[48,128,128]{2,1,0:T(8,128)(2,1)S(1)}, u32[]{:S(2)}, u32[]{:S(2)}) collective-permute-start(bf16[48,128,128]{2,1,0:T(8,128)(2,1)} %bitcast.19), channel_id=1, source_target_pairs={{0,32},{32,64},{64,96},{96,0},{1,33},{33,65},{65,97},{97,1},{2,34}... | collective-permute-start | bytes 4718600 | tf_op jit(solution)/shard_map/ppermute | solution.py:114
  8.6 62.8 %collective-permute-start.9 = (bf16[48,128,128]{2,1,0:T(8,128)(2,1)}, bf16[48,128,128]{2,1,0:T(8,128)(2,1)}, u32[]{:S(2)}, u32[]{:S(2)}) collective-permute-start(bf16[48,128,128]{2,1,0:T(8,128)(2,1)} %bitcast.21), channel_id=1, source_target_pairs={{0,16},{16,0},{1,17},{17,1},{2,18},{18,2},{3,19},{19,3},{4,20},{20... | collective-permute-start | bytes 4718600 | tf_op jit(solution)/shard_map/ppermute | solution.py:114
  8.6 43.4 %collective-permute-start.4 = (s32[48]{0:T(128)}, s32[48]{0:T(128)S(1)}, u32[]{:S(2)}, u32[]{:S(2)}) collective-permute-start(s32[48]{0:T(128)} %bitcast.24), channel_id=1, source_target_pairs={{0,16},{16,0},{1,17},{17,1},{2,18},{18,2},{3,19},{19,3},{4,20},{20... | collective-permute-start | bytes 584 | tf_op jit(solution)/shard_map/ppermute | solution.py:114
  9.1 40.9 %collective-permute-start.1 = (s32[48]{0:T(128)}, s32[48]{0:T(128)S(1)}, u32[]{:S(2)}, u32[]{:S(2)}) collective-permute-start(s32[48]{0:T(128)} %bitcast.27), channel_id=1, source_target_pairs={{0,96},{32,0},{64,32},{96,64},{1,97},{33,1},{65,33},{97,65},{2,98}... | collective-permute-start | bytes 584 | tf_op jit(solution)/shard_map/ppermute | solution.py:114
  11.0 36.0 %copy-start.1 = (s32[1,1,1,4]{3,2,1,0:T(1,128)S(1)}, s32[1,1,1,4]{3,2,1,0:T(1,128)}, u32[]{:S(2)}) copy-start(s32[1,1,1,4]{3,2,1,0:T(1,128)} %param.16) | copy-start | bytes 52
  11.0 37.2 %copy-start.4 = (s32[1,1,1,4,192]{4,3,2,1,0:T(4,128)S(1)}, s32[1,1,1,4,192]{4,3,2,1,0:T(4,128)}, u32[]{:S(2)}) copy-start(s32[1,1,1,4,192]{4,3,2,1,0:T(4,128)} %param.14) | copy-start | bytes 9220
  11.0 38.9 %copy-start.6 = (s32[1,1,1,48]{3,2,1,0:T(1,128)S(1)}, s32[1,1,1,48]{3,2,1,0:T(1,128)}, u32[]{:S(2)}) copy-start(s32[1,1,1,48]{3,2,1,0:T(1,128)} %param.11) | copy-start | bytes 580
  11.1 55.1 %copy-start.5 = (s32[1,1,1,48]{3,2,1,0:T(1,128)S(1)}, s32[1,1,1,48]{3,2,1,0:T(1,128)}, u32[]{:S(2)}) copy-start(s32[1,1,1,48]{3,2,1,0:T(1,128)} %param.13) | copy-start | bytes 580
  42.9 3.0 %copy-start.2 = (bf16[48,128,128]{2,1,0:T(8,128)(2,1)}, bf16[48,128,128]{2,1,0:T(8,128)(2,1)S(1)}, u32[]{:S(2)}) copy-start(bf16[48,128,128]{2,1,0:T(8,128)(2,1)S(1)} %collective-permute-done.6.refs_2_) | copy-start | bytes 4718596
  43.9 27.4 %collective-permute-start.8 = (bf16[24,128,128]{2,1,0:T(8,128)(2,1)}, bf16[24,128,128]{2,1,0:T(8,128)(2,1)}, u32[]{:S(2)}, u32[]{:S(2)}) collective-permute-start(bf16[24,128,128]{2,1,0:T(8,128)(2,1)} %slice.23), channel_id=1, source_target_pairs={{0,96},{32,0},{64,32},{96,64},{1,97},{33,1},{65,33},{97,65},{2,98}... | collective-permute-start | bytes 2359304 | tf_op jit(solution)/shard_map/ppermute | solution.py:114
  44.8 26.5 %copy-start.3 = (bf16[48,128,128]{2,1,0:T(8,128)(2,1)}, bf16[48,128,128]{2,1,0:T(8,128)(2,1)S(1)}, u32[]{:S(2)}) copy-start(bf16[48,128,128]{2,1,0:T(8,128)(2,1)S(1)} %collective-permute-done.5.refs_1_) | copy-start | bytes 4718596
  45.9 25.4 %collective-permute-start.7 = (bf16[24,128,128]{2,1,0:T(8,128)(2,1)}, bf16[24,128,128]{2,1,0:T(8,128)(2,1)}, u32[]{:S(2)}, u32[]{:S(2)}) collective-permute-start(bf16[24,128,128]{2,1,0:T(8,128)(2,1)} %slice.22), channel_id=1, source_target_pairs={{0,32},{32,64},{64,96},{96,0},{1,33},{33,65},{65,97},{97,1},{2,34}... | collective-permute-start | bytes 2359304 | tf_op jit(solution)/shard_map/ppermute | solution.py:114
  50.0 16.2 %collective-permute-start = (s32[48]{0:T(128)S(1)}, s32[48]{0:T(128)S(1)}, u32[]{:S(2)}, u32[]{:S(2)}) collective-permute-start(s32[48]{0:T(128)S(1)} %bitcast.28), channel_id=1, source_target_pairs={{0,32},{32,64},{64,96},{96,0},{1,33},{33,65},{65,97},{97,1},{2,34}... | collective-permute-start | bytes 584 | tf_op jit(solution)/shard_map/ppermute | solution.py:114
  51.9 14.8 %collective-permute-start.3 = (s32[24]{0:T(128)S(1)}, s32[24]{0:T(128)S(1)}, u32[]{:S(2)}, u32[]{:S(2)}) collective-permute-start(s32[24]{0:T(128)S(1)} %slice.13), channel_id=1, source_target_pairs={{0,96},{32,0},{64,32},{96,64},{1,97},{33,1},{65,33},{97,65},{2,98}... | collective-permute-start | bytes 296 | tf_op jit(solution)/shard_map/ppermute | solution.py:114
  66.2 4.5 %collective-permute-start.2 = (s32[24]{0:T(128)S(1)}, s32[24]{0:T(128)S(1)}, u32[]{:S(2)}, u32[]{:S(2)}) collective-permute-start(s32[24]{0:T(128)S(1)} %bitcast.31), channel_id=1, source_target_pairs={{0,32},{32,64},{64,96},{96,0},{1,33},{33,65},{65,97},{97,1},{2,34}... | collective-permute-start | bytes 296 | tf_op jit(solution)/shard_map/ppermute | solution.py:114
Sparse Core Ops, SparseCore 0:
  87.8 114.9 reduce-scatter.1

commit v8 on v7

--- a/solution.py
+++ b/solution.py
@@ -126,8 +126,9 @@
     own_left = (left_blocks.reshape(left_cap, block_size, block_size), left_rows.reshape(left_cap))
     own_right = (right_blocks.reshape(right_cap, block_size, block_size), right_cols.reshape(right_cap))
 
-    from_below = shifted(own_left, "row", 1)
-    from_above = shifted(own_left, "row", -1)
+    left_ids_all = lax.all_gather(own_left[1], "row")
+    from_below = shifted(own_left[0], "row", 1)
+    from_above = shifted(own_left[0], "row", -1)
     other_right = shifted(own_right, "col", 1)
 
     slots_left_all = pair_left.reshape(piece_count, -1)
@@ -140,15 +141,14 @@
                 jnp.take(counts_all, piece, axis=0))
 
     half = left_cap // 2
-    far_low = shifted(jax.tree.map(lambda a: a[:half], from_below), "row", 1)
-    far_high = shifted(jax.tree.map(lambda a: a[half:], from_above), "row", -1)
-    far_ids = jnp.concatenate([far_low[1], far_high[1]])
+    far_low = shifted(from_below[:half], "row", 1)
+    far_high = shifted(from_above[half:], "row", -1)
     sl, sr, cn = pieces_for([0, -1, 1, 2])
-    left_id_stack = jnp.stack([own_left[1], from_below[1], from_above[1], far_ids])
+    offsets = jnp.array([0, -1, 1, 2], jnp.int32)
+    left_id_stack = jnp.take(left_ids_all, (row_here + offsets) % piece_count, axis=0)
     right_id_stack = jnp.stack([own_right[1], other_right[1]])
     totals = pair_products(sl, sr, cn, left_id_stack, right_id_stack,
-                           ((own_left[0],), (from_below[0],), (from_above[0],),
-                            (far_low[0], far_high[0])),
+                           ((own_left[0],), (from_below,), (from_above,), (far_low, far_high)),
                            (own_right[0], other_right[0]), (0, 1, 1, 0), targets)
     owned = lax.psum_scatter(totals, "layer", scatter_dimension=0, tiled=True)
     return owned.reshape(1, 1, -1, block_size, block_size)

time: 211 us -> 211 us (level)
  blocking collectives: 0 us -> 21.9 us
  waiting for transfers between devices: 165 us -> 145 us
  starting transfers between devices: 8.35 us -> 4.56 us
    all_gather x0 -> x1, blocking collectives: none -> 21.9 us  [on_device(): left_ids_all = lax.all_gather(own_left[1], 'row')]
    ppermute x10 -> x6, waiting for transfers between devices: 49.3 us -> 33.1 us  [shifted(): return lax.ppermute(value, axis, pairs)]
    ppermute x10 -> x6, starting transfers between devices: 8.35 us -> 4.56 us  [shifted(): return lax.ppermute(value, axis, pairs)]
    reduce_scatter x1, waiting for transfers between devices: 115 us -> 112 us  [on_device(): owned = lax.psum_scatter(totals, 'layer', scatter_dimension=0, tiled=True)]
  transfers between devices with their start and end apart: 11 -> 7, of which waited for: 4 -> 2; matrix products, arithmetic and copies ran while one was open for 3% -> 4% of each run, Pallas kernels for 0% -> 0%
where the time goes in v8:
time: 211 us; the launch traced here: 210 us
  waiting for transfers between devices  145 us (69%)
  blocking collectives  21.9 us (10%)
  Pallas kernels  17.8 us (8%)
  between operations  13.5 us (6%)
  starting transfers between devices  4.56 us (2%)
  local copies, waits for them, and re-layouts  4.49 us (2%)
  other arithmetic  3.1 us (1%)
    reduce_scatter x1, waiting for transfers between devices, on_device(): owned = lax.psum_scatter(totals, 'layer', scatter_dimension=0, tiled=True)  112 us
    ppermute x6, waiting for transfers between devices, shifted(): return lax.ppermute(value, axis, pairs)  33.1 us
    all_gather x1, blocking collectives, on_device(): left_ids_all = lax.all_gather(own_left[1], 'row')  21.9 us
    pallas_call x1, Pallas kernels, pair_products(): pl.pallas_call(make_pair_kernel(right_pick, [tuple(range(len(parts))) for...  17.8 us
    ppermute x6, starting transfers between devices, shifted(): return lax.ppermute(value, axis, pairs)  4.56 us
  transfers between devices with their start and end apart: 7, of which 2 were waited for; matrix products, arithmetic and copies ran while one was open for 4% of the time, Pallas kernels for 0%

profile of v8, /device:TPU:26, one launch (start us, length us, event | category | flops | bytes accessed | tf_op | source)
XLA Modules:
  0.0 210.1 jit_solution(8339386661995875211)
XLA Ops:
  6.5 0.0 copy-start
  6.5 0.0 reduce-scatter.2.cloned.1.call-start
  6.5 0.5 collective-permute-start.2
  7.1 1.5 collective-permute-start.1
  8.6 0.0 collective-permute-start.5
  8.6 0.5 collective-permute-start
  9.1 0.7 compare_and_fusion.1
  9.8 0.0 copy-start.1
  9.8 0.0 copy-start.4
  9.8 0.0 copy-start.5
  9.8 0.0 copy-start.6
  9.8 33.1 %collective-permute-done.2.refs_2_ = bf16[48,128,128]{2,1,0:T(8,128)(2,1)S(1)} collective-permute-done((bf16[48,128,128]{2,1,0:T(8,128)(2,1)}, bf16[48,128,128]{2,1,0:T(8,128)(2,1)S(1)}, u32[]{:S(2)}, u32[]{:S(2)}) %collective-permute-start.2) | collective-permute-done | bytes 1572896 | tf_op jit(solution)/shard_map/ppermute | solution.py:114
  42.9 0.0 copy-start.2
  42.9 1.1 slice.17
  44.0 0.9 collective-permute-start.4
  44.9 0.0 collective-permute-done.1.refs_1_
  44.9 0.0 copy-start.3
  44.9 1.0 slice.16
  45.9 0.0 copy-done.2
  45.9 1.1 collective-permute-start.3
  47.1 0.0 copy-done.1
  47.1 0.6 gather_fusion
  47.7 0.0 copy-done
  47.7 0.6 gather_fusion.3
  48.3 0.0 copy-done.4
  48.3 0.6 gather_fusion.2
  48.8 0.0 copy-done.5
  48.8 21.9 %all-gather = s32[4,1,1,48]{3,2,1,0:T(1,128)S(1)} all-gather(s32[1,1,1,48]{3,2,1,0:T(1,128)S(1)} %copy-done.5), channel_id=2, replica_groups=mesh['row'=4,'col'=2,'layer'=16] {'row'}, dimensions={0}, use_global_device_ids=true | all-gather | bytes 960 | tf_op jit(solution)/shard_map/all_gather | solution.py:129
  70.7 0.6 gather_fusion.1
  71.3 0.6 broadcast_select_fusion.2.left_ids
  71.9 0.7 broadcast_select_fusion
  72.5 0.6 broadcast_select_fusion.3.counts
  73.1 0.0 collective-permute-done
  73.1 0.0 copy-done.6
  73.1 0.6 pad_add_fusion.right_ids
  73.7 0.0 collective-permute-done.5.refs_6_
  73.7 0.0 collective-permute-done.4.refs_4_
  73.7 0.0 collective-permute-done.3.refs_3_
  73.7 0.0 copy-done.3
  73.7 17.8 %shard_map.91 = f32[256,128,128]{2,1,0:T(8,128)} custom-call(s32[4,192]{1,0:T(4,128)} %get-tuple-element.13.slots_left, s32[4,192]{1,0:T(4,128)} %get-tuple-element.12.slots_right, s32[4]{0:T(128)} %broadcast_select_fusion.3.counts, s32[4,48]{1,0:T(4,128)} %broadcast_select_fusion.2.left_ids, s32[2,48]{1,0:T(2,128)} %pad_add_fusion.right_ids, ...), custom_call_target="tpu_custom_call" | custom-call | tf_op jit(solution)/shard_map/pallas_call | solution.py:97
  91.5 0.0 reduce-scatter.2.cloned.1.call-update
  91.5 111.7 %reduce-scatter.2.cloned.1.call-done = f32[16,128,128]{2,1,0:T(8,128)} async-done(((f32[256,128,128]{2,1,0:T(8,128)}), f32[16,128,128]{2,1,0:T(8,128)}) %reduce-scatter.2.cloned.1.call-update) | async-done | bytes 1048592 | tf_op jit(solution)/shard_map/reduce_scatter | solution.py:153
  (2 shorter events, 0.0 us)
Async XLA Ops:
  6.5 41.2 %copy-start = (s32[1,1,1,4,192]{4,3,2,1,0:T(4,128)S(1)}, s32[1,1,1,4,192]{4,3,2,1,0:T(4,128)}, u32[]{:S(2)}) copy-start(s32[1,1,1,4,192]{4,3,2,1,0:T(4,128)} %param.16) | copy-start | bytes 9220
  6.5 196.7 %reduce-scatter.2.cloned.1.call-start = ((), (), s32[]{:S(2)}) async-start(), calls=%async_computation.1 | async-start | bytes 17825792 | tf_op jit(solution)/shard_map/reduce_scatter | solution.py:153
  6.5 36.3 %collective-permute-start.2 = (bf16[48,128,128]{2,1,0:T(8,128)(2,1)}, bf16[48,128,128]{2,1,0:T(8,128)(2,1)S(1)}, u32[]{:S(2)}, u32[]{:S(2)}) collective-permute-start(bf16[48,128,128]{2,1,0:T(8,128)(2,1)} %bitcast.12), channel_id=1, source_target_pairs={{0,96},{32,0},{64,32},{96,64},{1,97},{33,1},{65,33},{97,65},{2,98}... | collective-permute-start | bytes 4718600 | tf_op jit(solution)/shard_map/ppermute | solution.py:114
  7.1 37.8 %collective-permute-start.1 = (bf16[48,128,128]{2,1,0:T(8,128)(2,1)}, bf16[48,128,128]{2,1,0:T(8,128)(2,1)S(1)}, u32[]{:S(2)}, u32[]{:S(2)}) collective-permute-start(bf16[48,128,128]{2,1,0:T(8,128)(2,1)} %bitcast.13), channel_id=1, source_target_pairs={{0,32},{32,64},{64,96},{96,0},{1,33},{33,65},{65,97},{97,1},{2,34}... | collective-permute-start | bytes 4718600 | tf_op jit(solution)/shard_map/ppermute | solution.py:114
  8.6 65.1 %collective-permute-start.5 = (bf16[48,128,128]{2,1,0:T(8,128)(2,1)}, bf16[48,128,128]{2,1,0:T(8,128)(2,1)}, u32[]{:S(2)}, u32[]{:S(2)}) collective-permute-start(bf16[48,128,128]{2,1,0:T(8,128)(2,1)} %bitcast.15), channel_id=1, source_target_pairs={{0,16},{16,0},{1,17},{17,1},{2,18},{18,2},{3,19},{19,3},{4,20},{20... | collective-permute-start | bytes 4718600 | tf_op jit(solution)/shard_map/ppermute | solution.py:114
  8.6 64.5 %collective-permute-start = (s32[48]{0:T(128)}, s32[48]{0:T(128)S(1)}, u32[]{:S(2)}, u32[]{:S(2)}) collective-permute-start(s32[48]{0:T(128)} %bitcast.19), channel_id=1, source_target_pairs={{0,16},{16,0},{1,17},{17,1},{2,18},{18,2},{3,19},{19,3},{4,20},{20... | collective-permute-start | bytes 584 | tf_op jit(solution)/shard_map/ppermute | solution.py:114
  9.8 37.3 %copy-start.1 = (s32[1,1,1,4]{3,2,1,0:T(1,128)S(1)}, s32[1,1,1,4]{3,2,1,0:T(1,128)}, u32[]{:S(2)}) copy-start(s32[1,1,1,4]{3,2,1,0:T(1,128)} %param.17) | copy-start | bytes 52
  9.8 38.5 %copy-start.4 = (s32[1,1,1,4,192]{4,3,2,1,0:T(4,128)S(1)}, s32[1,1,1,4,192]{4,3,2,1,0:T(4,128)}, u32[]{:S(2)}) copy-start(s32[1,1,1,4,192]{4,3,2,1,0:T(4,128)} %param.15) | copy-start | bytes 9220
  9.8 39.1 %copy-start.5 = (s32[1,1,1,48]{3,2,1,0:T(1,128)S(1)}, s32[1,1,1,48]{3,2,1,0:T(1,128)}, u32[]{:S(2)}) copy-start(s32[1,1,1,48]{3,2,1,0:T(1,128)} %param.12) | copy-start | bytes 580
  9.8 63.3 %copy-start.6 = (s32[1,1,1,48]{3,2,1,0:T(1,128)S(1)}, s32[1,1,1,48]{3,2,1,0:T(1,128)}, u32[]{:S(2)}) copy-start(s32[1,1,1,48]{3,2,1,0:T(1,128)} %param.14) | copy-start | bytes 580
  42.9 3.1 %copy-start.2 = (bf16[48,128,128]{2,1,0:T(8,128)(2,1)}, bf16[48,128,128]{2,1,0:T(8,128)(2,1)S(1)}, u32[]{:S(2)}) copy-start(bf16[48,128,128]{2,1,0:T(8,128)(2,1)S(1)} %collective-permute-done.2.refs_2_) | copy-start | bytes 4718596
  44.0 29.7 %collective-permute-start.4 = (bf16[24,128,128]{2,1,0:T(8,128)(2,1)}, bf16[24,128,128]{2,1,0:T(8,128)(2,1)}, u32[]{:S(2)}, u32[]{:S(2)}) collective-permute-start(bf16[24,128,128]{2,1,0:T(8,128)(2,1)} %slice.17), channel_id=1, source_target_pairs={{0,96},{32,0},{64,32},{96,64},{1,97},{33,1},{65,33},{97,65},{2,98}... | collective-permute-start | bytes 2359304 | tf_op jit(solution)/shard_map/ppermute | solution.py:114
  44.9 28.8 %copy-start.3 = (bf16[48,128,128]{2,1,0:T(8,128)(2,1)}, bf16[48,128,128]{2,1,0:T(8,128)(2,1)S(1)}, u32[]{:S(2)}) copy-start(bf16[48,128,128]{2,1,0:T(8,128)(2,1)S(1)} %collective-permute-done.1.refs_1_) | copy-start | bytes 4718596
  45.9 27.8 %collective-permute-start.3 = (bf16[24,128,128]{2,1,0:T(8,128)(2,1)}, bf16[24,128,128]{2,1,0:T(8,128)(2,1)}, u32[]{:S(2)}, u32[]{:S(2)}) collective-permute-start(bf16[24,128,128]{2,1,0:T(8,128)(2,1)} %slice.16), channel_id=1, source_target_pairs={{0,32},{32,64},{64,96},{96,0},{1,33},{33,65},{65,97},{97,1},{2,34}... | collective-permute-start | bytes 2359304 | tf_op jit(solution)/shard_map/ppermute | solution.py:114
Sparse Core Ops, SparseCore 0:
  91.7 111.5 reduce-scatter.1

commit v9 on v0

v9 whole, which is shorter than its diff:
```python
import jax
import jax.numpy as jnp
from jax import lax
from jax.experimental import pallas as pl
from jax.experimental.pallas import tpu as pltpu
from jax.sharding import Mesh, PartitionSpec as P

SLAB = 128
ROWS_GROUP = 8
UNROLL = 16


def pair_kernel(slots_left, slots_right, counts, left_ids, right_ids, pick,
                own_left, from_below, from_above, left_pair, own_right, right_pair,
                totals, left_lists, right_lists, sems):
    slab_width = totals.shape[0] // ROWS_GROUP
    block_size = totals.shape[-1]
    copies = [
        [pltpu.make_async_copy(own_left, left_lists.at[0], sems.at[0]),
         pltpu.make_async_copy(own_right, right_lists.at[0], sems.at[1])],
        [pltpu.make_async_copy(from_below, left_lists.at[1], sems.at[2]),
         pltpu.make_async_copy(right_pair.at[pick[0]], right_lists.at[1], sems.at[3])],
        [pltpu.make_async_copy(from_above, left_lists.at[2], sems.at[4])],
        [pltpu.make_async_copy(left_pair.at[pick[1]], left_lists.at[3], sems.at[5])],
    ]
    for group in copies:
        for copy in group:
            copy.start()

    def clear(t, carry):
        totals[t] = jnp.zeros((block_size, block_size), jnp.float32)
        return carry

    lax.fori_loop(0, totals.shape[0], clear, 0)

    for u, v in enumerate((0, 1, 1, 0)):
        for copy in copies[u]:
            copy.wait()

        def one_term(j, u=u, v=v):
            i = slots_left[u, j]
            k = slots_right[u, j]
            t = left_ids[u, i] * slab_width + right_ids[v, k]
            term = jnp.dot(left_lists[u, i], right_lists[v, k], preferred_element_type=jnp.float32)
            return t, term

        def add_group(g, carry, one_term=one_term):
            made = [one_term(g * UNROLL + q) for q in range(UNROLL)]
            for t, term in made:
                totals[t] = totals[t] + term
            return carry

        def add_single(j, carry, one_term=one_term):
            t, term = one_term(j)
            totals[t] = totals[t] + term
            return carry

        count = counts[u]
        groups = count // UNROLL
        lax.fori_loop(0, groups, add_group, 0)
        lax.fori_loop(groups * UNROLL, count, add_single, 0)


def pair_products(scalars, lists, targets):
    own_left = lists[0]
    list_cap, block_size = own_left.shape[0], own_left.shape[-1]
    smem = pl.BlockSpec(memory_space=pltpu.SMEM)
    hbm = pl.BlockSpec(memory_space=pl.ANY)
    return pl.pallas_call(
        pair_kernel,
        out_shape=jax.ShapeDtypeStruct((targets, block_size, block_size), jnp.float32),
        in_specs=[smem] * len(scalars) + [hbm] * len(lists),
        out_specs=pl.BlockSpec(memory_space=pltpu.VMEM),
        scratch_shapes=[
            pltpu.VMEM((4, list_cap, block_size, block_size), jnp.bfloat16),
            pltpu.VMEM((2, list_cap, block_size, block_size), jnp.bfloat16),
            pltpu.SemaphoreType.DMA((6,)),
        ],
        compiler_params=pltpu.CompilerParams(vmem_limit_bytes=60 * 1024 * 1024),
    )(*scalars, *lists)


def shifted(value, axis, steps):
    count = lax.axis_size(axis)
    pairs = [(source, (source + steps) % count) for source in range(count)]
    return lax.ppermute(value, axis, pairs)


ROW = ("row_high", "row_low")
LAYER = ("layer_high", "layer_low")


def on_device(left_blocks, left_rows, right_blocks, right_cols, pair_left, pair_right, pair_count):
    block_size = left_blocks.shape[-1]
    left_cap = left_blocks.shape[3]
    right_cap = right_blocks.shape[3]
    low_count = lax.axis_size("row_low")
    piece_count = lax.axis_size("row_high") * low_count
    slab_width = SLAB // piece_count
    targets = ROWS_GROUP * slab_width
    row_high = lax.axis_index("row_high")
    row_here = row_high * low_count + lax.axis_index("row_low")
    col_here = lax.axis_index("col")
    own_left = left_blocks.reshape(left_cap, block_size, block_size)
    own_right = right_blocks.reshape(right_cap, block_size, block_size)

    from_below = shifted(own_left, ROW, 1)
    from_above = shifted(own_left, ROW, -1)
    left_pair = lax.all_gather(own_left, "row_high")
    right_pair = lax.all_gather(own_right, "col")
    left_ids_all = lax.all_gather(left_rows.reshape(left_cap), ROW)
    right_ids_pair = lax.all_gather(right_cols.reshape(right_cap), "col")

    slots_left_all = pair_left.reshape(piece_count, -1)
    slots_right_all = pair_right.reshape(piece_count, -1)
    counts_all = pair_count.reshape(piece_count)
    offsets = jnp.array([0, -1, 1, 2], jnp.int32)
    piece = (row_here + col_here + offsets) % piece_count
    left_id_stack = jnp.take(left_ids_all, (row_here + offsets) % piece_count, axis=0)
    right_id_stack = jnp.take(right_ids_pair, jnp.stack([col_here, 1 - col_here]), axis=0)
    pick = jnp.stack([1 - col_here, 1 - row_high]).astype(jnp.int32)
    scalars = (jnp.take(slots_left_all, piece, axis=0), jnp.take(slots_right_all, piece, axis=0),
               jnp.take(counts_all, piece, axis=0), left_id_stack, right_id_stack, pick)
    totals = pair_products(scalars, (own_left, from_below, from_above, left_pair, own_right,
                                     right_pair), targets)
    owned = lax.psum_scatter(totals, LAYER, scatter_dimension=0, tiled=True)
    return owned.reshape(1, 1, -1, block_size, block_size)


def solution(mesh):
    devices = mesh.devices
    rows, cols, layers = devices.shape
    split = Mesh(devices.reshape(2, rows // 2, cols, 4, layers // 4),
                 ROW + ("col",) + LAYER)
    in_specs = (
        P(ROW, "col", LAYER, None, None, None),
        P(ROW, "col", LAYER, None),
        P(ROW, "col", LAYER, None, None, None),
        P(ROW, "col", LAYER, None),
        P(ROW, "col", LAYER, None, None),
        P(ROW, "col", LAYER, None, None),
        P(ROW, "col", LAYER, None),
    )
    out_specs = P("col", ROW, LAYER, None, None)
    return jax.shard_map(
        on_device, mesh=split, in_specs=in_specs, out_specs=out_specs, check_vma=False
    )
```

time: 269 us -> 236 us (0.88)
  waiting for transfers between devices: 192 us -> 124 us
  blocking collectives: 9.94 us -> 71.2 us
  Pallas kernels: 49 us -> 17.9 us
    all_gather x2, waiting for transfers between devices: 73.2 us -> 10.5 us  [the longest x1 10.5 us: on_device(): right_pair = lax.all_gather(own_right, 'col')]
    all_gather x2, blocking collectives: 9.94 us -> 71.2 us  [the longest x1 69.4 us: on_device(): left_ids_all = lax.all_gather(left_rows.reshape(left_cap), ROW)]
    pallas_call x1, Pallas kernels: 49 us -> 17.9 us  [pair_products(): pl.pallas_call(pair_kernel, out_shape=jax.ShapeDtypeStruct((targets, bloc...]
    reduce_scatter x1, waiting for transfers between devices: 117 us -> 112 us  [on_device(): owned = lax.psum_scatter(totals, LAYER, scatter_dimension=0, tiled=True)]
  transfers between devices with their start and end apart: 3 -> 5, of which waited for: 3 -> 2; matrix products, arithmetic and copies ran while one was open for 1% -> 3% of each run, Pallas kernels for 0% -> 0%
where the time goes in v9:
time: 236 us; the launch traced here: 235 us
  waiting for transfers between devices  124 us (53%)
  blocking collectives  71.2 us (30%)
  Pallas kernels  17.9 us (8%)
  between operations  13.2 us (6%)
  other arithmetic  3.31 us (1%)
  local copies, waits for them, and re-layouts  2.91 us (1%)
    reduce_scatter x1, waiting for transfers between devices, on_device(): owned = lax.psum_scatter(totals, LAYER, scatter_dimension=0, tiled=True)  112 us
    all_gather x1, blocking collectives, on_device(): left_ids_all = lax.all_gather(left_rows.reshape(left_cap), ROW)  69.4 us
    pallas_call x1, Pallas kernels, pair_products(): pl.pallas_call(pair_kernel, out_shape=jax.ShapeDtypeStruct((targets, bloc...  17.9 us
    all_gather x1, waiting for transfers between devices, on_device(): right_pair = lax.all_gather(own_right, 'col')  10.5 us
  transfers between devices with their start and end apart: 5, of which 2 were waited for; matrix products, arithmetic and copies ran while one was open for 3% of the time, Pallas kernels for 0%

profile of v9, /device:TPU:26, one launch (start us, length us, event | category | flops | bytes accessed | tf_op | source)
XLA Modules:
  0.0 234.9 jit_solution(9431468804777959716)
XLA Ops:
  6.5 0.0 copy-start
  6.5 0.0 copy-start.2
  6.5 0.0 copy-start.6
  6.5 0.0 copy-start.1
  6.5 0.0 copy-start.4
  6.5 0.0 copy-start.7
  6.6 0.0 copy-start.5
  6.6 0.0 all-gather.7.cloned.1.call-start
  6.6 0.7 all-gather.7.cloned.1.call-update
  7.3 0.0 all-gather.9.cloned.1.call-start
  7.3 0.7 all-gather.9.cloned.1.call-update
  8.1 0.0 reduce-scatter.2.cloned.1.call-start
  8.1 0.0 copy-done.2
  8.1 0.6 collective-permute-start.1
  8.7 1.5 collective-permute-start
  10.2 0.0 copy-done.6
  10.2 0.0 copy-done.1
  10.3 0.6 gather_fusion
  10.9 0.0 copy-done
  10.9 0.6 gather_fusion.4
  11.5 0.0 copy-done.4
  11.5 0.6 gather_fusion.3
  12.0 0.0 copy-done.7
  12.0 1.8 all-gather.1
  13.8 0.1 fusion.2
  13.9 0.6 gather_fusion.2
  14.5 0.0 copy-done.5
  14.5 69.4 %all-gather = s32[4,1,1,48]{3,2,1,0:T(1,128)S(1)} all-gather(s32[1,1,1,48]{3,2,1,0:T(1,128)S(1)} %copy-done.5), channel_id=2, replica_groups=mesh['row_high'=2,'row_low'=2,'col'=2,'layer_high'=4,'layer_low'=4] {'ro..., dimensions={0}, use_global_device_ids=true | all-gather | bytes 960 | tf_op jit(solution)/shard_map/all_gather | solution.py:111
  83.9 0.6 gather_fusion.1
  84.4 0.6 pad_add_fusion.pick
  85.0 0.1 compare_and_fusion.1
  85.1 0.5 broadcast_select_fusion.4.counts
  85.7 0.7 broadcast_select_fusion.3.right_ids
  86.3 0.7 broadcast_select_fusion.2.left_ids
  87.0 0.7 broadcast_select_fusion
  87.6 0.0 collective-permute-done.1.from_above
  87.6 0.0 copy-start.3
  87.6 0.0 collective-permute-done.from_below
  87.6 0.0 all-gather.7.cloned.1.call-done
  87.7 10.5 %all-gather.9.cloned.1.call-done = bf16[2,1,1,48,128,128]{5,4,3,2,1,0:T(8,128)(2,1)} async-done(((bf16[1,1,1,48,128,128]{5,4,3,2,1,0:T(8,128)(2,1)}), bf16[2,1,1,48,128,128]{5,4,3,2,1,0:T(8,128)(2,1)}) %all-gather.9.cloned.1.call-update) | async-done | bytes 3145744 | tf_op jit(solution)/shard_map/all_gather | solution.py:110
  98.2 0.0 copy-done.3
  98.2 17.9 %shard_map.82 = f32[256,128,128]{2,1,0:T(8,128)} custom-call(s32[4,192]{1,0:T(4,128)} %get-tuple-element.13.slots_left, s32[4,192]{1,0:T(4,128)} %get-tuple-element.12.slots_right, s32[4]{0:T(128)} %broadcast_select_fusion.4.counts, s32[4,48]{1,0:T(4,128)} %broadcast_select_fusion.2.left_ids, s32[2,48]{1,0:T(2,128)} %broadcast_select_fusion.3.right_ids, ...), custom_call_target="tpu_custom_call" | custom-call | tf_op jit(solution)/shard_map/pallas_call | solution.py:69
  116.1 0.0 reduce-scatter.2.cloned.1.call-update
  116.1 112.2 %reduce-scatter.2.cloned.1.call-done = f32[16,128,128]{2,1,0:T(8,128)} async-done(((f32[256,128,128]{2,1,0:T(8,128)}), f32[16,128,128]{2,1,0:T(8,128)}) %reduce-scatter.2.cloned.1.call-update) | async-done | bytes 1048592 | tf_op jit(solution)/shard_map/reduce_scatter | solution.py:126
  (4 shorter events, 0.0 us)
Async XLA Ops:
  6.5 4.4 %copy-start = (s32[1,1,1,4,192]{4,3,2,1,0:T(4,128)S(1)}, s32[1,1,1,4,192]{4,3,2,1,0:T(4,128)}, u32[]{:S(2)}) copy-start(s32[1,1,1,4,192]{4,3,2,1,0:T(4,128)} %param.15) | copy-start | bytes 9220
  6.5 1.6 copy-start.2
  6.5 3.7 %copy-start.6 = (s32[4]{0:T(128)S(1)}, s32[4]{0:T(128)}, u32[]{:S(2)}) copy-start(s32[4]{0:T(128)} %constant.87.clone) | copy-start | bytes 52
  6.5 3.7 %copy-start.1 = (s32[1,1,1,4]{3,2,1,0:T(1,128)S(1)}, s32[1,1,1,4]{3,2,1,0:T(1,128)}, u32[]{:S(2)}) copy-start(s32[1,1,1,4]{3,2,1,0:T(1,128)} %param.16) | copy-start | bytes 52
  6.5 4.9 %copy-start.4 = (s32[1,1,1,4,192]{4,3,2,1,0:T(4,128)S(1)}, s32[1,1,1,4,192]{4,3,2,1,0:T(4,128)}, u32[]{:S(2)}) copy-start(s32[1,1,1,4,192]{4,3,2,1,0:T(4,128)} %param.14) | copy-start | bytes 9220
  6.5 5.5 %copy-start.7 = (s32[1,1,1,48]{3,2,1,0:T(1,128)S(1)}, s32[1,1,1,48]{3,2,1,0:T(1,128)}, u32[]{:S(2)}) copy-start(s32[1,1,1,48]{3,2,1,0:T(1,128)} %param.13) | copy-start | bytes 580
  6.6 7.9 %copy-start.5 = (s32[1,1,1,48]{3,2,1,0:T(1,128)S(1)}, s32[1,1,1,48]{3,2,1,0:T(1,128)}, u32[]{:S(2)}) copy-start(s32[1,1,1,48]{3,2,1,0:T(1,128)} %param.11) | copy-start | bytes 580
  6.6 81.1 %all-gather.7.cloned.1.call-start = ((), (), s32[]{:S(2)}) async-start(), calls=%async_computation.2 | async-start | bytes 4718592 | tf_op jit(solution)/shard_map/all_gather | solution.py:109
  7.3 90.9 %all-gather.9.cloned.1.call-start = ((), (), s32[]{:S(2)}) async-start(), calls=%async_computation.3 | async-start | bytes 4718592 | tf_op jit(solution)/shard_map/all_gather | solution.py:110
  8.1 220.3 %reduce-scatter.2.cloned.1.call-start = ((), (), s32[]{:S(2)}) async-start(), calls=%async_computation.1 | async-start | bytes 17825792 | tf_op jit(solution)/shard_map/reduce_scatter | solution.py:126
  8.1 79.5 %collective-permute-start.1 = (bf16[48,128,128]{2,1,0:T(8,128)(2,1)S(1)}, bf16[48,128,128]{2,1,0:T(8,128)(2,1)S(1)}, u32[]{:S(2)}, u32[]{:S(2)}) collective-permute-start(bf16[48,128,128]{2,1,0:T(8,128)(2,1)S(1)} %bitcast.20), channel_id=1, source_target_pairs={{0,96},{32,0},{64,32},{96,64},{1,97},{33,1},{65,33},{97,65},{2,98}... | collective-permute-start | bytes 4718600 | tf_op jit(solution)/shard_map/ppermute | solution.py:86
  8.7 78.9 %collective-permute-start = (bf16[48,128,128]{2,1,0:T(8,128)(2,1)S(1)}, bf16[48,128,128]{2,1,0:T(8,128)(2,1)}, u32[]{:S(2)}, u32[]{:S(2)}) collective-permute-start(bf16[48,128,128]{2,1,0:T(8,128)(2,1)S(1)} %bitcast.21), channel_id=1, source_target_pairs={{0,32},{32,64},{64,96},{96,0},{1,33},{33,65},{65,97},{97,1},{2,34}... | collective-permute-start | bytes 4718600 | tf_op jit(solution)/shard_map/ppermute | solution.py:86
  87.6 10.6 %copy-start.3 = (bf16[48,128,128]{2,1,0:T(8,128)(2,1)}, bf16[48,128,128]{2,1,0:T(8,128)(2,1)S(1)}, u32[]{:S(2)}) copy-start(bf16[48,128,128]{2,1,0:T(8,128)(2,1)S(1)} %collective-permute-done.1.from_above) | copy-start | bytes 4718596
Sparse Core Ops, SparseCore 0:
  9.1 70.0 all-gather.6
  80.9 17.2 all-gather.8
  116.2 112.0 reduce-scatter.1

commit v10 on v9

v10 whole, which is shorter than its diff:
```python
import jax
import jax.numpy as jnp
from jax import lax
from jax.experimental import pallas as pl
from jax.experimental.pallas import tpu as pltpu
from jax.sharding import PartitionSpec as P

SLAB = 128
ROWS_GROUP = 8
UNROLL = 16


def pair_kernel(slots_left, slots_right, counts, left_ids, right_ids, pick,
                own_left, from_below, from_above, far_low, far_high, own_right, right_pair,
                totals, left_lists, right_lists, sems):
    half = far_low.shape[0]
    slab_width = totals.shape[0] // ROWS_GROUP
    block_size = totals.shape[-1]
    copies = [
        [pltpu.make_async_copy(own_left, left_lists.at[0], sems.at[0]),
         pltpu.make_async_copy(own_right, right_lists.at[0], sems.at[1])],
        [pltpu.make_async_copy(from_below, left_lists.at[1], sems.at[2]),
         pltpu.make_async_copy(right_pair.at[pick[0]], right_lists.at[1], sems.at[3])],
        [pltpu.make_async_copy(from_above, left_lists.at[2], sems.at[4])],
        [pltpu.make_async_copy(far_low, left_lists.at[3, pl.ds(0, half)], sems.at[5]),
         pltpu.make_async_copy(far_high, left_lists.at[3, pl.ds(half, half)], sems.at[6])],
    ]
    for group in copies:
        for copy in group:
            copy.start()

    def clear(t, carry):
        totals[t] = jnp.zeros((block_size, block_size), jnp.float32)
        return carry

    lax.fori_loop(0, totals.shape[0], clear, 0)

    for u, v in enumerate((0, 1, 1, 0)):
        for copy in copies[u]:
            copy.wait()

        def one_term(j, u=u, v=v):
            i = slots_left[u, j]
            k = slots_right[u, j]
            t = left_ids[u, i] * slab_width + right_ids[v, k]
            term = jnp.dot(left_lists[u, i], right_lists[v, k], preferred_element_type=jnp.float32)
            return t, term

        def add_group(g, carry, one_term=one_term):
            made = [one_term(g * UNROLL + q) for q in range(UNROLL)]
            for t, term in made:
                totals[t] = totals[t] + term
            return carry

        def add_single(j, carry, one_term=one_term):
            t, term = one_term(j)
            totals[t] = totals[t] + term
            return carry

        count = counts[u]
        groups = count // UNROLL
        lax.fori_loop(0, groups, add_group, 0)
        lax.fori_loop(groups * UNROLL, count, add_single, 0)


def pair_products(scalars, lists, targets):
    own_left = lists[0]
    list_cap, block_size = own_left.shape[0], own_left.shape[-1]
    smem = pl.BlockSpec(memory_space=pltpu.SMEM)
    hbm = pl.BlockSpec(memory_space=pl.ANY)
    return pl.pallas_call(
        pair_kernel,
        out_shape=jax.ShapeDtypeStruct((targets, block_size, block_size), jnp.float32),
        in_specs=[smem] * len(scalars) + [hbm] * len(lists),
        out_specs=pl.BlockSpec(memory_space=pltpu.VMEM),
        scratch_shapes=[
            pltpu.VMEM((4, list_cap, block_size, block_size), jnp.bfloat16),
            pltpu.VMEM((2, list_cap, block_size, block_size), jnp.bfloat16),
            pltpu.SemaphoreType.DMA((7,)),
        ],
        compiler_params=pltpu.CompilerParams(vmem_limit_bytes=60 * 1024 * 1024),
    )(*scalars, *lists)


def shifted(value, axis, steps):
    count = lax.axis_size(axis)
    pairs = [(source, (source + steps) % count) for source in range(count)]
    return lax.ppermute(value, axis, pairs)


def on_device(left_blocks, left_rows, right_blocks, right_cols, pair_left, pair_right, pair_count):
    block_size = left_blocks.shape[-1]
    left_cap = left_blocks.shape[3]
    right_cap = right_blocks.shape[3]
    piece_count = lax.axis_size("row")
    slab_width = SLAB // piece_count
    targets = ROWS_GROUP * slab_width
    row_here = lax.axis_index("row")
    col_here = lax.axis_index("col")
    own_left = left_blocks.reshape(left_cap, block_size, block_size)
    own_right = right_blocks.reshape(right_cap, block_size, block_size)
    own_ids = left_rows.reshape(left_cap)

    ids_below = shifted(own_ids, "row", 1)
    ids_above = shifted(own_ids, "row", -1)
    ids_far = shifted(own_ids, "row", 2)
    from_below = shifted(own_left, "row", 1)
    from_above = shifted(own_left, "row", -1)
    right_pair = lax.all_gather(own_right, "col")
    right_ids_pair = lax.all_gather(right_cols.reshape(right_cap), "col")
    half = left_cap // 2
    far_low = shifted(from_below[:half], "row", 1)
    far_high = shifted(from_above[half:], "row", -1)

    slots_left_all = pair_left.reshape(piece_count, -1)
    slots_right_all = pair_right.reshape(piece_count, -1)
    counts_all = pair_count.reshape(piece_count)
    offsets = jnp.array([0, -1, 1, 2], jnp.int32)
    piece = (row_here + col_here + offsets) % piece_count
    left_id_stack = jnp.stack([own_ids, ids_below, ids_above, ids_far])
    right_id_stack = jnp.take(right_ids_pair, jnp.stack([col_here, 1 - col_here]), axis=0)
    pick = jnp.stack([1 - col_here, col_here]).astype(jnp.int32)
    scalars = (jnp.take(slots_left_all, piece, axis=0), jnp.take(slots_right_all, piece, axis=0),
               jnp.take(counts_all, piece, axis=0), left_id_stack, right_id_stack, pick)
    totals = pair_products(scalars, (own_left, from_below, from_above, far_low, far_high,
                                     own_right, right_pair), targets)
    owned = lax.psum_scatter(totals, "layer", scatter_dimension=0, tiled=True)
    return owned.reshape(1, 1, -1, block_size, block_size)


def solution(mesh):
    in_specs = (
        P("row", "col", "layer", None, None, None),
        P("row", "col", "layer", None),
        P("row", "col", "layer", None, None, None),
        P("row", "col", "layer", None),
        P("row", "col", "layer", None, None),
        P("row", "col", "layer", None, None),
        P("row", "col", "layer", None),
    )
    out_specs = P("col", "row", "layer", None, None)
    return jax.shard_map(
        on_device, mesh=mesh, in_specs=in_specs, out_specs=out_specs, check_vma=False
    )
```

time: 236 us -> 206 us (0.87)
  blocking collectives: 71.2 us -> 1.77 us
  waiting for transfers between devices: 124 us -> 154 us
  starting transfers between devices: 2.21 us -> 9.55 us
    all_gather x1 -> x0, blocking collectives: 69.4 us -> none  [on_device(): left_ids_all = lax.all_gather(left_rows.reshape(left_cap), ROW)]
    ppermute x2 -> x7, waiting for transfers between devices: 0.01 us -> 40.7 us  [shifted(): return lax.ppermute(value, axis, pairs)]
    all_gather x1, waiting for transfers between devices: 10.5 us -> 0.01 us  [on_device(): right_pair = lax.all_gather(own_right, 'col')]
    ppermute x2 -> x7, starting transfers between devices: 2.09 us -> 9.48 us  [shifted(): return lax.ppermute(value, axis, pairs)]
  transfers between devices with their start and end apart: 5 -> 9, of which waited for: 2 -> 4; matrix products, arithmetic and copies ran while one was open for 3% -> 4% of each run, Pallas kernels for 0% -> 0%
where the time goes in v10:
time: 206 us; the launch traced here: 204 us
  waiting for transfers between devices  154 us (75%)
  Pallas kernels  18.1 us (9%)
  between operations  13.5 us (7%)
  starting transfers between devices  9.55 us (5%)
  local copies, waits for them, and re-layouts  4.36 us (2%)
  other arithmetic  3.25 us (2%)
    reduce_scatter x1, waiting for transfers between devices, on_device(): owned = lax.psum_scatter(totals, 'layer', scatter_dimension=0, tiled=True)  112 us
    ppermute x7, waiting for transfers between devices, shifted(): return lax.ppermute(value, axis, pairs)  40.7 us
    pallas_call x1, Pallas kernels, pair_products(): pl.pallas_call(pair_kernel, out_shape=jax.ShapeDtypeStruct((targets, bloc...  18.1 us
    ppermute x7, starting transfers between devices, shifted(): return lax.ppermute(value, axis, pairs)  9.48 us
  transfers between devices with their start and end apart: 9, of which 4 were waited for; matrix products, arithmetic and copies ran while one was open for 4% of the time, Pallas kernels for 0%

profile of v10, /device:TPU:26, one launch (start us, length us, event | category | flops | bytes accessed | tf_op | source)
XLA Modules:
  0.0 204.4 jit_solution(13057113077703723249)
XLA Ops:
  6.5 0.0 copy-start
  6.5 0.0 copy-start.5
  6.5 0.0 copy-start.6
  6.5 0.0 copy-start.1
  6.5 0.0 all-gather.4.cloned.1.call-start
  6.6 0.7 all-gather.4.cloned.1.call-update
  7.3 0.0 reduce-scatter.2.cloned.1.call-start
  7.3 0.6 collective-permute-start.4
  7.9 1.5 collective-permute-start.3
  9.4 0.0 copy-done.6
  9.4 3.3 %collective-permute-start.2 = (s32[48]{0:T(128)S(1)}, s32[48]{0:T(128)S(1)}, u32[]{:S(2)}, u32[]{:S(2)}) collective-permute-start(s32[48]{0:T(128)S(1)} %bitcast.25), channel_id=1, source_target_pairs={{0,64},{32,96},{64,0},{96,32},{1,65},{33,97},{65,1},{97,33},{2,66}... | collective-permute-start | bytes 584 | tf_op jit(solution)/shard_map/ppermute | solution.py:88
  12.8 0.2 collective-permute-start.1
  13.0 1.8 collective-permute-start
  14.8 0.0 copy-done.5
  14.8 0.0 copy-done.1
  14.8 0.6 gather_fusion
  15.5 0.1 fusion.1
  15.5 0.5 broadcast_select_fusion.3.counts
  16.1 0.0 copy-start.4
  16.1 0.0 copy-start.7
  16.1 27.7 %collective-permute-done.4.from_above = bf16[48,128,128]{2,1,0:T(8,128)(2,1)S(1)} collective-permute-done((bf16[48,128,128]{2,1,0:T(8,128)(2,1)}, bf16[48,128,128]{2,1,0:T(8,128)(2,1)S(1)}, u32[]{:S(2)}, u32[]{:S(2)}) %collective-permute-start.4) | collective-permute-done | bytes 1572896 | tf_op jit(solution)/shard_map/ppermute | solution.py:88
  43.7 1.0 slice.17
  44.7 0.9 collective-permute-start.6
  45.7 0.0 collective-permute-done.3.from_below
  45.7 1.0 slice.16
  46.7 1.1 collective-permute-start.5
  47.8 0.0 copy-done.2
  47.8 0.0 copy-done
  47.8 0.6 gather_fusion.3
  48.4 0.0 copy-done.4
  48.4 0.6 gather_fusion.2
  48.9 0.0 copy-done.7
  48.9 1.8 all-gather
  50.7 0.6 gather_fusion.1
  51.3 0.1 compare_and_fusion.1
  51.4 0.7 broadcast_select_fusion.2.right_ids
  52.0 0.7 broadcast_select_fusion
  52.7 0.6 pad_add_fusion.1.pick
  53.3 0.0 collective-permute-done.2
  53.3 0.0 collective-permute-done.1
  53.3 0.0 collective-permute-done
  53.3 0.6 pad_add_fusion.left_ids
  53.9 9.5 %collective-permute-done.6.far_high = bf16[24,128,128]{2,1,0:T(8,128)(2,1)} collective-permute-done((bf16[24,128,128]{2,1,0:T(8,128)(2,1)}, bf16[24,128,128]{2,1,0:T(8,128)(2,1)}, u32[]{:S(2)}, u32[]{:S(2)}) %collective-permute-start.6) | collective-permute-done | bytes 786464 | tf_op jit(solution)/shard_map/ppermute | solution.py:88
  63.5 3.5 %collective-permute-done.5.far_low = bf16[24,128,128]{2,1,0:T(8,128)(2,1)} collective-permute-done((bf16[24,128,128]{2,1,0:T(8,128)(2,1)}, bf16[24,128,128]{2,1,0:T(8,128)(2,1)}, u32[]{:S(2)}, u32[]{:S(2)}) %collective-permute-start.5) | collective-permute-done | bytes 786464 | tf_op jit(solution)/shard_map/ppermute | solution.py:88
  67.0 0.0 copy-done.3
  67.0 18.1 %shard_map.82 = f32[256,128,128]{2,1,0:T(8,128)} custom-call(s32[4,192]{1,0:T(4,128)} %get-tuple-element.9.slots_left, s32[4,192]{1,0:T(4,128)} %get-tuple-element.8.slots_right, s32[4]{0:T(128)} %broadcast_select_fusion.3.counts, s32[4,48]{1,0:T(4,128)} %pad_add_fusion.left_ids, s32[2,48]{1,0:T(2,128)} %broadcast_select_fusion.2.right_ids, ...), custom_call_target="tpu_custom_call" | custom-call | tf_op jit(solution)/shard_map/pallas_call | solution.py:71
  85.1 0.0 reduce-scatter.2.cloned.1.call-update
  85.1 112.4 %reduce-scatter.2.cloned.1.call-done = f32[16,128,128]{2,1,0:T(8,128)} async-done(((f32[256,128,128]{2,1,0:T(8,128)}), f32[16,128,128]{2,1,0:T(8,128)}) %reduce-scatter.2.cloned.1.call-update) | async-done | bytes 1048592 | tf_op jit(solution)/shard_map/reduce_scatter | solution.py:127
  (6 shorter events, 0.0 us)
Async XLA Ops:
  6.5 41.3 %copy-start = (s32[1,1,1,4,192]{4,3,2,1,0:T(4,128)S(1)}, s32[1,1,1,4,192]{4,3,2,1,0:T(4,128)}, u32[]{:S(2)}) copy-start(s32[1,1,1,4,192]{4,3,2,1,0:T(4,128)} %param.15) | copy-start | bytes 9220
  6.5 8.2 %copy-start.5 = (s32[4]{0:T(128)S(1)}, s32[4]{0:T(128)}, u32[]{:S(2)}) copy-start(s32[4]{0:T(128)} %constant.67.clone) | copy-start | bytes 52
  6.5 2.9 %copy-start.6 = (s32[1,1,1,48]{3,2,1,0:T(1,128)S(1)}, s32[1,1,1,48]{3,2,1,0:T(1,128)}, u32[]{:S(2)}) copy-start(s32[1,1,1,48]{3,2,1,0:T(1,128)} %param.11) | copy-start | bytes 580
  6.5 8.3 %copy-start.1 = (s32[1,1,1,4]{3,2,1,0:T(1,128)S(1)}, s32[1,1,1,4]{3,2,1,0:T(1,128)}, u32[]{:S(2)}) copy-start(s32[1,1,1,4]{3,2,1,0:T(1,128)} %param.16) | copy-start | bytes 52
  6.5 60.4 %all-gather.4.cloned.1.call-start = ((), (), s32[]{:S(2)}) async-start(), calls=%async_computation.2 | async-start | bytes 4718592 | tf_op jit(solution)/shard_map/all_gather | solution.py:109
  7.3 190.3 %reduce-scatter.2.cloned.1.call-start = ((), (), s32[]{:S(2)}) async-start(), calls=%async_computation.1 | async-start | bytes 17825792 | tf_op jit(solution)/shard_map/reduce_scatter | solution.py:127
  7.3 36.4 %collective-permute-start.4 = (bf16[48,128,128]{2,1,0:T(8,128)(2,1)}, bf16[48,128,128]{2,1,0:T(8,128)(2,1)S(1)}, u32[]{:S(2)}, u32[]{:S(2)}) collective-permute-start(bf16[48,128,128]{2,1,0:T(8,128)(2,1)} %bitcast.14.own_left), channel_id=1, source_target_pairs={{0,96},{32,0},{64,32},{96,64},{1,97},{33,1},{65,33},{97,65},{2,98}... | collective-permute-start | bytes 4718600 | tf_op jit(solution)/shard_map/ppermute | solution.py:88
  7.9 37.8 %collective-permute-start.3 = (bf16[48,128,128]{2,1,0:T(8,128)(2,1)}, bf16[48,128,128]{2,1,0:T(8,128)(2,1)S(1)}, u32[]{:S(2)}, u32[]{:S(2)}) collective-permute-start(bf16[48,128,128]{2,1,0:T(8,128)(2,1)} %bitcast.14.own_left), channel_id=1, source_target_pairs={{0,32},{32,64},{64,96},{96,0},{1,33},{33,65},{65,97},{97,1},{2,34}... | collective-permute-start | bytes 4718600 | tf_op jit(solution)/shard_map/ppermute | solution.py:88
  9.4 43.9 %collective-permute-start.2 = (s32[48]{0:T(128)S(1)}, s32[48]{0:T(128)S(1)}, u32[]{:S(2)}, u32[]{:S(2)}) collective-permute-start(s32[48]{0:T(128)S(1)} %bitcast.25), channel_id=1, source_target_pairs={{0,64},{32,96},{64,0},{96,32},{1,65},{33,97},{65,1},{97,33},{2,66}... | collective-permute-start | bytes 584 | tf_op jit(solution)/shard_map/ppermute | solution.py:88
  12.8 40.6 %collective-permute-start.1 = (s32[48]{0:T(128)S(1)}, s32[48]{0:T(128)S(1)}, u32[]{:S(2)}, u32[]{:S(2)}) collective-permute-start(s32[48]{0:T(128)S(1)} %bitcast.26), channel_id=1, source_target_pairs={{0,96},{32,0},{64,32},{96,64},{1,97},{33,1},{65,33},{97,65},{2,98}... | collective-permute-start | bytes 584 | tf_op jit(solution)/shard_map/ppermute | solution.py:88
  13.0 40.3 %collective-permute-start = (s32[48]{0:T(128)S(1)}, s32[48]{0:T(128)S(1)}, u32[]{:S(2)}, u32[]{:S(2)}) collective-permute-start(s32[48]{0:T(128)S(1)} %bitcast.27), channel_id=1, source_target_pairs={{0,32},{32,64},{64,96},{96,0},{1,33},{33,65},{65,97},{97,1},{2,34}... | collective-permute-start | bytes 584 | tf_op jit(solution)/shard_map/ppermute | solution.py:88
  16.1 32.3 %copy-start.4 = (s32[1,1,1,4,192]{4,3,2,1,0:T(4,128)S(1)}, s32[1,1,1,4,192]{4,3,2,1,0:T(4,128)}, u32[]{:S(2)}) copy-start(s32[1,1,1,4,192]{4,3,2,1,0:T(4,128)} %param.14) | copy-start | bytes 9220
  16.1 32.9 %copy-start.7 = (s32[1,1,1,48]{3,2,1,0:T(1,128)S(1)}, s32[1,1,1,48]{3,2,1,0:T(1,128)}, u32[]{:S(2)}) copy-start(s32[1,1,1,48]{3,2,1,0:T(1,128)} %param.13) | copy-start | bytes 580
  43.7 4.0 %copy-start.2 = (bf16[48,128,128]{2,1,0:T(8,128)(2,1)}, bf16[48,128,128]{2,1,0:T(8,128)(2,1)S(1)}, u32[]{:S(2)}) copy-start(bf16[48,128,128]{2,1,0:T(8,128)(2,1)S(1)} %collective-permute-done.4.from_above) | copy-start | bytes 4718596
  44.7 18.7 %collective-permute-start.6 = (bf16[24,128,128]{2,1,0:T(8,128)(2,1)}, bf16[24,128,128]{2,1,0:T(8,128)(2,1)}, u32[]{:S(2)}, u32[]{:S(2)}) collective-permute-start(bf16[24,128,128]{2,1,0:T(8,128)(2,1)} %slice.17), channel_id=1, source_target_pairs={{0,96},{32,0},{64,32},{96,64},{1,97},{33,1},{65,33},{97,65},{2,98}... | collective-permute-start | bytes 2359304 | tf_op jit(solution)/shard_map/ppermute | solution.py:88
  45.7 21.3 %copy-start.3 = (bf16[48,128,128]{2,1,0:T(8,128)(2,1)}, bf16[48,128,128]{2,1,0:T(8,128)(2,1)S(1)}, u32[]{:S(2)}) copy-start(bf16[48,128,128]{2,1,0:T(8,128)(2,1)S(1)} %collective-permute-done.3.from_below) | copy-start | bytes 4718596
  46.7 20.3 %collective-permute-start.5 = (bf16[24,128,128]{2,1,0:T(8,128)(2,1)}, bf16[24,128,128]{2,1,0:T(8,128)(2,1)}, u32[]{:S(2)}, u32[]{:S(2)}) collective-permute-start(bf16[24,128,128]{2,1,0:T(8,128)(2,1)} %slice.16), channel_id=1, source_target_pairs={{0,32},{32,64},{64,96},{96,0},{1,33},{33,65},{65,97},{97,1},{2,34}... | collective-permute-start | bytes 2359304 | tf_op jit(solution)/shard_map/ppermute | solution.py:88
Sparse Core Ops, SparseCore 0:
  9.0 16.9 all-gather.3
  85.2 112.2 reduce-scatter.1

commit v11 on v10

--- a/solution.py
+++ b/solution.py
@@ -11,17 +11,19 @@
 
 
 def pair_kernel(slots_left, slots_right, counts, left_ids, right_ids, pick,
-                own_left, from_below, from_above, far_low, far_high, own_right, right_pair,
-                totals, left_lists, right_lists, sems):
+                own_left, below_low, below_high, above_low, above_high, far_low, far_high,
+                own_right, right_pair, totals, left_lists, right_lists, sems):
     half = far_low.shape[0]
     slab_width = totals.shape[0] // ROWS_GROUP
     block_size = totals.shape[-1]
     copies = [
         [pltpu.make_async_copy(own_left, left_lists.at[0], sems.at[0]),
          pltpu.make_async_copy(own_right, right_lists.at[0], sems.at[1])],
-        [pltpu.make_async_copy(from_below, left_lists.at[1], sems.at[2]),
+        [pltpu.make_async_copy(below_low, left_lists.at[1, pl.ds(0, half)], sems.at[2]),
+         pltpu.make_async_copy(below_high, left_lists.at[1, pl.ds(half, half)], sems.at[7]),
          pltpu.make_async_copy(right_pair.at[pick[0]], right_lists.at[1], sems.at[3])],
-        [pltpu.make_async_copy(from_above, left_lists.at[2], sems.at[4])],
+        [pltpu.make_async_copy(above_low, left_lists.at[2, pl.ds(0, half)], sems.at[4]),
+         pltpu.make_async_copy(above_high, left_lists.at[2, pl.ds(half, half)], sems.at[8])],
         [pltpu.make_async_copy(far_low, left_lists.at[3, pl.ds(0, half)], sems.at[5]),
          pltpu.make_async_copy(far_high, left_lists.at[3, pl.ds(half, half)], sems.at[6])],
     ]
@@ -76,7 +78,7 @@
         scratch_shapes=[
             pltpu.VMEM((4, list_cap, block_size, block_size), jnp.bfloat16),
             pltpu.VMEM((2, list_cap, block_size, block_size), jnp.bfloat16),
-            pltpu.SemaphoreType.DMA((7,)),
+            pltpu.SemaphoreType.DMA((9,)),
         ],
         compiler_params=pltpu.CompilerParams(vmem_limit_bytes=60 * 1024 * 1024),
     )(*scalars, *lists)
@@ -104,13 +106,19 @@
     ids_below = shifted(own_ids, "row", 1)
     ids_above = shifted(own_ids, "row", -1)
     ids_far = shifted(own_ids, "row", 2)
-    from_below = shifted(own_left, "row", 1)
-    from_above = shifted(own_left, "row", -1)
+    half = left_cap // 2
+    own_low, own_high = own_left[:half], own_left[half:]
+    below_low = shifted(own_low, "row", 1)
+    above_high = shifted(own_high, "row", -1)
     right_pair = lax.all_gather(own_right, "col")
     right_ids_pair = lax.all_gather(right_cols.reshape(right_cap), "col")
-    half = left_cap // 2
-    far_low = shifted(from_below[:half], "row", 1)
-    far_high = shifted(from_above[half:], "row", -1)
+    below_low, above_high, own_low, own_high, ids_below, ids_above, ids_far = (
+        lax.optimization_barrier(
+            (below_low, above_high, own_low, own_high, ids_below, ids_above, ids_far)))
+    below_high = shifted(own_high, "row", 1)
+    above_low = shifted(own_low, "row", -1)
+    far_low = shifted(below_low, "row", 1)
+    far_high = shifted(above_high, "row", -1)
 
     slots_left_all = pair_left.reshape(piece_count, -1)
     slots_right_all = pair_right.reshape(piece_count, -1)
@@ -122,8 +130,8 @@
     pick = jnp.stack([1 - col_here, col_here]).astype(jnp.int32)
     scalars = (jnp.take(slots_left_all, piece, axis=0), jnp.take(slots_right_all, piece, axis=0),
                jnp.take(counts_all, piece, axis=0), left_id_stack, right_id_stack, pick)
-    totals = pair_products(scalars, (own_left, from_below, from_above, far_low, far_high,
-                                     own_right, right_pair), targets)
+    totals = pair_products(scalars, (own_left, below_low, below_high, above_low, above_high,
+                                     far_low, far_high, own_right, right_pair), targets)
     owned = lax.psum_scatter(totals, "layer", scatter_dimension=0, tiled=True)
     return owned.reshape(1, 1, -1, block_size, block_size)
 

time: 206 us -> 208 us (level)
  starting transfers between devices: 9.55 us -> 13.7 us
  waiting for transfers between devices: 154 us -> 151 us
    ppermute x7 -> x9, waiting for transfers between devices: 40.7 us -> 36 us  [shifted(): return lax.ppermute(value, axis, pairs)]
    ppermute x7 -> x9, starting transfers between devices: 9.48 us -> 13.6 us  [shifted(): return lax.ppermute(value, axis, pairs)]
    reduce_scatter x1, waiting for transfers between devices: 112 us -> 115 us  [on_device(): owned = lax.psum_scatter(totals, 'layer', scatter_dimension=0, tiled=True)]
  transfers between devices with their start and end apart: 9 -> 11, of which waited for: 4 -> 6; matrix products, arithmetic and copies ran while one was open for 4% -> 3% of each run, Pallas kernels for 0% -> 0%
where the time goes in v11:
time: 208 us; the launch traced here: 206 us
  waiting for transfers between devices  151 us (73%)
  Pallas kernels  18.4 us (9%)
  starting transfers between devices  13.7 us (7%)
  between operations  13.5 us (6%)
  local copies, waits for them, and re-layouts  3.99 us (2%)
  other arithmetic  3.31 us (2%)
    reduce_scatter x1, waiting for transfers between devices, on_device(): owned = lax.psum_scatter(totals, 'layer', scatter_dimension=0, tiled=True)  115 us
    ppermute x9, waiting for transfers between devices, shifted(): return lax.ppermute(value, axis, pairs)  36 us
    pallas_call x1, Pallas kernels, pair_products(): pl.pallas_call(pair_kernel, out_shape=jax.ShapeDtypeStruct((targets, bloc...  18.4 us
    ppermute x9, starting transfers between devices, shifted(): return lax.ppermute(value, axis, pairs)  13.6 us
  transfers between devices with their start and end apart: 11, of which 6 were waited for; matrix products, arithmetic and copies ran while one was open for 3% of the time, Pallas kernels for 0%

profile of v11, /device:TPU:26, one launch (start us, length us, event | category | flops | bytes accessed | tf_op | source)
XLA Modules:
  0.0 206.0 jit_solution(8709085538612622576)
XLA Ops:
  6.5 0.0 copy-start
  6.5 0.0 all-gather.4.cloned.1.call-start
  6.5 0.7 all-gather.4.cloned.1.call-update
  7.3 0.0 copy-start.10
  7.3 0.0 copy-start.9
  7.3 0.0 copy-start.1
  7.3 0.0 copy-start.8
  7.3 0.0 copy-start.11
  7.3 0.0 reduce-scatter.2.cloned.1.call-start
  7.4 0.6 copy-done.2
  8.0 1.0 slice_bitcast_fusion
  9.0 0.5 collective-permute-start.1
  9.5 1.5 collective-permute-start
  11.0 0.0 copy-done.10
  11.0 3.3 %collective-permute-start.4 = (s32[48]{0:T(128)S(1)}, s32[48]{0:T(128)S(1)}, u32[]{:S(2)}, u32[]{:S(2)}) collective-permute-start(s32[48]{0:T(128)S(1)} %bitcast.30), channel_id=1, source_target_pairs={{0,64},{32,96},{64,0},{96,32},{1,65},{33,97},{65,1},{97,33},{2,66}... | collective-permute-start | bytes 584 | tf_op jit(solution)/shard_map/ppermute | solution.py:90
  14.3 0.2 collective-permute-start.3
  14.6 1.8 collective-permute-start.2
  16.4 0.1 fusion.1
  16.5 0.0 copy-done.9
  16.5 0.6 pad_add_fusion.1.pick
  17.1 12.3 %collective-permute-done.4 = s32[48]{0:T(128)S(1)} collective-permute-done((s32[48]{0:T(128)S(1)}, s32[48]{0:T(128)S(1)}, u32[]{:S(2)}, u32[]{:S(2)}) %collective-permute-start.4) | collective-permute-done | bytes 224 | tf_op jit(solution)/shard_map/ppermute | solution.py:90
  29.4 0.0 collective-permute-done.3
  29.4 0.2 collective-permute-done.2
  29.6 0.0 collective-permute-done.1.above_high
  29.6 0.0 collective-permute-done.below_low
  29.6 0.0 copy-start.4
  29.6 1.5 collective-permute-start.5
  31.1 1.6 collective-permute-start.6
  32.7 0.4 collective-permute-start.7
  33.1 2.8 %collective-permute-start.8 = (bf16[24,128,128]{2,1,0:T(8,128)(2,1)S(1)}, bf16[24,128,128]{2,1,0:T(8,128)(2,1)}, u32[]{:S(2)}, u32[]{:S(2)}) collective-permute-start(bf16[24,128,128]{2,1,0:T(8,128)(2,1)S(1)} %collective-permute-done.1.above_high), channel_id=1, source_target_pairs={{0,96},{32,0},{64,32},{96,64},{1,97},{33,1},{65,33},{97,65},{2,98}... | collective-permute-start | bytes 2359304 | tf_op jit(solution)/shard_map/ppermute | solution.py:90
  35.9 0.1 compare_and_fusion.1
  36.0 0.6 gather_fusion
  36.6 0.0 copy-done
  36.6 0.6 gather_fusion.3
  37.2 0.6 gather_fusion.2
  37.8 1.8 all-gather
  39.5 0.6 gather_fusion.1
  40.1 0.6 broadcast_select_fusion.3.counts
  40.7 0.7 broadcast_select_fusion.2.right_ids
  41.3 0.7 broadcast_select_fusion
  42.0 0.6 pad_add_fusion.left_ids
  42.6 8.7 %collective-permute-done.5.below_high = bf16[24,128,128]{2,1,0:T(8,128)(2,1)S(1)} collective-permute-done((bf16[24,128,128]{2,1,0:T(8,128)(2,1)}, bf16[24,128,128]{2,1,0:T(8,128)(2,1)S(1)}, u32[]{:S(2)}, u32[]{:S(2)}) %collective-permute-start.5) | collective-permute-done | bytes 786464 | tf_op jit(solution)/shard_map/ppermute | solution.py:90
  51.3 0.5 collective-permute-done.6.above_low
  51.8 14.3 %collective-permute-done.7.far_low = bf16[24,128,128]{2,1,0:T(8,128)(2,1)} collective-permute-done((bf16[24,128,128]{2,1,0:T(8,128)(2,1)S(1)}, bf16[24,128,128]{2,1,0:T(8,128)(2,1)}, u32[]{:S(2)}, u32[]{:S(2)}) %collective-permute-start.7) | collective-permute-done | bytes 786464 | tf_op jit(solution)/shard_map/ppermute | solution.py:90
  66.1 0.0 collective-permute-done.8.far_high
  66.2 18.4 %shard_map.82 = f32[256,128,128]{2,1,0:T(8,128)} custom-call(s32[4,192]{1,0:T(4,128)} %get-tuple-element.25.slots_left, s32[4,192]{1,0:T(4,128)} %get-tuple-element.24.slots_right, s32[4]{0:T(128)} %broadcast_select_fusion.3.counts, s32[4,48]{1,0:T(4,128)} %pad_add_fusion.left_ids, s32[2,48]{1,0:T(2,128)} %broadcast_select_fusion.2.right_ids, ...), custom_call_target="tpu_custom_call" | custom-call | tf_op jit(solution)/shard_map/pallas_call | solution.py:73
  84.5 0.0 reduce-scatter.2.cloned.1.call-update
  84.6 114.6 %reduce-scatter.2.cloned.1.call-done = f32[16,128,128]{2,1,0:T(8,128)} async-done(((f32[256,128,128]{2,1,0:T(8,128)}), f32[16,128,128]{2,1,0:T(8,128)}) %reduce-scatter.2.cloned.1.call-update) | async-done | bytes 1048592 | tf_op jit(solution)/shard_map/reduce_scatter | solution.py:135
  (17 shorter events, 0.1 us)
Async XLA Ops:
  6.5 30.1 %copy-start = (s32[1,1,1,4,192]{4,3,2,1,0:T(4,128)S(1)}, s32[1,1,1,4,192]{4,3,2,1,0:T(4,128)}, u32[]{:S(2)}) copy-start(s32[1,1,1,4,192]{4,3,2,1,0:T(4,128)} %param.15) | copy-start | bytes 9220
  6.5 1.4 copy-start.2
  6.5 59.6 %all-gather.4.cloned.1.call-start = ((), (), s32[]{:S(2)}) async-start(), calls=%async_computation.2 | async-start | bytes 4718592 | tf_op jit(solution)/shard_map/all_gather | solution.py:113
  7.3 3.8 %copy-start.10 = (s32[1,1,1,48]{3,2,1,0:T(1,128)S(1)}, s32[1,1,1,48]{3,2,1,0:T(1,128)}, u32[]{:S(2)}) copy-start(s32[1,1,1,48]{3,2,1,0:T(1,128)} %param.11) | copy-start | bytes 580
  7.3 9.2 %copy-start.9 = (s32[4]{0:T(128)S(1)}, s32[4]{0:T(128)}, u32[]{:S(2)}) copy-start(s32[4]{0:T(128)} %constant.67.clone) | copy-start | bytes 52
  7.3 28.7 %copy-start.1 = (s32[1,1,1,4]{3,2,1,0:T(1,128)S(1)}, s32[1,1,1,4]{3,2,1,0:T(1,128)}, u32[]{:S(2)}) copy-start(s32[1,1,1,4]{3,2,1,0:T(1,128)} %param.16) | copy-start | bytes 52
  7.3 29.9 %copy-start.8 = (s32[1,1,1,4,192]{4,3,2,1,0:T(4,128)S(1)}, s32[1,1,1,4,192]{4,3,2,1,0:T(4,128)}, u32[]{:S(2)}) copy-start(s32[1,1,1,4,192]{4,3,2,1,0:T(4,128)} %param.14) | copy-start | bytes 9220
  7.3 30.5 %copy-start.11 = (s32[1,1,1,48]{3,2,1,0:T(1,128)S(1)}, s32[1,1,1,48]{3,2,1,0:T(1,128)}, u32[]{:S(2)}) copy-start(s32[1,1,1,48]{3,2,1,0:T(1,128)} %param.13) | copy-start | bytes 580
  7.3 191.9 %reduce-scatter.2.cloned.1.call-start = ((), (), s32[]{:S(2)}) async-start(), calls=%async_computation.1 | async-start | bytes 17825792 | tf_op jit(solution)/shard_map/reduce_scatter | solution.py:135
  9.0 20.6 %copy-start.7 = (bf16[24,128,128]{2,1,0:T(8,128)(2,1)}, bf16[24,128,128]{2,1,0:T(8,128)(2,1)S(1)}, u32[]{:S(2)}) copy-start(bf16[24,128,128]{2,1,0:T(8,128)(2,1)S(1)} %get-tuple-element.18) | copy-start | bytes 2359300
  9.0 20.6 %collective-permute-start.1 = (bf16[24,128,128]{2,1,0:T(8,128)(2,1)}, bf16[24,128,128]{2,1,0:T(8,128)(2,1)S(1)}, u32[]{:S(2)}, u32[]{:S(2)}) collective-permute-start(bf16[24,128,128]{2,1,0:T(8,128)(2,1)} %get-tuple-element.17), channel_id=1, source_target_pairs={{0,96},{32,0},{64,32},{96,64},{1,97},{33,1},{65,33},{97,65},{2,98}... | collective-permute-start | bytes 2359304 | tf_op jit(solution)/shard_map/ppermute | solution.py:90
  9.5 20.1 %collective-permute-start = (bf16[24,128,128]{2,1,0:T(8,128)(2,1)S(1)}, bf16[24,128,128]{2,1,0:T(8,128)(2,1)S(1)}, u32[]{:S(2)}, u32[]{:S(2)}) collective-permute-start(bf16[24,128,128]{2,1,0:T(8,128)(2,1)S(1)} %get-tuple-element.18), channel_id=1, source_target_pairs={{0,32},{32,64},{64,96},{96,0},{1,33},{33,65},{65,97},{97,1},{2,34}... | collective-permute-start | bytes 2359304 | tf_op jit(solution)/shard_map/ppermute | solution.py:90
  11.0 18.4 %collective-permute-start.4 = (s32[48]{0:T(128)S(1)}, s32[48]{0:T(128)S(1)}, u32[]{:S(2)}, u32[]{:S(2)}) collective-permute-start(s32[48]{0:T(128)S(1)} %bitcast.30), channel_id=1, source_target_pairs={{0,64},{32,96},{64,0},{96,32},{1,65},{33,97},{65,1},{97,33},{2,66}... | collective-permute-start | bytes 584 | tf_op jit(solution)/shard_map/ppermute | solution.py:90
  14.3 15.0 %collective-permute-start.3 = (s32[48]{0:T(128)S(1)}, s32[48]{0:T(128)S(1)}, u32[]{:S(2)}, u32[]{:S(2)}) collective-permute-start(s32[48]{0:T(128)S(1)} %bitcast.31), channel_id=1, source_target_pairs={{0,96},{32,0},{64,32},{96,64},{1,97},{33,1},{65,33},{97,65},{2,98}... | collective-permute-start | bytes 584 | tf_op jit(solution)/shard_map/ppermute | solution.py:90
  14.6 15.0 %collective-permute-start.2 = (s32[48]{0:T(128)S(1)}, s32[48]{0:T(128)S(1)}, u32[]{:S(2)}, u32[]{:S(2)}) collective-permute-start(s32[48]{0:T(128)S(1)} %bitcast.32), channel_id=1, source_target_pairs={{0,32},{32,64},{64,96},{96,0},{1,33},{33,65},{65,97},{97,1},{2,34}... | collective-permute-start | bytes 584 | tf_op jit(solution)/shard_map/ppermute | solution.py:90
  29.6 36.5 %copy-start.3 = (bf16[24,128,128]{2,1,0:T(8,128)(2,1)}, bf16[24,128,128]{2,1,0:T(8,128)(2,1)S(1)}, u32[]{:S(2)}) copy-start(bf16[24,128,128]{2,1,0:T(8,128)(2,1)S(1)} %collective-permute-done.1.above_high) | copy-start | bytes 2359300
  29.6 36.5 %copy-start.4 = (bf16[24,128,128]{2,1,0:T(8,128)(2,1)}, bf16[24,128,128]{2,1,0:T(8,128)(2,1)S(1)}, u32[]{:S(2)}) copy-start(bf16[24,128,128]{2,1,0:T(8,128)(2,1)S(1)} %collective-permute-done.below_low) | copy-start | bytes 2359300
  29.6 21.7 %collective-permute-start.5 = (bf16[24,128,128]{2,1,0:T(8,128)(2,1)}, bf16[24,128,128]{2,1,0:T(8,128)(2,1)S(1)}, u32[]{:S(2)}, u32[]{:S(2)}) collective-permute-start(bf16[24,128,128]{2,1,0:T(8,128)(2,1)} %get-tuple-element.17), channel_id=1, source_target_pairs={{0,32},{32,64},{64,96},{96,0},{1,33},{33,65},{65,97},{97,1},{2,34}... | collective-permute-start | bytes 2359304 | tf_op jit(solution)/shard_map/ppermute | solution.py:90
  31.1 20.7 %collective-permute-start.6 = (bf16[24,128,128]{2,1,0:T(8,128)(2,1)}, bf16[24,128,128]{2,1,0:T(8,128)(2,1)S(1)}, u32[]{:S(2)}, u32[]{:S(2)}) collective-permute-start(bf16[24,128,128]{2,1,0:T(8,128)(2,1)} %copy-done.7), channel_id=1, source_target_pairs={{0,96},{32,0},{64,32},{96,64},{1,97},{33,1},{65,33},{97,65},{2,98}... | collective-permute-start | bytes 2359304 | tf_op jit(solution)/shard_map/ppermute | solution.py:90
  32.7 33.4 %collective-permute-start.7 = (bf16[24,128,128]{2,1,0:T(8,128)(2,1)S(1)}, bf16[24,128,128]{2,1,0:T(8,128)(2,1)}, u32[]{:S(2)}, u32[]{:S(2)}) collective-permute-start(bf16[24,128,128]{2,1,0:T(8,128)(2,1)S(1)} %collective-permute-done.below_low), channel_id=1, source_target_pairs={{0,32},{32,64},{64,96},{96,0},{1,33},{33,65},{65,97},{97,1},{2,34}... | collective-permute-start | bytes 2359304 | tf_op jit(solution)/shard_map/ppermute | solution.py:90
  33.1 33.0 %collective-permute-start.8 = (bf16[24,128,128]{2,1,0:T(8,128)(2,1)S(1)}, bf16[24,128,128]{2,1,0:T(8,128)(2,1)}, u32[]{:S(2)}, u32[]{:S(2)}) collective-permute-start(bf16[24,128,128]{2,1,0:T(8,128)(2,1)S(1)} %collective-permute-done.1.above_high), channel_id=1, source_target_pairs={{0,96},{32,0},{64,32},{96,64},{1,97},{33,1},{65,33},{97,65},{2,98}... | collective-permute-start | bytes 2359304 | tf_op jit(solution)/shard_map/ppermute | solution.py:90
  51.3 14.8 %copy-start.5 = (bf16[24,128,128]{2,1,0:T(8,128)(2,1)}, bf16[24,128,128]{2,1,0:T(8,128)(2,1)S(1)}, u32[]{:S(2)}) copy-start(bf16[24,128,128]{2,1,0:T(8,128)(2,1)S(1)} %collective-permute-done.5.below_high) | copy-start | bytes 2359300
  51.8 14.3 %copy-start.6 = (bf16[24,128,128]{2,1,0:T(8,128)(2,1)}, bf16[24,128,128]{2,1,0:T(8,128)(2,1)S(1)}, u32[]{:S(2)}) copy-start(bf16[24,128,128]{2,1,0:T(8,128)(2,1)S(1)} %collective-permute-done.6.above_low) | copy-start | bytes 2359300
Sparse Core Ops, SparseCore 0:
  9.0 16.9 all-gather.3
  84.7 114.4 reduce-scatter.1

commit v12 on v1

v12 whole, which is shorter than its diff:
```python
import jax
import jax.numpy as jnp
from jax import lax
from jax.experimental import pallas as pl
from jax.experimental.pallas import tpu as pltpu
from jax.sharding import PartitionSpec as P

SLAB = 128
ROWS_GROUP = 8
UNROLL = 16


def make_pair_kernel(parts, right_of, right_count, has_start):
    left_count = sum(parts)

    def pair_kernel(slots_left, slots_right, counts, left_ids, right_ids, pick, *refs):
        left_refs = refs[:left_count]
        right_refs = refs[left_count:left_count + right_count]
        start = refs[left_count + right_count] if has_start else None
        totals, left_lists, right_lists, sems = refs[-4:]
        slab_width = totals.shape[0] // ROWS_GROUP
        block_size = totals.shape[-1]
        copies = []
        position = 0
        for u, count in enumerate(parts):
            offset = 0
            group = []
            for _ in range(count):
                size = left_refs[position].shape[0]
                group.append(pltpu.make_async_copy(
                    left_refs[position], left_lists.at[u, pl.ds(offset, size)], sems.at[position]))
                offset += size
                position += 1
            copies.append(group)
        right_copies = [pltpu.make_async_copy(right_refs[0], right_lists.at[0], sems.at[left_count])]
        if right_count > 1:
            right_copies.append(pltpu.make_async_copy(
                right_refs[1].at[pick[0]], right_lists.at[1], sems.at[left_count + 1]))
        if has_start:
            start_copy = pltpu.make_async_copy(start, totals, sems.at[left_count + right_count])
            start_copy.start()
        for u, group in enumerate(copies):
            for copy in group:
                copy.start()
            if u == 0:
                for copy in right_copies:
                    copy.start()

        if has_start:
            start_copy.wait()
        else:
            def clear(t, carry):
                totals[t] = jnp.zeros((block_size, block_size), jnp.float32)
                return carry

            lax.fori_loop(0, totals.shape[0], clear, 0)

        for u, group in enumerate(copies):
            v = right_of[u]
            for copy in group:
                copy.wait()
            if u == 0:
                for copy in right_copies:
                    copy.wait()

            def one_term(j, u=u, v=v):
                i = slots_left[u, j]
                k = slots_right[u, j]
                t = left_ids[u, i] * slab_width + right_ids[v, k]
                term = jnp.dot(left_lists[u, i], right_lists[v, k],
                               preferred_element_type=jnp.float32)
                return t, term

            def add_group(g, carry, one_term=one_term):
                made = [one_term(g * UNROLL + q) for q in range(UNROLL)]
                for t, term in made:
                    totals[t] = totals[t] + term
                return carry

            def add_single(j, carry, one_term=one_term):
                t, term = one_term(j)
                totals[t] = totals[t] + term
                return carry

            count = counts[u]
            groups = count // UNROLL
            lax.fori_loop(0, groups, add_group, 0)
            lax.fori_loop(groups * UNROLL, count, add_single, 0)

    return pair_kernel


def pair_products(scalars, left_parts, right_lists, right_of, targets, start=None):
    own_left = left_parts[0][0]
    list_cap, block_size = own_left.shape[0] * len(left_parts[0]), own_left.shape[-1]
    smem = pl.BlockSpec(memory_space=pltpu.SMEM)
    hbm = pl.BlockSpec(memory_space=pl.ANY)
    flat = [part for parts in left_parts for part in parts]
    extra = [] if start is None else [start]
    operands = flat + list(right_lists) + extra
    return pl.pallas_call(
        make_pair_kernel([len(parts) for parts in left_parts], right_of, len(right_lists),
                         start is not None),
        out_shape=jax.ShapeDtypeStruct((targets, block_size, block_size), jnp.float32),
        in_specs=[smem] * len(scalars) + [hbm] * len(operands),
        out_specs=pl.BlockSpec(memory_space=pltpu.VMEM),
        scratch_shapes=[
            pltpu.VMEM((len(left_parts), list_cap, block_size, block_size), jnp.bfloat16),
            pltpu.VMEM((2, list_cap, block_size, block_size), jnp.bfloat16),
            pltpu.SemaphoreType.DMA((len(operands),)),
        ],
        compiler_params=pltpu.CompilerParams(vmem_limit_bytes=60 * 1024 * 1024),
    )(*scalars, *operands)


def shifted(value, axis, steps):
    count = lax.axis_size(axis)
    pairs = [(source, (source + steps) % count) for source in range(count)]
    return lax.ppermute(value, axis, pairs)


def on_device(left_blocks, left_rows, right_blocks, right_cols, pair_left, pair_right, pair_count):
    block_size = left_blocks.shape[-1]
    left_cap = left_blocks.shape[3]
    right_cap = right_blocks.shape[3]
    piece_count = lax.axis_size("row")
    slab_width = SLAB // piece_count
    targets = ROWS_GROUP * slab_width
    row_here = lax.axis_index("row")
    col_here = lax.axis_index("col")
    own_left = left_blocks.reshape(left_cap, block_size, block_size)
    own_right = right_blocks.reshape(right_cap, block_size, block_size)
    own_ids = left_rows.reshape(left_cap)

    ids_below = shifted(own_ids, "row", 1)
    ids_above = shifted(own_ids, "row", -1)
    ids_far = shifted(own_ids, "row", 2)
    half = left_cap // 2
    own_low, own_high = own_left[:half], own_left[half:]
    below_low = shifted(own_low, "row", 1)
    above_high = shifted(own_high, "row", -1)
    right_pair = lax.all_gather(own_right, "col")
    right_ids_pair = lax.all_gather(right_cols.reshape(right_cap), "col")
    below_low, above_high, own_low, own_high, ids_below, ids_above, ids_far = (
        lax.optimization_barrier(
            (below_low, above_high, own_low, own_high, ids_below, ids_above, ids_far)))
    below_high = shifted(own_high, "row", 1)
    above_low = shifted(own_low, "row", -1)
    far_low = shifted(below_low, "row", 1)
    far_high = shifted(above_high, "row", -1)

    slots_left_all = pair_left.reshape(piece_count, -1)
    slots_right_all = pair_right.reshape(piece_count, -1)
    counts_all = pair_count.reshape(piece_count)
    right_id_stack = jnp.take(right_ids_pair, jnp.stack([col_here, 1 - col_here]), axis=0)
    pick = jnp.stack([1 - col_here, col_here]).astype(jnp.int32)

    def scalars_for(offsets, id_lists):
        piece = (row_here + col_here + jnp.array(offsets, jnp.int32)) % piece_count
        return (jnp.take(slots_left_all, piece, axis=0), jnp.take(slots_right_all, piece, axis=0),
                jnp.take(counts_all, piece, axis=0), jnp.stack(id_lists), right_id_stack, pick)

    totals = pair_products(scalars_for([0, -1, 1], [own_ids, ids_below, ids_above]),
                           ((own_left,), (below_low, below_high), (above_low, above_high)),
                           (own_right, right_pair), (0, 1, 1), targets)
    totals = pair_products(scalars_for([2], [ids_far]), ((far_low, far_high),),
                           (own_right,), (0,), targets, start=totals)
    owned = lax.psum_scatter(totals, "layer", scatter_dimension=0, tiled=True)
    return owned.reshape(1, 1, -1, block_size, block_size)


def solution(mesh):
    in_specs = (
        P("row", "col", "layer", None, None, None),
        P("row", "col", "layer", None),
        P("row", "col", "layer", None, None, None),
        P("row", "col", "layer", None),
        P("row", "col", "layer", None, None),
        P("row", "col", "layer", None, None),
        P("row", "col", "layer", None),
    )
    out_specs = P("col", "row", "layer", None, None)
    return jax.shard_map(
        on_device, mesh=mesh, in_specs=in_specs, out_specs=out_specs, check_vma=False
    )
```

time: 234 us -> 212 us (0.906)
  waiting for transfers between devices: 155 us -> 142 us
  Pallas kernels: 38.4 us -> 29.9 us
  other arithmetic: 11.2 us -> 3.82 us
  starting transfers between devices: 9.83 us -> 12.5 us
    ppermute x10 -> x9, waiting for transfers between devices: 34.8 us -> 24.5 us  [shifted(): return lax.ppermute(value, axis, pairs)]
    pallas_call x2, Pallas kernels: 38.4 us -> 29.9 us  [pair_products(): pl.pallas_call(make_pair_kernel([len(parts) for parts in left_parts], rig...]
    another operation x6 -> x2, other arithmetic: 8.66 us -> 1.25 us  [the longest x1 0.67 us: on_device(): pick = jnp.stack([1 - col_here, col_here]).astype(jnp.int32)]
    reduce_scatter x1, waiting for transfers between devices: 120 us -> 116 us  [on_device(): owned = lax.psum_scatter(totals, 'layer', scatter_dimension=0, tiled=True)]
    ppermute x10 -> x9, starting transfers between devices: 9.82 us -> 12.4 us  [shifted(): return lax.ppermute(value, axis, pairs)]
  transfers between devices with their start and end apart: 11 -> 11, of which waited for: 5 -> 4; matrix products, arithmetic and copies ran while one was open for 5% -> 4% of each run, Pallas kernels for 8% -> 6%
where the time goes in v12:
time: 212 us; the launch traced here: 210 us
  waiting for transfers between devices  142 us (67%)
  Pallas kernels  29.9 us (14%)
  between operations  14.1 us (7%)
  starting transfers between devices  12.5 us (6%)
  local copies, waits for them, and re-layouts  6.45 us (3%)
  other arithmetic  3.82 us (2%)
    reduce_scatter x1, waiting for transfers between devices, on_device(): owned = lax.psum_scatter(totals, 'layer', scatter_dimension=0, tiled=True)  116 us
    pallas_call x2, Pallas kernels, pair_products(): pl.pallas_call(make_pair_kernel([len(parts) for parts in left_parts], rig...  29.9 us
    ppermute x9, waiting for transfers between devices, shifted(): return lax.ppermute(value, axis, pairs)  24.5 us
    ppermute x9, starting transfers between devices, shifted(): return lax.ppermute(value, axis, pairs)  12.4 us
  transfers between devices with their start and end apart: 11, of which 4 were waited for; matrix products, arithmetic and copies ran while one was open for 4% of the time, Pallas kernels for 6%

profile of v12, /device:TPU:26, one launch (start us, length us, event | category | flops | bytes accessed | tf_op | source)
XLA Modules:
  0.0 210.3 jit_solution(13070519150926116526)
XLA Ops:
  6.5 0.0 copy-start
  6.5 0.0 copy-start.11
  6.6 0.0 all-gather.4.cloned.1.call-start
  6.6 0.7 all-gather.4.cloned.1.call-update
  7.3 0.0 reduce-scatter.2.cloned.1.call-start
  7.3 2.2 %collective-permute-start.4 = (s32[48]{0:T(128)}, s32[48]{0:T(128)S(1)}, u32[]{:S(2)}, u32[]{:S(2)}) collective-permute-start(s32[48]{0:T(128)} %bitcast.38), channel_id=1, source_target_pairs={{0,64},{32,96},{64,0},{96,32},{1,65},{33,97},{65,1},{97,33},{2,66}... | collective-permute-start | bytes 584 | tf_op jit(solution)/shard_map/ppermute | solution.py:119
  9.5 1.4 collective-permute-start.3
  11.0 0.6 collective-permute-start.2
  11.6 2.4 %slice_bitcast_fusion = (bf16[24,128,128]{2,1,0:T(8,128)(2,1)}, bf16[24,128,128]{2,1,0:T(8,128)(2,1)S(1)}) fusion(bf16[1,1,1,48,128,128]{5,4,3,2,1,0:T(8,128)(2,1)} %param.13), kind=kLoop, calls=%fused_computation.4 | loop fusion | bytes 3145728 | tf_op jit(solution)/shard_map/slice | solution.py:139
  14.0 1.4 collective-permute-start.1
  15.4 0.6 collective-permute-start
  16.0 0.1 fusion.1
  16.1 0.0 copy-done.7
  16.1 0.6 broadcast_select_fusion.2
  16.7 0.7 pad_add_fusion.1.pick
  17.4 0.0 collective-permute-done.4
  17.4 0.0 collective-permute-done.3
  17.4 0.0 collective-permute-done.2
  17.4 15.2 %collective-permute-done.1.refs_4_ = bf16[24,128,128]{2,1,0:T(8,128)(2,1)S(1)} collective-permute-done((bf16[24,128,128]{2,1,0:T(8,128)(2,1)}, bf16[24,128,128]{2,1,0:T(8,128)(2,1)S(1)}, u32[]{:S(2)}, u32[]{:S(2)}) %collective-permute-start.1) | collective-permute-done | bytes 786464 | tf_op jit(solution)/shard_map/ppermute | solution.py:119
  32.6 1.5 collective-permute-done.refs_1_
  34.2 0.0 collective-permute-start.7
  34.2 3.0 %collective-permute-start.8 = (bf16[24,128,128]{2,1,0:T(8,128)(2,1)}, bf16[24,128,128]{2,1,0:T(8,128)(2,1)S(1)}, u32[]{:S(2)}, u32[]{:S(2)}) collective-permute-start(bf16[24,128,128]{2,1,0:T(8,128)(2,1)} %copy-done.5), channel_id=1, source_target_pairs={{0,96},{32,0},{64,32},{96,64},{1,97},{33,1},{65,33},{97,65},{2,98}... | collective-permute-start | bytes 2359304 | tf_op jit(solution)/shard_map/ppermute | solution.py:119
  37.1 0.0 collective-permute-start.5
  37.1 3.2 %collective-permute-start.6 = (bf16[24,128,128]{2,1,0:T(8,128)(2,1)S(1)}, bf16[24,128,128]{2,1,0:T(8,128)(2,1)}, u32[]{:S(2)}, u32[]{:S(2)}) collective-permute-start(bf16[24,128,128]{2,1,0:T(8,128)(2,1)S(1)} %collective-permute-done.1.refs_4_), channel_id=1, source_target_pairs={{0,96},{32,0},{64,32},{96,64},{1,97},{33,1},{65,33},{97,65},{2,98}... | collective-permute-start | bytes 2359304 | tf_op jit(solution)/shard_map/ppermute | solution.py:119
  40.4 0.1 compare_and_fusion.1
  40.4 0.6 gather_fusion.3
  41.0 0.6 gather_fusion.2
  41.6 0.6 constant_dynamic-slice_fusion
  42.2 0.6 gather_fusion.1
  43.4 1.8 all-gather
  45.2 0.6 gather_fusion
  45.7 0.5 broadcast_select_fusion.5.counts
  46.3 0.6 broadcast_select_fusion.4.right_ids
  46.9 0.7 broadcast_select_fusion
  47.5 0.6 pad_add_fusion.left_ids
  48.1 7.7 %collective-permute-done.7.refs_2_ = bf16[24,128,128]{2,1,0:T(8,128)(2,1)S(1)} collective-permute-done((bf16[24,128,128]{2,1,0:T(8,128)(2,1)}, bf16[24,128,128]{2,1,0:T(8,128)(2,1)S(1)}, u32[]{:S(2)}, u32[]{:S(2)}) %collective-permute-start.7) | collective-permute-done | bytes 786464 | tf_op jit(solution)/shard_map/ppermute | solution.py:119
  55.8 0.0 collective-permute-done.8.refs_3_
  55.8 0.0 all-gather.4.cloned.1.call-done
  55.8 0.0 copy-done.1
  55.8 0.0 copy-done.2
  55.8 0.8 copy-done.3
  56.7 0.3 copy-done.4
  56.9 13.2 %shard_map.91.refs_3_ = f32[256,128,128]{2,1,0:T(8,128)} custom-call(s32[3,192]{1,0:T(4,128)} %get-tuple-element.48.slots_left, s32[3,192]{1,0:T(4,128)} %get-tuple-element.47.slots_right, s32[3]{0:T(128)} %broadcast_select_fusion.5.counts, s32[3,48]{1,0:T(4,128)} %pad_add_fusion.left_ids, s32[2,48]{1,0:T(2,128)} %broadcast_select_fusion.4.right_ids, ...), custom_call_target="tpu_custom_call" | custom-call | tf_op jit(solution)/shard_map/pallas_call | solution.py:101
  70.1 0.0 collective-permute-done.5.refs_0_
  70.1 0.0 collective-permute-done.6.refs_1_
  70.2 16.8 %shard_map.92 = f32[256,128,128]{2,1,0:T(8,128)} custom-call(s32[1,192]{1,0:T(1,128)} %get-tuple-element.50.slots_left, s32[1,192]{1,0:T(1,128)} %get-tuple-element.49.slots_right, s32[1]{0:T(128)S(6)} %select_n.73.counts, s32[1,48]{1,0:T(1,128)} %bitcast.37, s32[2,48]{1,0:T(2,128)} %broadcast_select_fusion.4.right_ids, s32[2]{0:T(128)} %pad_add_fusion.1.pick, ...), custom_call_target="tpu_custom_call" | custom-call | tf_op jit(solution)/shard_map/pallas_call | solution.py:101
  86.9 0.0 reduce-scatter.2.cloned.1.call-update
  87.0 116.5 %reduce-scatter.2.cloned.1.call-done = f32[16,128,128]{2,1,0:T(8,128)} async-done(((f32[256,128,128]{2,1,0:T(8,128)}), f32[16,128,128]{2,1,0:T(8,128)}) %reduce-scatter.2.cloned.1.call-update) | async-done | bytes 1048592 | tf_op jit(solution)/shard_map/reduce_scatter | solution.py:168
  (20 shorter events, 0.1 us)
Async XLA Ops:
  6.5 35.0 %copy-start = (s32[1,1,1,4]{3,2,1,0:T(1,128)S(1)}, s32[1,1,1,4]{3,2,1,0:T(1,128)}, u32[]{:S(2)}) copy-start(s32[1,1,1,4]{3,2,1,0:T(1,128)} %param.19) | copy-start | bytes 52
  6.5 10.1 %copy-start.10 = (s32[3]{0:T(128)S(1)}, s32[3]{0:T(128)}, u32[]{:S(2)}) copy-start(s32[3]{0:T(128)} %constant.110.clone) | copy-start | bytes 40
  6.5 41.0 %copy-start.9 = (s32[1,1,1,48]{3,2,1,0:T(1,128)S(1)}, s32[1,1,1,48]{3,2,1,0:T(1,128)}, u32[]{:S(2)}) copy-start(s32[1,1,1,48]{3,2,1,0:T(1,128)} %param.14) | copy-start | bytes 580
  6.5 9.5 %copy-start.6 = (s32[1,1,1,4,192]{4,3,2,1,0:T(4,128)S(1)}, s32[1,1,1,4,192]{4,3,2,1,0:T(4,128)}, u32[]{:S(2)}) copy-start(s32[1,1,1,4,192]{4,3,2,1,0:T(4,128)} %param.18) | copy-start | bytes 9220
  6.5 9.5 %copy-start.7 = (s32[1,1,1,4,192]{4,3,2,1,0:T(4,128)S(1)}, s32[1,1,1,4,192]{4,3,2,1,0:T(4,128)}, u32[]{:S(2)}) copy-start(s32[1,1,1,4,192]{4,3,2,1,0:T(4,128)} %param.17) | copy-start | bytes 9220
  6.5 36.8 %copy-start.11 = (s32[1,1,1,48]{3,2,1,0:T(1,128)S(1)}, s32[1,1,1,48]{3,2,1,0:T(1,128)}, u32[]{:S(2)}) copy-start(s32[1,1,1,48]{3,2,1,0:T(1,128)} %param.16) | copy-start | bytes 580
  6.6 49.3 %all-gather.4.cloned.1.call-start = ((), (), s32[]{:S(2)}) async-start(), calls=%async_computation.2 | async-start | bytes 4718592 | tf_op jit(solution)/shard_map/all_gather | solution.py:142
  7.3 196.1 %reduce-scatter.2.cloned.1.call-start = ((), (), s32[]{:S(2)}) async-start(), calls=%async_computation.1 | async-start | bytes 17825792 | tf_op jit(solution)/shard_map/reduce_scatter | solution.py:168
  7.3 10.0 %collective-permute-start.4 = (s32[48]{0:T(128)}, s32[48]{0:T(128)S(1)}, u32[]{:S(2)}, u32[]{:S(2)}) collective-permute-start(s32[48]{0:T(128)} %bitcast.38), channel_id=1, source_target_pairs={{0,64},{32,96},{64,0},{96,32},{1,65},{33,97},{65,1},{97,33},{2,66}... | collective-permute-start | bytes 584 | tf_op jit(solution)/shard_map/ppermute | solution.py:119
  9.5 7.8 %collective-permute-start.3 = (s32[48]{0:T(128)}, s32[48]{0:T(128)S(1)}, u32[]{:S(2)}, u32[]{:S(2)}) collective-permute-start(s32[48]{0:T(128)} %bitcast.39), channel_id=1, source_target_pairs={{0,96},{32,0},{64,32},{96,64},{1,97},{33,1},{65,33},{97,65},{2,98}... | collective-permute-start | bytes 584 | tf_op jit(solution)/shard_map/ppermute | solution.py:119
  11.0 6.4 %collective-permute-start.2 = (s32[48]{0:T(128)}, s32[48]{0:T(128)S(1)}, u32[]{:S(2)}, u32[]{:S(2)}) collective-permute-start(s32[48]{0:T(128)} %bitcast.40), channel_id=1, source_target_pairs={{0,32},{32,64},{64,96},{96,0},{1,33},{33,65},{65,97},{97,1},{2,34}... | collective-permute-start | bytes 584 | tf_op jit(solution)/shard_map/ppermute | solution.py:119
  14.0 18.7 %copy-start.5 = (bf16[24,128,128]{2,1,0:T(8,128)(2,1)}, bf16[24,128,128]{2,1,0:T(8,128)(2,1)S(1)}, u32[]{:S(2)}) copy-start(bf16[24,128,128]{2,1,0:T(8,128)(2,1)S(1)} %get-tuple-element.20) | copy-start | bytes 2359300
  14.0 18.7 %collective-permute-start.1 = (bf16[24,128,128]{2,1,0:T(8,128)(2,1)}, bf16[24,128,128]{2,1,0:T(8,128)(2,1)S(1)}, u32[]{:S(2)}, u32[]{:S(2)}) collective-permute-start(bf16[24,128,128]{2,1,0:T(8,128)(2,1)} %get-tuple-element.19), channel_id=1, source_target_pairs={{0,96},{32,0},{64,32},{96,64},{1,97},{33,1},{65,33},{97,65},{2,98}... | collective-permute-start | bytes 2359304 | tf_op jit(solution)/shard_map/ppermute | solution.py:119
  15.4 18.8 %collective-permute-start = (bf16[24,128,128]{2,1,0:T(8,128)(2,1)S(1)}, bf16[24,128,128]{2,1,0:T(8,128)(2,1)S(1)}, u32[]{:S(2)}, u32[]{:S(2)}) collective-permute-start(bf16[24,128,128]{2,1,0:T(8,128)(2,1)S(1)} %get-tuple-element.20), channel_id=1, source_target_pairs={{0,32},{32,64},{64,96},{96,0},{1,33},{33,65},{65,97},{97,1},{2,34}... | collective-permute-start | bytes 2359304 | tf_op jit(solution)/shard_map/ppermute | solution.py:119
  17.4 52.8 %copy-start.8 = (s32[48]{0:T(128)}, s32[48]{0:T(128)S(1)}, u32[]{:S(2)}) copy-start(s32[48]{0:T(128)S(1)} %collective-permute-done.4) | copy-start | bytes 580
  32.6 23.2 %copy-start.1 = (bf16[24,128,128]{2,1,0:T(8,128)(2,1)}, bf16[24,128,128]{2,1,0:T(8,128)(2,1)S(1)}, u32[]{:S(2)}) copy-start(bf16[24,128,128]{2,1,0:T(8,128)(2,1)S(1)} %collective-permute-done.1.refs_4_) | copy-start | bytes 2359300
  34.2 21.7 %copy-start.2 = (bf16[24,128,128]{2,1,0:T(8,128)(2,1)}, bf16[24,128,128]{2,1,0:T(8,128)(2,1)S(1)}, u32[]{:S(2)}) copy-start(bf16[24,128,128]{2,1,0:T(8,128)(2,1)S(1)} %collective-permute-done.refs_1_) | copy-start | bytes 2359300
  34.2 21.6 %collective-permute-start.7 = (bf16[24,128,128]{2,1,0:T(8,128)(2,1)}, bf16[24,128,128]{2,1,0:T(8,128)(2,1)S(1)}, u32[]{:S(2)}, u32[]{:S(2)}) collective-permute-start(bf16[24,128,128]{2,1,0:T(8,128)(2,1)} %get-tuple-element.19), channel_id=1, source_target_pairs={{0,32},{32,64},{64,96},{96,0},{1,33},{33,65},{65,97},{97,1},{2,34}... | collective-permute-start | bytes 2359304 | tf_op jit(solution)/shard_map/ppermute | solution.py:119
  34.2 21.6 %collective-permute-start.8 = (bf16[24,128,128]{2,1,0:T(8,128)(2,1)}, bf16[24,128,128]{2,1,0:T(8,128)(2,1)S(1)}, u32[]{:S(2)}, u32[]{:S(2)}) collective-permute-start(bf16[24,128,128]{2,1,0:T(8,128)(2,1)} %copy-done.5), channel_id=1, source_target_pairs={{0,96},{32,0},{64,32},{96,64},{1,97},{33,1},{65,33},{97,65},{2,98}... | collective-permute-start | bytes 2359304 | tf_op jit(solution)/shard_map/ppermute | solution.py:119
  37.1 33.0 %collective-permute-start.5 = (bf16[24,128,128]{2,1,0:T(8,128)(2,1)S(1)}, bf16[24,128,128]{2,1,0:T(8,128)(2,1)}, u32[]{:S(2)}, u32[]{:S(2)}) collective-permute-start(bf16[24,128,128]{2,1,0:T(8,128)(2,1)S(1)} %collective-permute-done.refs_1_), channel_id=1, source_target_pairs={{0,32},{32,64},{64,96},{96,0},{1,33},{33,65},{65,97},{97,1},{2,34}... | collective-permute-start | bytes 2359304 | tf_op jit(solution)/shard_map/ppermute | solution.py:119
  37.1 33.0 %collective-permute-start.6 = (bf16[24,128,128]{2,1,0:T(8,128)(2,1)S(1)}, bf16[24,128,128]{2,1,0:T(8,128)(2,1)}, u32[]{:S(2)}, u32[]{:S(2)}) collective-permute-start(bf16[24,128,128]{2,1,0:T(8,128)(2,1)S(1)} %collective-permute-done.1.refs_4_), channel_id=1, source_target_pairs={{0,96},{32,0},{64,32},{96,64},{1,97},{33,1},{65,33},{97,65},{2,98}... | collective-permute-start | bytes 2359304 | tf_op jit(solution)/shard_map/ppermute | solution.py:119
  55.8 0.9 copy-start.3
  55.8 1.2 copy-start.4
Sparse Core Ops, SparseCore 0:
  9.0 16.9 all-gather.3
  87.1 116.3 reduce-scatter.1

commit v13 on v11

--- a/solution.py
+++ b/solution.py
@@ -10,11 +10,10 @@
 UNROLL = 16
 
 
-def pair_kernel(slots_left, slots_right, counts, left_ids, right_ids, pick,
+def pair_kernel(slots_left, slots_right, counts, places, pick,
                 own_left, below_low, below_high, above_low, above_high, far_low, far_high,
                 own_right, right_pair, totals, left_lists, right_lists, sems):
     half = far_low.shape[0]
-    slab_width = totals.shape[0] // ROWS_GROUP
     block_size = totals.shape[-1]
     copies = [
         [pltpu.make_async_copy(own_left, left_lists.at[0], sems.at[0]),
@@ -44,7 +43,7 @@
         def one_term(j, u=u, v=v):
             i = slots_left[u, j]
             k = slots_right[u, j]
-            t = left_ids[u, i] * slab_width + right_ids[v, k]
+            t = places[u, j]
             term = jnp.dot(left_lists[u, i], right_lists[v, k], preferred_element_type=jnp.float32)
             return t, term
 
@@ -128,8 +127,12 @@
     left_id_stack = jnp.stack([own_ids, ids_below, ids_above, ids_far])
     right_id_stack = jnp.take(right_ids_pair, jnp.stack([col_here, 1 - col_here]), axis=0)
     pick = jnp.stack([1 - col_here, col_here]).astype(jnp.int32)
-    scalars = (jnp.take(slots_left_all, piece, axis=0), jnp.take(slots_right_all, piece, axis=0),
-               jnp.take(counts_all, piece, axis=0), left_id_stack, right_id_stack, pick)
+    slots_left = jnp.take(slots_left_all, piece, axis=0)
+    slots_right = jnp.take(slots_right_all, piece, axis=0)
+    right_of = jnp.array([0, 1, 1, 0], jnp.int32)
+    places = (jnp.take_along_axis(left_id_stack, slots_left, axis=1) * slab_width
+              + jnp.take_along_axis(right_id_stack[right_of], slots_right, axis=1))
+    scalars = (slots_left, slots_right, jnp.take(counts_all, piece, axis=0), places, pick)
     totals = pair_products(scalars, (own_left, below_low, below_high, above_low, above_high,
                                      far_low, far_high, own_right, right_pair), targets)
     owned = lax.psum_scatter(totals, "layer", scatter_dimension=0, tiled=True)

time: 208 us -> 210 us (level)
  local copies, waits for them, and re-layouts: 3.99 us -> 17.5 us
  waiting for transfers between devices: 151 us -> 143 us
    gather x2 -> x9, local copies, waits for them, and re-layouts: 1.13 us -> 15.2 us  [the longest x3 6.77 us: on_device(): jnp.take_along_axis(left_id_stack, slots_left, axis=1) * slab_width]
    ppermute x9, waiting for transfers between devices: 36 us -> 27.2 us  [shifted(): return lax.ppermute(value, axis, pairs)]
  transfers between devices with their start and end apart: 11 -> 11, of which waited for: 6 -> 4; matrix products, arithmetic and copies ran while one was open for 3% -> 9% of each run, Pallas kernels for 0% -> 0%
where the time goes in v13:
time: 210 us; the launch traced here: 208 us
  waiting for transfers between devices  143 us (68%)
  Pallas kernels  18.2 us (9%)
  local copies, waits for them, and re-layouts  17.5 us (8%)
  between operations  13.6 us (6%)
  starting transfers between devices  12.5 us (6%)
    reduce_scatter x1, waiting for transfers between devices, on_device(): owned = lax.psum_scatter(totals, 'layer', scatter_dimension=0, tiled=True)  115 us
    ppermute x9, waiting for transfers between devices, shifted(): return lax.ppermute(value, axis, pairs)  27.2 us
    pallas_call x1, Pallas kernels, pair_products(): pl.pallas_call(pair_kernel, out_shape=jax.ShapeDtypeStruct((targets, bloc...  18.2 us
    ppermute x9, starting transfers between devices, shifted(): return lax.ppermute(value, axis, pairs)  12.4 us
    gather x3, local copies, waits for them, and re-layouts, on_device(): jnp.take_along_axis(left_id_stack, slots_left, axis=1) * slab_width  6.77 us
    gather x3, local copies, waits for them, and re-layouts, on_device(): jnp.take_along_axis(right_id_stack[right_of], slots_right, axis=1)  6.77 us
  transfers between devices with their start and end apart: 11, of which 4 were waited for; matrix products, arithmetic and copies ran while one was open for 9% of the time, Pallas kernels for 0%

profile of v13, /device:TPU:26, one launch (start us, length us, event | category | flops | bytes accessed | tf_op | source)
XLA Modules:
  0.0 208.2 jit_solution(4829705970521535264)
XLA Ops:
  6.5 0.7 all-gather.4.cloned.1.call-update
  7.3 0.0 reduce-scatter.2.cloned.1.call-start
  7.3 0.0 copy-start.12
  7.3 0.0 copy-start.8
  7.3 0.0 copy-start.14
  7.4 0.0 copy-start.1
  7.4 0.0 copy-start.11
  7.4 2.2 %collective-permute-start.4 = (s32[48]{0:T(128)S(1)}, s32[48]{0:T(128)S(1)}, u32[]{:S(2)}, u32[]{:S(2)}) collective-permute-start(s32[48]{0:T(128)S(1)} %bitcast.38), channel_id=1, source_target_pairs={{0,64},{32,96},{64,0},{96,32},{1,65},{33,97},{65,1},{97,33},{2,66}... | collective-permute-start | bytes 584 | tf_op jit(solution)/shard_map/ppermute | solution.py:89
  9.6 1.4 collective-permute-start.3
  11.0 0.6 collective-permute-start.2
  11.6 1.0 slice_bitcast_fusion
  12.6 1.4 collective-permute-start.1
  14.1 0.6 collective-permute-start
  14.7 0.6 gather_fusion.4
  15.3 0.6 gather_fusion.3
  15.8 0.1 compare_and_fusion.1
  15.9 0.1 fusion.1
  16.0 0.1 bitcast_or_fusion
  16.1 1.8 all-gather
  17.9 0.6 gather_fusion.1
  18.4 0.0 collective-permute-done.4
  18.4 0.0 collective-permute-done.3
  18.4 0.0 collective-permute-done.2
  18.5 12.8 %collective-permute-done.1.above_high = bf16[24,128,128]{2,1,0:T(8,128)(2,1)S(1)} collective-permute-done((bf16[24,128,128]{2,1,0:T(8,128)(2,1)}, bf16[24,128,128]{2,1,0:T(8,128)(2,1)S(1)}, u32[]{:S(2)}, u32[]{:S(2)}) %collective-permute-start.1) | collective-permute-done | bytes 786464 | tf_op jit(solution)/shard_map/ppermute | solution.py:89
  31.3 1.5 collective-permute-done.below_low
  32.8 0.0 collective-permute-start.5
  32.8 3.0 %collective-permute-start.6 = (bf16[24,128,128]{2,1,0:T(8,128)(2,1)}, bf16[24,128,128]{2,1,0:T(8,128)(2,1)S(1)}, u32[]{:S(2)}, u32[]{:S(2)}) collective-permute-start(bf16[24,128,128]{2,1,0:T(8,128)(2,1)} %copy-done.7), channel_id=1, source_target_pairs={{0,96},{32,0},{64,32},{96,64},{1,97},{33,1},{65,33},{97,65},{2,98}... | collective-permute-start | bytes 2359304 | tf_op jit(solution)/shard_map/ppermute | solution.py:89
  35.8 0.0 collective-permute-start.7
  35.8 3.2 %collective-permute-start.8 = (bf16[24,128,128]{2,1,0:T(8,128)(2,1)S(1)}, bf16[24,128,128]{2,1,0:T(8,128)(2,1)}, u32[]{:S(2)}, u32[]{:S(2)}) collective-permute-start(bf16[24,128,128]{2,1,0:T(8,128)(2,1)S(1)} %collective-permute-done.1.above_high), channel_id=1, source_target_pairs={{0,96},{32,0},{64,32},{96,64},{1,97},{33,1},{65,33},{97,65},{2,98}... | collective-permute-start | bytes 2359304 | tf_op jit(solution)/shard_map/ppermute | solution.py:89
  39.0 0.1 broadcast_select_fusion.2
  39.1 0.6 gather_fusion
  39.7 0.1 reshape.223
  39.8 0.6 gather_fusion.2
  40.4 6.6 %gather_fusion.6 = s32[768]{0:T(1024)S(1)} fusion(s32[4,48]{1,0:T(4,128)S(1)} %gather_fusion.2, s32[768]{0:T(1024)S(1)} %reshape.223), kind=kCustom, calls=%fused_computation.3.clone | custom fusion | bytes 12288 | tf_op jit(solution)/shard_map/jit(take_along_axis)/gather | solution.py:134
  47.0 0.1 reshape.226
  47.1 0.1 reshape.218
  47.2 0.6 pad_add_fusion.1.pick
  47.8 0.5 broadcast_select_fusion.3.counts
  48.3 6.6 %gather_fusion.5 = s32[768]{0:T(1024)S(1)} fusion(s32[4,48]{1,0:T(4,128)S(1)} %pad_add_fusion, s32[768]{0:T(1024)S(1)} %reshape.218), kind=kCustom, calls=%fused_computation.1.clone | custom fusion | bytes 12288 | tf_op jit(solution)/shard_map/jit(take_along_axis)/gather | solution.py:133
  55.0 0.1 reshape.221
  55.0 0.6 select_add_fusion.places
  55.7 0.0 collective-permute-done.5.below_high
  55.7 0.0 collective-permute-done.6.above_low
  55.7 12.8 %collective-permute-done.7.far_low = bf16[24,128,128]{2,1,0:T(8,128)(2,1)} collective-permute-done((bf16[24,128,128]{2,1,0:T(8,128)(2,1)S(1)}, bf16[24,128,128]{2,1,0:T(8,128)(2,1)}, u32[]{:S(2)}, u32[]{:S(2)}) %collective-permute-start.7) | collective-permute-done | bytes 786464 | tf_op jit(solution)/shard_map/ppermute | solution.py:89
  68.5 0.0 collective-permute-done.8.far_high
  68.5 18.2 %shard_map.91 = f32[256,128,128]{2,1,0:T(8,128)} custom-call(s32[4,192]{1,0:T(4,128)} %copy-done.10, s32[4,192]{1,0:T(4,128)} %copy-done.9, s32[4]{0:T(128)} %broadcast_select_fusion.3.counts, s32[4,192]{1,0:T(4,128)} %select_add_fusion.places, s32[2]{0:T(128)} %pad_add_fusion.1.pick, bf16[48,128,128]{2,1,0:T(8,128)(2,1)} %bitcast.34, ...), custom_call_target="tpu_custom_call" | custom-call | tf_op jit(solution)/shard_map/pallas_call | solution.py:72
  86.7 0.0 reduce-scatter.2.cloned.1.call-update
  86.7 114.7 %reduce-scatter.2.cloned.1.call-done = f32[16,128,128]{2,1,0:T(8,128)} async-done(((f32[256,128,128]{2,1,0:T(8,128)}), f32[16,128,128]{2,1,0:T(8,128)}) %reduce-scatter.2.cloned.1.call-update) | async-done | bytes 1048592 | tf_op jit(solution)/shard_map/reduce_scatter | solution.py:138
  (32 shorter events, 0.1 us)
Async XLA Ops:
  6.5 8.2 %copy-start = (s32[1,1,1,4,192]{4,3,2,1,0:T(4,128)S(1)}, s32[1,1,1,4,192]{4,3,2,1,0:T(4,128)}, u32[]{:S(2)}) copy-start(s32[1,1,1,4,192]{4,3,2,1,0:T(4,128)} %param.18) | copy-start | bytes 9220
  6.5 0.8 copy-start.13
  6.5 5.1 %copy-start.2 = (bf16[1,1,1,48,128,128]{5,4,3,2,1,0:T(8,128)(2,1)S(1)}, bf16[1,1,1,48,128,128]{5,4,3,2,1,0:T(8,128)(2,1)}, u32[]{:S(2)}) copy-start(bf16[1,1,1,48,128,128]{5,4,3,2,1,0:T(8,128)(2,1)} %param.13) | copy-start | bytes 4718596
  6.5 61.9 %all-gather.4.cloned.1.call-start = ((), (), s32[]{:S(2)}) async-start(), calls=%async_computation.2 | async-start | bytes 4718592 | tf_op jit(solution)/shard_map/all_gather | solution.py:112
  7.3 194.1 %reduce-scatter.2.cloned.1.call-start = ((), (), s32[]{:S(2)}) async-start(), calls=%async_computation.1 | async-start | bytes 17825792 | tf_op jit(solution)/shard_map/reduce_scatter | solution.py:138
  7.3 7.3 %copy-start.12 = (s32[4]{0:T(128)S(1)}, s32[4]{0:T(128)}, u32[]{:S(2)}) copy-start(s32[4]{0:T(128)} %constant.83.clone) | copy-start | bytes 52
  7.3 7.9 %copy-start.8 = (s32[1,1,1,4,192]{4,3,2,1,0:T(4,128)S(1)}, s32[1,1,1,4,192]{4,3,2,1,0:T(4,128)}, u32[]{:S(2)}) copy-start(s32[1,1,1,4,192]{4,3,2,1,0:T(4,128)} %param.17) | copy-start | bytes 9220
  7.3 8.7 %copy-start.14 = (s32[1,1,1,48]{3,2,1,0:T(1,128)S(1)}, s32[1,1,1,48]{3,2,1,0:T(1,128)}, u32[]{:S(2)}) copy-start(s32[1,1,1,48]{3,2,1,0:T(1,128)} %param.16) | copy-start | bytes 580
  7.4 31.8 %copy-start.1 = (s32[1,1,1,4]{3,2,1,0:T(1,128)S(1)}, s32[1,1,1,4]{3,2,1,0:T(1,128)}, u32[]{:S(2)}) copy-start(s32[1,1,1,4]{3,2,1,0:T(1,128)} %param.19) | copy-start | bytes 52
  7.4 32.5 %copy-start.11 = (s32[4]{0:T(128)S(1)}, s32[4]{0:T(128)}, u32[]{:S(2)}) copy-start(s32[4]{0:T(128)} %constant.122) | copy-start | bytes 52
  7.4 11.1 %collective-permute-start.4 = (s32[48]{0:T(128)S(1)}, s32[48]{0:T(128)S(1)}, u32[]{:S(2)}, u32[]{:S(2)}) collective-permute-start(s32[48]{0:T(128)S(1)} %bitcast.38), channel_id=1, source_target_pairs={{0,64},{32,96},{64,0},{96,32},{1,65},{33,97},{65,1},{97,33},{2,66}... | collective-permute-start | bytes 584 | tf_op jit(solution)/shard_map/ppermute | solution.py:89
  9.6 8.9 %collective-permute-start.3 = (s32[48]{0:T(128)S(1)}, s32[48]{0:T(128)S(1)}, u32[]{:S(2)}, u32[]{:S(2)}) collective-permute-start(s32[48]{0:T(128)S(1)} %bitcast.39), channel_id=1, source_target_pairs={{0,96},{32,0},{64,32},{96,64},{1,97},{33,1},{65,33},{97,65},{2,98}... | collective-permute-start | bytes 584 | tf_op jit(solution)/shard_map/ppermute | solution.py:89
  11.0 7.4 %collective-permute-start.2 = (s32[48]{0:T(128)S(1)}, s32[48]{0:T(128)S(1)}, u32[]{:S(2)}, u32[]{:S(2)}) collective-permute-start(s32[48]{0:T(128)S(1)} %bitcast.40), channel_id=1, source_target_pairs={{0,32},{32,64},{64,96},{96,0},{1,33},{33,65},{65,97},{97,1},{2,34}... | collective-permute-start | bytes 584 | tf_op jit(solution)/shard_map/ppermute | solution.py:89
  12.6 18.7 %copy-start.7 = (bf16[24,128,128]{2,1,0:T(8,128)(2,1)}, bf16[24,128,128]{2,1,0:T(8,128)(2,1)S(1)}, u32[]{:S(2)}) copy-start(bf16[24,128,128]{2,1,0:T(8,128)(2,1)S(1)} %get-tuple-element.19) | copy-start | bytes 2359300
  12.6 18.7 %collective-permute-start.1 = (bf16[24,128,128]{2,1,0:T(8,128)(2,1)}, bf16[24,128,128]{2,1,0:T(8,128)(2,1)S(1)}, u32[]{:S(2)}, u32[]{:S(2)}) collective-permute-start(bf16[24,128,128]{2,1,0:T(8,128)(2,1)} %get-tuple-element.18), channel_id=1, source_target_pairs={{0,96},{32,0},{64,32},{96,64},{1,97},{33,1},{65,33},{97,65},{2,98}... | collective-permute-start | bytes 2359304 | tf_op jit(solution)/shard_map/ppermute | solution.py:89
  14.1 18.8 %collective-permute-start = (bf16[24,128,128]{2,1,0:T(8,128)(2,1)S(1)}, bf16[24,128,128]{2,1,0:T(8,128)(2,1)S(1)}, u32[]{:S(2)}, u32[]{:S(2)}) collective-permute-start(bf16[24,128,128]{2,1,0:T(8,128)(2,1)S(1)} %get-tuple-element.19), channel_id=1, source_target_pairs={{0,32},{32,64},{64,96},{96,0},{1,33},{33,65},{65,97},{97,1},{2,34}... | collective-permute-start | bytes 2359304 | tf_op jit(solution)/shard_map/ppermute | solution.py:89
  16.1 39.0 %copy-start.9 = (s32[4,192]{1,0:T(4,128)}, s32[4,192]{1,0:T(4,128)S(1)}, u32[]{:S(2)}) copy-start(s32[4,192]{1,0:T(4,128)S(1)} %get-tuple-element.24.slots_right) | copy-start | bytes 9220
  16.1 39.0 %copy-start.10 = (s32[4,192]{1,0:T(4,128)}, s32[4,192]{1,0:T(4,128)S(1)}, u32[]{:S(2)}) copy-start(s32[4,192]{1,0:T(4,128)S(1)} %get-tuple-element.30.slots_left) | copy-start | bytes 9220
  31.3 15.7 %copy-start.3 = (bf16[24,128,128]{2,1,0:T(8,128)(2,1)}, bf16[24,128,128]{2,1,0:T(8,128)(2,1)S(1)}, u32[]{:S(2)}) copy-start(bf16[24,128,128]{2,1,0:T(8,128)(2,1)S(1)} %collective-permute-done.1.above_high) | copy-start | bytes 2359300
  32.8 14.2 %copy-start.4 = (bf16[24,128,128]{2,1,0:T(8,128)(2,1)}, bf16[24,128,128]{2,1,0:T(8,128)(2,1)S(1)}, u32[]{:S(2)}) copy-start(bf16[24,128,128]{2,1,0:T(8,128)(2,1)S(1)} %collective-permute-done.below_low) | copy-start | bytes 2359300
  32.8 22.8 %collective-permute-start.5 = (bf16[24,128,128]{2,1,0:T(8,128)(2,1)}, bf16[24,128,128]{2,1,0:T(8,128)(2,1)S(1)}, u32[]{:S(2)}, u32[]{:S(2)}) collective-permute-start(bf16[24,128,128]{2,1,0:T(8,128)(2,1)} %get-tuple-element.18), channel_id=1, source_target_pairs={{0,32},{32,64},{64,96},{96,0},{1,33},{33,65},{65,97},{97,1},{2,34}... | collective-permute-start | bytes 2359304 | tf_op jit(solution)/shard_map/ppermute | solution.py:89
  32.8 22.8 %collective-permute-start.6 = (bf16[24,128,128]{2,1,0:T(8,128)(2,1)}, bf16[24,128,128]{2,1,0:T(8,128)(2,1)S(1)}, u32[]{:S(2)}, u32[]{:S(2)}) collective-permute-start(bf16[24,128,128]{2,1,0:T(8,128)(2,1)} %copy-done.7), channel_id=1, source_target_pairs={{0,96},{32,0},{64,32},{96,64},{1,97},{33,1},{65,33},{97,65},{2,98}... | collective-permute-start | bytes 2359304 | tf_op jit(solution)/shard_map/ppermute | solution.py:89
  35.8 32.7 %collective-permute-start.7 = (bf16[24,128,128]{2,1,0:T(8,128)(2,1)S(1)}, bf16[24,128,128]{2,1,0:T(8,128)(2,1)}, u32[]{:S(2)}, u32[]{:S(2)}) collective-permute-start(bf16[24,128,128]{2,1,0:T(8,128)(2,1)S(1)} %collective-permute-done.below_low), channel_id=1, source_target_pairs={{0,32},{32,64},{64,96},{96,0},{1,33},{33,65},{65,97},{97,1},{2,34}... | collective-permute-start | bytes 2359304 | tf_op jit(solution)/shard_map/ppermute | solution.py:89
  35.8 32.7 %collective-permute-start.8 = (bf16[24,128,128]{2,1,0:T(8,128)(2,1)S(1)}, bf16[24,128,128]{2,1,0:T(8,128)(2,1)}, u32[]{:S(2)}, u32[]{:S(2)}) collective-permute-start(bf16[24,128,128]{2,1,0:T(8,128)(2,1)S(1)} %collective-permute-done.1.above_high), channel_id=1, source_target_pairs={{0,96},{32,0},{64,32},{96,64},{1,97},{33,1},{65,33},{97,65},{2,98}... | collective-permute-start | bytes 2359304 | tf_op jit(solution)/shard_map/ppermute | solution.py:89
  55.7 12.8 %copy-start.5 = (bf16[24,128,128]{2,1,0:T(8,128)(2,1)}, bf16[24,128,128]{2,1,0:T(8,128)(2,1)S(1)}, u32[]{:S(2)}) copy-start(bf16[24,128,128]{2,1,0:T(8,128)(2,1)S(1)} %collective-permute-done.5.below_high) | copy-start | bytes 2359300
  55.7 12.8 %copy-start.6 = (bf16[24,128,128]{2,1,0:T(8,128)(2,1)}, bf16[24,128,128]{2,1,0:T(8,128)(2,1)S(1)}, u32[]{:S(2)}) copy-start(bf16[24,128,128]{2,1,0:T(8,128)(2,1)S(1)} %collective-permute-done.6.above_low) | copy-start | bytes 2359300
Sparse Core Ops, SparseCore 0:
  9.0 16.9 all-gather.3
  86.8 114.5 reduce-scatter.1

commit v14 on v11

--- a/solution.py
+++ b/solution.py
@@ -112,11 +112,10 @@
     above_high = shifted(own_high, "row", -1)
     right_pair = lax.all_gather(own_right, "col")
     right_ids_pair = lax.all_gather(right_cols.reshape(right_cap), "col")
-    below_low, above_high, own_low, own_high, ids_below, ids_above, ids_far = (
-        lax.optimization_barrier(
-            (below_low, above_high, own_low, own_high, ids_below, ids_above, ids_far)))
     below_high = shifted(own_high, "row", 1)
     above_low = shifted(own_low, "row", -1)
+    below_low, above_high, ids_below, ids_above, ids_far = lax.optimization_barrier(
+        (below_low, above_high, ids_below, ids_above, ids_far))
     far_low = shifted(below_low, "row", 1)
     far_high = shifted(above_high, "row", -1)
 

time: 208 us -> 207 us (level)
  no operation moved by 1% of the time
where the time goes in v14:
time: 207 us; the launch traced here: 206 us
  waiting for transfers between devices  152 us (73%)
  Pallas kernels  18.2 us (9%)
  between operations  13.5 us (7%)
  starting transfers between devices  13.2 us (6%)
  local copies, waits for them, and re-layouts  4.22 us (2%)
  other arithmetic  3.33 us (2%)
    reduce_scatter x1, waiting for transfers between devices, on_device(): owned = lax.psum_scatter(totals, 'layer', scatter_dimension=0, tiled=True)  115 us
    ppermute x9, waiting for transfers between devices, shifted(): return lax.ppermute(value, axis, pairs)  36.6 us
    pallas_call x1, Pallas kernels, pair_products(): pl.pallas_call(pair_kernel, out_shape=jax.ShapeDtypeStruct((targets, bloc...  18.2 us
    ppermute x9, starting transfers between devices, shifted(): return lax.ppermute(value, axis, pairs)  13.1 us
  transfers between devices with their start and end apart: 11, of which 6 were waited for; matrix products, arithmetic and copies ran while one was open for 3% of the time, Pallas kernels for 0%

profile of v14, /device:TPU:26, one launch (start us, length us, event | category | flops | bytes accessed | tf_op | source)
XLA Modules:
  0.0 206.4 jit_solution(1079000876619947379)
XLA Ops:
  6.5 0.0 copy-start
  6.5 0.0 all-gather.4.cloned.1.call-start
  6.5 0.7 all-gather.4.cloned.1.call-update
  7.3 0.0 copy-start.9
  7.3 0.0 copy-start.8
  7.3 0.0 copy-start.1
  7.3 0.0 copy-start.7
  7.3 0.0 copy-start.10
  7.3 0.0 reduce-scatter.2.cloned.1.call-start
  7.4 0.6 copy-done.2
  8.0 1.3 slice_bitcast_fusion
  9.2 0.5 collective-permute-start.1
  9.7 1.5 collective-permute-start
  11.2 0.0 copy-done.9
  11.2 3.3 %collective-permute-start.4 = (s32[48]{0:T(128)S(1)}, s32[48]{0:T(128)S(1)}, u32[]{:S(2)}, u32[]{:S(2)}) collective-permute-start(s32[48]{0:T(128)S(1)} %bitcast.30), channel_id=1, source_target_pairs={{0,64},{32,96},{64,0},{96,32},{1,65},{33,97},{65,1},{97,33},{2,66}... | collective-permute-start | bytes 584 | tf_op jit(solution)/shard_map/ppermute | solution.py:90
  14.6 0.2 collective-permute-start.3
  14.8 1.8 collective-permute-start.2
  16.6 0.1 fusion.1
  16.7 0.0 copy-done.8
  16.7 0.7 pad_add_fusion.1.pick
  17.4 12.2 %collective-permute-done.4 = s32[48]{0:T(128)S(1)} collective-permute-done((s32[48]{0:T(128)S(1)}, s32[48]{0:T(128)S(1)}, u32[]{:S(2)}, u32[]{:S(2)}) %collective-permute-start.4) | collective-permute-done | bytes 224 | tf_op jit(solution)/shard_map/ppermute | solution.py:90
  29.6 1.8 collective-permute-start.5
  31.4 0.0 collective-permute-done.3
  31.4 0.6 collective-permute-start.6
  32.0 0.0 collective-permute-done.2
  32.0 0.0 collective-permute-done.1.above_high
  32.0 0.0 collective-permute-done.below_low
  32.0 1.5 collective-permute-start.7
  33.6 1.8 collective-permute-start.8
  35.4 0.1 compare_and_fusion.1
  35.5 0.6 gather_fusion
  36.1 0.6 gather_fusion.3
  36.7 0.6 gather_fusion.2
  37.3 1.8 all-gather
  39.0 0.6 gather_fusion.1
  39.6 0.5 broadcast_select_fusion.3.counts
  40.1 0.7 broadcast_select_fusion.2.right_ids
  40.8 0.7 broadcast_select_fusion
  41.5 0.6 pad_add_fusion.left_ids
  42.1 8.6 %collective-permute-done.5.below_high = bf16[24,128,128]{2,1,0:T(8,128)(2,1)S(1)} collective-permute-done((bf16[24,128,128]{2,1,0:T(8,128)(2,1)}, bf16[24,128,128]{2,1,0:T(8,128)(2,1)S(1)}, u32[]{:S(2)}, u32[]{:S(2)}) %collective-permute-start.5) | collective-permute-done | bytes 786464 | tf_op jit(solution)/shard_map/ppermute | solution.py:90
  50.6 1.5 collective-permute-done.6.above_low
  52.1 13.1 %collective-permute-done.7.far_low = bf16[24,128,128]{2,1,0:T(8,128)(2,1)} collective-permute-done((bf16[24,128,128]{2,1,0:T(8,128)(2,1)S(1)}, bf16[24,128,128]{2,1,0:T(8,128)(2,1)}, u32[]{:S(2)}, u32[]{:S(2)}) %collective-permute-start.7) | collective-permute-done | bytes 786464 | tf_op jit(solution)/shard_map/ppermute | solution.py:90
  65.2 1.2 collective-permute-done.8.far_high
  66.4 0.0 copy-done.4
  66.4 0.0 copy-done.6
  66.5 18.2 %shard_map.82 = f32[256,128,128]{2,1,0:T(8,128)} custom-call(s32[4,192]{1,0:T(4,128)} %get-tuple-element.21.slots_left, s32[4,192]{1,0:T(4,128)} %get-tuple-element.20.slots_right, s32[4]{0:T(128)} %broadcast_select_fusion.3.counts, s32[4,48]{1,0:T(4,128)} %pad_add_fusion.left_ids, s32[2,48]{1,0:T(2,128)} %broadcast_select_fusion.2.right_ids, ...), custom_call_target="tpu_custom_call" | custom-call | tf_op jit(solution)/shard_map/pallas_call | solution.py:73
  84.7 0.0 reduce-scatter.2.cloned.1.call-update
  84.7 114.8 %reduce-scatter.2.cloned.1.call-done = f32[16,128,128]{2,1,0:T(8,128)} async-done(((f32[256,128,128]{2,1,0:T(8,128)}), f32[16,128,128]{2,1,0:T(8,128)}) %reduce-scatter.2.cloned.1.call-update) | async-done | bytes 1048592 | tf_op jit(solution)/shard_map/reduce_scatter | solution.py:134
  (15 shorter events, 0.1 us)
Async XLA Ops:
  6.5 29.6 %copy-start = (s32[1,1,1,4,192]{4,3,2,1,0:T(4,128)S(1)}, s32[1,1,1,4,192]{4,3,2,1,0:T(4,128)}, u32[]{:S(2)}) copy-start(s32[1,1,1,4,192]{4,3,2,1,0:T(4,128)} %param.15) | copy-start | bytes 9220
  6.5 1.4 copy-start.2
  6.5 59.9 %all-gather.4.cloned.1.call-start = ((), (), s32[]{:S(2)}) async-start(), calls=%async_computation.2 | async-start | bytes 4718592 | tf_op jit(solution)/shard_map/all_gather | solution.py:113
  7.3 4.0 %copy-start.9 = (s32[1,1,1,48]{3,2,1,0:T(1,128)S(1)}, s32[1,1,1,48]{3,2,1,0:T(1,128)}, u32[]{:S(2)}) copy-start(s32[1,1,1,48]{3,2,1,0:T(1,128)} %param.11) | copy-start | bytes 580
  7.3 9.4 %copy-start.8 = (s32[4]{0:T(128)S(1)}, s32[4]{0:T(128)}, u32[]{:S(2)}) copy-start(s32[4]{0:T(128)} %constant.67.clone) | copy-start | bytes 52
  7.3 28.2 %copy-start.1 = (s32[1,1,1,4]{3,2,1,0:T(1,128)S(1)}, s32[1,1,1,4]{3,2,1,0:T(1,128)}, u32[]{:S(2)}) copy-start(s32[1,1,1,4]{3,2,1,0:T(1,128)} %param.16) | copy-start | bytes 52
  7.3 29.4 %copy-start.7 = (s32[1,1,1,4,192]{4,3,2,1,0:T(4,128)S(1)}, s32[1,1,1,4,192]{4,3,2,1,0:T(4,128)}, u32[]{:S(2)}) copy-start(s32[1,1,1,4,192]{4,3,2,1,0:T(4,128)} %param.14) | copy-start | bytes 9220
  7.3 30.0 %copy-start.10 = (s32[1,1,1,48]{3,2,1,0:T(1,128)S(1)}, s32[1,1,1,48]{3,2,1,0:T(1,128)}, u32[]{:S(2)}) copy-start(s32[1,1,1,48]{3,2,1,0:T(1,128)} %param.13) | copy-start | bytes 580
  7.3 192.2 %reduce-scatter.2.cloned.1.call-start = ((), (), s32[]{:S(2)}) async-start(), calls=%async_computation.1 | async-start | bytes 17825792 | tf_op jit(solution)/shard_map/reduce_scatter | solution.py:134
  9.2 22.8 %collective-permute-start.1 = (bf16[24,128,128]{2,1,0:T(8,128)(2,1)}, bf16[24,128,128]{2,1,0:T(8,128)(2,1)S(1)}, u32[]{:S(2)}, u32[]{:S(2)}) collective-permute-start(bf16[24,128,128]{2,1,0:T(8,128)(2,1)} %get-tuple-element.18), channel_id=1, source_target_pairs={{0,96},{32,0},{64,32},{96,64},{1,97},{33,1},{65,33},{97,65},{2,98}... | collective-permute-start | bytes 2359304 | tf_op jit(solution)/shard_map/ppermute | solution.py:90
  9.7 22.2 %collective-permute-start = (bf16[24,128,128]{2,1,0:T(8,128)(2,1)}, bf16[24,128,128]{2,1,0:T(8,128)(2,1)S(1)}, u32[]{:S(2)}, u32[]{:S(2)}) collective-permute-start(bf16[24,128,128]{2,1,0:T(8,128)(2,1)} %get-tuple-element.19), channel_id=1, source_target_pairs={{0,32},{32,64},{64,96},{96,0},{1,33},{33,65},{65,97},{97,1},{2,34}... | collective-permute-start | bytes 2359304 | tf_op jit(solution)/shard_map/ppermute | solution.py:90
  11.2 18.4 %collective-permute-start.4 = (s32[48]{0:T(128)S(1)}, s32[48]{0:T(128)S(1)}, u32[]{:S(2)}, u32[]{:S(2)}) collective-permute-start(s32[48]{0:T(128)S(1)} %bitcast.30), channel_id=1, source_target_pairs={{0,64},{32,96},{64,0},{96,32},{1,65},{33,97},{65,1},{97,33},{2,66}... | collective-permute-start | bytes 584 | tf_op jit(solution)/shard_map/ppermute | solution.py:90
  14.6 16.9 %collective-permute-start.3 = (s32[48]{0:T(128)S(1)}, s32[48]{0:T(128)S(1)}, u32[]{:S(2)}, u32[]{:S(2)}) collective-permute-start(s32[48]{0:T(128)S(1)} %bitcast.31), channel_id=1, source_target_pairs={{0,96},{32,0},{64,32},{96,64},{1,97},{33,1},{65,33},{97,65},{2,98}... | collective-permute-start | bytes 584 | tf_op jit(solution)/shard_map/ppermute | solution.py:90
  14.8 17.2 %collective-permute-start.2 = (s32[48]{0:T(128)S(1)}, s32[48]{0:T(128)S(1)}, u32[]{:S(2)}, u32[]{:S(2)}) collective-permute-start(s32[48]{0:T(128)S(1)} %bitcast.32), channel_id=1, source_target_pairs={{0,32},{32,64},{64,96},{96,0},{1,33},{33,65},{65,97},{97,1},{2,34}... | collective-permute-start | bytes 584 | tf_op jit(solution)/shard_map/ppermute | solution.py:90
  29.6 21.0 %collective-permute-start.5 = (bf16[24,128,128]{2,1,0:T(8,128)(2,1)}, bf16[24,128,128]{2,1,0:T(8,128)(2,1)S(1)}, u32[]{:S(2)}, u32[]{:S(2)}) collective-permute-start(bf16[24,128,128]{2,1,0:T(8,128)(2,1)} %get-tuple-element.18), channel_id=1, source_target_pairs={{0,32},{32,64},{64,96},{96,0},{1,33},{33,65},{65,97},{97,1},{2,34}... | collective-permute-start | bytes 2359304 | tf_op jit(solution)/shard_map/ppermute | solution.py:90
  31.4 20.7 %collective-permute-start.6 = (bf16[24,128,128]{2,1,0:T(8,128)(2,1)}, bf16[24,128,128]{2,1,0:T(8,128)(2,1)S(1)}, u32[]{:S(2)}, u32[]{:S(2)}) collective-permute-start(bf16[24,128,128]{2,1,0:T(8,128)(2,1)} %get-tuple-element.19), channel_id=1, source_target_pairs={{0,96},{32,0},{64,32},{96,64},{1,97},{33,1},{65,33},{97,65},{2,98}... | collective-permute-start | bytes 2359304 | tf_op jit(solution)/shard_map/ppermute | solution.py:90
  32.0 34.4 %copy-start.3 = (bf16[24,128,128]{2,1,0:T(8,128)(2,1)}, bf16[24,128,128]{2,1,0:T(8,128)(2,1)S(1)}, u32[]{:S(2)}) copy-start(bf16[24,128,128]{2,1,0:T(8,128)(2,1)S(1)} %collective-permute-done.1.above_high) | copy-start | bytes 2359300
  32.0 34.4 %copy-start.4 = (bf16[24,128,128]{2,1,0:T(8,128)(2,1)}, bf16[24,128,128]{2,1,0:T(8,128)(2,1)S(1)}, u32[]{:S(2)}) copy-start(bf16[24,128,128]{2,1,0:T(8,128)(2,1)S(1)} %collective-permute-done.below_low) | copy-start | bytes 2359300
  32.0 33.2 %collective-permute-start.7 = (bf16[24,128,128]{2,1,0:T(8,128)(2,1)S(1)}, bf16[24,128,128]{2,1,0:T(8,128)(2,1)}, u32[]{:S(2)}, u32[]{:S(2)}) collective-permute-start(bf16[24,128,128]{2,1,0:T(8,128)(2,1)S(1)} %collective-permute-done.below_low), channel_id=1, source_target_pairs={{0,32},{32,64},{64,96},{96,0},{1,33},{33,65},{65,97},{97,1},{2,34}... | collective-permute-start | bytes 2359304 | tf_op jit(solution)/shard_map/ppermute | solution.py:90
  33.6 32.9 %collective-permute-start.8 = (bf16[24,128,128]{2,1,0:T(8,128)(2,1)S(1)}, bf16[24,128,128]{2,1,0:T(8,128)(2,1)}, u32[]{:S(2)}, u32[]{:S(2)}) collective-permute-start(bf16[24,128,128]{2,1,0:T(8,128)(2,1)S(1)} %collective-permute-done.1.above_high), channel_id=1, source_target_pairs={{0,96},{32,0},{64,32},{96,64},{1,97},{33,1},{65,33},{97,65},{2,98}... | collective-permute-start | bytes 2359304 | tf_op jit(solution)/shard_map/ppermute | solution.py:90
  50.6 15.8 %copy-start.5 = (bf16[24,128,128]{2,1,0:T(8,128)(2,1)}, bf16[24,128,128]{2,1,0:T(8,128)(2,1)S(1)}, u32[]{:S(2)}) copy-start(bf16[24,128,128]{2,1,0:T(8,128)(2,1)S(1)} %collective-permute-done.5.below_high) | copy-start | bytes 2359300
  52.1 14.3 %copy-start.6 = (bf16[24,128,128]{2,1,0:T(8,128)(2,1)}, bf16[24,128,128]{2,1,0:T(8,128)(2,1)S(1)}, u32[]{:S(2)}) copy-start(bf16[24,128,128]{2,1,0:T(8,128)(2,1)S(1)} %collective-permute-done.6.above_low) | copy-start | bytes 2359300
Sparse Core Ops, SparseCore 0:
  9.0 16.9 all-gather.3
  84.8 114.6 reduce-scatter.1

commit v15 on v13

--- a/solution.py
+++ b/solution.py
@@ -10,10 +10,11 @@
 UNROLL = 16
 
 
-def pair_kernel(slots_left, slots_right, counts, places, pick,
+def pair_kernel(slots_left, slots_right, counts, left_ids, right_ids, pick, order, bounds,
                 own_left, below_low, below_high, above_low, above_high, far_low, far_high,
-                own_right, right_pair, totals, left_lists, right_lists, sems):
+                own_right, right_pair, out, totals, left_lists, right_lists, sems, out_sem):
     half = far_low.shape[0]
+    slab_width = totals.shape[0] // ROWS_GROUP
     block_size = totals.shape[-1]
     copies = [
         [pltpu.make_async_copy(own_left, left_lists.at[0], sems.at[0]),
@@ -36,6 +37,16 @@
 
     lax.fori_loop(0, totals.shape[0], clear, 0)
 
+    def flush(group):
+        def one(n, carry):
+            t = order[n]
+            pltpu.make_async_copy(totals.at[t], out.at[t], out_sem.at[0]).start()
+            return carry
+
+        lax.fori_loop(bounds[group], bounds[group + 1], one, 0)
+
+    flush(0)
+
     for u, v in enumerate((0, 1, 1, 0)):
         for copy in copies[u]:
             copy.wait()
@@ -43,7 +54,7 @@
         def one_term(j, u=u, v=v):
             i = slots_left[u, j]
             k = slots_right[u, j]
-            t = places[u, j]
+            t = left_ids[u, i] * slab_width + right_ids[v, k]
             term = jnp.dot(left_lists[u, i], right_lists[v, k], preferred_element_type=jnp.float32)
             return t, term
 
@@ -62,6 +73,9 @@
         groups = count // UNROLL
         lax.fori_loop(0, groups, add_group, 0)
         lax.fori_loop(groups * UNROLL, count, add_single, 0)
+        flush(u + 1)
+
+    pltpu.make_async_copy(totals, out, out_sem.at[0]).wait()
 
 
 def pair_products(scalars, lists, targets):
@@ -73,11 +87,13 @@
         pair_kernel,
         out_shape=jax.ShapeDtypeStruct((targets, block_size, block_size), jnp.float32),
         in_specs=[smem] * len(scalars) + [hbm] * len(lists),
-        out_specs=pl.BlockSpec(memory_space=pltpu.VMEM),
+        out_specs=hbm,
         scratch_shapes=[
+            pltpu.VMEM((targets, block_size, block_size), jnp.float32),
             pltpu.VMEM((4, list_cap, block_size, block_size), jnp.bfloat16),
             pltpu.VMEM((2, list_cap, block_size, block_size), jnp.bfloat16),
             pltpu.SemaphoreType.DMA((9,)),
+            pltpu.SemaphoreType.DMA((1,)),
         ],
         compiler_params=pltpu.CompilerParams(vmem_limit_bytes=60 * 1024 * 1024),
     )(*scalars, *lists)
@@ -129,10 +145,21 @@
     pick = jnp.stack([1 - col_here, col_here]).astype(jnp.int32)
     slots_left = jnp.take(slots_left_all, piece, axis=0)
     slots_right = jnp.take(slots_right_all, piece, axis=0)
+    counts = jnp.take(counts_all, piece, axis=0)
     right_of = jnp.array([0, 1, 1, 0], jnp.int32)
     places = (jnp.take_along_axis(left_id_stack, slots_left, axis=1) * slab_width
               + jnp.take_along_axis(right_id_stack[right_of], slots_right, axis=1))
-    scalars = (slots_left, slots_right, jnp.take(counts_all, piece, axis=0), places, pick)
+    live = jnp.arange(slots_left.shape[1], dtype=jnp.int32)[None, :] < counts[:, None]
+    lists = jnp.arange(4, dtype=jnp.int32)[:, None] + jnp.zeros_like(places)
+    last = jnp.full((targets,), -1, jnp.int32).at[places.reshape(-1)].max(
+        jnp.where(live, lists, -1).reshape(-1))
+    member = (last[:, None] == jnp.arange(-1, 4, dtype=jnp.int32)[None, :]).astype(jnp.int32)
+    sizes = member.sum(axis=0)
+    bounds = jnp.concatenate([jnp.zeros((1,), jnp.int32), jnp.cumsum(sizes)]).astype(jnp.int32)
+    rank = jnp.sum((jnp.cumsum(member, axis=0) - 1) * member, axis=1)
+    slot = jnp.take(bounds, last + 1) + rank
+    order = jnp.zeros((targets,), jnp.int32).at[slot].set(jnp.arange(targets, dtype=jnp.int32))
+    scalars = (slots_left, slots_right, counts, left_id_stack, right_id_stack, pick, order, bounds)
     totals = pair_products(scalars, (own_left, below_low, below_high, above_low, above_high,
                                      far_low, far_high, own_right, right_pair), targets)
     owned = lax.psum_scatter(totals, "layer", scatter_dimension=0, tiled=True)

time: 210 us -> 220 us (1.048)
  other arithmetic: 2.09 us -> 12.8 us
  Pallas kernels: 18.2 us -> 14.6 us
  local copies, waits for them, and re-layouts: 17.5 us -> 20.6 us
    another operation x0 -> x4, other arithmetic: none -> 7.57 us  [the longest x1 5.85 us: on_device(): jnp.full((targets,), -1, jnp.int32).at[places.reshape(-1)]]
    pallas_call x1, Pallas kernels: 18.2 us -> 14.6 us  [pair_products(): pl.pallas_call(pair_kernel, out_shape=jax.ShapeDtypeStruct((targets, bloc...]
    select_n x1 -> x4, other arithmetic: 0.54 us -> 3.28 us  [the longest x1 3.19 us: on_device(): jnp.zeros((targets,), jnp.int32).at[slot]]
  transfers between devices with their start and end apart: 11 -> 11, of which waited for: 4 -> 5; matrix products, arithmetic and copies ran while one was open for 9% -> 15% of each run, Pallas kernels for 0% -> 0%
where the time goes in v15:
time: 220 us; the launch traced here: 219 us
  waiting for transfers between devices  143 us (65%)
  local copies, waits for them, and re-layouts  20.6 us (9%)
  Pallas kernels  14.6 us (7%)
  between operations  13.7 us (6%)
  other arithmetic  12.8 us (6%)
  starting transfers between devices  12.5 us (6%)
    reduce_scatter x1, waiting for transfers between devices, on_device(): owned = lax.psum_scatter(totals, 'layer', scatter_dimension=0, tiled=True)  115 us
    ppermute x9, waiting for transfers between devices, shifted(): return lax.ppermute(value, axis, pairs)  27.9 us
    pallas_call x1, Pallas kernels, pair_products(): pl.pallas_call(pair_kernel, out_shape=jax.ShapeDtypeStruct((targets, bloc...  14.6 us
    ppermute x9, starting transfers between devices, shifted(): return lax.ppermute(value, axis, pairs)  12.4 us
    gather x3, local copies, waits for them, and re-layouts, on_device(): jnp.take_along_axis(left_id_stack, slots_left, axis=1) * slab_width  6.77 us
    gather x3, local copies, waits for them, and re-layouts, on_device(): jnp.take_along_axis(right_id_stack[right_of], slots_right, axis=1)  6.77 us
    another operation x1, other arithmetic, on_device(): jnp.full((targets,), -1, jnp.int32).at[places.reshape(-1)]  5.85 us
  transfers between devices with their start and end apart: 11, of which 5 were waited for; matrix products, arithmetic and copies ran while one was open for 15% of the time, Pallas kernels for 0%

profile of v15, /device:TPU:26, one launch (start us, length us, event | category | flops | bytes accessed | tf_op | source)
XLA Modules:
  0.0 218.7 jit_solution(5173273976093030720)
XLA Ops:
  6.5 2.1 collective-permute-start.4
  8.7 1.4 collective-permute-start.3
  10.1 0.6 collective-permute-start.2
  10.8 0.0 reduce-scatter.2.cloned.1.call-start
  10.8 1.0 slice_bitcast_fusion
  11.8 1.4 collective-permute-start.1
  13.3 0.6 collective-permute-start
  13.9 0.6 gather_fusion
  14.6 0.6 gather_fusion.4
  15.1 0.6 gather_fusion.3
  15.7 0.1 iota_select_fusion
  15.8 0.1 bitcast_or_fusion
  15.9 0.1 fusion.5
  16.0 0.1 reshape.321
  16.0 0.1 reshape.370
  16.1 1.8 all-gather
  17.9 0.6 gather_fusion.1
  18.4 0.1 compare_and_fusion.1
  18.5 0.1 broadcast_select_fusion.2.right_ids
  18.6 0.6 gather_fusion.2
  19.2 6.6 %gather_fusion.6 = s32[768]{0:T(1024)S(1)} fusion(s32[4,48]{1,0:T(4,128)S(1)} %gather_fusion.2, s32[768]{0:T(1024)S(1)} %reshape.370), kind=kCustom, calls=%fused_computation.3.clone | custom fusion | bytes 12288 | tf_op jit(solution)/shard_map/jit(take_along_axis)/gather | solution.py:151
  25.8 0.6 pad_add_fusion.1.pick
  26.5 0.1 reshape.373
  26.5 0.1 reshape.365
  26.6 3.9 %collective-permute-done.1.above_high = bf16[24,128,128]{2,1,0:T(8,128)(2,1)S(1)} collective-permute-done((bf16[24,128,128]{2,1,0:T(8,128)(2,1)}, bf16[24,128,128]{2,1,0:T(8,128)(2,1)S(1)}, u32[]{:S(2)}, u32[]{:S(2)}) %collective-permute-start.1) | collective-permute-done | bytes 786464 | tf_op jit(solution)/shard_map/ppermute | solution.py:105
  30.5 1.5 collective-permute-done.below_low
  32.1 6.6 %gather_fusion.5 = s32[768]{0:T(1024)S(1)} fusion(s32[4,48]{1,0:T(4,128)S(1)} %pad_add_fusion.left_ids, s32[768]{0:T(1024)S(1)} %reshape.365), kind=kCustom, calls=%fused_computation.1.clone | custom fusion | bytes 12288 | tf_op jit(solution)/shard_map/jit(take_along_axis)/gather | solution.py:150
  38.7 0.1 reshape.368
  38.8 0.1 reshape.244
  38.9 5.8 %scatter_custom_fusion = s32[256]{0:T(256)S(1)} fusion(s32[768]{0:T(1024)S(1)} %fusion.2, s32[768]{0:T(1024)S(1)} %reshape.321, s32[]{:T(128)} %constant.114.clone.1), kind=kCustom, calls=%fused_computation.58 | custom fusion | flops 768 | bytes 1028 | tf_op jit(solution)/shard_map/scatter-max | solution.py:154
  44.8 0.1 compare_convert_fusion.1
  44.8 1.5 reduce-window.20
  46.4 0.1 slice.55
  46.4 0.1 copy.16
  46.6 0.1 copy.17
  46.7 3.0 %collective-permute-start.6 = (bf16[24,128,128]{2,1,0:T(8,128)(2,1)}, bf16[24,128,128]{2,1,0:T(8,128)(2,1)S(1)}, u32[]{:S(2)}, u32[]{:S(2)}) collective-permute-start(bf16[24,128,128]{2,1,0:T(8,128)(2,1)} %copy-done.8), channel_id=1, source_target_pairs={{0,96},{32,0},{64,32},{96,64},{1,97},{33,1},{65,33},{97,65},{2,98}... | collective-permute-start | bytes 2359304 | tf_op jit(solution)/shard_map/ppermute | solution.py:105
  49.7 3.2 %collective-permute-start.8 = (bf16[24,128,128]{2,1,0:T(8,128)(2,1)S(1)}, bf16[24,128,128]{2,1,0:T(8,128)(2,1)}, u32[]{:S(2)}, u32[]{:S(2)}) collective-permute-start(bf16[24,128,128]{2,1,0:T(8,128)(2,1)S(1)} %collective-permute-done.1.above_high), channel_id=1, source_target_pairs={{0,96},{32,0},{64,32},{96,64},{1,97},{33,1},{65,33},{97,65},{2,98}... | collective-permute-start | bytes 2359304 | tf_op jit(solution)/shard_map/ppermute | solution.py:105
  52.9 0.1 add_bitcast_fusion
  53.0 0.2 fusion
  53.2 0.2 reduce-window.19
  53.4 0.7 fusion.10
  54.1 3.2 %compare_select_fusion.4 = s32[256]{0:T(256)S(1)} fusion(s32[256]{0:T(256)S(1)} %get-tuple-element.22, s32[256]{0:T(256)S(1)} %scatter_custom_fusion, s32[]{:T(128)} %bitcast.19, s32[]{:T(128)} %bitcast.20, s32[]{:T(128)} %bitcast.21, s32[]{:T(128)} %bitcast.22, s32[]{:T(128)} %bitcast.23), kind=kLoop, calls=%fused_computation.31 | loop fusion | flops 5632 | bytes 3092 | tf_op jit(solution)/shard_map/select_n | solution.py:161
  57.3 2.0 scatter_custom_fusion.1.order
  59.2 0.6 pad_add_fusion.2.bounds
  59.8 8.5 %collective-permute-done.5.below_high = bf16[24,128,128]{2,1,0:T(8,128)(2,1)S(1)} collective-permute-done((bf16[24,128,128]{2,1,0:T(8,128)(2,1)}, bf16[24,128,128]{2,1,0:T(8,128)(2,1)S(1)}, u32[]{:S(2)}, u32[]{:S(2)}) %collective-permute-start.5) | collective-permute-done | bytes 786464 | tf_op jit(solution)/shard_map/ppermute | solution.py:105
  68.3 14.0 %collective-permute-done.7.far_low = bf16[24,128,128]{2,1,0:T(8,128)(2,1)} collective-permute-done((bf16[24,128,128]{2,1,0:T(8,128)(2,1)S(1)}, bf16[24,128,128]{2,1,0:T(8,128)(2,1)}, u32[]{:S(2)}, u32[]{:S(2)}) %collective-permute-start.7) | collective-permute-done | bytes 786464 | tf_op jit(solution)/shard_map/ppermute | solution.py:105
  82.3 14.6 %shard_map.91 = f32[256,128,128]{2,1,0:T(8,128)} custom-call(s32[4,192]{1,0:T(4,128)} %copy-done.12, s32[4,192]{1,0:T(4,128)} %copy-done.11, s32[4]{0:T(128)} %copy-done.13, s32[4,48]{1,0:T(4,128)} %copy-done.1, s32[2,48]{1,0:T(2,128)} %copy-done.9, s32[2]{0:T(128)} %pad_add_fusion.1.pick, s32[256]{0:T(256)} %scatter_custom_fusion.1.order, ...), custom_call_target="tpu_custom_call" | custom-call | tf_op jit(solution)/shard_map/pallas_call | solution.py:86
  96.9 115.0 %reduce-scatter.2.cloned.1.call-done = f32[16,128,128]{2,1,0:T(8,128)} async-done(((f32[256,128,128]{2,1,0:T(8,128)}), f32[16,128,128]{2,1,0:T(8,128)}) %reduce-scatter.2.cloned.1.call-update) | async-done | bytes 1048592 | tf_op jit(solution)/shard_map/reduce_scatter | solution.py:165
  (59 shorter events, 0.3 us)
Async XLA Ops:
  6.5 8.0 %copy-start = (s32[1,1,1,4,192]{4,3,2,1,0:T(4,128)S(1)}, s32[1,1,1,4,192]{4,3,2,1,0:T(4,128)}, u32[]{:S(2)}) copy-start(s32[1,1,1,4,192]{4,3,2,1,0:T(4,128)} %param.18) | copy-start | bytes 9220
  6.5 4.3 %copy-start.3 = (bf16[1,1,1,48,128,128]{5,4,3,2,1,0:T(8,128)(2,1)S(1)}, bf16[1,1,1,48,128,128]{5,4,3,2,1,0:T(8,128)(2,1)}, u32[]{:S(2)}) copy-start(bf16[1,1,1,48,128,128]{5,4,3,2,1,0:T(8,128)(2,1)} %param.13) | copy-start | bytes 4718596
  6.5 75.8 %all-gather.4.cloned.1.call-start = ((), (), s32[]{:S(2)}) async-start(), calls=%async_computation.2 | async-start | bytes 4718592 | tf_op jit(solution)/shard_map/all_gather | solution.py:128
  6.5 20.1 %collective-permute-start.4 = (s32[48]{0:T(128)}, s32[48]{0:T(128)S(1)}, u32[]{:S(2)}, u32[]{:S(2)}) collective-permute-start(s32[48]{0:T(128)} %bitcast.62), channel_id=1, source_target_pairs={{0,64},{32,96},{64,0},{96,32},{1,65},{33,97},{65,1},{97,33},{2,66}... | collective-permute-start | bytes 584 | tf_op jit(solution)/shard_map/ppermute | solution.py:105
  8.7 18.0 %collective-permute-start.3 = (s32[48]{0:T(128)}, s32[48]{0:T(128)S(1)}, u32[]{:S(2)}, u32[]{:S(2)}) collective-permute-start(s32[48]{0:T(128)} %bitcast.63), channel_id=1, source_target_pairs={{0,96},{32,0},{64,32},{96,64},{1,97},{33,1},{65,33},{97,65},{2,98}... | collective-permute-start | bytes 584 | tf_op jit(solution)/shard_map/ppermute | solution.py:105
  10.1 16.5 %collective-permute-start.2 = (s32[48]{0:T(128)}, s32[48]{0:T(128)S(1)}, u32[]{:S(2)}, u32[]{:S(2)}) collective-permute-start(s32[48]{0:T(128)} %bitcast.64), channel_id=1, source_target_pairs={{0,32},{32,64},{64,96},{96,0},{1,33},{33,65},{65,97},{97,1},{2,34}... | collective-permute-start | bytes 584 | tf_op jit(solution)/shard_map/ppermute | solution.py:105
  10.7 3.2 %copy-start.15 = (s32[4]{0:T(128)S(1)}, s32[4]{0:T(128)}, u32[]{:S(2)}) copy-start(s32[4]{0:T(128)} %constant.120.clone) | copy-start | bytes 52
  10.7 3.2 %copy-start.2 = (s32[1,1,1,4]{3,2,1,0:T(1,128)S(1)}, s32[1,1,1,4]{3,2,1,0:T(1,128)}, u32[]{:S(2)}) copy-start(s32[1,1,1,4]{3,2,1,0:T(1,128)} %param.19) | copy-start | bytes 52
  10.7 4.4 %copy-start.10 = (s32[1,1,1,4,192]{4,3,2,1,0:T(4,128)S(1)}, s32[1,1,1,4,192]{4,3,2,1,0:T(4,128)}, u32[]{:S(2)}) copy-start(s32[1,1,1,4,192]{4,3,2,1,0:T(4,128)} %param.17) | copy-start | bytes 9220
  10.8 5.4 %copy-start.17 = (s32[1,1,1,48]{3,2,1,0:T(1,128)S(1)}, s32[1,1,1,48]{3,2,1,0:T(1,128)}, u32[]{:S(2)}) copy-start(s32[1,1,1,48]{3,2,1,0:T(1,128)} %param.16) | copy-start | bytes 580
  10.8 7.8 %copy-start.14 = (s32[4]{0:T(128)S(1)}, s32[4]{0:T(128)}, u32[]{:S(2)}) copy-start(s32[4]{0:T(128)} %constant.165) | copy-start | bytes 52
  10.8 201.1 %reduce-scatter.2.cloned.1.call-start = ((), (), s32[]{:S(2)}) async-start(), calls=%async_computation.1 | async-start | bytes 17825792 | tf_op jit(solution)/shard_map/reduce_scatter | solution.py:165
  11.8 14.0 %copy-start.8 = (bf16[24,128,128]{2,1,0:T(8,128)(2,1)}, bf16[24,128,128]{2,1,0:T(8,128)(2,1)S(1)}, u32[]{:S(2)}) copy-start(bf16[24,128,128]{2,1,0:T(8,128)(2,1)S(1)} %get-tuple-element.19) | copy-start | bytes 2359300
  11.8 18.7 %collective-permute-start.1 = (bf16[24,128,128]{2,1,0:T(8,128)(2,1)}, bf16[24,128,128]{2,1,0:T(8,128)(2,1)S(1)}, u32[]{:S(2)}, u32[]{:S(2)}) collective-permute-start(bf16[24,128,128]{2,1,0:T(8,128)(2,1)} %get-tuple-element.18), channel_id=1, source_target_pairs={{0,96},{32,0},{64,32},{96,64},{1,97},{33,1},{65,33},{97,65},{2,98}... | collective-permute-start | bytes 2359304 | tf_op jit(solution)/shard_map/ppermute | solution.py:105
  13.3 18.8 %collective-permute-start = (bf16[24,128,128]{2,1,0:T(8,128)(2,1)S(1)}, bf16[24,128,128]{2,1,0:T(8,128)(2,1)S(1)}, u32[]{:S(2)}, u32[]{:S(2)}) collective-permute-start(bf16[24,128,128]{2,1,0:T(8,128)(2,1)S(1)} %get-tuple-element.19), channel_id=1, source_target_pairs={{0,32},{32,64},{64,96},{96,0},{1,33},{33,65},{65,97},{97,1},{2,34}... | collective-permute-start | bytes 2359304 | tf_op jit(solution)/shard_map/ppermute | solution.py:105
  15.7 10.1 %copy-start.13 = (s32[4]{0:T(128)}, s32[4]{0:T(128)S(1)}, u32[]{:S(2)}) copy-start(s32[4]{0:T(128)S(1)} %broadcast_select_fusion.3.counts) | copy-start | bytes 52
  15.9 22.9 %copy-start.11 = (s32[4,192]{1,0:T(4,128)}, s32[4,192]{1,0:T(4,128)S(1)}, u32[]{:S(2)}) copy-start(s32[4,192]{1,0:T(4,128)S(1)} %get-tuple-element.26.slots_right) | copy-start | bytes 9220
  15.9 22.9 %copy-start.12 = (s32[4,192]{1,0:T(4,128)}, s32[4,192]{1,0:T(4,128)S(1)}, u32[]{:S(2)}) copy-start(s32[4,192]{1,0:T(4,128)S(1)} %get-tuple-element.37.slots_left) | copy-start | bytes 9220
  18.6 7.2 %copy-start.9 = (s32[2,48]{1,0:T(2,128)}, s32[2,48]{1,0:T(2,128)S(1)}, u32[]{:S(2)}) copy-start(s32[2,48]{1,0:T(2,128)S(1)} %broadcast_select_fusion.2.right_ids) | copy-start | bytes 1156
  19.2 12.9 %copy-start.16 = (s32[1,1,1,48]{3,2,1,0:T(1,128)S(1)}, s32[1,1,1,48]{3,2,1,0:T(1,128)}, u32[]{:S(2)}) copy-start(s32[1,1,1,48]{3,2,1,0:T(1,128)} %param.14) | copy-start | bytes 580
  30.5 19.2 %copy-start.4 = (bf16[24,128,128]{2,1,0:T(8,128)(2,1)}, bf16[24,128,128]{2,1,0:T(8,128)(2,1)S(1)}, u32[]{:S(2)}) copy-start(bf16[24,128,128]{2,1,0:T(8,128)(2,1)S(1)} %collective-permute-done.1.above_high) | copy-start | bytes 2359300
  32.1 17.6 %copy-start.5 = (bf16[24,128,128]{2,1,0:T(8,128)(2,1)}, bf16[24,128,128]{2,1,0:T(8,128)(2,1)S(1)}, u32[]{:S(2)}) copy-start(bf16[24,128,128]{2,1,0:T(8,128)(2,1)S(1)} %collective-permute-done.below_low) | copy-start | bytes 2359300
  32.1 6.6 %copy-start.1 = (s32[4,48]{1,0:T(4,128)}, s32[4,48]{1,0:T(4,128)S(1)}, u32[]{:S(2)}) copy-start(s32[4,48]{1,0:T(4,128)S(1)} %pad_add_fusion.left_ids) | copy-start | bytes 2308
  46.7 21.6 %collective-permute-start.5 = (bf16[24,128,128]{2,1,0:T(8,128)(2,1)}, bf16[24,128,128]{2,1,0:T(8,128)(2,1)S(1)}, u32[]{:S(2)}, u32[]{:S(2)}) collective-permute-start(bf16[24,128,128]{2,1,0:T(8,128)(2,1)} %get-tuple-element.18), channel_id=1, source_target_pairs={{0,32},{32,64},{64,96},{96,0},{1,33},{33,65},{65,97},{97,1},{2,34}... | collective-permute-start | bytes 2359304 | tf_op jit(solution)/shard_map/ppermute | solution.py:105
  46.7 21.6 %collective-permute-start.6 = (bf16[24,128,128]{2,1,0:T(8,128)(2,1)}, bf16[24,128,128]{2,1,0:T(8,128)(2,1)S(1)}, u32[]{:S(2)}, u32[]{:S(2)}) collective-permute-start(bf16[24,128,128]{2,1,0:T(8,128)(2,1)} %copy-done.8), channel_id=1, source_target_pairs={{0,96},{32,0},{64,32},{96,64},{1,97},{33,1},{65,33},{97,65},{2,98}... | collective-permute-start | bytes 2359304 | tf_op jit(solution)/shard_map/ppermute | solution.py:105
  49.7 32.6 %collective-permute-start.7 = (bf16[24,128,128]{2,1,0:T(8,128)(2,1)S(1)}, bf16[24,128,128]{2,1,0:T(8,128)(2,1)}, u32[]{:S(2)}, u32[]{:S(2)}) collective-permute-start(bf16[24,128,128]{2,1,0:T(8,128)(2,1)S(1)} %collective-permute-done.below_low), channel_id=1, source_target_pairs={{0,32},{32,64},{64,96},{96,0},{1,33},{33,65},{65,97},{97,1},{2,34}... | collective-permute-start | bytes 2359304 | tf_op jit(solution)/shard_map/ppermute | solution.py:105
  49.7 32.6 %collective-permute-start.8 = (bf16[24,128,128]{2,1,0:T(8,128)(2,1)S(1)}, bf16[24,128,128]{2,1,0:T(8,128)(2,1)}, u32[]{:S(2)}, u32[]{:S(2)}) collective-permute-start(bf16[24,128,128]{2,1,0:T(8,128)(2,1)S(1)} %collective-permute-done.1.above_high), channel_id=1, source_target_pairs={{0,96},{32,0},{64,32},{96,64},{1,97},{33,1},{65,33},{97,65},{2,98}... | collective-permute-start | bytes 2359304 | tf_op jit(solution)/shard_map/ppermute | solution.py:105
  68.3 14.0 %copy-start.6 = (bf16[24,128,128]{2,1,0:T(8,128)(2,1)}, bf16[24,128,128]{2,1,0:T(8,128)(2,1)S(1)}, u32[]{:S(2)}) copy-start(bf16[24,128,128]{2,1,0:T(8,128)(2,1)S(1)} %collective-permute-done.5.below_high) | copy-start | bytes 2359300
  68.3 14.0 %copy-start.7 = (bf16[24,128,128]{2,1,0:T(8,128)(2,1)}, bf16[24,128,128]{2,1,0:T(8,128)(2,1)S(1)}, u32[]{:S(2)}) copy-start(bf16[24,128,128]{2,1,0:T(8,128)(2,1)S(1)} %collective-permute-done.6.above_low) | copy-start | bytes 2359300
Sparse Core Ops, SparseCore 0:
  10.8 17.1 all-gather.3
  97.0 114.7 reduce-scatter.1

commit v16 on v15

--- a/solution.py
+++ b/solution.py
@@ -143,6 +143,9 @@
     left_id_stack = jnp.stack([own_ids, ids_below, ids_above, ids_far])
     right_id_stack = jnp.take(right_ids_pair, jnp.stack([col_here, 1 - col_here]), axis=0)
     pick = jnp.stack([1 - col_here, col_here]).astype(jnp.int32)
+    below_high, left_id_stack, right_id_stack, slots_left_all, slots_right_all, counts_all = (
+        lax.optimization_barrier((below_high, left_id_stack, right_id_stack, slots_left_all,
+                                  slots_right_all, counts_all)))
     slots_left = jnp.take(slots_left_all, piece, axis=0)
     slots_right = jnp.take(slots_right_all, piece, axis=0)
     counts = jnp.take(counts_all, piece, axis=0)

time: 220 us -> 219 us (level)
  waiting for transfers between devices: 143 us -> 139 us
    ppermute x9, waiting for transfers between devices: 27.9 us -> 25.3 us  [shifted(): return lax.ppermute(value, axis, pairs)]
  transfers between devices with their start and end apart: 11 -> 11, of which waited for: 5 -> 4; matrix products, arithmetic and copies ran while one was open for 15% -> 15% of each run, Pallas kernels for 0% -> 0%
where the time goes in v16:
time: 219 us; the launch traced here: 217 us
  waiting for transfers between devices  139 us (63%)
  local copies, waits for them, and re-layouts  21.9 us (10%)
  Pallas kernels  14.1 us (6%)
  starting transfers between devices  13.8 us (6%)
  between operations  13.7 us (6%)
  other arithmetic  12.8 us (6%)
    reduce_scatter x1, waiting for transfers between devices, on_device(): owned = lax.psum_scatter(totals, 'layer', scatter_dimension=0, tiled=True)  114 us
    ppermute x9, waiting for transfers between devices, shifted(): return lax.ppermute(value, axis, pairs)  25.3 us
    pallas_call x1, Pallas kernels, pair_products(): pl.pallas_call(pair_kernel, out_shape=jax.ShapeDtypeStruct((targets, bloc...  14.1 us
    ppermute x9, starting transfers between devices, shifted(): return lax.ppermute(value, axis, pairs)  13.7 us
    gather x3, local copies, waits for them, and re-layouts, on_device(): jnp.take_along_axis(right_id_stack[right_of], slots_right, axis=1)  6.77 us
    gather x3, local copies, waits for them, and re-layouts, on_device(): jnp.take_along_axis(left_id_stack, slots_left, axis=1) * slab_width  6.76 us
    another operation x1, other arithmetic, on_device(): jnp.full((targets,), -1, jnp.int32).at[places.reshape(-1)]  5.85 us
  transfers between devices with their start and end apart: 11, of which 4 were waited for; matrix products, arithmetic and copies ran while one was open for 15% of the time, Pallas kernels for 0%

profile of v16, /device:TPU:26, one launch (start us, length us, event | category | flops | bytes accessed | tf_op | source)
XLA Modules:
  0.0 217.2 jit_solution(11281348741051951125)
XLA Ops:
  6.5 1.5 slice_bitcast_fusion
  8.1 0.6 collective-permute-start.1
  8.7 1.5 collective-permute-start
  10.2 3.3 %collective-permute-start.4 = (s32[48]{0:T(128)S(1)}, s32[48]{0:T(128)S(1)}, u32[]{:S(2)}, u32[]{:S(2)}) collective-permute-start(s32[48]{0:T(128)S(1)} %bitcast.62), channel_id=1, source_target_pairs={{0,64},{32,96},{64,0},{96,32},{1,65},{33,97},{65,1},{97,33},{2,66}... | collective-permute-start | bytes 584 | tf_op jit(solution)/shard_map/ppermute | solution.py:105
  13.6 0.2 collective-permute-start.3
  13.8 1.8 collective-permute-start.2
  15.7 0.1 fusion.5
  15.8 0.6 pad_add_fusion.1.pick
  16.4 12.0 %collective-permute-done.4 = s32[48]{0:T(128)S(1)} collective-permute-done((s32[48]{0:T(128)S(1)}, s32[48]{0:T(128)S(1)}, u32[]{:S(2)}, u32[]{:S(2)}) %collective-permute-start.4) | collective-permute-done | bytes 224 | tf_op jit(solution)/shard_map/ppermute | solution.py:105
  28.4 0.4 collective-permute-done.2
  28.9 1.5 collective-permute-start.5
  30.3 0.1 compare_and_fusion.1
  30.4 1.8 all-gather
  32.2 0.6 gather_fusion
  32.8 0.1 broadcast_select_fusion.2.right_ids
  32.9 1.6 collective-permute-start.6
  34.5 0.5 collective-permute-start.7
  34.9 2.8 %collective-permute-start.8 = (bf16[24,128,128]{2,1,0:T(8,128)(2,1)S(1)}, bf16[24,128,128]{2,1,0:T(8,128)(2,1)}, u32[]{:S(2)}, u32[]{:S(2)}) collective-permute-start(bf16[24,128,128]{2,1,0:T(8,128)(2,1)S(1)} %collective-permute-done.1.above_high), channel_id=1, source_target_pairs={{0,96},{32,0},{64,32},{96,64},{1,97},{33,1},{65,33},{97,65},{2,98}... | collective-permute-start | bytes 2359304 | tf_op jit(solution)/shard_map/ppermute | solution.py:105
  37.7 12.8 %collective-permute-done.5.below_high = bf16[24,128,128]{2,1,0:T(8,128)(2,1)S(1)} collective-permute-done((bf16[24,128,128]{2,1,0:T(8,128)(2,1)}, bf16[24,128,128]{2,1,0:T(8,128)(2,1)S(1)}, u32[]{:S(2)}, u32[]{:S(2)}) %collective-permute-start.5) | collective-permute-done | bytes 786464 | tf_op jit(solution)/shard_map/ppermute | solution.py:105
  50.6 0.6 gather_fusion.1
  51.3 0.1 reshape.321
  51.4 0.6 gather_fusion.3
  51.9 0.6 gather_fusion.4
  52.5 0.1 bitcast_or_fusion
  52.6 0.1 reshape.370
  52.7 0.6 gather_fusion.2
  53.2 6.6 %gather_fusion.6 = s32[768]{0:T(1024)S(1)} fusion(s32[4,48]{1,0:T(4,128)S(1)} %gather_fusion.2, s32[768]{0:T(1024)S(1)} %reshape.370), kind=kCustom, calls=%fused_computation.3.clone | custom fusion | bytes 12288 | tf_op jit(solution)/shard_map/jit(take_along_axis)/gather | solution.py:154
  59.9 0.1 reshape.373
  60.0 0.1 reshape.365
  60.1 6.6 %gather_fusion.5 = s32[768]{0:T(1024)S(1)} fusion(s32[4,48]{1,0:T(4,128)S(1)} %pad_add_fusion.left_ids, s32[768]{0:T(1024)S(1)} %reshape.365), kind=kCustom, calls=%fused_computation.1.clone | custom fusion | bytes 12288 | tf_op jit(solution)/shard_map/jit(take_along_axis)/gather | solution.py:153
  66.7 0.1 reshape.368
  66.8 0.1 reshape.244
  66.9 5.8 %scatter_custom_fusion = s32[256]{0:T(256)S(1)} fusion(s32[768]{0:T(1024)S(1)} %fusion.2, s32[768]{0:T(1024)S(1)} %reshape.321, s32[]{:T(128)} %constant.114.clone.1), kind=kCustom, calls=%fused_computation.58 | custom fusion | flops 768 | bytes 1028 | tf_op jit(solution)/shard_map/scatter-max | solution.py:157
  72.7 0.1 compare_convert_fusion.1
  72.8 1.5 reduce-window.20
  74.3 0.1 slice.55
  74.4 0.1 copy.16
  74.5 0.1 copy.17
  74.6 0.1 add_bitcast_fusion
  74.7 0.2 fusion
  74.9 0.2 reduce-window.19
  75.1 0.7 fusion.10
  75.7 3.2 %compare_select_fusion.4 = s32[256]{0:T(256)S(1)} fusion(s32[256]{0:T(256)S(1)} %get-tuple-element.34, s32[256]{0:T(256)S(1)} %scatter_custom_fusion, s32[]{:T(128)} %bitcast.19, s32[]{:T(128)} %bitcast.20, s32[]{:T(128)} %bitcast.21, s32[]{:T(128)} %bitcast.22, s32[]{:T(128)} %bitcast.23), kind=kLoop, calls=%fused_computation.31 | loop fusion | flops 5632 | bytes 3092 | tf_op jit(solution)/shard_map/select_n | solution.py:164
  78.9 2.0 scatter_custom_fusion.1.order
  80.9 0.6 pad_add_fusion.2.bounds
  81.6 0.9 copy-done.6
  82.4 14.1 %shard_map.91 = f32[256,128,128]{2,1,0:T(8,128)} custom-call(s32[4,192]{1,0:T(4,128)} %copy-done.12, s32[4,192]{1,0:T(4,128)} %copy-done.11, s32[4]{0:T(128)} %copy-done.13, s32[4,48]{1,0:T(4,128)} %copy-done.1, s32[2,48]{1,0:T(2,128)} %copy-done.9, s32[2]{0:T(128)} %pad_add_fusion.1.pick, s32[256]{0:T(256)} %scatter_custom_fusion.1.order, ...), custom_call_target="tpu_custom_call" | custom-call | tf_op jit(solution)/shard_map/pallas_call | solution.py:86
  96.6 113.8 %reduce-scatter.2.cloned.1.call-done = f32[16,128,128]{2,1,0:T(8,128)} async-done(((f32[256,128,128]{2,1,0:T(8,128)}), f32[16,128,128]{2,1,0:T(8,128)}) %reduce-scatter.2.cloned.1.call-update) | async-done | bytes 1048592 | tf_op jit(solution)/shard_map/reduce_scatter | solution.py:168
  (59 shorter events, 0.4 us)
Async XLA Ops:
  6.5 44.0 %copy-start = (s32[1,1,1,4,192]{4,3,2,1,0:T(4,128)S(1)}, s32[1,1,1,4,192]{4,3,2,1,0:T(4,128)}, u32[]{:S(2)}) copy-start(s32[1,1,1,4,192]{4,3,2,1,0:T(4,128)} %param.17) | copy-start | bytes 9220
  6.5 3.7 %copy-start.16 = (s32[1,1,1,48]{3,2,1,0:T(1,128)S(1)}, s32[1,1,1,48]{3,2,1,0:T(1,128)}, u32[]{:S(2)}) copy-start(s32[1,1,1,48]{3,2,1,0:T(1,128)} %param.14) | copy-start | bytes 580
  6.5 75.0 %all-gather.4.cloned.1.call-start = ((), (), s32[]{:S(2)}) async-start(), calls=%async_computation.2 | async-start | bytes 4718592 | tf_op jit(solution)/shard_map/all_gather | solution.py:128
  8.0 20.8 %copy-start.8 = (bf16[24,128,128]{2,1,0:T(8,128)(2,1)}, bf16[24,128,128]{2,1,0:T(8,128)(2,1)S(1)}, u32[]{:S(2)}) copy-start(bf16[24,128,128]{2,1,0:T(8,128)(2,1)S(1)} %get-tuple-element.20) | copy-start | bytes 2359300
  8.1 24.7 %copy-start.7 = (bf16[24,128,128]{2,1,0:T(8,128)(2,1)}, bf16[24,128,128]{2,1,0:T(8,128)(2,1)S(1)}, u32[]{:S(2)}) copy-start(bf16[24,128,128]{2,1,0:T(8,128)(2,1)S(1)} %get-tuple-element.31) | copy-start | bytes 2359300
  8.1 22.3 %copy-start.17 = (s32[1,1,1,48]{3,2,1,0:T(1,128)S(1)}, s32[1,1,1,48]{3,2,1,0:T(1,128)}, u32[]{:S(2)}) copy-start(s32[1,1,1,48]{3,2,1,0:T(1,128)} %param.16) | copy-start | bytes 580
  8.1 24.6 %copy-start.15 = (s32[4]{0:T(128)S(1)}, s32[4]{0:T(128)}, u32[]{:S(2)}) copy-start(s32[4]{0:T(128)} %constant.120.clone) | copy-start | bytes 52
  8.1 24.7 %copy-start.14 = (s32[4]{0:T(128)S(1)}, s32[4]{0:T(128)}, u32[]{:S(2)}) copy-start(s32[4]{0:T(128)} %constant.165) | copy-start | bytes 52
  8.1 42.5 %copy-start.2 = (s32[1,1,1,4]{3,2,1,0:T(1,128)S(1)}, s32[1,1,1,4]{3,2,1,0:T(1,128)}, u32[]{:S(2)}) copy-start(s32[1,1,1,4]{3,2,1,0:T(1,128)} %param.19) | copy-start | bytes 52
  8.1 43.8 %copy-start.10 = (s32[1,1,1,4,192]{4,3,2,1,0:T(4,128)S(1)}, s32[1,1,1,4,192]{4,3,2,1,0:T(4,128)}, u32[]{:S(2)}) copy-start(s32[1,1,1,4,192]{4,3,2,1,0:T(4,128)} %param.18) | copy-start | bytes 9220
  8.1 20.7 %collective-permute-start.1 = (bf16[24,128,128]{2,1,0:T(8,128)(2,1)S(1)}, bf16[24,128,128]{2,1,0:T(8,128)(2,1)S(1)}, u32[]{:S(2)}, u32[]{:S(2)}) collective-permute-start(bf16[24,128,128]{2,1,0:T(8,128)(2,1)S(1)} %get-tuple-element.20), channel_id=1, source_target_pairs={{0,96},{32,0},{64,32},{96,64},{1,97},{33,1},{65,33},{97,65},{2,98}... | collective-permute-start | bytes 2359304 | tf_op jit(solution)/shard_map/ppermute | solution.py:105
  8.7 20.1 %collective-permute-start = (bf16[24,128,128]{2,1,0:T(8,128)(2,1)S(1)}, bf16[24,128,128]{2,1,0:T(8,128)(2,1)S(1)}, u32[]{:S(2)}, u32[]{:S(2)}) collective-permute-start(bf16[24,128,128]{2,1,0:T(8,128)(2,1)S(1)} %get-tuple-element.31), channel_id=1, source_target_pairs={{0,32},{32,64},{64,96},{96,0},{1,33},{33,65},{65,97},{97,1},{2,34}... | collective-permute-start | bytes 2359304 | tf_op jit(solution)/shard_map/ppermute | solution.py:105
  10.2 18.2 %collective-permute-start.4 = (s32[48]{0:T(128)S(1)}, s32[48]{0:T(128)S(1)}, u32[]{:S(2)}, u32[]{:S(2)}) collective-permute-start(s32[48]{0:T(128)S(1)} %bitcast.62), channel_id=1, source_target_pairs={{0,64},{32,96},{64,0},{96,32},{1,65},{33,97},{65,1},{97,33},{2,66}... | collective-permute-start | bytes 584 | tf_op jit(solution)/shard_map/ppermute | solution.py:105
  13.6 14.8 %collective-permute-start.3 = (s32[48]{0:T(128)S(1)}, s32[48]{0:T(128)S(1)}, u32[]{:S(2)}, u32[]{:S(2)}) collective-permute-start(s32[48]{0:T(128)S(1)} %bitcast.63), channel_id=1, source_target_pairs={{0,96},{32,0},{64,32},{96,64},{1,97},{33,1},{65,33},{97,65},{2,98}... | collective-permute-start | bytes 584 | tf_op jit(solution)/shard_map/ppermute | solution.py:105
  13.8 15.0 %collective-permute-start.2 = (s32[48]{0:T(128)S(1)}, s32[48]{0:T(128)S(1)}, u32[]{:S(2)}, u32[]{:S(2)}) collective-permute-start(s32[48]{0:T(128)S(1)} %bitcast.64), channel_id=1, source_target_pairs={{0,32},{32,64},{64,96},{96,0},{1,33},{33,65},{65,97},{97,1},{2,34}... | collective-permute-start | bytes 584 | tf_op jit(solution)/shard_map/ppermute | solution.py:105
  15.6 194.8 %reduce-scatter.2.cloned.1.call-start = ((), (), s32[]{:S(2)}) async-start(), calls=%async_computation.1 | async-start | bytes 17825792 | tf_op jit(solution)/shard_map/reduce_scatter | solution.py:168
  28.8 31.0 %copy-start.3 = (bf16[24,128,128]{2,1,0:T(8,128)(2,1)}, bf16[24,128,128]{2,1,0:T(8,128)(2,1)S(1)}, u32[]{:S(2)}) copy-start(bf16[24,128,128]{2,1,0:T(8,128)(2,1)S(1)} %collective-permute-done.1.above_high) | copy-start | bytes 2359300
  28.8 31.0 %copy-start.4 = (bf16[24,128,128]{2,1,0:T(8,128)(2,1)}, bf16[24,128,128]{2,1,0:T(8,128)(2,1)S(1)}, u32[]{:S(2)}) copy-start(bf16[24,128,128]{2,1,0:T(8,128)(2,1)S(1)} %collective-permute-done.below_low) | copy-start | bytes 2359300
  28.9 21.7 %collective-permute-start.5 = (bf16[24,128,128]{2,1,0:T(8,128)(2,1)}, bf16[24,128,128]{2,1,0:T(8,128)(2,1)S(1)}, u32[]{:S(2)}, u32[]{:S(2)}) collective-permute-start(bf16[24,128,128]{2,1,0:T(8,128)(2,1)} %copy-done.8), channel_id=1, source_target_pairs={{0,32},{32,64},{64,96},{96,0},{1,33},{33,65},{65,97},{97,1},{2,34}... | collective-permute-start | bytes 2359304 | tf_op jit(solution)/shard_map/ppermute | solution.py:105
  32.9 27.0 %copy-start.9 = (s32[2,48]{1,0:T(2,128)}, s32[2,48]{1,0:T(2,128)S(1)}, u32[]{:S(2)}) copy-start(s32[2,48]{1,0:T(2,128)S(1)} %broadcast_select_fusion.2.right_ids) | copy-start | bytes 1156
  32.9 48.7 %collective-permute-start.6 = (bf16[24,128,128]{2,1,0:T(8,128)(2,1)}, bf16[24,128,128]{2,1,0:T(8,128)(2,1)S(1)}, u32[]{:S(2)}, u32[]{:S(2)}) collective-permute-start(bf16[24,128,128]{2,1,0:T(8,128)(2,1)} %copy-done.7), channel_id=1, source_target_pairs={{0,96},{32,0},{64,32},{96,64},{1,97},{33,1},{65,33},{97,65},{2,98}... | collective-permute-start | bytes 2359304 | tf_op jit(solution)/shard_map/ppermute | solution.py:105
  34.5 47.1 %collective-permute-start.7 = (bf16[24,128,128]{2,1,0:T(8,128)(2,1)S(1)}, bf16[24,128,128]{2,1,0:T(8,128)(2,1)}, u32[]{:S(2)}, u32[]{:S(2)}) collective-permute-start(bf16[24,128,128]{2,1,0:T(8,128)(2,1)S(1)} %collective-permute-done.below_low), channel_id=1, source_target_pairs={{0,32},{32,64},{64,96},{96,0},{1,33},{33,65},{65,97},{97,1},{2,34}... | collective-permute-start | bytes 2359304 | tf_op jit(solution)/shard_map/ppermute | solution.py:105
  34.9 46.6 %collective-permute-start.8 = (bf16[24,128,128]{2,1,0:T(8,128)(2,1)S(1)}, bf16[24,128,128]{2,1,0:T(8,128)(2,1)}, u32[]{:S(2)}, u32[]{:S(2)}) collective-permute-start(bf16[24,128,128]{2,1,0:T(8,128)(2,1)S(1)} %collective-permute-done.1.above_high), channel_id=1, source_target_pairs={{0,96},{32,0},{64,32},{96,64},{1,97},{33,1},{65,33},{97,65},{2,98}... | collective-permute-start | bytes 2359304 | tf_op jit(solution)/shard_map/ppermute | solution.py:105
  37.7 22.4 %copy-start.1 = (s32[4,48]{1,0:T(4,128)}, s32[4,48]{1,0:T(4,128)S(1)}, u32[]{:S(2)}) copy-start(s32[4,48]{1,0:T(4,128)S(1)} %pad_add_fusion.left_ids) | copy-start | bytes 2308
  50.5 9.3 %copy-start.5 = (bf16[24,128,128]{2,1,0:T(8,128)(2,1)}, bf16[24,128,128]{2,1,0:T(8,128)(2,1)S(1)}, u32[]{:S(2)}) copy-start(bf16[24,128,128]{2,1,0:T(8,128)(2,1)S(1)} %collective-permute-done.5.below_high) | copy-start | bytes 2359300
  51.2 8.7 %copy-start.13 = (s32[4]{0:T(128)}, s32[4]{0:T(128)S(1)}, u32[]{:S(2)}) copy-start(s32[4]{0:T(128)S(1)} %broadcast_select_fusion.3.counts) | copy-start | bytes 52
  52.6 14.2 %copy-start.11 = (s32[4,192]{1,0:T(4,128)}, s32[4,192]{1,0:T(4,128)S(1)}, u32[]{:S(2)}) copy-start(s32[4,192]{1,0:T(4,128)S(1)} %get-tuple-element.38.slots_right) | copy-start | bytes 9220
  52.6 14.2 %copy-start.12 = (s32[4,192]{1,0:T(4,128)}, s32[4,192]{1,0:T(4,128)S(1)}, u32[]{:S(2)}) copy-start(s32[4,192]{1,0:T(4,128)S(1)} %get-tuple-element.49.slots_left) | copy-start | bytes 9220
  81.5 0.9 copy-start.6
Sparse Core Ops, SparseCore 0:
  15.7 15.9 all-gather.3
  96.7 113.6 reduce-scatter.1

commit v17 on v11

--- a/solution.py
+++ b/solution.py
@@ -12,7 +12,7 @@
 
 def pair_kernel(slots_left, slots_right, counts, left_ids, right_ids, pick,
                 own_left, below_low, below_high, above_low, above_high, far_low, far_high,
-                own_right, right_pair, totals, left_lists, right_lists, sems):
+                own_right, right_pair, out, totals, left_lists, right_lists, sems, out_sem, touched):
     half = far_low.shape[0]
     slab_width = totals.shape[0] // ROWS_GROUP
     block_size = totals.shape[-1]
@@ -36,6 +36,28 @@
         return carry
 
     lax.fori_loop(0, totals.shape[0], clear, 0)
+
+    def unmark(t, carry):
+        touched[t] = 0
+        return carry
+
+    lax.fori_loop(0, totals.shape[0], unmark, 0)
+
+    def mark(j, carry):
+        t = left_ids[3, slots_left[3, j]] * slab_width + right_ids[0, slots_right[3, j]]
+        touched[t] = 1
+        return carry
+
+    lax.fori_loop(0, counts[3], mark, 0)
+
+    def flush(flag):
+        def one(t, carry):
+            @pl.when(touched[t] == flag)
+            def _():
+                pltpu.make_async_copy(totals.at[t], out.at[t], out_sem.at[0]).start()
+            return carry
+
+        lax.fori_loop(0, totals.shape[0], one, 0)
 
     for u, v in enumerate((0, 1, 1, 0)):
         for copy in copies[u]:
@@ -63,6 +85,10 @@
         groups = count // UNROLL
         lax.fori_loop(0, groups, add_group, 0)
         lax.fori_loop(groups * UNROLL, count, add_single, 0)
+        if u >= 2:
+            flush(u - 2)
+
+    pltpu.make_async_copy(totals, out, out_sem.at[0]).wait()
 
 
 def pair_products(scalars, lists, targets):
@@ -74,11 +100,14 @@
         pair_kernel,
         out_shape=jax.ShapeDtypeStruct((targets, block_size, block_size), jnp.float32),
         in_specs=[smem] * len(scalars) + [hbm] * len(lists),
-        out_specs=pl.BlockSpec(memory_space=pltpu.VMEM),
+        out_specs=hbm,
         scratch_shapes=[
+            pltpu.VMEM((targets, block_size, block_size), jnp.float32),
             pltpu.VMEM((4, list_cap, block_size, block_size), jnp.bfloat16),
             pltpu.VMEM((2, list_cap, block_size, block_size), jnp.bfloat16),
             pltpu.SemaphoreType.DMA((9,)),
+            pltpu.SemaphoreType.DMA((1,)),
+            pltpu.SMEM((targets,), jnp.int32),
         ],
         compiler_params=pltpu.CompilerParams(vmem_limit_bytes=60 * 1024 * 1024),
     )(*scalars, *lists)

time: 208 us -> 210 us (level)
  Pallas kernels: 18.4 us -> 20.9 us
    pallas_call x1, Pallas kernels: 18.4 us -> 20.9 us  [pair_products(): pl.pallas_call(pair_kernel, out_shape=jax.ShapeDtypeStruct((targets, bloc...]
where the time goes in v17:
time: 210 us; the launch traced here: 208 us
  waiting for transfers between devices  151 us (72%)
  Pallas kernels  20.9 us (10%)
  starting transfers between devices  13.7 us (7%)
  between operations  13.5 us (6%)
  local copies, waits for them, and re-layouts  3.99 us (2%)
  other arithmetic  3.31 us (2%)
    reduce_scatter x1, waiting for transfers between devices, on_device(): owned = lax.psum_scatter(totals, 'layer', scatter_dimension=0, tiled=True)  115 us
    ppermute x9, waiting for transfers between devices, shifted(): return lax.ppermute(value, axis, pairs)  36 us
    pallas_call x1, Pallas kernels, pair_products(): pl.pallas_call(pair_kernel, out_shape=jax.ShapeDtypeStruct((targets, bloc...  20.9 us
    ppermute x9, starting transfers between devices, shifted(): return lax.ppermute(value, axis, pairs)  13.6 us
  transfers between devices with their start and end apart: 11, of which 6 were waited for; matrix products, arithmetic and copies ran while one was open for 3% of the time, Pallas kernels for 0%

profile of v17, /device:TPU:26, one launch (start us, length us, event | category | flops | bytes accessed | tf_op | source)
XLA Modules:
  0.0 208.4 jit_solution(3979526991667921447)
XLA Ops:
  6.5 0.0 copy-start
  6.5 0.0 all-gather.4.cloned.1.call-start
  6.5 0.7 all-gather.4.cloned.1.call-update
  7.3 0.0 copy-start.10
  7.3 0.0 copy-start.9
  7.3 0.0 copy-start.1
  7.3 0.0 copy-start.8
  7.3 0.0 copy-start.11
  7.3 0.0 reduce-scatter.2.cloned.1.call-start
  7.4 0.6 copy-done.2
  8.0 1.0 slice_bitcast_fusion
  9.0 0.5 collective-permute-start.1
  9.5 1.5 collective-permute-start
  11.0 3.3 %collective-permute-start.4 = (s32[48]{0:T(128)S(1)}, s32[48]{0:T(128)S(1)}, u32[]{:S(2)}, u32[]{:S(2)}) collective-permute-start(s32[48]{0:T(128)S(1)} %bitcast.30), channel_id=1, source_target_pairs={{0,64},{32,96},{64,0},{96,32},{1,65},{33,97},{65,1},{97,33},{2,66}... | collective-permute-start | bytes 584 | tf_op jit(solution)/shard_map/ppermute | solution.py:119
  14.3 0.2 collective-permute-start.3
  14.6 1.8 collective-permute-start.2
  16.4 0.1 fusion.1
  16.5 0.6 pad_add_fusion.1.pick
  17.1 12.3 %collective-permute-done.4 = s32[48]{0:T(128)S(1)} collective-permute-done((s32[48]{0:T(128)S(1)}, s32[48]{0:T(128)S(1)}, u32[]{:S(2)}, u32[]{:S(2)}) %collective-permute-start.4) | collective-permute-done | bytes 224 | tf_op jit(solution)/shard_map/ppermute | solution.py:119
  29.4 0.0 collective-permute-done.3
  29.4 0.2 collective-permute-done.2
  29.6 0.0 collective-permute-done.1.above_high
  29.6 0.0 copy-done.7
  29.6 0.0 collective-permute-done.below_low
  29.6 1.5 collective-permute-start.5
  31.1 1.6 collective-permute-start.6
  32.7 0.4 collective-permute-start.7
  33.1 2.8 %collective-permute-start.8 = (bf16[24,128,128]{2,1,0:T(8,128)(2,1)S(1)}, bf16[24,128,128]{2,1,0:T(8,128)(2,1)}, u32[]{:S(2)}, u32[]{:S(2)}) collective-permute-start(bf16[24,128,128]{2,1,0:T(8,128)(2,1)S(1)} %collective-permute-done.1.above_high), channel_id=1, source_target_pairs={{0,96},{32,0},{64,32},{96,64},{1,97},{33,1},{65,33},{97,65},{2,98}... | collective-permute-start | bytes 2359304 | tf_op jit(solution)/shard_map/ppermute | solution.py:119
  35.9 0.1 compare_and_fusion.1
  36.0 0.6 gather_fusion
  36.6 0.0 copy-done
  36.6 0.6 gather_fusion.3
  37.2 0.0 copy-done.8
  37.2 0.6 gather_fusion.2
  37.8 0.0 copy-done.11
  37.8 1.8 all-gather
  39.5 0.6 gather_fusion.1
  40.1 0.6 broadcast_select_fusion.3.counts
  40.7 0.7 broadcast_select_fusion.2.right_ids
  41.3 0.7 broadcast_select_fusion
  42.0 0.6 pad_add_fusion.left_ids
  42.6 8.7 %collective-permute-done.5.below_high = bf16[24,128,128]{2,1,0:T(8,128)(2,1)S(1)} collective-permute-done((bf16[24,128,128]{2,1,0:T(8,128)(2,1)}, bf16[24,128,128]{2,1,0:T(8,128)(2,1)S(1)}, u32[]{:S(2)}, u32[]{:S(2)}) %collective-permute-start.5) | collective-permute-done | bytes 786464 | tf_op jit(solution)/shard_map/ppermute | solution.py:119
  51.3 0.5 collective-permute-done.6.above_low
  51.8 14.3 %collective-permute-done.7.far_low = bf16[24,128,128]{2,1,0:T(8,128)(2,1)} collective-permute-done((bf16[24,128,128]{2,1,0:T(8,128)(2,1)S(1)}, bf16[24,128,128]{2,1,0:T(8,128)(2,1)}, u32[]{:S(2)}, u32[]{:S(2)}) %collective-permute-start.7) | collective-permute-done | bytes 786464 | tf_op jit(solution)/shard_map/ppermute | solution.py:119
  66.1 0.0 collective-permute-done.8.far_high
  66.2 20.9 %shard_map.82 = f32[256,128,128]{2,1,0:T(8,128)} custom-call(s32[4,192]{1,0:T(4,128)} %get-tuple-element.25.slots_left, s32[4,192]{1,0:T(4,128)} %get-tuple-element.24.slots_right, s32[4]{0:T(128)} %broadcast_select_fusion.3.counts, s32[4,48]{1,0:T(4,128)} %pad_add_fusion.left_ids, s32[2,48]{1,0:T(2,128)} %broadcast_select_fusion.2.right_ids, ...), custom_call_target="tpu_custom_call" | custom-call | tf_op jit(solution)/shard_map/pallas_call | solution.py:99
  87.0 0.0 reduce-scatter.2.cloned.1.call-update
  87.1 114.5 %reduce-scatter.2.cloned.1.call-done = f32[16,128,128]{2,1,0:T(8,128)} async-done(((f32[256,128,128]{2,1,0:T(8,128)}), f32[16,128,128]{2,1,0:T(8,128)}) %reduce-scatter.2.cloned.1.call-update) | async-done | bytes 1048592 | tf_op jit(solution)/shard_map/reduce_scatter | solution.py:164
  (17 shorter events, 0.1 us)
Async XLA Ops:
  6.5 30.1 %copy-start = (s32[1,1,1,4,192]{4,3,2,1,0:T(4,128)S(1)}, s32[1,1,1,4,192]{4,3,2,1,0:T(4,128)}, u32[]{:S(2)}) copy-start(s32[1,1,1,4,192]{4,3,2,1,0:T(4,128)} %param.15) | copy-start | bytes 9220
  6.5 1.4 copy-start.2
  6.5 59.6 %all-gather.4.cloned.1.call-start = ((), (), s32[]{:S(2)}) async-start(), calls=%async_computation.2 | async-start | bytes 4718592 | tf_op jit(solution)/shard_map/all_gather | solution.py:142
  7.3 3.8 %copy-start.10 = (s32[1,1,1,48]{3,2,1,0:T(1,128)S(1)}, s32[1,1,1,48]{3,2,1,0:T(1,128)}, u32[]{:S(2)}) copy-start(s32[1,1,1,48]{3,2,1,0:T(1,128)} %param.11) | copy-start | bytes 580
  7.3 9.2 %copy-start.9 = (s32[4]{0:T(128)S(1)}, s32[4]{0:T(128)}, u32[]{:S(2)}) copy-start(s32[4]{0:T(128)} %constant.67.clone) | copy-start | bytes 52
  7.3 28.7 %copy-start.1 = (s32[1,1,1,4]{3,2,1,0:T(1,128)S(1)}, s32[1,1,1,4]{3,2,1,0:T(1,128)}, u32[]{:S(2)}) copy-start(s32[1,1,1,4]{3,2,1,0:T(1,128)} %param.16) | copy-start | bytes 52
  7.3 29.9 %copy-start.8 = (s32[1,1,1,4,192]{4,3,2,1,0:T(4,128)S(1)}, s32[1,1,1,4,192]{4,3,2,1,0:T(4,128)}, u32[]{:S(2)}) copy-start(s32[1,1,1,4,192]{4,3,2,1,0:T(4,128)} %param.14) | copy-start | bytes 9220
  7.3 30.5 %copy-start.11 = (s32[1,1,1,48]{3,2,1,0:T(1,128)S(1)}, s32[1,1,1,48]{3,2,1,0:T(1,128)}, u32[]{:S(2)}) copy-start(s32[1,1,1,48]{3,2,1,0:T(1,128)} %param.13) | copy-start | bytes 580
  7.3 194.3 %reduce-scatter.2.cloned.1.call-start = ((), (), s32[]{:S(2)}) async-start(), calls=%async_computation.1 | async-start | bytes 17825792 | tf_op jit(solution)/shard_map/reduce_scatter | solution.py:164
  9.0 20.6 %copy-start.7 = (bf16[24,128,128]{2,1,0:T(8,128)(2,1)}, bf16[24,128,128]{2,1,0:T(8,128)(2,1)S(1)}, u32[]{:S(2)}) copy-start(bf16[24,128,128]{2,1,0:T(8,128)(2,1)S(1)} %get-tuple-element.18) | copy-start | bytes 2359300
  9.0 20.6 %collective-permute-start.1 = (bf16[24,128,128]{2,1,0:T(8,128)(2,1)}, bf16[24,128,128]{2,1,0:T(8,128)(2,1)S(1)}, u32[]{:S(2)}, u32[]{:S(2)}) collective-permute-start(bf16[24,128,128]{2,1,0:T(8,128)(2,1)} %get-tuple-element.17), channel_id=1, source_target_pairs={{0,96},{32,0},{64,32},{96,64},{1,97},{33,1},{65,33},{97,65},{2,98}... | collective-permute-start | bytes 2359304 | tf_op jit(solution)/shard_map/ppermute | solution.py:119
  9.5 20.1 %collective-permute-start = (bf16[24,128,128]{2,1,0:T(8,128)(2,1)S(1)}, bf16[24,128,128]{2,1,0:T(8,128)(2,1)S(1)}, u32[]{:S(2)}, u32[]{:S(2)}) collective-permute-start(bf16[24,128,128]{2,1,0:T(8,128)(2,1)S(1)} %get-tuple-element.18), channel_id=1, source_target_pairs={{0,32},{32,64},{64,96},{96,0},{1,33},{33,65},{65,97},{97,1},{2,34}... | collective-permute-start | bytes 2359304 | tf_op jit(solution)/shard_map/ppermute | solution.py:119
  11.0 18.4 %collective-permute-start.4 = (s32[48]{0:T(128)S(1)}, s32[48]{0:T(128)S(1)}, u32[]{:S(2)}, u32[]{:S(2)}) collective-permute-start(s32[48]{0:T(128)S(1)} %bitcast.30), channel_id=1, source_target_pairs={{0,64},{32,96},{64,0},{96,32},{1,65},{33,97},{65,1},{97,33},{2,66}... | collective-permute-start | bytes 584 | tf_op jit(solution)/shard_map/ppermute | solution.py:119
  14.3 15.0 %collective-permute-start.3 = (s32[48]{0:T(128)S(1)}, s32[48]{0:T(128)S(1)}, u32[]{:S(2)}, u32[]{:S(2)}) collective-permute-start(s32[48]{0:T(128)S(1)} %bitcast.31), channel_id=1, source_target_pairs={{0,96},{32,0},{64,32},{96,64},{1,97},{33,1},{65,33},{97,65},{2,98}... | collective-permute-start | bytes 584 | tf_op jit(solution)/shard_map/ppermute | solution.py:119
  14.6 15.0 %collective-permute-start.2 = (s32[48]{0:T(128)S(1)}, s32[48]{0:T(128)S(1)}, u32[]{:S(2)}, u32[]{:S(2)}) collective-permute-start(s32[48]{0:T(128)S(1)} %bitcast.32), channel_id=1, source_target_pairs={{0,32},{32,64},{64,96},{96,0},{1,33},{33,65},{65,97},{97,1},{2,34}... | collective-permute-start | bytes 584 | tf_op jit(solution)/shard_map/ppermute | solution.py:119
  29.6 36.5 %copy-start.3 = (bf16[24,128,128]{2,1,0:T(8,128)(2,1)}, bf16[24,128,128]{2,1,0:T(8,128)(2,1)S(1)}, u32[]{:S(2)}) copy-start(bf16[24,128,128]{2,1,0:T(8,128)(2,1)S(1)} %collective-permute-done.1.above_high) | copy-start | bytes 2359300
  29.6 36.5 %copy-start.4 = (bf16[24,128,128]{2,1,0:T(8,128)(2,1)}, bf16[24,128,128]{2,1,0:T(8,128)(2,1)S(1)}, u32[]{:S(2)}) copy-start(bf16[24,128,128]{2,1,0:T(8,128)(2,1)S(1)} %collective-permute-done.below_low) | copy-start | bytes 2359300
  29.6 21.7 %collective-permute-start.5 = (bf16[24,128,128]{2,1,0:T(8,128)(2,1)}, bf16[24,128,128]{2,1,0:T(8,128)(2,1)S(1)}, u32[]{:S(2)}, u32[]{:S(2)}) collective-permute-start(bf16[24,128,128]{2,1,0:T(8,128)(2,1)} %get-tuple-element.17), channel_id=1, source_target_pairs={{0,32},{32,64},{64,96},{96,0},{1,33},{33,65},{65,97},{97,1},{2,34}... | collective-permute-start | bytes 2359304 | tf_op jit(solution)/shard_map/ppermute | solution.py:119
  31.1 20.7 %collective-permute-start.6 = (bf16[24,128,128]{2,1,0:T(8,128)(2,1)}, bf16[24,128,128]{2,1,0:T(8,128)(2,1)S(1)}, u32[]{:S(2)}, u32[]{:S(2)}) collective-permute-start(bf16[24,128,128]{2,1,0:T(8,128)(2,1)} %copy-done.7), channel_id=1, source_target_pairs={{0,96},{32,0},{64,32},{96,64},{1,97},{33,1},{65,33},{97,65},{2,98}... | collective-permute-start | bytes 2359304 | tf_op jit(solution)/shard_map/ppermute | solution.py:119
  32.7 33.4 %collective-permute-start.7 = (bf16[24,128,128]{2,1,0:T(8,128)(2,1)S(1)}, bf16[24,128,128]{2,1,0:T(8,128)(2,1)}, u32[]{:S(2)}, u32[]{:S(2)}) collective-permute-start(bf16[24,128,128]{2,1,0:T(8,128)(2,1)S(1)} %collective-permute-done.below_low), channel_id=1, source_target_pairs={{0,32},{32,64},{64,96},{96,0},{1,33},{33,65},{65,97},{97,1},{2,34}... | collective-permute-start | bytes 2359304 | tf_op jit(solution)/shard_map/ppermute | solution.py:119
  33.1 33.0 %collective-permute-start.8 = (bf16[24,128,128]{2,1,0:T(8,128)(2,1)S(1)}, bf16[24,128,128]{2,1,0:T(8,128)(2,1)}, u32[]{:S(2)}, u32[]{:S(2)}) collective-permute-start(bf16[24,128,128]{2,1,0:T(8,128)(2,1)S(1)} %collective-permute-done.1.above_high), channel_id=1, source_target_pairs={{0,96},{32,0},{64,32},{96,64},{1,97},{33,1},{65,33},{97,65},{2,98}... | collective-permute-start | bytes 2359304 | tf_op jit(solution)/shard_map/ppermute | solution.py:119
  51.3 14.8 %copy-start.5 = (bf16[24,128,128]{2,1,0:T(8,128)(2,1)}, bf16[24,128,128]{2,1,0:T(8,128)(2,1)S(1)}, u32[]{:S(2)}) copy-start(bf16[24,128,128]{2,1,0:T(8,128)(2,1)S(1)} %collective-permute-done.5.below_high) | copy-start | bytes 2359300
  51.8 14.3 %copy-start.6 = (bf16[24,128,128]{2,1,0:T(8,128)(2,1)}, bf16[24,128,128]{2,1,0:T(8,128)(2,1)S(1)}, u32[]{:S(2)}) copy-start(bf16[24,128,128]{2,1,0:T(8,128)(2,1)S(1)} %collective-permute-done.6.above_low) | copy-start | bytes 2359300
Sparse Core Ops, SparseCore 0:
  9.0 16.9 all-gather.3
  87.2 114.3 reduce-scatter.1

commit v18 on v11

--- a/solution.py
+++ b/solution.py
@@ -12,7 +12,7 @@
 
 def pair_kernel(slots_left, slots_right, counts, left_ids, right_ids, pick,
                 own_left, below_low, below_high, above_low, above_high, far_low, far_high,
-                own_right, right_pair, totals, left_lists, right_lists, sems):
+                own_right, right_pair, out, totals, left_lists, right_lists, sems, out_sems):
     half = far_low.shape[0]
     slab_width = totals.shape[0] // ROWS_GROUP
     block_size = totals.shape[-1]
@@ -64,6 +64,15 @@
         lax.fori_loop(0, groups, add_group, 0)
         lax.fori_loop(groups * UNROLL, count, add_single, 0)
 
+    part = totals.shape[0] // 4
+    out_copies = [pltpu.make_async_copy(totals.at[pl.ds(q * part, part)],
+                                        out.at[pl.ds(q * part, part)], out_sems.at[q])
+                  for q in range(4)]
+    for copy in out_copies:
+        copy.start()
+    for copy in out_copies:
+        copy.wait()
+
 
 def pair_products(scalars, lists, targets):
     own_left = lists[0]
@@ -74,11 +83,13 @@
         pair_kernel,
         out_shape=jax.ShapeDtypeStruct((targets, block_size, block_size), jnp.float32),
         in_specs=[smem] * len(scalars) + [hbm] * len(lists),
-        out_specs=pl.BlockSpec(memory_space=pltpu.VMEM),
+        out_specs=hbm,
         scratch_shapes=[
+            pltpu.VMEM((targets, block_size, block_size), jnp.float32),
             pltpu.VMEM((4, list_cap, block_size, block_size), jnp.bfloat16),
             pltpu.VMEM((2, list_cap, block_size, block_size), jnp.bfloat16),
             pltpu.SemaphoreType.DMA((9,)),
+            pltpu.SemaphoreType.DMA((4,)),
         ],
         compiler_params=pltpu.CompilerParams(vmem_limit_bytes=60 * 1024 * 1024),
     )(*scalars, *lists)

time: 208 us -> 208 us (level)
  no operation moved by 1% of the time
where the time goes in v18:
time: 208 us; the launch traced here: 206 us
  waiting for transfers between devices  151 us (73%)
  Pallas kernels  18.5 us (9%)
  starting transfers between devices  13.7 us (7%)
  between operations  13.5 us (6%)
  local copies, waits for them, and re-layouts  3.99 us (2%)
  other arithmetic  3.31 us (2%)
    reduce_scatter x1, waiting for transfers between devices, on_device(): owned = lax.psum_scatter(totals, 'layer', scatter_dimension=0, tiled=True)  115 us
    ppermute x9, waiting for transfers between devices, shifted(): return lax.ppermute(value, axis, pairs)  36 us
    pallas_call x1, Pallas kernels, pair_products(): pl.pallas_call(pair_kernel, out_shape=jax.ShapeDtypeStruct((targets, bloc...  18.5 us
    ppermute x9, starting transfers between devices, shifted(): return lax.ppermute(value, axis, pairs)  13.6 us
  transfers between devices with their start and end apart: 11, of which 6 were waited for; matrix products, arithmetic and copies ran while one was open for 3% of the time, Pallas kernels for 0%

profile of v18, /device:TPU:26, one launch (start us, length us, event | category | flops | bytes accessed | tf_op | source)
XLA Modules:
  0.0 206.3 jit_solution(9324913006149576181)
XLA Ops:
  6.5 0.0 copy-start
  6.5 0.0 all-gather.4.cloned.1.call-start
  6.5 0.7 all-gather.4.cloned.1.call-update
  7.3 0.0 copy-start.10
  7.3 0.0 copy-start.9
  7.3 0.0 copy-start.1
  7.3 0.0 copy-start.8
  7.3 0.0 copy-start.11
  7.3 0.0 reduce-scatter.2.cloned.1.call-start
  7.4 0.6 copy-done.2
  8.0 1.0 slice_bitcast_fusion
  9.0 0.5 collective-permute-start.1
  9.5 1.5 collective-permute-start
  11.0 3.3 %collective-permute-start.4 = (s32[48]{0:T(128)S(1)}, s32[48]{0:T(128)S(1)}, u32[]{:S(2)}, u32[]{:S(2)}) collective-permute-start(s32[48]{0:T(128)S(1)} %bitcast.30), channel_id=1, source_target_pairs={{0,64},{32,96},{64,0},{96,32},{1,65},{33,97},{65,1},{97,33},{2,66}... | collective-permute-start | bytes 584 | tf_op jit(solution)/shard_map/ppermute | solution.py:101
  14.3 0.2 collective-permute-start.3
  14.6 1.8 collective-permute-start.2
  16.4 0.1 fusion.1
  16.5 0.0 copy-done.9
  16.5 0.6 pad_add_fusion.1.pick
  17.1 12.3 %collective-permute-done.4 = s32[48]{0:T(128)S(1)} collective-permute-done((s32[48]{0:T(128)S(1)}, s32[48]{0:T(128)S(1)}, u32[]{:S(2)}, u32[]{:S(2)}) %collective-permute-start.4) | collective-permute-done | bytes 224 | tf_op jit(solution)/shard_map/ppermute | solution.py:101
  29.4 0.0 collective-permute-done.3
  29.4 0.2 collective-permute-done.2
  29.6 0.0 collective-permute-done.1.above_high
  29.6 0.0 collective-permute-done.below_low
  29.6 1.5 collective-permute-start.5
  31.1 1.6 collective-permute-start.6
  32.7 0.4 collective-permute-start.7
  33.1 2.8 %collective-permute-start.8 = (bf16[24,128,128]{2,1,0:T(8,128)(2,1)S(1)}, bf16[24,128,128]{2,1,0:T(8,128)(2,1)}, u32[]{:S(2)}, u32[]{:S(2)}) collective-permute-start(bf16[24,128,128]{2,1,0:T(8,128)(2,1)S(1)} %collective-permute-done.1.above_high), channel_id=1, source_target_pairs={{0,96},{32,0},{64,32},{96,64},{1,97},{33,1},{65,33},{97,65},{2,98}... | collective-permute-start | bytes 2359304 | tf_op jit(solution)/shard_map/ppermute | solution.py:101
  35.9 0.1 compare_and_fusion.1
  36.0 0.6 gather_fusion
  36.6 0.6 gather_fusion.3
  37.2 0.6 gather_fusion.2
  37.8 1.8 all-gather
  39.5 0.6 gather_fusion.1
  40.1 0.6 broadcast_select_fusion.3.counts
  40.7 0.7 broadcast_select_fusion.2.right_ids
  41.3 0.7 broadcast_select_fusion
  42.0 0.6 pad_add_fusion.left_ids
  42.6 8.7 %collective-permute-done.5.below_high = bf16[24,128,128]{2,1,0:T(8,128)(2,1)S(1)} collective-permute-done((bf16[24,128,128]{2,1,0:T(8,128)(2,1)}, bf16[24,128,128]{2,1,0:T(8,128)(2,1)S(1)}, u32[]{:S(2)}, u32[]{:S(2)}) %collective-permute-start.5) | collective-permute-done | bytes 786464 | tf_op jit(solution)/shard_map/ppermute | solution.py:101
  51.3 0.5 collective-permute-done.6.above_low
  51.8 14.3 %collective-permute-done.7.far_low = bf16[24,128,128]{2,1,0:T(8,128)(2,1)} collective-permute-done((bf16[24,128,128]{2,1,0:T(8,128)(2,1)S(1)}, bf16[24,128,128]{2,1,0:T(8,128)(2,1)}, u32[]{:S(2)}, u32[]{:S(2)}) %collective-permute-start.7) | collective-permute-done | bytes 786464 | tf_op jit(solution)/shard_map/ppermute | solution.py:101
  66.1 0.0 collective-permute-done.8.far_high
  66.1 0.0 copy-done.4
  66.1 0.0 copy-done.5
  66.1 0.0 copy-done.6
  66.2 18.5 %shard_map.82 = f32[256,128,128]{2,1,0:T(8,128)} custom-call(s32[4,192]{1,0:T(4,128)} %get-tuple-element.25.slots_left, s32[4,192]{1,0:T(4,128)} %get-tuple-element.24.slots_right, s32[4]{0:T(128)} %broadcast_select_fusion.3.counts, s32[4,48]{1,0:T(4,128)} %pad_add_fusion.left_ids, s32[2,48]{1,0:T(2,128)} %broadcast_select_fusion.2.right_ids, ...), custom_call_target="tpu_custom_call" | custom-call | tf_op jit(solution)/shard_map/pallas_call | solution.py:82
  84.7 0.0 reduce-scatter.2.cloned.1.call-update
  84.7 114.8 %reduce-scatter.2.cloned.1.call-done = f32[16,128,128]{2,1,0:T(8,128)} async-done(((f32[256,128,128]{2,1,0:T(8,128)}), f32[16,128,128]{2,1,0:T(8,128)}) %reduce-scatter.2.cloned.1.call-update) | async-done | bytes 1048592 | tf_op jit(solution)/shard_map/reduce_scatter | solution.py:146
  (17 shorter events, 0.1 us)
Async XLA Ops:
  6.5 30.1 %copy-start = (s32[1,1,1,4,192]{4,3,2,1,0:T(4,128)S(1)}, s32[1,1,1,4,192]{4,3,2,1,0:T(4,128)}, u32[]{:S(2)}) copy-start(s32[1,1,1,4,192]{4,3,2,1,0:T(4,128)} %param.15) | copy-start | bytes 9220
  6.5 1.4 copy-start.2
  6.5 59.6 %all-gather.4.cloned.1.call-start = ((), (), s32[]{:S(2)}) async-start(), calls=%async_computation.2 | async-start | bytes 4718592 | tf_op jit(solution)/shard_map/all_gather | solution.py:124
  7.3 3.8 %copy-start.10 = (s32[1,1,1,48]{3,2,1,0:T(1,128)S(1)}, s32[1,1,1,48]{3,2,1,0:T(1,128)}, u32[]{:S(2)}) copy-start(s32[1,1,1,48]{3,2,1,0:T(1,128)} %param.11) | copy-start | bytes 580
  7.3 9.2 %copy-start.9 = (s32[4]{0:T(128)S(1)}, s32[4]{0:T(128)}, u32[]{:S(2)}) copy-start(s32[4]{0:T(128)} %constant.67.clone) | copy-start | bytes 52
  7.3 28.7 %copy-start.1 = (s32[1,1,1,4]{3,2,1,0:T(1,128)S(1)}, s32[1,1,1,4]{3,2,1,0:T(1,128)}, u32[]{:S(2)}) copy-start(s32[1,1,1,4]{3,2,1,0:T(1,128)} %param.16) | copy-start | bytes 52
  7.3 29.9 %copy-start.8 = (s32[1,1,1,4,192]{4,3,2,1,0:T(4,128)S(1)}, s32[1,1,1,4,192]{4,3,2,1,0:T(4,128)}, u32[]{:S(2)}) copy-start(s32[1,1,1,4,192]{4,3,2,1,0:T(4,128)} %param.14) | copy-start | bytes 9220
  7.3 30.5 %copy-start.11 = (s32[1,1,1,48]{3,2,1,0:T(1,128)S(1)}, s32[1,1,1,48]{3,2,1,0:T(1,128)}, u32[]{:S(2)}) copy-start(s32[1,1,1,48]{3,2,1,0:T(1,128)} %param.13) | copy-start | bytes 580
  7.3 192.2 %reduce-scatter.2.cloned.1.call-start = ((), (), s32[]{:S(2)}) async-start(), calls=%async_computation.1 | async-start | bytes 17825792 | tf_op jit(solution)/shard_map/reduce_scatter | solution.py:146
  9.0 20.6 %copy-start.7 = (bf16[24,128,128]{2,1,0:T(8,128)(2,1)}, bf16[24,128,128]{2,1,0:T(8,128)(2,1)S(1)}, u32[]{:S(2)}) copy-start(bf16[24,128,128]{2,1,0:T(8,128)(2,1)S(1)} %get-tuple-element.18) | copy-start | bytes 2359300
  9.0 20.6 %collective-permute-start.1 = (bf16[24,128,128]{2,1,0:T(8,128)(2,1)}, bf16[24,128,128]{2,1,0:T(8,128)(2,1)S(1)}, u32[]{:S(2)}, u32[]{:S(2)}) collective-permute-start(bf16[24,128,128]{2,1,0:T(8,128)(2,1)} %get-tuple-element.17), channel_id=1, source_target_pairs={{0,96},{32,0},{64,32},{96,64},{1,97},{33,1},{65,33},{97,65},{2,98}... | collective-permute-start | bytes 2359304 | tf_op jit(solution)/shard_map/ppermute | solution.py:101
  9.5 20.1 %collective-permute-start = (bf16[24,128,128]{2,1,0:T(8,128)(2,1)S(1)}, bf16[24,128,128]{2,1,0:T(8,128)(2,1)S(1)}, u32[]{:S(2)}, u32[]{:S(2)}) collective-permute-start(bf16[24,128,128]{2,1,0:T(8,128)(2,1)S(1)} %get-tuple-element.18), channel_id=1, source_target_pairs={{0,32},{32,64},{64,96},{96,0},{1,33},{33,65},{65,97},{97,1},{2,34}... | collective-permute-start | bytes 2359304 | tf_op jit(solution)/shard_map/ppermute | solution.py:101
  11.0 18.4 %collective-permute-start.4 = (s32[48]{0:T(128)S(1)}, s32[48]{0:T(128)S(1)}, u32[]{:S(2)}, u32[]{:S(2)}) collective-permute-start(s32[48]{0:T(128)S(1)} %bitcast.30), channel_id=1, source_target_pairs={{0,64},{32,96},{64,0},{96,32},{1,65},{33,97},{65,1},{97,33},{2,66}... | collective-permute-start | bytes 584 | tf_op jit(solution)/shard_map/ppermute | solution.py:101
  14.3 15.0 %collective-permute-start.3 = (s32[48]{0:T(128)S(1)}, s32[48]{0:T(128)S(1)}, u32[]{:S(2)}, u32[]{:S(2)}) collective-permute-start(s32[48]{0:T(128)S(1)} %bitcast.31), channel_id=1, source_target_pairs={{0,96},{32,0},{64,32},{96,64},{1,97},{33,1},{65,33},{97,65},{2,98}... | collective-permute-start | bytes 584 | tf_op jit(solution)/shard_map/ppermute | solution.py:101
  14.6 15.0 %collective-permute-start.2 = (s32[48]{0:T(128)S(1)}, s32[48]{0:T(128)S(1)}, u32[]{:S(2)}, u32[]{:S(2)}) collective-permute-start(s32[48]{0:T(128)S(1)} %bitcast.32), channel_id=1, source_target_pairs={{0,32},{32,64},{64,96},{96,0},{1,33},{33,65},{65,97},{97,1},{2,34}... | collective-permute-start | bytes 584 | tf_op jit(solution)/shard_map/ppermute | solution.py:101
  29.6 36.5 %copy-start.3 = (bf16[24,128,128]{2,1,0:T(8,128)(2,1)}, bf16[24,128,128]{2,1,0:T(8,128)(2,1)S(1)}, u32[]{:S(2)}) copy-start(bf16[24,128,128]{2,1,0:T(8,128)(2,1)S(1)} %collective-permute-done.1.above_high) | copy-start | bytes 2359300
  29.6 36.5 %copy-start.4 = (bf16[24,128,128]{2,1,0:T(8,128)(2,1)}, bf16[24,128,128]{2,1,0:T(8,128)(2,1)S(1)}, u32[]{:S(2)}) copy-start(bf16[24,128,128]{2,1,0:T(8,128)(2,1)S(1)} %collective-permute-done.below_low) | copy-start | bytes 2359300
  29.6 21.7 %collective-permute-start.5 = (bf16[24,128,128]{2,1,0:T(8,128)(2,1)}, bf16[24,128,128]{2,1,0:T(8,128)(2,1)S(1)}, u32[]{:S(2)}, u32[]{:S(2)}) collective-permute-start(bf16[24,128,128]{2,1,0:T(8,128)(2,1)} %get-tuple-element.17), channel_id=1, source_target_pairs={{0,32},{32,64},{64,96},{96,0},{1,33},{33,65},{65,97},{97,1},{2,34}... | collective-permute-start | bytes 2359304 | tf_op jit(solution)/shard_map/ppermute | solution.py:101
  31.1 20.7 %collective-permute-start.6 = (bf16[24,128,128]{2,1,0:T(8,128)(2,1)}, bf16[24,128,128]{2,1,0:T(8,128)(2,1)S(1)}, u32[]{:S(2)}, u32[]{:S(2)}) collective-permute-start(bf16[24,128,128]{2,1,0:T(8,128)(2,1)} %copy-done.7), channel_id=1, source_target_pairs={{0,96},{32,0},{64,32},{96,64},{1,97},{33,1},{65,33},{97,65},{2,98}... | collective-permute-start | bytes 2359304 | tf_op jit(solution)/shard_map/ppermute | solution.py:101
  32.7 33.4 %collective-permute-start.7 = (bf16[24,128,128]{2,1,0:T(8,128)(2,1)S(1)}, bf16[24,128,128]{2,1,0:T(8,128)(2,1)}, u32[]{:S(2)}, u32[]{:S(2)}) collective-permute-start(bf16[24,128,128]{2,1,0:T(8,128)(2,1)S(1)} %collective-permute-done.below_low), channel_id=1, source_target_pairs={{0,32},{32,64},{64,96},{96,0},{1,33},{33,65},{65,97},{97,1},{2,34}... | collective-permute-start | bytes 2359304 | tf_op jit(solution)/shard_map/ppermute | solution.py:101
  33.1 33.0 %collective-permute-start.8 = (bf16[24,128,128]{2,1,0:T(8,128)(2,1)S(1)}, bf16[24,128,128]{2,1,0:T(8,128)(2,1)}, u32[]{:S(2)}, u32[]{:S(2)}) collective-permute-start(bf16[24,128,128]{2,1,0:T(8,128)(2,1)S(1)} %collective-permute-done.1.above_high), channel_id=1, source_target_pairs={{0,96},{32,0},{64,32},{96,64},{1,97},{33,1},{65,33},{97,65},{2,98}... | collective-permute-start | bytes 2359304 | tf_op jit(solution)/shard_map/ppermute | solution.py:101
  51.3 14.8 %copy-start.5 = (bf16[24,128,128]{2,1,0:T(8,128)(2,1)}, bf16[24,128,128]{2,1,0:T(8,128)(2,1)S(1)}, u32[]{:S(2)}) copy-start(bf16[24,128,128]{2,1,0:T(8,128)(2,1)S(1)} %collective-permute-done.5.below_high) | copy-start | bytes 2359300
  51.8 14.3 %copy-start.6 = (bf16[24,128,128]{2,1,0:T(8,128)(2,1)}, bf16[24,128,128]{2,1,0:T(8,128)(2,1)S(1)}, u32[]{:S(2)}) copy-start(bf16[24,128,128]{2,1,0:T(8,128)(2,1)S(1)} %collective-permute-done.6.above_low) | copy-start | bytes 2359300
Sparse Core Ops, SparseCore 0:
  9.0 16.9 all-gather.3
  84.8 114.6 reduce-scatter.1

commit v19 on v11

--- a/solution.py
+++ b/solution.py
@@ -7,7 +7,7 @@
 
 SLAB = 128
 ROWS_GROUP = 8
-UNROLL = 16
+UNROLL = 20
 
 
 def pair_kernel(slots_left, slots_right, counts, left_ids, right_ids, pick,

time: 208 us -> 209 us (level)
  no operation moved by 1% of the time
where the time goes in v19:
time: 209 us; the launch traced here: 208 us
  waiting for transfers between devices  153 us (73%)
  Pallas kernels  19.1 us (9%)
  starting transfers between devices  13.7 us (7%)
  between operations  13.5 us (6%)
  local copies, waits for them, and re-layouts  3.99 us (2%)
  other arithmetic  3.31 us (2%)
    reduce_scatter x1, waiting for transfers between devices, on_device(): owned = lax.psum_scatter(totals, 'layer', scatter_dimension=0, tiled=True)  116 us
    ppermute x9, waiting for transfers between devices, shifted(): return lax.ppermute(value, axis, pairs)  36 us
    pallas_call x1, Pallas kernels, pair_products(): pl.pallas_call(pair_kernel, out_shape=jax.ShapeDtypeStruct((targets, bloc...  19.1 us
    ppermute x9, starting transfers between devices, shifted(): return lax.ppermute(value, axis, pairs)  13.6 us
  transfers between devices with their start and end apart: 11, of which 6 were waited for; matrix products, arithmetic and copies ran while one was open for 3% of the time, Pallas kernels for 0%

profile of v19, /device:TPU:26, one launch (start us, length us, event | category | flops | bytes accessed | tf_op | source)
XLA Modules:
  0.0 208.3 jit_solution(13987936010217340773)
XLA Ops:
  6.5 0.0 copy-start
  6.5 0.0 all-gather.4.cloned.1.call-start
  6.5 0.7 all-gather.4.cloned.1.call-update
  7.3 0.0 copy-start.10
  7.3 0.0 copy-start.9
  7.3 0.0 copy-start.1
  7.3 0.0 copy-start.8
  7.3 0.0 copy-start.11
  7.3 0.0 reduce-scatter.2.cloned.1.call-start
  7.4 0.6 copy-done.2
  8.0 1.0 slice_bitcast_fusion
  9.0 0.5 collective-permute-start.1
  9.5 1.5 collective-permute-start
  11.0 0.0 copy-done.10
  11.0 3.3 %collective-permute-start.4 = (s32[48]{0:T(128)S(1)}, s32[48]{0:T(128)S(1)}, u32[]{:S(2)}, u32[]{:S(2)}) collective-permute-start(s32[48]{0:T(128)S(1)} %bitcast.30), channel_id=1, source_target_pairs={{0,64},{32,96},{64,0},{96,32},{1,65},{33,97},{65,1},{97,33},{2,66}... | collective-permute-start | bytes 584 | tf_op jit(solution)/shard_map/ppermute | solution.py:90
  14.3 0.2 collective-permute-start.3
  14.6 1.8 collective-permute-start.2
  16.4 0.1 fusion.1
  16.5 0.0 copy-done.9
  16.5 0.6 pad_add_fusion.1.pick
  17.1 12.3 %collective-permute-done.4 = s32[48]{0:T(128)S(1)} collective-permute-done((s32[48]{0:T(128)S(1)}, s32[48]{0:T(128)S(1)}, u32[]{:S(2)}, u32[]{:S(2)}) %collective-permute-start.4) | collective-permute-done | bytes 224 | tf_op jit(solution)/shard_map/ppermute | solution.py:90
  29.4 0.0 collective-permute-done.3
  29.4 0.2 collective-permute-done.2
  29.6 0.0 collective-permute-done.1.above_high
  29.6 0.0 copy-done.7
  29.6 0.0 collective-permute-done.below_low
  29.6 0.0 copy-start.4
  29.6 1.5 collective-permute-start.5
  31.1 1.6 collective-permute-start.6
  32.7 0.4 collective-permute-start.7
  33.1 2.8 %collective-permute-start.8 = (bf16[24,128,128]{2,1,0:T(8,128)(2,1)S(1)}, bf16[24,128,128]{2,1,0:T(8,128)(2,1)}, u32[]{:S(2)}, u32[]{:S(2)}) collective-permute-start(bf16[24,128,128]{2,1,0:T(8,128)(2,1)S(1)} %collective-permute-done.1.above_high), channel_id=1, source_target_pairs={{0,96},{32,0},{64,32},{96,64},{1,97},{33,1},{65,33},{97,65},{2,98}... | collective-permute-start | bytes 2359304 | tf_op jit(solution)/shard_map/ppermute | solution.py:90
  35.9 0.1 compare_and_fusion.1
  36.0 0.6 gather_fusion
  36.6 0.6 gather_fusion.3
  37.2 0.6 gather_fusion.2
  37.8 1.8 all-gather
  39.5 0.6 gather_fusion.1
  40.1 0.6 broadcast_select_fusion.3.counts
  40.7 0.7 broadcast_select_fusion.2.right_ids
  41.3 0.7 broadcast_select_fusion
  42.0 0.6 pad_add_fusion.left_ids
  42.6 8.7 %collective-permute-done.5.below_high = bf16[24,128,128]{2,1,0:T(8,128)(2,1)S(1)} collective-permute-done((bf16[24,128,128]{2,1,0:T(8,128)(2,1)}, bf16[24,128,128]{2,1,0:T(8,128)(2,1)S(1)}, u32[]{:S(2)}, u32[]{:S(2)}) %collective-permute-start.5) | collective-permute-done | bytes 786464 | tf_op jit(solution)/shard_map/ppermute | solution.py:90
  51.3 0.5 collective-permute-done.6.above_low
  51.8 14.3 %collective-permute-done.7.far_low = bf16[24,128,128]{2,1,0:T(8,128)(2,1)} collective-permute-done((bf16[24,128,128]{2,1,0:T(8,128)(2,1)S(1)}, bf16[24,128,128]{2,1,0:T(8,128)(2,1)}, u32[]{:S(2)}, u32[]{:S(2)}) %collective-permute-start.7) | collective-permute-done | bytes 786464 | tf_op jit(solution)/shard_map/ppermute | solution.py:90
  66.1 0.0 collective-permute-done.8.far_high
  66.2 19.1 %shard_map.82 = f32[256,128,128]{2,1,0:T(8,128)} custom-call(s32[4,192]{1,0:T(4,128)} %get-tuple-element.25.slots_left, s32[4,192]{1,0:T(4,128)} %get-tuple-element.24.slots_right, s32[4]{0:T(128)} %broadcast_select_fusion.3.counts, s32[4,48]{1,0:T(4,128)} %pad_add_fusion.left_ids, s32[2,48]{1,0:T(2,128)} %broadcast_select_fusion.2.right_ids, ...), custom_call_target="tpu_custom_call" | custom-call | tf_op jit(solution)/shard_map/pallas_call | solution.py:73
  85.3 0.0 reduce-scatter.2.cloned.1.call-update
  85.3 116.2 %reduce-scatter.2.cloned.1.call-done = f32[16,128,128]{2,1,0:T(8,128)} async-done(((f32[256,128,128]{2,1,0:T(8,128)}), f32[16,128,128]{2,1,0:T(8,128)}) %reduce-scatter.2.cloned.1.call-update) | async-done | bytes 1048592 | tf_op jit(solution)/shard_map/reduce_scatter | solution.py:135
  (17 shorter events, 0.1 us)
Async XLA Ops:
  6.5 30.1 %copy-start = (s32[1,1,1,4,192]{4,3,2,1,0:T(4,128)S(1)}, s32[1,1,1,4,192]{4,3,2,1,0:T(4,128)}, u32[]{:S(2)}) copy-start(s32[1,1,1,4,192]{4,3,2,1,0:T(4,128)} %param.15) | copy-start | bytes 9220
  6.5 1.4 copy-start.2
  6.5 59.6 %all-gather.4.cloned.1.call-start = ((), (), s32[]{:S(2)}) async-start(), calls=%async_computation.2 | async-start | bytes 4718592 | tf_op jit(solution)/shard_map/all_gather | solution.py:113
  7.3 3.8 %copy-start.10 = (s32[1,1,1,48]{3,2,1,0:T(1,128)S(1)}, s32[1,1,1,48]{3,2,1,0:T(1,128)}, u32[]{:S(2)}) copy-start(s32[1,1,1,48]{3,2,1,0:T(1,128)} %param.11) | copy-start | bytes 580
  7.3 9.2 %copy-start.9 = (s32[4]{0:T(128)S(1)}, s32[4]{0:T(128)}, u32[]{:S(2)}) copy-start(s32[4]{0:T(128)} %constant.67.clone) | copy-start | bytes 52
  7.3 28.7 %copy-start.1 = (s32[1,1,1,4]{3,2,1,0:T(1,128)S(1)}, s32[1,1,1,4]{3,2,1,0:T(1,128)}, u32[]{:S(2)}) copy-start(s32[1,1,1,4]{3,2,1,0:T(1,128)} %param.16) | copy-start | bytes 52
  7.3 29.9 %copy-start.8 = (s32[1,1,1,4,192]{4,3,2,1,0:T(4,128)S(1)}, s32[1,1,1,4,192]{4,3,2,1,0:T(4,128)}, u32[]{:S(2)}) copy-start(s32[1,1,1,4,192]{4,3,2,1,0:T(4,128)} %param.14) | copy-start | bytes 9220
  7.3 30.5 %copy-start.11 = (s32[1,1,1,48]{3,2,1,0:T(1,128)S(1)}, s32[1,1,1,48]{3,2,1,0:T(1,128)}, u32[]{:S(2)}) copy-start(s32[1,1,1,48]{3,2,1,0:T(1,128)} %param.13) | copy-start | bytes 580
  7.3 194.2 %reduce-scatter.2.cloned.1.call-start = ((), (), s32[]{:S(2)}) async-start(), calls=%async_computation.1 | async-start | bytes 17825792 | tf_op jit(solution)/shard_map/reduce_scatter | solution.py:135
  9.0 20.6 %copy-start.7 = (bf16[24,128,128]{2,1,0:T(8,128)(2,1)}, bf16[24,128,128]{2,1,0:T(8,128)(2,1)S(1)}, u32[]{:S(2)}) copy-start(bf16[24,128,128]{2,1,0:T(8,128)(2,1)S(1)} %get-tuple-element.18) | copy-start | bytes 2359300
  9.0 20.6 %collective-permute-start.1 = (bf16[24,128,128]{2,1,0:T(8,128)(2,1)}, bf16[24,128,128]{2,1,0:T(8,128)(2,1)S(1)}, u32[]{:S(2)}, u32[]{:S(2)}) collective-permute-start(bf16[24,128,128]{2,1,0:T(8,128)(2,1)} %get-tuple-element.17), channel_id=1, source_target_pairs={{0,96},{32,0},{64,32},{96,64},{1,97},{33,1},{65,33},{97,65},{2,98}... | collective-permute-start | bytes 2359304 | tf_op jit(solution)/shard_map/ppermute | solution.py:90
  9.5 20.1 %collective-permute-start = (bf16[24,128,128]{2,1,0:T(8,128)(2,1)S(1)}, bf16[24,128,128]{2,1,0:T(8,128)(2,1)S(1)}, u32[]{:S(2)}, u32[]{:S(2)}) collective-permute-start(bf16[24,128,128]{2,1,0:T(8,128)(2,1)S(1)} %get-tuple-element.18), channel_id=1, source_target_pairs={{0,32},{32,64},{64,96},{96,0},{1,33},{33,65},{65,97},{97,1},{2,34}... | collective-permute-start | bytes 2359304 | tf_op jit(solution)/shard_map/ppermute | solution.py:90
  11.0 18.4 %collective-permute-start.4 = (s32[48]{0:T(128)S(1)}, s32[48]{0:T(128)S(1)}, u32[]{:S(2)}, u32[]{:S(2)}) collective-permute-start(s32[48]{0:T(128)S(1)} %bitcast.30), channel_id=1, source_target_pairs={{0,64},{32,96},{64,0},{96,32},{1,65},{33,97},{65,1},{97,33},{2,66}... | collective-permute-start | bytes 584 | tf_op jit(solution)/shard_map/ppermute | solution.py:90
  14.3 15.0 %collective-permute-start.3 = (s32[48]{0:T(128)S(1)}, s32[48]{0:T(128)S(1)}, u32[]{:S(2)}, u32[]{:S(2)}) collective-permute-start(s32[48]{0:T(128)S(1)} %bitcast.31), channel_id=1, source_target_pairs={{0,96},{32,0},{64,32},{96,64},{1,97},{33,1},{65,33},{97,65},{2,98}... | collective-permute-start | bytes 584 | tf_op jit(solution)/shard_map/ppermute | solution.py:90
  14.6 15.0 %collective-permute-start.2 = (s32[48]{0:T(128)S(1)}, s32[48]{0:T(128)S(1)}, u32[]{:S(2)}, u32[]{:S(2)}) collective-permute-start(s32[48]{0:T(128)S(1)} %bitcast.32), channel_id=1, source_target_pairs={{0,32},{32,64},{64,96},{96,0},{1,33},{33,65},{65,97},{97,1},{2,34}... | collective-permute-start | bytes 584 | tf_op jit(solution)/shard_map/ppermute | solution.py:90
  29.6 36.5 %copy-start.3 = (bf16[24,128,128]{2,1,0:T(8,128)(2,1)}, bf16[24,128,128]{2,1,0:T(8,128)(2,1)S(1)}, u32[]{:S(2)}) copy-start(bf16[24,128,128]{2,1,0:T(8,128)(2,1)S(1)} %collective-permute-done.1.above_high) | copy-start | bytes 2359300
  29.6 36.5 %copy-start.4 = (bf16[24,128,128]{2,1,0:T(8,128)(2,1)}, bf16[24,128,128]{2,1,0:T(8,128)(2,1)S(1)}, u32[]{:S(2)}) copy-start(bf16[24,128,128]{2,1,0:T(8,128)(2,1)S(1)} %collective-permute-done.below_low) | copy-start | bytes 2359300
  29.6 21.7 %collective-permute-start.5 = (bf16[24,128,128]{2,1,0:T(8,128)(2,1)}, bf16[24,128,128]{2,1,0:T(8,128)(2,1)S(1)}, u32[]{:S(2)}, u32[]{:S(2)}) collective-permute-start(bf16[24,128,128]{2,1,0:T(8,128)(2,1)} %get-tuple-element.17), channel_id=1, source_target_pairs={{0,32},{32,64},{64,96},{96,0},{1,33},{33,65},{65,97},{97,1},{2,34}... | collective-permute-start | bytes 2359304 | tf_op jit(solution)/shard_map/ppermute | solution.py:90
  31.1 20.7 %collective-permute-start.6 = (bf16[24,128,128]{2,1,0:T(8,128)(2,1)}, bf16[24,128,128]{2,1,0:T(8,128)(2,1)S(1)}, u32[]{:S(2)}, u32[]{:S(2)}) collective-permute-start(bf16[24,128,128]{2,1,0:T(8,128)(2,1)} %copy-done.7), channel_id=1, source_target_pairs={{0,96},{32,0},{64,32},{96,64},{1,97},{33,1},{65,33},{97,65},{2,98}... | collective-permute-start | bytes 2359304 | tf_op jit(solution)/shard_map/ppermute | solution.py:90
  32.7 33.4 %collective-permute-start.7 = (bf16[24,128,128]{2,1,0:T(8,128)(2,1)S(1)}, bf16[24,128,128]{2,1,0:T(8,128)(2,1)}, u32[]{:S(2)}, u32[]{:S(2)}) collective-permute-start(bf16[24,128,128]{2,1,0:T(8,128)(2,1)S(1)} %collective-permute-done.below_low), channel_id=1, source_target_pairs={{0,32},{32,64},{64,96},{96,0},{1,33},{33,65},{65,97},{97,1},{2,34}... | collective-permute-start | bytes 2359304 | tf_op jit(solution)/shard_map/ppermute | solution.py:90
  33.1 33.0 %collective-permute-start.8 = (bf16[24,128,128]{2,1,0:T(8,128)(2,1)S(1)}, bf16[24,128,128]{2,1,0:T(8,128)(2,1)}, u32[]{:S(2)}, u32[]{:S(2)}) collective-permute-start(bf16[24,128,128]{2,1,0:T(8,128)(2,1)S(1)} %collective-permute-done.1.above_high), channel_id=1, source_target_pairs={{0,96},{32,0},{64,32},{96,64},{1,97},{33,1},{65,33},{97,65},{2,98}... | collective-permute-start | bytes 2359304 | tf_op jit(solution)/shard_map/ppermute | solution.py:90
  51.3 14.8 %copy-start.5 = (bf16[24,128,128]{2,1,0:T(8,128)(2,1)}, bf16[24,128,128]{2,1,0:T(8,128)(2,1)S(1)}, u32[]{:S(2)}) copy-start(bf16[24,128,128]{2,1,0:T(8,128)(2,1)S(1)} %collective-permute-done.5.below_high) | copy-start | bytes 2359300
  51.8 14.3 %copy-start.6 = (bf16[24,128,128]{2,1,0:T(8,128)(2,1)}, bf16[24,128,128]{2,1,0:T(8,128)(2,1)S(1)}, u32[]{:S(2)}) copy-start(bf16[24,128,128]{2,1,0:T(8,128)(2,1)S(1)} %collective-permute-done.6.above_low) | copy-start | bytes 2359300
Sparse Core Ops, SparseCore 0:
  9.0 16.9 all-gather.3
  85.4 116.0 reduce-scatter.1

commit v20 on v11

--- a/solution.py
+++ b/solution.py
@@ -48,21 +48,17 @@
             term = jnp.dot(left_lists[u, i], right_lists[v, k], preferred_element_type=jnp.float32)
             return t, term
 
-        def add_group(g, carry, one_term=one_term):
-            made = [one_term(g * UNROLL + q) for q in range(UNROLL)]
-            for t, term in made:
-                totals[t] = totals[t] + term
+        count = counts[u]
+
+        def add_group(g, carry, one_term=one_term, count=count):
+            made = [(g * UNROLL + q, *one_term(g * UNROLL + q)) for q in range(UNROLL)]
+            for j, t, term in made:
+                @pl.when(j < count)
+                def _(t=t, term=term):
+                    totals[t] = totals[t] + term
             return carry
 
-        def add_single(j, carry, one_term=one_term):
-            t, term = one_term(j)
-            totals[t] = totals[t] + term
-            return carry
-
-        count = counts[u]
-        groups = count // UNROLL
-        lax.fori_loop(0, groups, add_group, 0)
-        lax.fori_loop(groups * UNROLL, count, add_single, 0)
+        lax.fori_loop(0, (count + UNROLL - 1) // UNROLL, add_group, 0)
 
 
 def pair_products(scalars, lists, targets):

time: 208 us -> 208 us (level)
  no operation moved by 1% of the time
where the time goes in v20:
time: 208 us; the launch traced here: 206 us
  waiting for transfers between devices  153 us (74%)
  Pallas kernels  17.4 us (8%)
  starting transfers between devices  13.7 us (7%)
  between operations  13.5 us (6%)
  local copies, waits for them, and re-layouts  3.99 us (2%)
  other arithmetic  3.31 us (2%)
    reduce_scatter x1, waiting for transfers between devices, on_device(): owned = lax.psum_scatter(totals, 'layer', scatter_dimension=0, tiled=True)  116 us
    ppermute x9, waiting for transfers between devices, shifted(): return lax.ppermute(value, axis, pairs)  36 us
    pallas_call x1, Pallas kernels, pair_products(): pl.pallas_call(pair_kernel, out_shape=jax.ShapeDtypeStruct((targets, bloc...  17.4 us
    ppermute x9, starting transfers between devices, shifted(): return lax.ppermute(value, axis, pairs)  13.6 us
  transfers between devices with their start and end apart: 11, of which 6 were waited for; matrix products, arithmetic and copies ran while one was open for 3% of the time, Pallas kernels for 0%

profile of v20, /device:TPU:26, one launch (start us, length us, event | category | flops | bytes accessed | tf_op | source)
XLA Modules:
  0.0 206.3 jit_solution(6425568100817812942)
XLA Ops:
  6.5 0.0 copy-start
  6.5 0.0 all-gather.4.cloned.1.call-start
  6.5 0.7 all-gather.4.cloned.1.call-update
  7.3 0.0 copy-start.10
  7.3 0.0 copy-start.9
  7.3 0.0 copy-start.1
  7.3 0.0 copy-start.8
  7.3 0.0 copy-start.11
  7.3 0.0 reduce-scatter.2.cloned.1.call-start
  7.4 0.6 copy-done.2
  8.0 1.0 slice_bitcast_fusion
  9.0 0.5 collective-permute-start.1
  9.5 1.5 collective-permute-start
  11.0 3.3 %collective-permute-start.4 = (s32[48]{0:T(128)S(1)}, s32[48]{0:T(128)S(1)}, u32[]{:S(2)}, u32[]{:S(2)}) collective-permute-start(s32[48]{0:T(128)S(1)} %bitcast.30), channel_id=1, source_target_pairs={{0,64},{32,96},{64,0},{96,32},{1,65},{33,97},{65,1},{97,33},{2,66}... | collective-permute-start | bytes 584 | tf_op jit(solution)/shard_map/ppermute | solution.py:86
  14.3 0.2 collective-permute-start.3
  14.6 1.8 collective-permute-start.2
  16.4 0.1 fusion.1
  16.5 0.0 copy-done.9
  16.5 0.6 pad_add_fusion.1.pick
  17.1 12.3 %collective-permute-done.4 = s32[48]{0:T(128)S(1)} collective-permute-done((s32[48]{0:T(128)S(1)}, s32[48]{0:T(128)S(1)}, u32[]{:S(2)}, u32[]{:S(2)}) %collective-permute-start.4) | collective-permute-done | bytes 224 | tf_op jit(solution)/shard_map/ppermute | solution.py:86
  29.4 0.0 collective-permute-done.3
  29.4 0.2 collective-permute-done.2
  29.6 0.0 collective-permute-done.1.above_high
  29.6 0.0 collective-permute-done.below_low
  29.6 1.5 collective-permute-start.5
  31.1 1.6 collective-permute-start.6
  32.7 0.4 collective-permute-start.7
  33.1 2.8 %collective-permute-start.8 = (bf16[24,128,128]{2,1,0:T(8,128)(2,1)S(1)}, bf16[24,128,128]{2,1,0:T(8,128)(2,1)}, u32[]{:S(2)}, u32[]{:S(2)}) collective-permute-start(bf16[24,128,128]{2,1,0:T(8,128)(2,1)S(1)} %collective-permute-done.1.above_high), channel_id=1, source_target_pairs={{0,96},{32,0},{64,32},{96,64},{1,97},{33,1},{65,33},{97,65},{2,98}... | collective-permute-start | bytes 2359304 | tf_op jit(solution)/shard_map/ppermute | solution.py:86
  35.9 0.1 compare_and_fusion.1
  36.0 0.6 gather_fusion
  36.6 0.6 gather_fusion.3
  37.2 0.6 gather_fusion.2
  37.8 1.8 all-gather
  39.5 0.6 gather_fusion.1
  40.1 0.6 broadcast_select_fusion.3.counts
  40.7 0.7 broadcast_select_fusion.2.right_ids
  41.3 0.7 broadcast_select_fusion
  42.0 0.6 pad_add_fusion.left_ids
  42.6 8.7 %collective-permute-done.5.below_high = bf16[24,128,128]{2,1,0:T(8,128)(2,1)S(1)} collective-permute-done((bf16[24,128,128]{2,1,0:T(8,128)(2,1)}, bf16[24,128,128]{2,1,0:T(8,128)(2,1)S(1)}, u32[]{:S(2)}, u32[]{:S(2)}) %collective-permute-start.5) | collective-permute-done | bytes 786464 | tf_op jit(solution)/shard_map/ppermute | solution.py:86
  51.3 0.5 collective-permute-done.6.above_low
  51.8 14.3 %collective-permute-done.7.far_low = bf16[24,128,128]{2,1,0:T(8,128)(2,1)} collective-permute-done((bf16[24,128,128]{2,1,0:T(8,128)(2,1)S(1)}, bf16[24,128,128]{2,1,0:T(8,128)(2,1)}, u32[]{:S(2)}, u32[]{:S(2)}) %collective-permute-start.7) | collective-permute-done | bytes 786464 | tf_op jit(solution)/shard_map/ppermute | solution.py:86
  66.1 0.0 collective-permute-done.8.far_high
  66.1 0.0 copy-done.4
  66.1 0.0 copy-done.5
  66.1 0.0 copy-done.6
  66.2 17.4 %shard_map.82 = f32[256,128,128]{2,1,0:T(8,128)} custom-call(s32[4,192]{1,0:T(4,128)} %get-tuple-element.25.slots_left, s32[4,192]{1,0:T(4,128)} %get-tuple-element.24.slots_right, s32[4]{0:T(128)} %broadcast_select_fusion.3.counts, s32[4,48]{1,0:T(4,128)} %pad_add_fusion.left_ids, s32[2,48]{1,0:T(2,128)} %broadcast_select_fusion.2.right_ids, ...), custom_call_target="tpu_custom_call" | custom-call | tf_op jit(solution)/shard_map/pallas_call | solution.py:69
  83.6 0.0 reduce-scatter.2.cloned.1.call-update
  83.6 115.8 %reduce-scatter.2.cloned.1.call-done = f32[16,128,128]{2,1,0:T(8,128)} async-done(((f32[256,128,128]{2,1,0:T(8,128)}), f32[16,128,128]{2,1,0:T(8,128)}) %reduce-scatter.2.cloned.1.call-update) | async-done | bytes 1048592 | tf_op jit(solution)/shard_map/reduce_scatter | solution.py:131
  (17 shorter events, 0.1 us)
Async XLA Ops:
  6.5 30.1 %copy-start = (s32[1,1,1,4,192]{4,3,2,1,0:T(4,128)S(1)}, s32[1,1,1,4,192]{4,3,2,1,0:T(4,128)}, u32[]{:S(2)}) copy-start(s32[1,1,1,4,192]{4,3,2,1,0:T(4,128)} %param.15) | copy-start | bytes 9220
  6.5 1.4 copy-start.2
  6.5 59.6 %all-gather.4.cloned.1.call-start = ((), (), s32[]{:S(2)}) async-start(), calls=%async_computation.2 | async-start | bytes 4718592 | tf_op jit(solution)/shard_map/all_gather | solution.py:109
  7.3 3.8 %copy-start.10 = (s32[1,1,1,48]{3,2,1,0:T(1,128)S(1)}, s32[1,1,1,48]{3,2,1,0:T(1,128)}, u32[]{:S(2)}) copy-start(s32[1,1,1,48]{3,2,1,0:T(1,128)} %param.11) | copy-start | bytes 580
  7.3 9.2 %copy-start.9 = (s32[4]{0:T(128)S(1)}, s32[4]{0:T(128)}, u32[]{:S(2)}) copy-start(s32[4]{0:T(128)} %constant.67.clone) | copy-start | bytes 52
  7.3 28.7 %copy-start.1 = (s32[1,1,1,4]{3,2,1,0:T(1,128)S(1)}, s32[1,1,1,4]{3,2,1,0:T(1,128)}, u32[]{:S(2)}) copy-start(s32[1,1,1,4]{3,2,1,0:T(1,128)} %param.16) | copy-start | bytes 52
  7.3 29.9 %copy-start.8 = (s32[1,1,1,4,192]{4,3,2,1,0:T(4,128)S(1)}, s32[1,1,1,4,192]{4,3,2,1,0:T(4,128)}, u32[]{:S(2)}) copy-start(s32[1,1,1,4,192]{4,3,2,1,0:T(4,128)} %param.14) | copy-start | bytes 9220
  7.3 30.5 %copy-start.11 = (s32[1,1,1,48]{3,2,1,0:T(1,128)S(1)}, s32[1,1,1,48]{3,2,1,0:T(1,128)}, u32[]{:S(2)}) copy-start(s32[1,1,1,48]{3,2,1,0:T(1,128)} %param.13) | copy-start | bytes 580
  7.3 192.1 %reduce-scatter.2.cloned.1.call-start = ((), (), s32[]{:S(2)}) async-start(), calls=%async_computation.1 | async-start | bytes 17825792 | tf_op jit(solution)/shard_map/reduce_scatter | solution.py:131
  9.0 20.6 %copy-start.7 = (bf16[24,128,128]{2,1,0:T(8,128)(2,1)}, bf16[24,128,128]{2,1,0:T(8,128)(2,1)S(1)}, u32[]{:S(2)}) copy-start(bf16[24,128,128]{2,1,0:T(8,128)(2,1)S(1)} %get-tuple-element.18) | copy-start | bytes 2359300
  9.0 20.6 %collective-permute-start.1 = (bf16[24,128,128]{2,1,0:T(8,128)(2,1)}, bf16[24,128,128]{2,1,0:T(8,128)(2,1)S(1)}, u32[]{:S(2)}, u32[]{:S(2)}) collective-permute-start(bf16[24,128,128]{2,1,0:T(8,128)(2,1)} %get-tuple-element.17), channel_id=1, source_target_pairs={{0,96},{32,0},{64,32},{96,64},{1,97},{33,1},{65,33},{97,65},{2,98}... | collective-permute-start | bytes 2359304 | tf_op jit(solution)/shard_map/ppermute | solution.py:86
  9.5 20.1 %collective-permute-start = (bf16[24,128,128]{2,1,0:T(8,128)(2,1)S(1)}, bf16[24,128,128]{2,1,0:T(8,128)(2,1)S(1)}, u32[]{:S(2)}, u32[]{:S(2)}) collective-permute-start(bf16[24,128,128]{2,1,0:T(8,128)(2,1)S(1)} %get-tuple-element.18), channel_id=1, source_target_pairs={{0,32},{32,64},{64,96},{96,0},{1,33},{33,65},{65,97},{97,1},{2,34}... | collective-permute-start | bytes 2359304 | tf_op jit(solution)/shard_map/ppermute | solution.py:86
  11.0 18.4 %collective-permute-start.4 = (s32[48]{0:T(128)S(1)}, s32[48]{0:T(128)S(1)}, u32[]{:S(2)}, u32[]{:S(2)}) collective-permute-start(s32[48]{0:T(128)S(1)} %bitcast.30), channel_id=1, source_target_pairs={{0,64},{32,96},{64,0},{96,32},{1,65},{33,97},{65,1},{97,33},{2,66}... | collective-permute-start | bytes 584 | tf_op jit(solution)/shard_map/ppermute | solution.py:86
  14.3 15.0 %collective-permute-start.3 = (s32[48]{0:T(128)S(1)}, s32[48]{0:T(128)S(1)}, u32[]{:S(2)}, u32[]{:S(2)}) collective-permute-start(s32[48]{0:T(128)S(1)} %bitcast.31), channel_id=1, source_target_pairs={{0,96},{32,0},{64,32},{96,64},{1,97},{33,1},{65,33},{97,65},{2,98}... | collective-permute-start | bytes 584 | tf_op jit(solution)/shard_map/ppermute | solution.py:86
  14.6 15.0 %collective-permute-start.2 = (s32[48]{0:T(128)S(1)}, s32[48]{0:T(128)S(1)}, u32[]{:S(2)}, u32[]{:S(2)}) collective-permute-start(s32[48]{0:T(128)S(1)} %bitcast.32), channel_id=1, source_target_pairs={{0,32},{32,64},{64,96},{96,0},{1,33},{33,65},{65,97},{97,1},{2,34}... | collective-permute-start | bytes 584 | tf_op jit(solution)/shard_map/ppermute | solution.py:86
  29.6 36.5 %copy-start.3 = (bf16[24,128,128]{2,1,0:T(8,128)(2,1)}, bf16[24,128,128]{2,1,0:T(8,128)(2,1)S(1)}, u32[]{:S(2)}) copy-start(bf16[24,128,128]{2,1,0:T(8,128)(2,1)S(1)} %collective-permute-done.1.above_high) | copy-start | bytes 2359300
  29.6 36.5 %copy-start.4 = (bf16[24,128,128]{2,1,0:T(8,128)(2,1)}, bf16[24,128,128]{2,1,0:T(8,128)(2,1)S(1)}, u32[]{:S(2)}) copy-start(bf16[24,128,128]{2,1,0:T(8,128)(2,1)S(1)} %collective-permute-done.below_low) | copy-start | bytes 2359300
  29.6 21.7 %collective-permute-start.5 = (bf16[24,128,128]{2,1,0:T(8,128)(2,1)}, bf16[24,128,128]{2,1,0:T(8,128)(2,1)S(1)}, u32[]{:S(2)}, u32[]{:S(2)}) collective-permute-start(bf16[24,128,128]{2,1,0:T(8,128)(2,1)} %get-tuple-element.17), channel_id=1, source_target_pairs={{0,32},{32,64},{64,96},{96,0},{1,33},{33,65},{65,97},{97,1},{2,34}... | collective-permute-start | bytes 2359304 | tf_op jit(solution)/shard_map/ppermute | solution.py:86
  31.1 20.7 %collective-permute-start.6 = (bf16[24,128,128]{2,1,0:T(8,128)(2,1)}, bf16[24,128,128]{2,1,0:T(8,128)(2,1)S(1)}, u32[]{:S(2)}, u32[]{:S(2)}) collective-permute-start(bf16[24,128,128]{2,1,0:T(8,128)(2,1)} %copy-done.7), channel_id=1, source_target_pairs={{0,96},{32,0},{64,32},{96,64},{1,97},{33,1},{65,33},{97,65},{2,98}... | collective-permute-start | bytes 2359304 | tf_op jit(solution)/shard_map/ppermute | solution.py:86
  32.7 33.4 %collective-permute-start.7 = (bf16[24,128,128]{2,1,0:T(8,128)(2,1)S(1)}, bf16[24,128,128]{2,1,0:T(8,128)(2,1)}, u32[]{:S(2)}, u32[]{:S(2)}) collective-permute-start(bf16[24,128,128]{2,1,0:T(8,128)(2,1)S(1)} %collective-permute-done.below_low), channel_id=1, source_target_pairs={{0,32},{32,64},{64,96},{96,0},{1,33},{33,65},{65,97},{97,1},{2,34}... | collective-permute-start | bytes 2359304 | tf_op jit(solution)/shard_map/ppermute | solution.py:86
  33.1 33.0 %collective-permute-start.8 = (bf16[24,128,128]{2,1,0:T(8,128)(2,1)S(1)}, bf16[24,128,128]{2,1,0:T(8,128)(2,1)}, u32[]{:S(2)}, u32[]{:S(2)}) collective-permute-start(bf16[24,128,128]{2,1,0:T(8,128)(2,1)S(1)} %collective-permute-done.1.above_high), channel_id=1, source_target_pairs={{0,96},{32,0},{64,32},{96,64},{1,97},{33,1},{65,33},{97,65},{2,98}... | collective-permute-start | bytes 2359304 | tf_op jit(solution)/shard_map/ppermute | solution.py:86
  51.3 14.8 %copy-start.5 = (bf16[24,128,128]{2,1,0:T(8,128)(2,1)}, bf16[24,128,128]{2,1,0:T(8,128)(2,1)S(1)}, u32[]{:S(2)}) copy-start(bf16[24,128,128]{2,1,0:T(8,128)(2,1)S(1)} %collective-permute-done.5.below_high) | copy-start | bytes 2359300
  51.8 14.3 %copy-start.6 = (bf16[24,128,128]{2,1,0:T(8,128)(2,1)}, bf16[24,128,128]{2,1,0:T(8,128)(2,1)S(1)}, u32[]{:S(2)}) copy-start(bf16[24,128,128]{2,1,0:T(8,128)(2,1)S(1)} %collective-permute-done.6.above_low) | copy-start | bytes 2359300
Sparse Core Ops, SparseCore 0:
  9.0 16.9 all-gather.3
  83.7 115.6 reduce-scatter.1
